TPU v7x, 512 devices: a whole 4x4x16 slice. The times are simulated.
512 devices in a mesh: gx: 16 (over y_hi, x, core), gy: 32 (over z, y_lo).
Axes of the slice: x: 4, y: 4 (y_hi: 2, y_lo: 2; y = y_hi * 2 + y_lo), z: 16, core: 2. Of those that a mesh axis runs over, the one named last changes fastest.
Arguments:
- e_field: float32 [3, 64, 128, 2048], P(None, 'gx', 'gy'), may hold values from -6 to 6
- h_field: float32 [3, 64, 128, 2048], P(None, 'gx', 'gy'), may hold values from -6 to 6
- polarization: float32 [4, 3, 64, 128, 2048], P(None, None, 'gx', 'gy'), may hold values from -3 to 3
- material: int32 [64, 128, 2048], P('gx', 'gy'), may hold values from 0 to 7
- eps_inf: float32 [8], replicated, may hold values from 3 to 12
- conductivity: float32 [8], replicated, may hold values from 0.05 to 1
- pole_strength: float32 [4, 8], replicated, may hold values from 0.1 to 1
- pole_decay: float32 [4, 8], replicated, may hold values from 0.2 to 0.95
- seg_owner: int32 [16, 16384, 1], P('gx', 'gy'), may hold values from 0 to 31; in each aligned block of 512 rows (0 to 511, 512 to 1023, ..., all dimensions but the last counted through in order) at most 32 rows name the same one
- seg_cell: int32 [16, 16384], P('gx', 'gy'), may hold values from 0 to 32767
- current: float32 [16, 16384], P('gx', 'gy'), may hold values from -6 to 6
- voltage: float32 [16, 16384], P('gx', 'gy'), may hold values from -6 to 6
- wire_gain: float32 [16, 16384], P('gx', 'gy'), may hold values from 0.05 to 0.5
- wire_cap: float32 [16, 16384], P('gx', 'gy'), may hold values from 0.05 to 0.5
Outputs:
- e_field_out: float32 [3, 64, 128, 2048], P(None, 'gx', 'gy')
- h_field_out: float32 [3, 64, 128, 2048], P(None, 'gx', 'gy')
- polarization_out: float32 [4, 3, 64, 128, 2048], P(None, None, 'gx', 'gy')
- current_out: float32 [16, 16384], P('gx', 'gy')
- voltage_out: float32 [16, 16384], P('gx', 'gy')
Inputs may be any that keep to these rules, and one draw needn't show every extreme that they name: `seg_owner`: in each aligned block of 512 rows (the segments of one device), no column is named by more than 32 rows, a bound that some block reaches.
All inputs are finite; a program needn't handle non-finite values.
Results may differ from a plain program's by a relative error of at most 0.0001.
Values sent between devices are 32-bit elements; how exact they have to be, the bound alone decides.
No kernel may reach another device: no remote copies, remote signals or barrier semaphores. Data moves between devices by JAX's collectives and lax.ppermute only.
A program may use at most 64 MiB of HBM per device.

v0:
```python
import jax
import jax.numpy as jnp
from jax import lax
from jax.sharding import PartitionSpec as P

STEPS = 2


TIME_STEP = 0.5


def passed_along(value, axis, steps):
    count = lax.axis_size(axis)
    first, last = (max(0, -steps), min(count, count - steps))
    return lax.ppermute(value, axis, [(source, source + steps) for source in range(first, last)])


def next_vertical(field):
    return jnp.concatenate([field[..., 1:], jnp.zeros_like(field[..., :1])], axis=-1)


def prev_vertical(field):
    return jnp.concatenate([jnp.zeros_like(field[..., :1]), field[..., :-1]], axis=-1)


def electric_rims(e_field):
    face_x = passed_along(e_field[1:3, :1], "gx", -1)
    plus_x = jnp.concatenate([e_field[1:3, 1:], face_x], axis=1)
    face_y = passed_along(e_field[0::2, :, :1], "gy", -1)
    plus_y = jnp.concatenate([e_field[0::2, :, 1:], face_y], axis=2)
    return (plus_x, plus_y)


def magnetic_rims(h_field):
    face_x = passed_along(h_field[1:3, -1:], "gx", 1)
    minus_x = jnp.concatenate([face_x, h_field[1:3, :-1]], axis=1)
    face_y = passed_along(h_field[0::2, :, -1:], "gy", 1)
    minus_y = jnp.concatenate([face_y, h_field[0::2, :, :-1]], axis=2)
    return (minus_x, minus_y)


def on_device(
    e_field,
    h_field,
    polarization,
    material,
    eps_inf,
    conductivity,
    pole_strength,
    pole_decay,
    seg_owner,
    seg_cell,
    current,
    voltage,
    wire_gain,
    wire_cap,
):
    n_gy = lax.axis_size("gy")
    seg_count = seg_owner.shape[1]
    capacity = max(2 * seg_count // n_gy, 16)
    owner_col = seg_owner[0, :, 0]
    cell_ids = seg_cell[0]
    owner_hot = (owner_col[:, None] == jnp.arange(n_gy, dtype=jnp.int32)[None, :]).astype(jnp.int32)
    rank_in = jnp.sum((jnp.cumsum(owner_hot, axis=0) - 1) * owner_hot, axis=1)
    slot_at = owner_col * capacity + rank_in
    cell_buffer = (
        jnp.full((n_gy * capacity,), -1, jnp.int32)
        .at[slot_at]
        .set(cell_ids)
        .reshape(n_gy, capacity)
    )
    recv_cells = lax.all_to_all(cell_buffer, "gy", split_axis=0, concat_axis=0, tiled=True)
    is_valid = recv_cells >= 0
    safe_cells = jnp.where(is_valid, recv_cells, 0).reshape(-1)
    grid_shape = material.shape
    cell_total = grid_shape[0] * grid_shape[1] * grid_shape[2]
    material_hot = (
        material[None] == jnp.arange(eps_inf.shape[0], dtype=jnp.int32)[:, None, None, None]
    ).astype(jnp.float32)
    highest = lax.Precision.HIGHEST
    eps_cell = jnp.einsum("m,mxyz->xyz", eps_inf, material_hot, precision=highest)
    sigma_cell = jnp.einsum("m,mxyz->xyz", conductivity, material_hot, precision=highest)
    strength_cell = jnp.einsum("pm,mxyz->pxyz", pole_strength, material_hot, precision=highest)
    decay_cell = jnp.einsum("pm,mxyz->pxyz", pole_decay, material_hot, precision=highest)
    gain_row = wire_gain[0]
    cap_row = wire_cap[0]
    single_zero = jnp.zeros((1,), jnp.float32)
    for step_index in range(STEPS):
        plus_x, plus_y = electric_rims(e_field)
        elec_x, elec_y, elec_z = (e_field[0], e_field[1], e_field[2])
        magn_x = h_field[0] - TIME_STEP * (plus_y[1] - elec_z - (next_vertical(elec_y) - elec_y))
        magn_y = h_field[1] - TIME_STEP * (next_vertical(elec_x) - elec_x - (plus_x[1] - elec_z))
        magn_z = h_field[2] - TIME_STEP * (plus_x[0] - elec_y - (plus_y[0] - elec_x))
        h_field = jnp.stack([magn_x, magn_y, magn_z])
        samples = jnp.where(is_valid, elec_z.reshape(-1)[safe_cells].reshape(n_gy, capacity), 0.0)
        returned = lax.all_to_all(samples, "gy", split_axis=0, concat_axis=0, tiled=True)
        seg_sample = returned.reshape(-1)[slot_at]
        volt_now = voltage[0]
        curr_now = current[0]
        volt_next = jnp.concatenate([volt_now[1:], single_zero])
        curr_now = curr_now + gain_row * (seg_sample - (volt_next - volt_now))
        curr_prev = jnp.concatenate([single_zero, curr_now[:-1]])
        volt_now = volt_now - cap_row * (curr_now - curr_prev)
        current = curr_now[None]
        voltage = volt_now[None]
        current_buffer = (
            jnp.zeros((n_gy * capacity,), jnp.float32)
            .at[slot_at]
            .set(curr_now)
            .reshape(n_gy, capacity)
        )
        recv_current = lax.all_to_all(current_buffer, "gy", split_axis=0, concat_axis=0, tiled=True)
        wire_flat = (
            jnp.zeros((cell_total,), jnp.float32).at[safe_cells].add(recv_current.reshape(-1))
        )
        wire_term = wire_flat.reshape(grid_shape)
        minus_x, minus_y = magnetic_rims(h_field)
        curl_x = magn_z - minus_y[1] - (magn_y - prev_vertical(magn_y))
        curl_y = magn_x - prev_vertical(magn_x) - (magn_z - minus_x[1])
        curl_z = magn_y - minus_x[0] - (magn_x - minus_y[0])
        curl_all = jnp.stack([curl_x, curl_y, curl_z])
        polar_new = (
            decay_cell[:, None] * polarization
            + (1.0 - decay_cell[:, None]) * strength_cell[:, None] * e_field[None]
        )
        change = jnp.sum(polar_new - polarization, axis=0)
        drive = TIME_STEP * curl_all - TIME_STEP * sigma_cell[None] * e_field - change
        drive = drive.at[2].add(-TIME_STEP * wire_term)
        e_field = e_field + drive / eps_cell[None]
        polarization = polar_new
    return (e_field, h_field, polarization, current, voltage)


def solution(mesh):
    return jax.shard_map(
        on_device,
        mesh=mesh,
        in_specs=(
            P(None, "gx", "gy", None),
            P(None, "gx", "gy", None),
            P(None, None, "gx", "gy", None),
            P("gx", "gy", None),
            P(),
            P(),
            P(),
            P(),
            P("gx", "gy", None),
            P("gx", "gy"),
            P("gx", "gy"),
            P("gx", "gy"),
            P("gx", "gy"),
            P("gx", "gy"),
        ),
        out_specs=(
            P(None, "gx", "gy", None),
            P(None, "gx", "gy", None),
            P(None, None, "gx", "gy", None),
            P("gx", "gy"),
            P("gx", "gy"),
        ),
        check_vma=False,
    )
```

profile of v0, /device:TPU:7, one launch (start us, length us, event | category | flops | bytes accessed | tf_op | source)
XLA Modules:
  0.0 195.2 jit_solution(9504304332624794891)
XLA Ops:
  0.7 0.7 fusion.77
  1.4 1.2 reduce-window.6
  2.8 0.8 fusion.72
  3.6 0.7 compare_select_fusion.4
  4.3 2.6 %scatter_custom_fusion = s32[1024]{0:T(1024)S(1)} fusion(s32[512]{0:T(512)S(1)} %bitcast.305, s32[512]{0:T(512)} %bitcast.312, s32[]{:T(128)} %constant.81.clone.1), kind=kCustom, calls=%fused_computation.190 | custom fusion | bytes 4608 | tf_op jit(solution)/shard_map/scatter | solution.py:69
  6.9 0.7 all_to_all.28
  7.6 16.2 %all-to-all-start = ((s32[32,1,32]{2,1,0:T(1,128)}), s32[32,1,32]{2,1,0:T(1,128)S(1)}, u32[]{:S(2)}, u32[]{:S(2)}) async-start(s32[32,1,32]{2,1,0:T(1,128)} %all_to_all.28), calls=%async_computation | async-start | bytes 32768 | tf_op jit(solution)/shard_map/all_to_all | solution.py:72
  23.8 1.5 slice.228
  25.3 3.0 %collective-permute-start = (f32[2,1,4,2048]{3,2,1,0:T(4,128)}, f32[2,1,4,2048]{3,2,1,0:T(4,128)S(1)}, u32[]{:S(2)}, u32[]{:S(2)}) collective-permute-start(f32[2,1,4,2048]{3,2,1,0:T(4,128)} %slice.228), channel_id=1, source_target_pairs={{32,0},{64,32},{96,64},{128,96},{160,128},{192,160},{224,192},{256... | collective-permute-start | bytes 196616 | tf_op jit(solution)/shard_map/ppermute | solution.py:15
  28.3 1.6 slice.232
  29.9 1.3 collective-permute-start.1
  31.2 1.5 fusion.1
  32.7 1.5 fusion.2
  34.1 0.7 bitcast_multiply_fusion
  34.9 0.6 convolution_bitcast_fusion.1
  35.8 0.6 fusion
  37.0 1.6 subtract_reduce_fusion.1
  38.8 0.7 copy.36
  40.0 0.7 reduce.21
  40.9 1.7 slice_bitcast_fusion.9
  42.6 6.2 %gather_fusion = f32[1024]{0:T(1024)S(1)} fusion(f32[32768]{0:T(1024)S(1)} %bitcast.261, s32[1024]{0:T(1024)S(1)} %broadcast_clamp_fusion), kind=kCustom, calls=%fused_computation | custom fusion | bytes 12288 | tf_op jit(solution)/shard_map/gather | solution.py:95
  48.9 0.6 compare_select_fusion.1
  49.5 13.7 %all-to-all-start.1 = ((f32[32,1,32]{2,1,0:T(1,128)}), f32[32,1,32]{2,1,0:T(1,128)S(1)}, u32[]{:S(2)}, u32[]{:S(2)}) async-start(f32[32,1,32]{2,1,0:T(1,128)} %compare_select_fusion.1), calls=%async_computation.1 | async-start | bytes 32768 | tf_op jit(solution)/shard_map/all_to_all | solution.py:96
  63.2 1.0 slice.297
  64.4 1.2 fusion.59
  65.8 0.6 pad_maximum_fusion.11
  66.4 0.7 slice.242
  67.1 0.7 slice.243
  67.8 7.2 %collective-permute-start.3 = (f32[2,1,4,2048]{3,2,1,0:T(4,128)}, f32[2,1,4,2048]{3,2,1,0:T(4,128)}, u32[]{:S(2)}, u32[]{:S(2)}) collective-permute-start(f32[2,1,4,2048]{3,2,1,0:T(4,128)} %pad_maximum_fusion.11), channel_id=1, source_target_pairs={{0,32},{32,64},{64,96},{96,128},{128,160},{160,192},{192,224},{224... | collective-permute-start | bytes 196616 | tf_op jit(solution)/shard_map/ppermute | solution.py:15
  75.0 3.4 %collective-permute-start.2 = (f32[2,4,1,2048]{3,2,1,0:T(1,128)}, f32[2,4,1,2048]{3,2,1,0:T(1,128)}, u32[]{:S(2)}, u32[]{:S(2)}) collective-permute-start(f32[2,4,1,2048]{3,2,1,0:T(1,128)} %slice.242), channel_id=1, source_target_pairs={{0,1},{1,2},{2,3},{3,4},{4,5},{5,6},{6,7},{7,8},{8,9},{9,10},{10,1... | collective-permute-start | bytes 196616 | tf_op jit(solution)/shard_map/ppermute | solution.py:15
  78.5 0.6 broadcast.249
  79.0 0.7 reduce.22
  79.9 2.3 %gather_fusion.1 = f32[512]{0:T(512)S(1)} fusion(f32[1024]{0:T(1024)S(1)} %reshape.251, s32[1024]{0:T(1024)S(1)} %pad_clamp_fusion), kind=kCustom, calls=%fused_computation.1 | custom fusion | bytes 6144 | tf_op jit(solution)/shard_map/gather | solution.py:97
  82.3 2.4 %scatter_custom_fusion.1 = f32[1024]{0:T(1024)S(1)} fusion(s32[512]{0:T(512)S(1)} %bitcast.307, f32[512]{0:T(512)S(1)} %fusion.89, f32[]{:T(128)} %constant.79.clone.1), kind=kCustom, calls=%fused_computation.188 | custom fusion | bytes 4100 | tf_op jit(solution)/shard_map/scatter | solution.py:109
  84.7 0.7 all_to_all.32
  85.4 11.6 %all-to-all-start.2 = ((f32[32,1,32]{2,1,0:T(1,128)}), f32[32,1,32]{2,1,0:T(1,128)S(1)}, u32[]{:S(2)}, u32[]{:S(2)}) async-start(f32[32,1,32]{2,1,0:T(1,128)} %all_to_all.32), calls=%async_computation.2 | async-start | bytes 32768 | tf_op jit(solution)/shard_map/all_to_all | solution.py:112
  97.1 0.7 slice.282
  97.7 11.2 %all-to-all-done.2 = f32[32,1,32]{2,1,0:T(1,128)S(1)} async-done(((f32[32,1,32]{2,1,0:T(1,128)}), f32[32,1,32]{2,1,0:T(1,128)S(1)}, u32[]{:S(2)}, u32[]{:S(2)}) %all-to-all-start.2) | async-done | bytes 4128 | tf_op jit(solution)/shard_map/all_to_all | solution.py:112
  108.9 0.7 reduce.23
  109.7 0.7 reshape.308
  110.3 7.0 %scatter_custom_fusion.2 = f32[32768]{0:T(1024)S(1)} fusion(s32[1024]{0:T(1024)} %bitcast.302, f32[1024]{0:T(1024)} %reshape.308, f32[]{:T(128)} %constant.79.clone.1), kind=kCustom, calls=%fused_computation.146 | custom fusion | flops 1024 | bytes 131584 | tf_op jit(solution)/shard_map/scatter-add | solution.py:114
  117.4 0.7 broadcast_multiply_fusion.1
  118.0 1.6 mul.179
  119.6 0.9 fusion.12
  120.6 1.5 fusion.24
  123.2 1.9 collective-permute-start.4
  125.1 1.3 collective-permute-start.5
  126.4 2.9 %subtract_reduce_fusion = (f32[3,4,4,2048]{3,2,1,0:T(4,128)}, f32[4,3,4,4,2048]{4,3,2,1,0:T(4,128)}) fusion(f32[4,3,4,4,2048]{4,3,2,1,0:T(4,128)S(1)} %copy-done.2, f32[3,4,4,2048]{3,2,1,0:T(4,128)S(1)} %copy-done.1, f32[4,4,4,2048]{3,2,1,0:T(4,128)S(1)} %copy-done.4, f32[4,4,4,2048]{3,2,1,0:T(4,128)S(1)} %copy.21, f32[3,4,4,2048]{3,2,1,0:T(4,128)S(1)} %bitcast.265), kind=kLoop, calls=%fused_computation.12 | loop fusion | flops 3047424 | bytes 5373952 | tf_op jit(solution)/shard_map/reduce_sum | solution.py:126
  129.5 2.9 %collective-permute-done.4 = f32[2,1,4,2048]{3,2,1,0:T(4,128)S(1)} collective-permute-done((f32[2,1,4,2048]{3,2,1,0:T(4,128)S(1)}, f32[2,1,4,2048]{3,2,1,0:T(4,128)S(1)}, u32[]{:S(2)}, u32[]{:S(2)}) %collective-permute-start.4) | collective-permute-done | bytes 65568 | tf_op jit(solution)/shard_map/ppermute | solution.py:15
  132.6 6.2 %gather_fusion.2 = f32[1024]{0:T(1024)S(1)} fusion(f32[32768]{0:T(1024)S(1)} %bitcast.260, s32[1024]{0:T(1024)S(1)} %broadcast_clamp_fusion), kind=kCustom, calls=%fused_computation.2 | custom fusion | bytes 12288 | tf_op jit(solution)/shard_map/gather | solution.py:95
  138.8 0.6 compare_select_fusion
  139.5 3.8 %all-to-all-start.3 = ((f32[32,1,32]{2,1,0:T(1,128)}), f32[32,1,32]{2,1,0:T(1,128)S(1)}, u32[]{:S(2)}, u32[]{:S(2)}) async-start(f32[32,1,32]{2,1,0:T(1,128)} %compare_select_fusion), calls=%async_computation.3 | async-start | bytes 32768 | tf_op jit(solution)/shard_map/all_to_all | solution.py:96
  144.1 7.7 %collective-permute-start.7 = (f32[2,1,4,2048]{3,2,1,0:T(4,128)S(1)}, f32[2,1,4,2048]{3,2,1,0:T(4,128)S(1)}, u32[]{:S(2)}, u32[]{:S(2)}) collective-permute-start(f32[2,1,4,2048]{3,2,1,0:T(4,128)S(1)} %pad_maximum_fusion.10), channel_id=1, source_target_pairs={{0,32},{32,64},{64,96},{96,128},{128,160},{160,192},{192,224},{224... | collective-permute-start | bytes 196616 | tf_op jit(solution)/shard_map/ppermute | solution.py:15
  151.8 2.8 %collective-permute-start.6 = (f32[2,4,1,2048]{3,2,1,0:T(1,128)S(1)}, f32[2,4,1,2048]{3,2,1,0:T(1,128)S(1)}, u32[]{:S(2)}, u32[]{:S(2)}) collective-permute-start(f32[2,4,1,2048]{3,2,1,0:T(1,128)S(1)} %slice.270), channel_id=1, source_target_pairs={{0,1},{1,2},{2,3},{3,4},{4,5},{5,6},{6,7},{7,8},{8,9},{9,10},{10,1... | collective-permute-start | bytes 196616 | tf_op jit(solution)/shard_map/ppermute | solution.py:15
  155.2 0.7 reduce.24
  156.0 2.3 %gather_fusion.3 = f32[512]{0:T(512)S(1)} fusion(f32[1024]{0:T(1024)S(1)} %reshape.254, s32[1024]{0:T(1024)S(1)} %copy-done.30), kind=kCustom, calls=%fused_computation.3 | custom fusion | bytes 6144 | tf_op jit(solution)/shard_map/gather | solution.py:97
  158.4 2.6 %scatter_custom_fusion.3 = f32[1024]{0:T(1024)S(1)} fusion(s32[512]{0:T(512)} %bitcast.308, f32[512]{0:T(512)S(1)} %fusion.93, f32[]{:T(128)} %constant.79.clone.1), kind=kCustom, calls=%fused_computation.186 | custom fusion | bytes 4608 | tf_op jit(solution)/shard_map/scatter | solution.py:109
  161.0 0.7 all_to_all.35
  161.7 11.6 %all-to-all-start.4 = ((f32[32,1,32]{2,1,0:T(1,128)}), f32[32,1,32]{2,1,0:T(1,128)S(1)}, u32[]{:S(2)}, u32[]{:S(2)}) async-start(f32[32,1,32]{2,1,0:T(1,128)} %all_to_all.35), calls=%async_computation.4 | async-start | bytes 32768 | tf_op jit(solution)/shard_map/all_to_all | solution.py:112
  173.4 0.7 fusion.104
  174.1 11.2 %all-to-all-done.4 = f32[32,1,32]{2,1,0:T(1,128)S(1)} async-done(((f32[32,1,32]{2,1,0:T(1,128)}), f32[32,1,32]{2,1,0:T(1,128)S(1)}, u32[]{:S(2)}, u32[]{:S(2)}) %all-to-all-start.4) | async-done | bytes 4128 | tf_op jit(solution)/shard_map/all_to_all | solution.py:112
  185.3 0.7 reduce.25
  186.1 6.9 %scatter_custom_fusion.4 = f32[32768]{0:T(1024)S(1)} fusion(s32[1024]{0:T(1024)} %bitcast.303, f32[1024]{0:T(1024)S(1)} %reshape.324, f32[]{:T(128)} %constant.79.clone.1), kind=kCustom, calls=%fused_computation.144 | custom fusion | flops 1024 | bytes 131584 | tf_op jit(solution)/shard_map/scatter-add | solution.py:114
  194.4 0.8 divide_add_fusion
  (132 shorter events, 6.8 us)
Async XLA Ops:
  0.6 34.2 %copy-start = (f32[4,8]{1,0:T(4,128)S(1)}, f32[4,8]{1,0:T(4,128)}, u32[]{:S(2)}) copy-start(f32[4,8]{1,0:T(4,128)} %param.25) | copy-start | bytes 388
  0.6 34.2 %copy-start.13 = (s32[4,4,2048]{2,1,0:T(4,128)S(1)}, s32[4,4,2048]{2,1,0:T(4,128)}, u32[]{:S(2)}) copy-start(s32[4,4,2048]{2,1,0:T(4,128)} %param.21) | copy-start | bytes 393220
  4.3 78.0 %copy-start.33 = (s32[512,1]{0,1:T(1,128)}, s32[512,1]{0,1:T(1,128)S(1)}, u32[]{:S(2)}) copy-start(s32[512,1]{0,1:T(1,128)S(1)} %compare_select_fusion.4) | copy-start | bytes 6148
  7.6 31.9 %all-to-all-start = ((s32[32,1,32]{2,1,0:T(1,128)}), s32[32,1,32]{2,1,0:T(1,128)S(1)}, u32[]{:S(2)}, u32[]{:S(2)}) async-start(s32[32,1,32]{2,1,0:T(1,128)} %all_to_all.28), calls=%async_computation | async-start | bytes 32768 | tf_op jit(solution)/shard_map/all_to_all | solution.py:72
  25.3 10.6 %copy-start.36 = (f32[4,8]{1,0:T(4,128)S(1)}, f32[4,8]{1,0:T(4,128)}, u32[]{:S(2)}) copy-start(f32[4,8]{1,0:T(4,128)} %param.24) | copy-start | bytes 388
  25.3 15.6 %collective-permute-start = (f32[2,1,4,2048]{3,2,1,0:T(4,128)}, f32[2,1,4,2048]{3,2,1,0:T(4,128)S(1)}, u32[]{:S(2)}, u32[]{:S(2)}) collective-permute-start(f32[2,1,4,2048]{3,2,1,0:T(4,128)} %slice.228), channel_id=1, source_target_pairs={{32,0},{64,32},{96,64},{128,96},{160,128},{192,160},{224,192},{256... | collective-permute-start | bytes 196616 | tf_op jit(solution)/shard_map/ppermute | solution.py:15
  29.9 11.0 %collective-permute-start.1 = (f32[2,4,1,2048]{3,2,1,0:T(1,128)}, f32[2,4,1,2048]{3,2,1,0:T(1,128)S(1)}, u32[]{:S(2)}, u32[]{:S(2)}) collective-permute-start(f32[2,4,1,2048]{3,2,1,0:T(1,128)} %slice.232), channel_id=1, source_target_pairs={{1,0},{2,1},{3,2},{4,3},{5,4},{6,5},{7,6},{8,7},{9,8},{10,9},{11,1... | collective-permute-start | bytes 196616 | tf_op jit(solution)/shard_map/ppermute | solution.py:15
  35.4 1.4 copy-start.1
  35.5 1.5 copy-start.2
  37.0 1.6 copy-start.3
  37.0 1.7 copy-start.17
  38.6 41.2 %copy-start.29 = (s32[1024]{0:T(1024)}, s32[1024]{0:T(1024)S(1)}, u32[]{:S(2)}) copy-start(s32[1024]{0:T(1024)S(1)} %pad_clamp_fusion) | copy-start | bytes 12292
  38.8 43.4 %copy-start.21 = (f32[1,511]{1,0:T(1,128)}, f32[1,511]{1,0:T(1,128)S(1)}, u32[]{:S(2)}) copy-start(f32[1,511]{1,0:T(1,128)S(1)} %slice.255) | copy-start | bytes 6136
  39.5 9.4 %copy-start.15 = (s32[32,1,32]{2,1,0:T(1,128)}, s32[32,1,32]{2,1,0:T(1,128)S(1)}, u32[]{:S(2)}) copy-start(s32[32,1,32]{2,1,0:T(1,128)S(1)} %all-to-all-done) | copy-start | bytes 12292
  40.8 8.0 %copy-start.28 = (s32[1024,1]{0,1:T(1,128)}, s32[1024,1]{0,1:T(1,128)S(1)}, u32[]{:S(2)}) copy-start(s32[1024,1]{0,1:T(1,128)S(1)} %compare_select_fusion.2) | copy-start | bytes 12292
  40.9 25.5 %copy-start.12 = (f32[2,4,1,2048]{3,2,1,0:T(1,128)}, f32[2,4,1,2048]{3,2,1,0:T(1,128)S(1)}, u32[]{:S(2)}) copy-start(f32[2,4,1,2048]{3,2,1,0:T(1,128)S(1)} %collective-permute-done.1) | copy-start | bytes 196612
  49.5 28.9 %all-to-all-start.1 = ((f32[32,1,32]{2,1,0:T(1,128)}), f32[32,1,32]{2,1,0:T(1,128)S(1)}, u32[]{:S(2)}, u32[]{:S(2)}) async-start(f32[32,1,32]{2,1,0:T(1,128)} %compare_select_fusion.1), calls=%async_computation.1 | async-start | bytes 32768 | tf_op jit(solution)/shard_map/all_to_all | solution.py:96
  65.7 16.4 %copy-start.19 = (f32[1,512]{1,0:T(1,128)S(1)}, f32[1,512]{1,0:T(1,128)}, u32[]{:S(2)}) copy-start(f32[1,512]{1,0:T(1,128)} %param.30) | copy-start | bytes 6148
  65.7 16.4 %copy-start.31 = (f32[1,512]{1,0:T(1,128)S(1)}, f32[1,512]{1,0:T(1,128)}, u32[]{:S(2)}) copy-start(f32[1,512]{1,0:T(1,128)} %param.28) | copy-start | bytes 6148
  65.8 31.2 %copy-start.34 = (f32[1,512]{1,0:T(1,128)S(1)}, f32[1,512]{1,0:T(1,128)}, u32[]{:S(2)}) copy-start(f32[1,512]{1,0:T(1,128)} %param.31) | copy-start | bytes 6148
  67.8 51.8 %collective-permute-start.3 = (f32[2,1,4,2048]{3,2,1,0:T(4,128)}, f32[2,1,4,2048]{3,2,1,0:T(4,128)}, u32[]{:S(2)}, u32[]{:S(2)}) collective-permute-start(f32[2,1,4,2048]{3,2,1,0:T(4,128)} %pad_maximum_fusion.11), channel_id=1, source_target_pairs={{0,32},{32,64},{64,96},{96,128},{128,160},{160,192},{192,224},{224... | collective-permute-start | bytes 196616 | tf_op jit(solution)/shard_map/ppermute | solution.py:15
  75.0 45.6 %collective-permute-start.2 = (f32[2,4,1,2048]{3,2,1,0:T(1,128)}, f32[2,4,1,2048]{3,2,1,0:T(1,128)}, u32[]{:S(2)}, u32[]{:S(2)}) collective-permute-start(f32[2,4,1,2048]{3,2,1,0:T(1,128)} %slice.242), channel_id=1, source_target_pairs={{0,1},{1,2},{2,3},{3,4},{4,5},{5,6},{6,7},{7,8},{8,9},{9,10},{10,1... | collective-permute-start | bytes 196616 | tf_op jit(solution)/shard_map/ppermute | solution.py:15
  82.1 27.5 %copy-start.26 = (f32[512]{0:T(512)}, f32[512]{0:T(512)S(1)}, u32[]{:S(2)}) copy-start(f32[512]{0:T(512)S(1)} %gather_fusion.1) | copy-start | bytes 6148
  85.4 23.5 %all-to-all-start.2 = ((f32[32,1,32]{2,1,0:T(1,128)}), f32[32,1,32]{2,1,0:T(1,128)S(1)}, u32[]{:S(2)}, u32[]{:S(2)}) async-start(f32[32,1,32]{2,1,0:T(1,128)} %all_to_all.32), calls=%async_computation.2 | async-start | bytes 32768 | tf_op jit(solution)/shard_map/all_to_all | solution.py:112
  97.1 25.0 %copy-start.24 = (f32[512]{0:T(512)}, f32[512]{0:T(512)S(1)}, u32[]{:S(2)}) copy-start(f32[512]{0:T(512)S(1)} %fusion.95) | copy-start | bytes 6148
  120.5 1.7 copy-start.5
  120.6 1.7 copy-start.10
  122.1 0.9 copy-start.14
  122.1 1.0 copy-start.8
  122.3 4.1 %copy-start.4 = (f32[4,4,4,2048]{3,2,1,0:T(4,128)S(1)}, f32[4,4,4,2048]{3,2,1,0:T(4,128)}, u32[]{:S(2)}) copy-start(f32[4,4,4,2048]{3,2,1,0:T(4,128)} %copy-done.3) | copy-start | bytes 1572868
  123.2 9.2 %collective-permute-start.4 = (f32[2,1,4,2048]{3,2,1,0:T(4,128)S(1)}, f32[2,1,4,2048]{3,2,1,0:T(4,128)S(1)}, u32[]{:S(2)}, u32[]{:S(2)}) collective-permute-start(f32[2,1,4,2048]{3,2,1,0:T(4,128)S(1)} %slice.307), channel_id=1, source_target_pairs={{32,0},{64,32},{96,64},{128,96},{160,128},{192,160},{224,192},{256... | collective-permute-start | bytes 196616 | tf_op jit(solution)/shard_map/ppermute | solution.py:15
  125.1 7.3 %collective-permute-start.5 = (f32[2,4,1,2048]{3,2,1,0:T(1,128)S(1)}, f32[2,4,1,2048]{3,2,1,0:T(1,128)S(1)}, u32[]{:S(2)}, u32[]{:S(2)}) collective-permute-start(f32[2,4,1,2048]{3,2,1,0:T(1,128)S(1)} %slice.262), channel_id=1, source_target_pairs={{1,0},{2,1},{3,2},{4,3},{5,4},{6,5},{7,6},{8,7},{9,8},{10,9},{11,1... | collective-permute-start | bytes 196616 | tf_op jit(solution)/shard_map/ppermute | solution.py:15
  132.6 6.3 %copy-start.16 = (s32[32,1,32]{2,1,0:T(1,128)S(1)}, s32[32,1,32]{2,1,0:T(1,128)}, u32[]{:S(2)}) copy-start(s32[32,1,32]{2,1,0:T(1,128)} %copy-done.15) | copy-start | bytes 12292
  139.5 15.8 %all-to-all-start.3 = ((f32[32,1,32]{2,1,0:T(1,128)}), f32[32,1,32]{2,1,0:T(1,128)S(1)}, u32[]{:S(2)}, u32[]{:S(2)}) async-start(f32[32,1,32]{2,1,0:T(1,128)} %compare_select_fusion), calls=%async_computation.3 | async-start | bytes 32768 | tf_op jit(solution)/shard_map/all_to_all | solution.py:96
  143.5 12.5 %copy-start.30 = (s32[1024]{0:T(1024)S(1)}, s32[1024]{0:T(1024)}, u32[]{:S(2)}) copy-start(s32[1024]{0:T(1024)} %copy-done.29) | copy-start | bytes 12292
  143.9 14.6 %copy-start.7 = (f32[3,4,4,2048]{3,2,1,0:T(4,128)}, f32[3,4,4,2048]{3,2,1,0:T(4,128)S(1)}, u32[]{:S(2)}) copy-start(f32[3,4,4,2048]{3,2,1,0:T(4,128)S(1)} %pad_maximum_fusion.1) | copy-start | bytes 1179652
  143.9 14.5 %copy-start.20 = (f32[1,512]{1,0:T(1,128)S(1)}, f32[1,512]{1,0:T(1,128)}, u32[]{:S(2)}) copy-start(f32[1,512]{1,0:T(1,128)} %param.30) | copy-start | bytes 6148
  143.9 14.4 %copy-start.23 = (f32[511]{0:T(512)S(1)}, f32[511]{0:T(512)}, u32[]{:S(2)}) copy-start(f32[511]{0:T(512)} %slice.282) | copy-start | bytes 6136
  143.9 14.4 %copy-start.25 = (f32[512]{0:T(512)S(1)}, f32[512]{0:T(512)}, u32[]{:S(2)}) copy-start(f32[512]{0:T(512)} %copy-done.24) | copy-start | bytes 6148
  143.9 29.4 %copy-start.18 = (f32[1,512]{1,0:T(1,128)S(1)}, f32[1,512]{1,0:T(1,128)}, u32[]{:S(2)}) copy-start(f32[1,512]{1,0:T(1,128)} %param.29) | copy-start | bytes 6148
  143.9 29.4 %copy-start.22 = (f32[1,511]{1,0:T(1,128)S(1)}, f32[1,511]{1,0:T(1,128)}, u32[]{:S(2)}) copy-start(f32[1,511]{1,0:T(1,128)} %copy-done.21) | copy-start | bytes 6136
  143.9 29.4 %copy-start.27 = (f32[512]{0:T(512)S(1)}, f32[512]{0:T(512)}, u32[]{:S(2)}) copy-start(f32[512]{0:T(512)} %copy-done.26) | copy-start | bytes 6148
  143.9 29.4 %copy-start.32 = (f32[1,512]{1,0:T(1,128)S(1)}, f32[1,512]{1,0:T(1,128)}, u32[]{:S(2)}) copy-start(f32[1,512]{1,0:T(1,128)} %param.28) | copy-start | bytes 6148
  144.0 29.4 %copy-start.35 = (f32[1,512]{1,0:T(1,128)S(1)}, f32[1,512]{1,0:T(1,128)}, u32[]{:S(2)}) copy-start(f32[1,512]{1,0:T(1,128)} %param.31) | copy-start | bytes 6148
  144.1 48.9 %collective-permute-start.7 = (f32[2,1,4,2048]{3,2,1,0:T(4,128)S(1)}, f32[2,1,4,2048]{3,2,1,0:T(4,128)S(1)}, u32[]{:S(2)}, u32[]{:S(2)}) collective-permute-start(f32[2,1,4,2048]{3,2,1,0:T(4,128)S(1)} %pad_maximum_fusion.10), channel_id=1, source_target_pairs={{0,32},{32,64},{64,96},{96,128},{128,160},{160,192},{192,224},{224... | collective-permute-start | bytes 196616 | tf_op jit(solution)/shard_map/ppermute | solution.py:15
  151.8 41.3 %collective-permute-start.6 = (f32[2,4,1,2048]{3,2,1,0:T(1,128)S(1)}, f32[2,4,1,2048]{3,2,1,0:T(1,128)S(1)}, u32[]{:S(2)}, u32[]{:S(2)}) collective-permute-start(f32[2,4,1,2048]{3,2,1,0:T(1,128)S(1)} %slice.270), channel_id=1, source_target_pairs={{0,1},{1,2},{2,3},{3,4},{4,5},{5,6},{6,7},{7,8},{8,9},{9,10},{10,1... | collective-permute-start | bytes 196616 | tf_op jit(solution)/shard_map/ppermute | solution.py:15
  161.7 23.6 %all-to-all-start.4 = ((f32[32,1,32]{2,1,0:T(1,128)}), f32[32,1,32]{2,1,0:T(1,128)S(1)}, u32[]{:S(2)}, u32[]{:S(2)}) async-start(f32[32,1,32]{2,1,0:T(1,128)} %all_to_all.35), calls=%async_computation.4 | async-start | bytes 32768 | tf_op jit(solution)/shard_map/all_to_all | solution.py:112
  193.1 1.0 copy-start.6
  193.1 1.0 copy-start.11
  193.5 0.9 copy-start.9
where the time goes:
time: 196 us; the launch traced here: 195 us
  starting transfers between devices  85.5 us (44%)
  local copies, waits for them, and re-layouts  40.4 us (21%)
  other arithmetic  37.6 us (19%)
  waiting for transfers between devices  26 us (13%)
  matrix products  4.15 us (2%)
    ppermute x8, starting transfers between devices, passed_along(): lax.ppermute(value, axis, [(source, source + steps) for source in range(f...  28.6 us
    all_to_all x2, starting transfers between devices, on_device(): lax.all_to_all(current_buffer, 'gy', split_axis=0, concat_axis=0, tiled=T...  23.2 us
    all_to_all x2, waiting for transfers between devices, on_device(): lax.all_to_all(current_buffer, 'gy', split_axis=0, concat_axis=0, tiled=T...  22.4 us
    all_to_all x2, starting transfers between devices, on_device(): lax.all_to_all(samples, 'gy', split_axis=0, concat_axis=0, tiled=True)  17.5 us
    all_to_all x1, starting transfers between devices, on_device(): lax.all_to_all(cell_buffer, 'gy', split_axis=0, concat_axis=0, tiled=True)  16.2 us
    scatter-add x2, other arithmetic, on_device(): jnp.zeros((cell_total,), jnp.float32).at[safe_cells]  13.9 us
    gather x2, local copies, waits for them, and re-layouts, on_device(): elec_z.reshape(-1)[safe_cells].reshape(n_gy, capacity)  12.3 us
    scatter x2, local copies, waits for them, and re-layouts, on_device(): current_buffer = jnp.zeros((n_gy * capacity,), jnp.float32).at[slot_at].s...  5.02 us
  transfers between devices with their start and end apart: 13, of which 4 were waited for; matrix products, arithmetic and copies ran while one was open for 27% of the time, Pallas kernels for 0%

commit v1 on v0

v1 whole, which is shorter than its diff:
```python
import jax
import jax.numpy as jnp
from jax import lax
from jax.sharding import PartitionSpec as P

STEPS = 2


TIME_STEP = 0.5


def passed_along(value, axis, steps):
    count = lax.axis_size(axis)
    first, last = (max(0, -steps), min(count, count - steps))
    return lax.ppermute(value, axis, [(source, source + steps) for source in range(first, last)])


def next_vertical(field):
    return jnp.concatenate([field[..., 1:], jnp.zeros_like(field[..., :1])], axis=-1)


def prev_vertical(field):
    return jnp.concatenate([jnp.zeros_like(field[..., :1]), field[..., :-1]], axis=-1)


def electric_rims(e_field):
    face_x = passed_along(e_field[1:3, :1], "gx", -1)
    plus_x = jnp.concatenate([e_field[1:3, 1:], face_x], axis=1)
    face_y = passed_along(e_field[0::2, :, :1], "gy", -1)
    plus_y = jnp.concatenate([e_field[0::2, :, 1:], face_y], axis=2)
    return (plus_x, plus_y)


def magnetic_rims(h_field):
    face_x = passed_along(h_field[1:3, -1:], "gx", 1)
    minus_x = jnp.concatenate([face_x, h_field[1:3, :-1]], axis=1)
    face_y = passed_along(h_field[0::2, :, -1:], "gy", 1)
    minus_y = jnp.concatenate([face_y, h_field[0::2, :, :-1]], axis=2)
    return (minus_x, minus_y)


def magnetic_update(e_field, h_field):
    plus_x, plus_y = electric_rims(e_field)
    elec_x, elec_y, elec_z = (e_field[0], e_field[1], e_field[2])
    magn_x = h_field[0] - TIME_STEP * (plus_y[1] - elec_z - (next_vertical(elec_y) - elec_y))
    magn_y = h_field[1] - TIME_STEP * (next_vertical(elec_x) - elec_x - (plus_x[1] - elec_z))
    magn_z = h_field[2] - TIME_STEP * (plus_x[0] - elec_y - (plus_y[0] - elec_x))
    return jnp.stack([magn_x, magn_y, magn_z])


def electric_update(e_field, h_field, polarization, wire_term, cells):
    eps_cell, sigma_cell, strength_cell, decay_cell = cells
    magn_x, magn_y, magn_z = (h_field[0], h_field[1], h_field[2])
    minus_x, minus_y = magnetic_rims(h_field)
    curl_x = magn_z - minus_y[1] - (magn_y - prev_vertical(magn_y))
    curl_y = magn_x - prev_vertical(magn_x) - (magn_z - minus_x[1])
    curl_z = magn_y - minus_x[0] - (magn_x - minus_y[0])
    curl_all = jnp.stack([curl_x, curl_y, curl_z])
    polar_new = (
        decay_cell[:, None] * polarization
        + (1.0 - decay_cell[:, None]) * strength_cell[:, None] * e_field[None]
    )
    change = jnp.sum(polar_new - polarization, axis=0)
    drive = TIME_STEP * curl_all - TIME_STEP * sigma_cell[None] * e_field - change
    drive = drive.at[2].add(-TIME_STEP * wire_term)
    return (e_field + drive / eps_cell[None], polar_new)


def on_device(
    e_field,
    h_field,
    polarization,
    material,
    eps_inf,
    conductivity,
    pole_strength,
    pole_decay,
    seg_owner,
    seg_cell,
    current,
    voltage,
    wire_gain,
    wire_cap,
):
    n_gy = lax.axis_size("gy")
    seg_count = seg_owner.shape[1]
    capacity = max(2 * seg_count // n_gy, 16)
    owner_col = seg_owner[0, :, 0]
    cell_ids = seg_cell[0]
    owner_hot = (owner_col[:, None] == jnp.arange(n_gy, dtype=jnp.int32)[None, :]).astype(jnp.int32)
    rank_in = jnp.sum((jnp.cumsum(owner_hot, axis=0) - 1) * owner_hot, axis=1)
    slot_at = owner_col * capacity + rank_in
    grid_shape = material.shape
    cell_total = grid_shape[0] * grid_shape[1] * grid_shape[2]
    single_zero = jnp.zeros((1,), jnp.float32)

    def to_slots(rows, fill):
        empty = jnp.broadcast_to(jnp.asarray(fill, jnp.float32)[:, None], (rows.shape[0], n_gy * capacity))
        buffer = empty.at[:, slot_at].set(rows)
        return buffer.reshape(rows.shape[0], n_gy, capacity).transpose(1, 0, 2)

    def exchange(blocks):
        return lax.all_to_all(blocks, "gy", split_axis=0, concat_axis=0, tiled=True)

    def from_slots(blocks):
        flat = blocks.transpose(1, 0, 2).reshape(blocks.shape[1], n_gy * capacity)
        return flat[:, slot_at]

    gain_row = wire_gain[0]
    cap_row = wire_cap[0]
    volt_0 = voltage[0]
    curr_0 = current[0]
    drop_0 = jnp.concatenate([volt_0[1:], single_zero]) - volt_0
    outgoing = to_slots(jnp.stack([cell_ids.astype(jnp.float32), curr_0, gain_row, drop_0]), [-1.0, 0.0, 0.0, 0.0])
    incoming = exchange(outgoing)
    recv_cells = incoming[:, 0, :].astype(jnp.int32)
    is_valid = recv_cells >= 0
    safe_cells = jnp.where(is_valid, recv_cells, 0).reshape(-1)
    recv_curr = incoming[:, 1, :].reshape(-1)
    recv_gain = incoming[:, 2, :].reshape(-1)
    recv_drop = incoming[:, 3, :].reshape(-1)
    valid_flat = is_valid.reshape(-1)

    material_hot = (
        material[None] == jnp.arange(eps_inf.shape[0], dtype=jnp.int32)[:, None, None, None]
    ).astype(jnp.float32)
    highest = lax.Precision.HIGHEST
    eps_cell = jnp.einsum("m,mxyz->xyz", eps_inf, material_hot, precision=highest)
    sigma_cell = jnp.einsum("m,mxyz->xyz", conductivity, material_hot, precision=highest)
    strength_cell = jnp.einsum("pm,mxyz->pxyz", pole_strength, material_hot, precision=highest)
    decay_cell = jnp.einsum("pm,mxyz->pxyz", pole_decay, material_hot, precision=highest)
    cells = (eps_cell, sigma_cell, strength_cell, decay_cell)

    def sample(e_now):
        return jnp.where(valid_flat, e_now[2].reshape(-1)[safe_cells], 0.0)

    def wire_of(values):
        return jnp.zeros((cell_total,), jnp.float32).at[safe_cells].add(values).reshape(grid_shape)

    sample_0 = sample(e_field)
    h_field = magnetic_update(e_field, h_field)
    curr_cell_1 = recv_curr + recv_gain * (sample_0 - recv_drop)
    e_field, polarization = electric_update(e_field, h_field, polarization, wire_of(curr_cell_1), cells)
    sample_1 = sample(e_field)

    returned = from_slots(exchange(jnp.stack([sample_0, sample_1]).reshape(2, n_gy, capacity).transpose(1, 0, 2)))
    seg_sample_0, seg_sample_1 = returned[0], returned[1]
    curr_1 = curr_0 + gain_row * (seg_sample_0 - drop_0)
    curr_prev = jnp.concatenate([single_zero, curr_1[:-1]])
    volt_1 = volt_0 - cap_row * (curr_1 - curr_prev)
    drop_1 = jnp.concatenate([volt_1[1:], single_zero]) - volt_1
    curr_2 = curr_1 + gain_row * (seg_sample_1 - drop_1)
    curr_prev = jnp.concatenate([single_zero, curr_2[:-1]])
    volt_2 = volt_1 - cap_row * (curr_2 - curr_prev)

    h_field = magnetic_update(e_field, h_field)
    recv_curr_2 = exchange(to_slots(curr_2[None], [0.0])).transpose(1, 0, 2).reshape(-1)
    e_field, polarization = electric_update(e_field, h_field, polarization, wire_of(recv_curr_2), cells)
    return (e_field, h_field, polarization, curr_2[None], volt_2[None])


def solution(mesh):
    return jax.shard_map(
        on_device,
        mesh=mesh,
        in_specs=(
            P(None, "gx", "gy", None),
            P(None, "gx", "gy", None),
            P(None, None, "gx", "gy", None),
            P("gx", "gy", None),
            P(),
            P(),
            P(),
            P(),
            P("gx", "gy", None),
            P("gx", "gy"),
            P("gx", "gy"),
            P("gx", "gy"),
            P("gx", "gy"),
            P("gx", "gy"),
        ),
        out_specs=(
            P(None, "gx", "gy", None),
            P(None, "gx", "gy", None),
            P(None, None, "gx", "gy", None),
            P("gx", "gy"),
            P("gx", "gy"),
        ),
        check_vma=False,
    )
```

time: 196 us -> 164 us (0.84)
  the two profiles are of different devices: /device:TPU:7 before, /device:TPU:16 now
where the time goes in v1:
time: 164 us; the launch traced here: 163 us
  starting transfers between devices  53.6 us (33%)
  other arithmetic  38.5 us (23%)
  local copies, waits for them, and re-layouts  35.9 us (22%)
  waiting for transfers between devices  31.4 us (19%)
  matrix products  2.33 us (1%)
    all_to_all x3, starting transfers between devices, exchange(): return lax.all_to_all(blocks, 'gy', split_axis=0, concat_axis=0, tiled=True)  30.7 us
    all_to_all x3, waiting for transfers between devices, exchange(): return lax.all_to_all(blocks, 'gy', split_axis=0, concat_axis=0, tiled=True)  27 us
    ppermute x8, starting transfers between devices, passed_along(): lax.ppermute(value, axis, [(source, source + steps) for source in range(f...  23 us
    scatter-add x2, other arithmetic, wire_of(): jnp.zeros((cell_total,), jnp.float32).at[safe_cells].add(values)  13 us
    gather x4, local copies, waits for them, and re-layouts, sample(): return jnp.where(valid_flat, e_now[2].reshape(-1)[safe_cells], 0.0)  12.4 us
    scatter x2, local copies, waits for them, and re-layouts, to_slots(): buffer = empty.at[:, slot_at].set(rows)  4.5 us
    ppermute x8, waiting for transfers between devices, passed_along(): lax.ppermute(value, axis, [(source, source + steps) for source in range(f...  4.37 us
    reduce_sum x2, other arithmetic, electric_update(): change = jnp.sum(polar_new - polarization, axis=0)  3.8 us
  transfers between devices with their start and end apart: 11, of which 5 were waited for; matrix products, arithmetic and copies ran while one was open for 23% of the time, Pallas kernels for 0%

profile of v1, /device:TPU:16, one launch (start us, length us, event | category | flops | bytes accessed | tf_op | source)
XLA Modules:
  0.0 163.3 jit_solution(13777256010692649013)
XLA Ops:
  0.7 0.9 slice.248
  1.6 4.0 %collective-permute-start = (f32[2,1,4,2048]{3,2,1,0:T(4,128)S(1)}, f32[2,1,4,2048]{3,2,1,0:T(4,128)S(1)}, u32[]{:S(2)}, u32[]{:S(2)}) collective-permute-start(f32[2,1,4,2048]{3,2,1,0:T(4,128)S(1)} %slice.248), channel_id=1, source_target_pairs={{32,0},{64,32},{96,64},{128,96},{160,128},{192,160},{224,192},{256... | collective-permute-start | bytes 196616 | tf_op jit(solution)/shard_map/ppermute | solution.py:15
  5.6 1.6 slice.252
  7.2 1.3 collective-permute-start.1
  8.5 0.8 slice.275
  9.3 0.7 convert_element_type.41
  10.0 0.7 fusion.77
  10.6 1.2 reduce-window.6
  12.1 0.8 fusion.72
  12.9 0.7 compare_select_fusion.2
  13.6 0.8 fusion.82
  14.3 0.7 maximum_bitcast_fusion.1
  15.2 0.7 broadcast_in_dim.15
  15.9 1.9 %scatter_fusion = f32[4,1024]{0,1:T(8,128)S(1)} fusion(f32[4,1024]{0,1:T(8,128)S(1)} %broadcast_in_dim.15, s32[512]{0:T(512)S(1)} %bitcast.321, f32[512,4]{1,0:T(8,128)S(1)} %copy.95), kind=kCustom, calls=%fused_computation.3 | custom fusion | bytes 26624 | tf_op jit(solution)/shard_map/scatter | solution.py:99
  18.1 0.7 reshape.367
  18.8 18.4 %all-to-all-start = ((f32[32,1,128]{2,1,0:T(1,128)}), f32[32,1,128]{2,1,0:T(1,128)}, u32[]{:S(2)}, u32[]{:S(2)}) async-start(f32[32,1,128]{2,1,0:T(1,128)} %reshape.367), calls=%async_computation | async-start | bytes 32768 | tf_op jit(solution)/shard_map/all_to_all | solution.py:103
  37.4 0.6 fusion.1
  38.6 0.7 bitcast_multiply_fusion
  39.3 0.6 convolution_bitcast_fusion.1
  40.3 0.6 fusion
  41.3 1.6 subtract_reduce_fusion.1
  42.9 0.6 pad_clamp_fusion
  43.5 6.7 %all-to-all-done = f32[32,1,128]{2,1,0:T(1,128)} async-done(((f32[32,1,128]{2,1,0:T(1,128)}), f32[32,1,128]{2,1,0:T(1,128)}, u32[]{:S(2)}, u32[]{:S(2)}) %all-to-all-start) | async-done | bytes 16416 | tf_op jit(solution)/shard_map/all_to_all | solution.py:103
  50.7 1.3 reduce.22
  52.4 0.7 reshape_squeeze.18
  53.1 0.7 reshape_squeeze.16
  53.7 0.7 reshape_squeeze.15
  54.4 1.7 %slice_bitcast_fusion.9 = (f32[4,16,4,128]{3,2,1,0:T(4,128)S(1)}, f32[1,4,4,2048]{3,2,1,0:T(4,128)S(1)}, f32[4,4,2048]{2,1,0:T(4,128)}, f32[4,4,2048]{2,1,0:T(4,128)S(1)}) fusion(f32[3,4,4,2048]{3,2,1,0:T(4,128)S(1)} %copy-done.1, f32[2,4,1,2048]{3,2,1,0:T(1,128)S(1)} %collective-permute-done.1, f32[2,4,3,2048]{3,2,1,0:T(4,128)S(1)} %slice.251, ...), kind=kLoop, calls=%fused_computation.130 | loop fusion | flops 229376 | bytes 1572864
  56.2 6.2 %gather_fusion = f32[1024]{0:T(1024)S(1)} fusion(f32[32768]{0:T(1024)S(1)} %bitcast.277, s32[1024]{0:T(1024)S(1)} %broadcast_clamp_fusion), kind=kCustom, calls=%fused_computation | custom fusion | bytes 12288 | tf_op jit(solution)/shard_map/gather | solution.py:135
  62.4 1.3 bitcast_select_fusion.1
  63.8 1.3 multiply_add_fusion.2
  65.1 6.5 %scatter_custom_fusion.1 = f32[32768]{0:T(1024)S(1)} fusion(s32[1024]{0:T(1024)} %bitcast.330, f32[1024]{0:T(1024)} %multiply_add_fusion.2, f32[]{:T(128)} %constant.82.clone.1), kind=kCustom, calls=%fused_computation.144 | custom fusion | flops 1024 | bytes 131584 | tf_op jit(solution)/shard_map/scatter-add | solution.py:138
  71.6 0.7 broadcast_multiply_fusion.1
  72.3 1.0 slice.321
  73.5 1.2 fusion.59
  74.7 0.6 pad_maximum_fusion.11
  75.3 1.9 %collective-permute-start.3 = (f32[2,1,4,2048]{3,2,1,0:T(4,128)}, f32[2,1,4,2048]{3,2,1,0:T(4,128)}, u32[]{:S(2)}, u32[]{:S(2)}) collective-permute-start(f32[2,1,4,2048]{3,2,1,0:T(4,128)} %pad_maximum_fusion.11), channel_id=1, source_target_pairs={{0,32},{32,64},{64,96},{96,128},{128,160},{160,192},{192,224},{224... | collective-permute-start | bytes 196616 | tf_op jit(solution)/shard_map/ppermute | solution.py:15
  77.3 0.7 slice.262
  78.0 0.7 slice.263
  78.8 1.6 mul.182
  80.4 3.1 %collective-permute-start.2 = (f32[2,4,1,2048]{3,2,1,0:T(1,128)}, f32[2,4,1,2048]{3,2,1,0:T(1,128)S(1)}, u32[]{:S(2)}, u32[]{:S(2)}) collective-permute-start(f32[2,4,1,2048]{3,2,1,0:T(1,128)} %slice.262), channel_id=1, source_target_pairs={{0,1},{1,2},{2,3},{3,4},{4,5},{5,6},{6,7},{7,8},{8,9},{9,10},{10,1... | collective-permute-start | bytes 196616 | tf_op jit(solution)/shard_map/ppermute | solution.py:15
  83.5 1.5 collective-permute-done.3
  84.9 0.9 fusion.12
  85.9 1.5 fusion.24
  88.5 5.7 %collective-permute-start.4 = (f32[2,1,4,2048]{3,2,1,0:T(4,128)S(1)}, f32[2,1,4,2048]{3,2,1,0:T(4,128)S(1)}, u32[]{:S(2)}, u32[]{:S(2)}) collective-permute-start(f32[2,1,4,2048]{3,2,1,0:T(4,128)S(1)} %slice.335), channel_id=1, source_target_pairs={{32,0},{64,32},{96,64},{128,96},{160,128},{192,160},{224,192},{256... | collective-permute-start | bytes 196616 | tf_op jit(solution)/shard_map/ppermute | solution.py:15
  94.2 1.5 collective-permute-start.5
  95.7 2.2 %subtract_reduce_fusion = (f32[3,4,4,2048]{3,2,1,0:T(4,128)S(1)}, f32[4,3,4,4,2048]{4,3,2,1,0:T(4,128)}) fusion(f32[4,3,4,4,2048]{4,3,2,1,0:T(4,128)S(1)} %copy-done.2, f32[3,4,4,2048]{3,2,1,0:T(4,128)S(1)} %copy-done.1, f32[4,4,4,2048]{3,2,1,0:T(4,128)S(1)} %copy-done.4, f32[4,4,4,2048]{3,2,1,0:T(4,128)S(1)} %copy.92, f32[3,4,4,2048]{3,2,1,0:T(4,128)S(1)} %bitcast.281), kind=kLoop, calls=%fused_computation.10 | loop fusion | flops 3047424 | bytes 5373952 | tf_op jit(solution)/shard_map/reduce_sum | solution.py:63
  98.0 2.9 %collective-permute-done.5 = f32[2,4,1,2048]{3,2,1,0:T(1,128)S(1)} collective-permute-done((f32[2,4,1,2048]{3,2,1,0:T(1,128)S(1)}, f32[2,4,1,2048]{3,2,1,0:T(1,128)S(1)}, u32[]{:S(2)}, u32[]{:S(2)}) %collective-permute-start.5) | collective-permute-done | bytes 65568 | tf_op jit(solution)/shard_map/ppermute | solution.py:15
  101.5 6.1 %gather_fusion.1 = f32[1024]{0:T(1024)S(1)} fusion(f32[32768]{0:T(1024)S(1)} %bitcast.276, s32[1024]{0:T(1024)S(1)} %broadcast_clamp_fusion), kind=kCustom, calls=%fused_computation.1 | custom fusion | bytes 12288 | tf_op jit(solution)/shard_map/gather | solution.py:135
  107.8 0.6 copy.98
  108.4 8.4 %all-to-all-start.1 = ((f32[32,2,32]{2,1,0:T(2,128)}), f32[32,2,32]{2,1,0:T(2,128)S(1)}, u32[]{:S(2)}, u32[]{:S(2)}) async-start(f32[32,2,32]{2,1,0:T(2,128)} %copy.98), calls=%async_computation.1 | async-start | bytes 65536 | tf_op jit(solution)/shard_map/all_to_all | solution.py:103
  117.6 12.7 %all-to-all-done.1 = f32[32,2,32]{2,1,0:T(2,128)S(1)} async-done(((f32[32,2,32]{2,1,0:T(2,128)}), f32[32,2,32]{2,1,0:T(2,128)S(1)}, u32[]{:S(2)}, u32[]{:S(2)}) %all-to-all-start.1) | async-done | bytes 8224 | tf_op jit(solution)/shard_map/all_to_all | solution.py:103
  130.5 1.0 gather_fusion.2
  132.1 0.7 fusion.99
  132.8 2.6 %scatter_custom_fusion.2 = f32[1024]{0:T(1024)S(1)} fusion(s32[512]{0:T(512)} %bitcast.323, f32[512]{0:T(512)S(1)} %bitcast.336, f32[]{:T(128)} %constant.82.clone.1), kind=kCustom, calls=%fused_computation.190 | custom fusion | bytes 4608 | tf_op jit(solution)/shard_map/scatter | solution.py:99
  135.4 0.7 transpose_reshape.3
  136.0 3.8 %all-to-all-start.2 = ((f32[32,1,32]{2,1,0:T(1,128)}), f32[32,1,32]{2,1,0:T(1,128)S(1)}, u32[]{:S(2)}, u32[]{:S(2)}) async-start(f32[32,1,32]{2,1,0:T(1,128)} %transpose_reshape.3), calls=%async_computation.2 | async-start | bytes 32768 | tf_op jit(solution)/shard_map/all_to_all | solution.py:103
  140.0 1.9 %collective-permute-start.7 = (f32[2,1,4,2048]{3,2,1,0:T(4,128)S(1)}, f32[2,1,4,2048]{3,2,1,0:T(4,128)S(1)}, u32[]{:S(2)}, u32[]{:S(2)}) collective-permute-start(f32[2,1,4,2048]{3,2,1,0:T(4,128)S(1)} %pad_maximum_fusion.10), channel_id=1, source_target_pairs={{0,32},{32,64},{64,96},{96,128},{128,160},{160,192},{192,224},{224... | collective-permute-start | bytes 196616 | tf_op jit(solution)/shard_map/ppermute | solution.py:15
  141.9 3.6 %collective-permute-start.6 = (f32[2,4,1,2048]{3,2,1,0:T(1,128)S(1)}, f32[2,4,1,2048]{3,2,1,0:T(1,128)S(1)}, u32[]{:S(2)}, u32[]{:S(2)}) collective-permute-start(f32[2,4,1,2048]{3,2,1,0:T(1,128)S(1)} %slice.293), channel_id=1, source_target_pairs={{0,1},{1,2},{2,3},{3,4},{4,5},{5,6},{6,7},{7,8},{8,9},{9,10},{10,1... | collective-permute-start | bytes 196616 | tf_op jit(solution)/shard_map/ppermute | solution.py:15
  145.5 7.6 %all-to-all-done.2 = f32[32,1,32]{2,1,0:T(1,128)S(1)} async-done(((f32[32,1,32]{2,1,0:T(1,128)}), f32[32,1,32]{2,1,0:T(1,128)S(1)}, u32[]{:S(2)}, u32[]{:S(2)}) %all-to-all-start.2) | async-done | bytes 4128 | tf_op jit(solution)/shard_map/all_to_all | solution.py:103
  153.2 0.6 broadcast.269
  153.7 0.7 reduce.21
  154.5 6.5 %scatter_custom_fusion.3 = f32[32768]{0:T(1024)S(1)} fusion(s32[1024]{0:T(1024)} %bitcast.331, f32[1024]{0:T(1024)S(1)} %reshape.325, f32[]{:T(128)} %constant.82.clone.1), kind=kCustom, calls=%fused_computation.142 | custom fusion | flops 1024 | bytes 131584 | tf_op jit(solution)/shard_map/scatter-add | solution.py:138
  162.5 0.8 divide_add_fusion
  (143 shorter events, 8.2 us)
Async XLA Ops:
  0.6 38.7 %copy-start = (f32[4,8]{1,0:T(4,128)S(1)}, f32[4,8]{1,0:T(4,128)}, u32[]{:S(2)}) copy-start(f32[4,8]{1,0:T(4,128)} %param.27) | copy-start | bytes 388
  0.6 36.6 %copy-start.1 = (f32[3,4,4,2048]{3,2,1,0:T(4,128)S(1)}, f32[3,4,4,2048]{3,2,1,0:T(4,128)}, u32[]{:S(2)}) copy-start(f32[3,4,4,2048]{3,2,1,0:T(4,128)} %param.20) | copy-start | bytes 1179652
  1.6 35.8 %copy-start.20 = (s32[4,4,2048]{2,1,0:T(4,128)S(1)}, s32[4,4,2048]{2,1,0:T(4,128)}, u32[]{:S(2)}) copy-start(s32[4,4,2048]{2,1,0:T(4,128)} %param.23) | copy-start | bytes 393220
  1.6 35.8 %copy-start.37 = (f32[8]{0:T(128)S(1)}, f32[8]{0:T(128)}, u32[]{:S(2)}) copy-start(f32[8]{0:T(128)} %param.24) | copy-start | bytes 100
  1.6 52.8 %collective-permute-start = (f32[2,1,4,2048]{3,2,1,0:T(4,128)S(1)}, f32[2,1,4,2048]{3,2,1,0:T(4,128)S(1)}, u32[]{:S(2)}, u32[]{:S(2)}) collective-permute-start(f32[2,1,4,2048]{3,2,1,0:T(4,128)S(1)} %slice.248), channel_id=1, source_target_pairs={{32,0},{64,32},{96,64},{128,96},{160,128},{192,160},{224,192},{256... | collective-permute-start | bytes 196616 | tf_op jit(solution)/shard_map/ppermute | solution.py:15
  7.2 47.2 %collective-permute-start.1 = (f32[2,4,1,2048]{3,2,1,0:T(1,128)}, f32[2,4,1,2048]{3,2,1,0:T(1,128)S(1)}, u32[]{:S(2)}, u32[]{:S(2)}) collective-permute-start(f32[2,4,1,2048]{3,2,1,0:T(1,128)} %slice.252), channel_id=1, source_target_pairs={{1,0},{2,1},{3,2},{4,3},{5,4},{6,5},{7,6},{8,7},{9,8},{10,9},{11,1... | collective-permute-start | bytes 196616 | tf_op jit(solution)/shard_map/ppermute | solution.py:15
  9.3 5.9 %copy-start.30 = (f32[1,511]{1,0:T(1,128)}, f32[1,511]{1,0:T(1,128)S(1)}, u32[]{:S(2)}) copy-start(f32[1,511]{1,0:T(1,128)S(1)} %slice.275) | copy-start | bytes 6136
  13.6 29.4 %copy-start.29 = (s32[512,1]{0,1:T(1,128)}, s32[512,1]{0,1:T(1,128)S(1)}, u32[]{:S(2)}) copy-start(s32[512,1]{0,1:T(1,128)S(1)} %compare_select_fusion.2) | copy-start | bytes 6148
  14.3 0.9 copy-start.27
  15.2 22.8 %copy-start.38 = (f32[8]{0:T(128)S(1)}, f32[8]{0:T(128)}, u32[]{:S(2)}) copy-start(f32[8]{0:T(128)} %param.25) | copy-start | bytes 100
  18.8 31.3 %all-to-all-start = ((f32[32,1,128]{2,1,0:T(1,128)}), f32[32,1,128]{2,1,0:T(1,128)}, u32[]{:S(2)}, u32[]{:S(2)}) async-start(f32[32,1,128]{2,1,0:T(1,128)} %reshape.367), calls=%async_computation | async-start | bytes 32768 | tf_op jit(solution)/shard_map/all_to_all | solution.py:103
  37.4 2.9 %copy-start.35 = (f32[4,8]{1,0:T(4,128)S(1)}, f32[4,8]{1,0:T(4,128)}, u32[]{:S(2)}) copy-start(f32[4,8]{1,0:T(4,128)} %param.26) | copy-start | bytes 388
  38.0 50.3 %copy-start.11 = (f32[1,4,4,2048]{3,2,1,0:T(4,128)}, f32[1,4,4,2048]{3,2,1,0:T(4,128)S(1)}, u32[]{:S(2)}) copy-start(f32[1,4,4,2048]{3,2,1,0:T(4,128)S(1)} %copy.114) | copy-start | bytes 393220
  39.9 1.4 copy-start.2
  41.3 1.6 copy-start.3
  52.3 2.1 %copy-start.22 = (f32[32,1,32]{2,1,0:T(1,128)}, f32[32,1,32]{2,1,0:T(1,128)S(1)}, u32[]{:S(2)}) copy-start(f32[32,1,32]{2,1,0:T(1,128)S(1)} %get-tuple-element.71) | copy-start | bytes 12292
  52.4 10.0 %copy-start.33 = (s32[1024,1]{0,1:T(1,128)}, s32[1024,1]{0,1:T(1,128)S(1)}, u32[]{:S(2)}) copy-start(s32[1024,1]{0,1:T(1,128)S(1)} %compare_select_fusion) | copy-start | bytes 12292
  54.4 1.8 %copy-start.15 = (f32[2,4,1,2048]{3,2,1,0:T(1,128)}, f32[2,4,1,2048]{3,2,1,0:T(1,128)S(1)}, u32[]{:S(2)}) copy-start(f32[2,4,1,2048]{3,2,1,0:T(1,128)S(1)} %collective-permute-done.1) | copy-start | bytes 196612
  56.2 28.8 %copy-start.5 = (f32[1,4,4,2048]{3,2,1,0:T(4,128)}, f32[1,4,4,2048]{3,2,1,0:T(4,128)S(1)}, u32[]{:S(2)}) copy-start(f32[1,4,4,2048]{3,2,1,0:T(4,128)S(1)} %get-tuple-element.68) | copy-start | bytes 393220
  75.3 9.6 %collective-permute-start.3 = (f32[2,1,4,2048]{3,2,1,0:T(4,128)}, f32[2,1,4,2048]{3,2,1,0:T(4,128)}, u32[]{:S(2)}, u32[]{:S(2)}) collective-permute-start(f32[2,1,4,2048]{3,2,1,0:T(4,128)} %pad_maximum_fusion.11), channel_id=1, source_target_pairs={{0,32},{32,64},{64,96},{96,128},{128,160},{160,192},{192,224},{224... | collective-permute-start | bytes 196616 | tf_op jit(solution)/shard_map/ppermute | solution.py:15
  80.4 5.5 %collective-permute-start.2 = (f32[2,4,1,2048]{3,2,1,0:T(1,128)}, f32[2,4,1,2048]{3,2,1,0:T(1,128)S(1)}, u32[]{:S(2)}, u32[]{:S(2)}) collective-permute-start(f32[2,4,1,2048]{3,2,1,0:T(1,128)} %slice.262), channel_id=1, source_target_pairs={{0,1},{1,2},{2,3},{3,4},{4,5},{5,6},{6,7},{7,8},{8,9},{9,10},{10,1... | collective-permute-start | bytes 196616 | tf_op jit(solution)/shard_map/ppermute | solution.py:15
  85.8 1.7 %copy-start.7 = (f32[3,4,4,2048]{3,2,1,0:T(4,128)S(1)}, f32[3,4,4,2048]{3,2,1,0:T(4,128)}, u32[]{:S(2)}) copy-start(f32[3,4,4,2048]{3,2,1,0:T(4,128)} %subtract_reduce_fusion.1) | copy-start | bytes 1179652
  85.8 1.7 %copy-start.13 = (f32[4,4,2048]{2,1,0:T(4,128)S(1)}, f32[4,4,2048]{2,1,0:T(4,128)}, u32[]{:S(2)}) copy-start(f32[4,4,2048]{2,1,0:T(4,128)} %bitcast_multiply_fusion) | copy-start | bytes 393220
  87.3 1.0 copy-start.9
  87.4 1.0 copy-start.21
  87.5 8.1 %copy-start.4 = (f32[4,4,4,2048]{3,2,1,0:T(4,128)S(1)}, f32[4,4,4,2048]{3,2,1,0:T(4,128)}, u32[]{:S(2)}) copy-start(f32[4,4,4,2048]{3,2,1,0:T(4,128)} %copy-done.3) | copy-start | bytes 1572868
  88.5 12.4 %copy-start.6 = (f32[1,4,4,2048]{3,2,1,0:T(4,128)S(1)}, f32[1,4,4,2048]{3,2,1,0:T(4,128)}, u32[]{:S(2)}) copy-start(f32[1,4,4,2048]{3,2,1,0:T(4,128)} %copy-done.5) | copy-start | bytes 393220
  88.5 9.5 %collective-permute-start.4 = (f32[2,1,4,2048]{3,2,1,0:T(4,128)S(1)}, f32[2,1,4,2048]{3,2,1,0:T(4,128)S(1)}, u32[]{:S(2)}, u32[]{:S(2)}) collective-permute-start(f32[2,1,4,2048]{3,2,1,0:T(4,128)S(1)} %slice.335), channel_id=1, source_target_pairs={{32,0},{64,32},{96,64},{128,96},{160,128},{192,160},{224,192},{256... | collective-permute-start | bytes 196616 | tf_op jit(solution)/shard_map/ppermute | solution.py:15
  94.2 6.7 %collective-permute-start.5 = (f32[2,4,1,2048]{3,2,1,0:T(1,128)S(1)}, f32[2,4,1,2048]{3,2,1,0:T(1,128)S(1)}, u32[]{:S(2)}, u32[]{:S(2)}) collective-permute-start(f32[2,4,1,2048]{3,2,1,0:T(1,128)S(1)} %slice.285), channel_id=1, source_target_pairs={{1,0},{2,1},{3,2},{4,3},{5,4},{6,5},{7,6},{8,7},{9,8},{10,9},{11,1... | collective-permute-start | bytes 196616 | tf_op jit(solution)/shard_map/ppermute | solution.py:15
  98.0 3.1 %copy-start.16 = (f32[2,1,4,2048]{3,2,1,0:T(4,128)}, f32[2,1,4,2048]{3,2,1,0:T(4,128)S(1)}, u32[]{:S(2)}) copy-start(f32[2,1,4,2048]{3,2,1,0:T(4,128)S(1)} %collective-permute-done.4) | copy-start | bytes 196612
  100.9 0.6 copy-start.18
  101.5 6.2 %copy-start.23 = (f32[1,32,32]{2,1,0:T(8,128)S(1)}, f32[1,32,32]{2,1,0:T(8,128)}, u32[]{:S(2)}) copy-start(f32[1,32,32]{2,1,0:T(8,128)} %get-tuple-element.49) | copy-start | bytes 12292
  101.5 15.6 %copy-start.17 = (f32[2,1,4,2048]{3,2,1,0:T(4,128)S(1)}, f32[2,1,4,2048]{3,2,1,0:T(4,128)}, u32[]{:S(2)}) copy-start(f32[2,1,4,2048]{3,2,1,0:T(4,128)} %copy-done.16) | copy-start | bytes 196612
  101.5 15.6 %copy-start.19 = (f32[2,4,1,2048]{3,2,1,0:T(1,128)S(1)}, f32[2,4,1,2048]{3,2,1,0:T(1,128)}, u32[]{:S(2)}) copy-start(f32[2,4,1,2048]{3,2,1,0:T(1,128)} %copy-done.18) | copy-start | bytes 196612
  108.4 21.8 %all-to-all-start.1 = ((f32[32,2,32]{2,1,0:T(2,128)}), f32[32,2,32]{2,1,0:T(2,128)S(1)}, u32[]{:S(2)}, u32[]{:S(2)}) async-start(f32[32,2,32]{2,1,0:T(2,128)} %copy.98), calls=%async_computation.1 | async-start | bytes 65536 | tf_op jit(solution)/shard_map/all_to_all | solution.py:103
  117.1 13.4 %copy-start.34 = (s32[1024]{0:T(1024)S(1)}, s32[1024]{0:T(1024)}, u32[]{:S(2)}) copy-start(s32[1024]{0:T(1024)} %pad_clamp_fusion) | copy-start | bytes 12292
  117.2 14.5 %copy-start.24 = (f32[1,512]{1,0:T(1,128)S(1)}, f32[1,512]{1,0:T(1,128)}, u32[]{:S(2)}) copy-start(f32[1,512]{1,0:T(1,128)} %param.31) | copy-start | bytes 6148
  117.2 14.5 %copy-start.25 = (f32[1,512]{1,0:T(1,128)S(1)}, f32[1,512]{1,0:T(1,128)}, u32[]{:S(2)}) copy-start(f32[1,512]{1,0:T(1,128)} %param.32) | copy-start | bytes 6148
  117.2 14.5 %copy-start.26 = (f32[1,512]{1,0:T(1,128)S(1)}, f32[1,512]{1,0:T(1,128)}, u32[]{:S(2)}) copy-start(f32[1,512]{1,0:T(1,128)} %param.30) | copy-start | bytes 6148
  117.2 14.5 %copy-start.31 = (f32[1,511]{1,0:T(1,128)S(1)}, f32[1,511]{1,0:T(1,128)}, u32[]{:S(2)}) copy-start(f32[1,511]{1,0:T(1,128)} %copy-done.30) | copy-start | bytes 6136
  117.2 14.6 %copy-start.32 = (f32[1,512]{1,0:T(1,128)S(1)}, f32[1,512]{1,0:T(1,128)}, u32[]{:S(2)}) copy-start(f32[1,512]{1,0:T(1,128)} %param.33) | copy-start | bytes 6148
  117.2 14.7 %copy-start.28 = (f32[1,512]{1,0:T(1,128)S(1)}, f32[1,512]{1,0:T(1,128)}, u32[]{:S(2)}) copy-start(f32[1,512]{1,0:T(1,128)} %copy-done.27) | copy-start | bytes 6148
  117.5 43.6 %copy-start.8 = (f32[3,4,4,2048]{3,2,1,0:T(4,128)}, f32[3,4,4,2048]{3,2,1,0:T(4,128)S(1)}, u32[]{:S(2)}) copy-start(f32[3,4,4,2048]{3,2,1,0:T(4,128)S(1)} %pad_maximum_fusion.1) | copy-start | bytes 1179652
  130.2 31.0 %copy-start.10 = (f32[4,4,2048]{2,1,0:T(4,128)S(1)}, f32[4,4,2048]{2,1,0:T(4,128)}, u32[]{:S(2)}) copy-start(f32[4,4,2048]{2,1,0:T(4,128)} %copy-done.9) | copy-start | bytes 393220
  132.8 28.8 %copy-start.36 = (f32[1,512]{1,0:T(1,128)}, f32[1,512]{1,0:T(1,128)S(1)}, u32[]{:S(2)}) copy-start(f32[1,512]{1,0:T(1,128)S(1)} %get-tuple-element.48) | copy-start | bytes 6148
  136.0 17.1 %all-to-all-start.2 = ((f32[32,1,32]{2,1,0:T(1,128)}), f32[32,1,32]{2,1,0:T(1,128)S(1)}, u32[]{:S(2)}, u32[]{:S(2)}) async-start(f32[32,1,32]{2,1,0:T(1,128)} %transpose_reshape.3), calls=%async_computation.2 | async-start | bytes 32768 | tf_op jit(solution)/shard_map/all_to_all | solution.py:103
  140.0 21.1 %collective-permute-start.7 = (f32[2,1,4,2048]{3,2,1,0:T(4,128)S(1)}, f32[2,1,4,2048]{3,2,1,0:T(4,128)S(1)}, u32[]{:S(2)}, u32[]{:S(2)}) collective-permute-start(f32[2,1,4,2048]{3,2,1,0:T(4,128)S(1)} %pad_maximum_fusion.10), channel_id=1, source_target_pairs={{0,32},{32,64},{64,96},{96,128},{128,160},{160,192},{192,224},{224... | collective-permute-start | bytes 196616 | tf_op jit(solution)/shard_map/ppermute | solution.py:15
  141.9 19.3 %collective-permute-start.6 = (f32[2,4,1,2048]{3,2,1,0:T(1,128)S(1)}, f32[2,4,1,2048]{3,2,1,0:T(1,128)S(1)}, u32[]{:S(2)}, u32[]{:S(2)}) collective-permute-start(f32[2,4,1,2048]{3,2,1,0:T(1,128)S(1)} %slice.293), channel_id=1, source_target_pairs={{0,1},{1,2},{2,3},{3,4},{4,5},{5,6},{6,7},{7,8},{8,9},{9,10},{10,1... | collective-permute-start | bytes 196616 | tf_op jit(solution)/shard_map/ppermute | solution.py:15
  161.2 0.9 copy-start.14
  161.6 0.9 copy-start.12

commit v2 on v1

--- a/solution.py
+++ b/solution.py
@@ -94,17 +94,22 @@
     cell_total = grid_shape[0] * grid_shape[1] * grid_shape[2]
     single_zero = jnp.zeros((1,), jnp.float32)
 
+    slot_total = n_gy * capacity
+    highest = lax.Precision.HIGHEST
+    slot_hot = (jnp.arange(slot_total, dtype=jnp.int32)[:, None] == slot_at[None, :]).astype(jnp.float32)
+    slot_used = jnp.sum(slot_hot, axis=1)
+
     def to_slots(rows, fill):
-        empty = jnp.broadcast_to(jnp.asarray(fill, jnp.float32)[:, None], (rows.shape[0], n_gy * capacity))
-        buffer = empty.at[:, slot_at].set(rows)
+        placed = jnp.einsum("fs,ts->ft", rows, slot_hot, precision=highest)
+        buffer = placed + jnp.asarray(fill, jnp.float32)[:, None] * (1.0 - slot_used)[None, :]
         return buffer.reshape(rows.shape[0], n_gy, capacity).transpose(1, 0, 2)
 
     def exchange(blocks):
         return lax.all_to_all(blocks, "gy", split_axis=0, concat_axis=0, tiled=True)
 
     def from_slots(blocks):
-        flat = blocks.transpose(1, 0, 2).reshape(blocks.shape[1], n_gy * capacity)
-        return flat[:, slot_at]
+        flat = blocks.transpose(1, 0, 2).reshape(blocks.shape[1], slot_total)
+        return jnp.einsum("ft,ts->fs", flat, slot_hot, precision=highest)
 
     gain_row = wire_gain[0]
     cap_row = wire_cap[0]
@@ -120,11 +125,15 @@
     recv_gain = incoming[:, 2, :].reshape(-1)
     recv_drop = incoming[:, 3, :].reshape(-1)
     valid_flat = is_valid.reshape(-1)
+    lanes = 128
+    plane_rows = cell_total // lanes
+    row_hot = ((safe_cells // lanes)[:, None] == jnp.arange(plane_rows, dtype=jnp.int32)[None, :]).astype(jnp.float32)
+    row_hot = row_hot * valid_flat.astype(jnp.float32)[:, None]
+    lane_hot = (safe_cells % lanes)[:, None] == jnp.arange(lanes, dtype=jnp.int32)[None, :]
 
     material_hot = (
         material[None] == jnp.arange(eps_inf.shape[0], dtype=jnp.int32)[:, None, None, None]
     ).astype(jnp.float32)
-    highest = lax.Precision.HIGHEST
     eps_cell = jnp.einsum("m,mxyz->xyz", eps_inf, material_hot, precision=highest)
     sigma_cell = jnp.einsum("m,mxyz->xyz", conductivity, material_hot, precision=highest)
     strength_cell = jnp.einsum("pm,mxyz->pxyz", pole_strength, material_hot, precision=highest)
@@ -132,10 +141,12 @@
     cells = (eps_cell, sigma_cell, strength_cell, decay_cell)
 
     def sample(e_now):
-        return jnp.where(valid_flat, e_now[2].reshape(-1)[safe_cells], 0.0)
+        picked = jnp.dot(row_hot, e_now[2].reshape(plane_rows, lanes), precision=highest)
+        return jnp.sum(jnp.where(lane_hot, picked, 0.0), axis=1)
 
     def wire_of(values):
-        return jnp.zeros((cell_total,), jnp.float32).at[safe_cells].add(values).reshape(grid_shape)
+        spread = jnp.where(lane_hot, values[:, None], 0.0)
+        return jnp.einsum("kr,kl->rl", row_hot, spread, precision=highest).reshape(grid_shape)
 
     sample_0 = sample(e_field)
     h_field = magnetic_update(e_field, h_field)

time: 164 us -> 146 us (0.89)
  local copies, waits for them, and re-layouts: 35.9 us -> 20.2 us
  other arithmetic: 38.5 us -> 23 us
  matrix products: 2.33 us -> 14.5 us
  starting transfers between devices: 53.6 us -> 59.5 us
  waiting for transfers between devices: 31.4 us -> 26.1 us
    gather x6 -> x0, local copies, waits for them, and re-layouts: 13.6 us -> none  [the longest x4 12.4 us: sample(): return jnp.where(valid_flat, e_now[2].reshape(-1)[safe_cells], 0.0)]
    scatter-add x2 -> x0, other arithmetic: 13 us -> none  [wire_of(): jnp.zeros((cell_total,), jnp.float32).at[safe_cells].add(values)]
    dot_general x0 -> x7, matrix products: none -> 11.3 us  [the longest x2 4.89 us: wire_of(): jnp.einsum('kr,kl->rl', row_hot, spread, precision=highest)]
    all_to_all x3, waiting for transfers between devices: 27 us -> 20.3 us  [exchange(): return lax.all_to_all(blocks, 'gy', split_axis=0, concat_axis=0, tiled=True)]
    scatter x2 -> x0, local copies, waits for them, and re-layouts: 4.5 us -> none  [to_slots(): buffer = empty.at[:, slot_at].set(rows)]
    all_to_all x3, starting transfers between devices: 30.7 us -> 35 us  [exchange(): return lax.all_to_all(blocks, 'gy', split_axis=0, concat_axis=0, tiled=True)]
    another operation x4 -> x6, local copies, waits for them, and re-layouts: 0.44 us -> 3.36 us  [the longest x2 1.7 us: sample(): e_now[2].reshape(plane_rows, lanes)]
    unnamed x2 -> x0, other arithmetic: 1.89 us -> none
  transfers between devices with their start and end apart: 11 -> 11, of which waited for: 5 -> 4; matrix products, arithmetic and copies ran while one was open for 23% -> 22% of each run, Pallas kernels for 0% -> 0%
where the time goes in v2:
time: 146 us; the launch traced here: 145 us
  starting transfers between devices  59.5 us (41%)
  waiting for transfers between devices  26.1 us (18%)
  other arithmetic  23 us (16%)
  local copies, waits for them, and re-layouts  20.2 us (14%)
  matrix products  14.5 us (10%)
  between operations  1.5 us (1%)
    all_to_all x3, starting transfers between devices, exchange(): return lax.all_to_all(blocks, 'gy', split_axis=0, concat_axis=0, tiled=True)  35 us
    ppermute x8, starting transfers between devices, passed_along(): lax.ppermute(value, axis, [(source, source + steps) for source in range(f...  24.5 us
    all_to_all x3, waiting for transfers between devices, exchange(): return lax.all_to_all(blocks, 'gy', split_axis=0, concat_axis=0, tiled=True)  20.3 us
    ppermute x8, waiting for transfers between devices, passed_along(): lax.ppermute(value, axis, [(source, source + steps) for source in range(f...  5.82 us
    dot_general x2, matrix products, wire_of(): jnp.einsum('kr,kl->rl', row_hot, spread, precision=highest)  4.89 us
    reduce_sum x2, other arithmetic, electric_update(): change = jnp.sum(polar_new - polarization, axis=0)  4.54 us
    dot_general x2, matrix products, sample(): jnp.dot(row_hot, e_now[2].reshape(plane_rows, lanes), precision=highest)  2.93 us
  transfers between devices with their start and end apart: 11, of which 4 were waited for; matrix products, arithmetic and copies ran while one was open for 22% of the time, Pallas kernels for 0%

profile of v2, /device:TPU:16, one launch (start us, length us, event | category | flops | bytes accessed | tf_op | source)
XLA Modules:
  0.0 144.8 jit_solution(258483171022923644)
XLA Ops:
  0.7 0.8 slice.273
  1.4 0.7 convert_element_type.39
  2.1 0.7 fusion.126
  2.8 1.2 reduce-window.6
  4.2 0.8 fusion.125
  5.0 0.7 multiply_add_fusion.6
  6.0 0.8 fusion.141
  6.8 1.7 %fusion.30 = f32[4,1024]{1,0:T(4,128)S(1)} fusion(s32[512]{0:T(512)S(1)} %multiply_add_fusion.6, f32[1,512]{1,0:T(1,128)S(1)} %fusion.141, f32[1,512]{1,0:T(1,128)} %param.32, f32[1,512]{1,0:T(1,128)} %param.30, f32[1,512]{1,0:T(1,128)S(1)} %convert_element_type.39, f32[1024]{0:T(1024)S(1)} %broadcast_subtract_fusion, f32[4]{0:T(128)} %constant.114.clone), kind=kOutput, calls=%fused_computation.26 | convolution fusion | flops 25704448 | bytes 30736 | tf_op jit(solution)/shard_map/fs,ts->ft/dot_general | solution.py:103
  8.7 0.7 reshape.290
  9.4 16.2 %all-to-all-start = ((f32[32,1,128]{2,1,0:T(1,128)}), f32[32,1,128]{2,1,0:T(1,128)S(1)}, u32[]{:S(2)}, u32[]{:S(2)}) async-start(f32[32,1,128]{2,1,0:T(1,128)} %reshape.290), calls=%async_computation | async-start | bytes 32768 | tf_op jit(solution)/shard_map/all_to_all | solution.py:108
  25.6 0.8 slice.248
  26.4 3.9 %collective-permute-start = (f32[2,1,4,2048]{3,2,1,0:T(4,128)S(1)}, f32[2,1,4,2048]{3,2,1,0:T(4,128)S(1)}, u32[]{:S(2)}, u32[]{:S(2)}) collective-permute-start(f32[2,1,4,2048]{3,2,1,0:T(4,128)S(1)} %slice.248), channel_id=1, source_target_pairs={{32,0},{64,32},{96,64},{128,96},{160,128},{192,160},{224,192},{256... | collective-permute-start | bytes 196616 | tf_op jit(solution)/shard_map/ppermute | solution.py:15
  30.3 1.0 slice.252
  31.3 1.3 collective-permute-start.1
  32.6 1.5 %fusion.35 = f32[1,4,4,2048]{3,0,2,1:T(1,128)S(1)} fusion(s32[4,4,2048]{2,1,0:T(4,128)} %param.23, f32[8]{0:T(128)} %param.25), kind=kOutput, calls=%fused_computation.33 | convolution fusion | flops 3407872 | bytes 262176 | tf_op jit(solution)/shard_map/m,mxyz->xyz/dot_general | solution.py:138
  34.1 0.7 bitcast_multiply_fusion
  34.8 0.6 convolution_bitcast_fusion.1
  35.8 0.6 fusion
  37.0 1.6 %subtract_reduce_fusion.1 = f32[3,4,4,2048]{3,2,1,0:T(4,128)} fusion(f32[4,3,4,4,2048]{4,3,2,1,0:T(4,128)S(1)} %copy-done.2, f32[3,4,4,2048]{3,2,1,0:T(4,128)S(1)} %copy-done.1, f32[4,4,4,2048]{3,2,1,0:T(4,128)S(1)} %copy.36, f32[4,4,4,2048]{3,2,1,0:T(4,128)S(1)} %copy.35), kind=kLoop, calls=%fused_computation.18 | loop fusion | flops 1867776 | bytes 3407872 | tf_op jit(solution)/shard_map/reduce_sum | solution.py:63
  38.6 0.6 fusion.34
  39.2 0.7 copy.51
  40.5 0.7 reduce.26
  41.4 0.6 compare_convert_fusion
  42.0 0.6 add_select_fusion
  42.7 0.7 reshape_squeeze.18
  43.4 0.7 reshape_squeeze.16
  44.1 0.7 reshape_squeeze.15
  44.7 1.7 %fusion.169 = (f32[1,4,4,2048]{3,2,1,0:T(4,128)}, f32[1,4,4,2048]{3,2,1,0:T(4,128)S(1)}, f32[4,4,2048]{2,1,0:T(4,128)S(1)}, f32[4,4,2048]{2,1,0:T(4,128)S(1)}) fusion(f32[3,4,4,2048]{3,2,1,0:T(4,128)S(1)} %copy-done.1, f32[2,4,1,2048]{3,2,1,0:T(1,128)S(1)} %collective-permute-done.1, f32[2,4,3,2048]{3,2,1,0:T(4,128)S(1)} %slice.251, ...), kind=kLoop, calls=%fused_computation.245 | loop fusion | flops 229376 | bytes 1572864 | tf_op jit(solution)/shard_map/slice | solution.py:44
  46.4 1.6 %reshape_squeeze.17 = f32[256,128]{1,0:T(8,128)} reshape(f32[1,4,4,2048]{3,2,1,0:T(4,128)} %get-tuple-element.50) | data formatting | bytes 262144 | tf_op jit(solution)/shard_map/reshape;squeeze | solution.py:144
  48.4 1.2 fusion.112
  49.6 0.6 pad_maximum_fusion.11
  50.3 1.9 %collective-permute-start.3 = (f32[2,1,4,2048]{3,2,1,0:T(4,128)}, f32[2,1,4,2048]{3,2,1,0:T(4,128)S(1)}, u32[]{:S(2)}, u32[]{:S(2)}) collective-permute-start(f32[2,1,4,2048]{3,2,1,0:T(4,128)} %pad_maximum_fusion.11), channel_id=1, source_target_pairs={{0,32},{32,64},{64,96},{96,128},{128,160},{160,192},{192,224},{224... | collective-permute-start | bytes 196616 | tf_op jit(solution)/shard_map/ppermute | solution.py:15
  52.2 0.8 pad_maximum_fusion
  53.0 1.5 %fusion.21 = f32[1024]{0:T(1024)S(1)} fusion(f32[256,128]{1,0:T(8,128)S(1)} %copy-done.15, f32[1024]{0:T(1024)S(1)} %copy-done.31, s32[1024]{0:T(1024)S(1)} %copy-done.29, s32[1024]{0:T(1024)S(1)} %copy-done.27), kind=kOutput, calls=%fused_computation.23 | convolution fusion | flops 403569664 | bytes 147456 | tf_op jit(solution)/shard_map/dot_general | solution.py:144
  54.6 0.6 copy-done.24
  55.1 2.8 %fusion.24 = f32[256,128]{1,0:T(8,128)} fusion(f32[1024]{0:T(1024)S(1)} %copy-done.31, s32[1024]{0:T(1024)S(1)} %copy-done.29, f32[1024]{0:T(1024)S(1)} %multiply_add_fusion.3, s32[1024]{0:T(1024)S(1)} %copy-done.27), kind=kOutput, calls=%fused_computation.24 | convolution fusion | flops 403472384 | bytes 147456 | tf_op jit(solution)/shard_map/kr,kl->rl/dot_general | solution.py:149
  57.9 1.4 stack.79
  59.3 1.7 %slice.262 = f32[2,4,1,2048]{3,2,1,0:T(1,128)} slice(f32[3,4,4,2048]{3,2,1,0:T(4,128)} %pad_maximum_fusion), slice={[0:3:2], [0:4:1], [3:4:1], [0:2048:1]} | slice | bytes 131072 | tf_op jit(solution)/shard_map/slice | solution.py:37
  60.9 1.7 %slice.263 = f32[2,4,3,2048]{3,2,1,0:T(4,128)} slice(f32[3,4,4,2048]{3,2,1,0:T(4,128)} %pad_maximum_fusion), slice={[0:3:2], [0:4:1], [0:3:1], [0:2048:1]} | slice | bytes 393216 | tf_op jit(solution)/shard_map/slice | solution.py:38
  62.6 1.6 %mul.216 = f32[1,4,4,2048]{3,2,1,0:T(4,128)} reshape(f32[256,128]{1,0:T(8,128)} %fusion.24) | data formatting | bytes 262144 | tf_op jit(solution)/shard_map/mul | solution.py:65
  64.2 4.8 %collective-permute-start.2 = (f32[2,4,1,2048]{3,2,1,0:T(1,128)}, f32[2,4,1,2048]{3,2,1,0:T(1,128)S(1)}, u32[]{:S(2)}, u32[]{:S(2)}) collective-permute-start(f32[2,4,1,2048]{3,2,1,0:T(1,128)} %slice.262), channel_id=1, source_target_pairs={{0,1},{1,2},{2,3},{3,4},{4,5},{5,6},{6,7},{7,8},{8,9},{9,10},{10,1... | collective-permute-start | bytes 196616 | tf_op jit(solution)/shard_map/ppermute | solution.py:15
  69.1 1.9 %collective-permute-done.2 = f32[2,4,1,2048]{3,2,1,0:T(1,128)S(1)} collective-permute-done((f32[2,4,1,2048]{3,2,1,0:T(1,128)}, f32[2,4,1,2048]{3,2,1,0:T(1,128)S(1)}, u32[]{:S(2)}, u32[]{:S(2)}) %collective-permute-start.2) | collective-permute-done | bytes 65568 | tf_op jit(solution)/shard_map/ppermute | solution.py:15
  71.0 1.4 fusion.77
  72.8 0.5 copy-done.14
  73.6 5.8 %collective-permute-start.4 = (f32[2,1,4,2048]{3,2,1,0:T(4,128)S(1)}, f32[2,1,4,2048]{3,2,1,0:T(4,128)S(1)}, u32[]{:S(2)}, u32[]{:S(2)}) collective-permute-start(f32[2,1,4,2048]{3,2,1,0:T(4,128)S(1)} %slice.329), channel_id=1, source_target_pairs={{32,0},{64,32},{96,64},{128,96},{160,128},{192,160},{224,192},{256... | collective-permute-start | bytes 196616 | tf_op jit(solution)/shard_map/ppermute | solution.py:15
  79.4 1.3 collective-permute-start.5
  80.7 2.9 %subtract_reduce_fusion = (f32[3,4,4,2048]{3,2,1,0:T(4,128)}, f32[4,3,4,4,2048]{4,3,2,1,0:T(4,128)}) fusion(f32[4,3,4,4,2048]{4,3,2,1,0:T(4,128)S(1)} %copy-done.2, f32[3,4,4,2048]{3,2,1,0:T(4,128)S(1)} %copy-done.1, f32[4,4,4,2048]{3,2,1,0:T(4,128)S(1)} %copy-done.4, f32[4,4,4,2048]{3,2,1,0:T(4,128)S(1)} %copy.35, f32[3,4,4,2048]{3,2,1,0:T(4,128)S(1)} %bitcast.260), kind=kLoop, calls=%fused_computation.16 | loop fusion | flops 3047424 | bytes 5373952 | tf_op jit(solution)/shard_map/reduce_sum | solution.py:63
  83.8 3.9 %collective-permute-done.5 = f32[2,4,1,2048]{3,2,1,0:T(1,128)S(1)} collective-permute-done((f32[2,4,1,2048]{3,2,1,0:T(1,128)S(1)}, f32[2,4,1,2048]{3,2,1,0:T(1,128)S(1)}, u32[]{:S(2)}, u32[]{:S(2)}) %collective-permute-start.5) | collective-permute-done | bytes 65568 | tf_op jit(solution)/shard_map/ppermute | solution.py:15
  87.9 1.5 %fusion.18 = f32[1024]{0:T(1024)S(1)} fusion(f32[256,128]{1,0:T(8,128)S(1)} %reshape_squeeze.19, f32[1024]{0:T(1024)S(1)} %copy-done.32, s32[1024]{0:T(1024)S(1)} %copy-done.30, s32[1024]{0:T(1024)S(1)} %copy-done.28), kind=kOutput, calls=%fused_computation.22 | convolution fusion | flops 403569664 | bytes 147456 | tf_op jit(solution)/shard_map/dot_general | solution.py:144
  89.5 0.7 maximum_bitcast_fusion
  90.1 15.0 %all-to-all-start.1 = ((f32[32,2,32]{2,1,0:T(2,128)}), f32[32,2,32]{2,1,0:T(2,128)S(1)}, u32[]{:S(2)}, u32[]{:S(2)}) async-start(f32[32,2,32]{2,1,0:T(2,128)} %maximum_bitcast_fusion), calls=%async_computation.1 | async-start | bytes 65536 | tf_op jit(solution)/shard_map/all_to_all | solution.py:108
  105.8 12.7 %all-to-all-done.1 = f32[32,2,32]{2,1,0:T(2,128)S(1)} async-done(((f32[32,2,32]{2,1,0:T(2,128)}), f32[32,2,32]{2,1,0:T(2,128)S(1)}, u32[]{:S(2)}, u32[]{:S(2)}) %all-to-all-start.1) | async-done | bytes 8224 | tf_op jit(solution)/shard_map/all_to_all | solution.py:108
  118.6 0.7 fusion.2
  119.8 0.7 fusion.157
  120.5 1.0 fusion.1
  121.5 0.7 transpose_reshape.3
  122.2 3.8 %all-to-all-start.2 = ((f32[32,1,32]{2,1,0:T(1,128)}), f32[32,1,32]{2,1,0:T(1,128)S(1)}, u32[]{:S(2)}, u32[]{:S(2)}) async-start(f32[32,1,32]{2,1,0:T(1,128)} %transpose_reshape.3), calls=%async_computation.2 | async-start | bytes 32768 | tf_op jit(solution)/shard_map/all_to_all | solution.py:108
  126.1 1.9 %collective-permute-start.7 = (f32[2,1,4,2048]{3,2,1,0:T(4,128)S(1)}, f32[2,1,4,2048]{3,2,1,0:T(4,128)S(1)}, u32[]{:S(2)}, u32[]{:S(2)}) collective-permute-start(f32[2,1,4,2048]{3,2,1,0:T(4,128)S(1)} %pad_maximum_fusion.10), channel_id=1, source_target_pairs={{0,32},{32,64},{64,96},{96,128},{128,160},{160,192},{192,224},{224... | collective-permute-start | bytes 196616 | tf_op jit(solution)/shard_map/ppermute | solution.py:15
  128.0 3.6 %collective-permute-start.6 = (f32[2,4,1,2048]{3,2,1,0:T(1,128)S(1)}, f32[2,4,1,2048]{3,2,1,0:T(1,128)S(1)}, u32[]{:S(2)}, u32[]{:S(2)}) collective-permute-start(f32[2,4,1,2048]{3,2,1,0:T(1,128)S(1)} %slice.293), channel_id=1, source_target_pairs={{0,1},{1,2},{2,3},{3,4},{4,5},{5,6},{6,7},{7,8},{8,9},{9,10},{10,1... | collective-permute-start | bytes 196616 | tf_op jit(solution)/shard_map/ppermute | solution.py:15
  131.6 7.6 %all-to-all-done.2 = f32[32,1,32]{2,1,0:T(1,128)S(1)} async-done(((f32[32,1,32]{2,1,0:T(1,128)}), f32[32,1,32]{2,1,0:T(1,128)S(1)}, u32[]{:S(2)}, u32[]{:S(2)}) %all-to-all-start.2) | async-done | bytes 4128 | tf_op jit(solution)/shard_map/all_to_all | solution.py:108
  139.2 0.5 broadcast.262
  139.7 0.7 reduce.25
  140.5 2.1 %fusion.27 = f32[256,128]{1,0:T(8,128)S(1)} fusion(f32[1024]{0:T(1024)S(1)} %copy-done.32, s32[1024]{0:T(1024)S(1)} %copy-done.30, f32[1024]{0:T(1024)S(1)} %broadcast_in_dim.27, s32[1024]{0:T(1024)S(1)} %copy-done.28), kind=kOutput, calls=%fused_computation.25 | convolution fusion | flops 403472384 | bytes 147456 | tf_op jit(solution)/shard_map/kr,kl->rl/dot_general | solution.py:149
  144.0 0.8 divide_add_fusion
  (131 shorter events, 6.5 us)
Async XLA Ops:
  0.6 34.2 %copy-start = (f32[4,8]{1,0:T(4,128)S(1)}, f32[4,8]{1,0:T(4,128)}, u32[]{:S(2)}) copy-start(f32[4,8]{1,0:T(4,128)} %param.27) | copy-start | bytes 388
  0.6 34.2 %copy-start.13 = (s32[4,4,2048]{2,1,0:T(4,128)S(1)}, s32[4,4,2048]{2,1,0:T(4,128)}, u32[]{:S(2)}) copy-start(s32[4,4,2048]{2,1,0:T(4,128)} %param.23) | copy-start | bytes 393220
  5.7 2.8 %copy-start.25 = (s32[512]{0:T(512)}, s32[512]{0:T(512)S(1)}, u32[]{:S(2)}) copy-start(s32[512]{0:T(512)S(1)} %multiply_add_fusion.6) | copy-start | bytes 6148
  8.5 27.3 %copy-start.33 = (f32[4,8]{1,0:T(4,128)S(1)}, f32[4,8]{1,0:T(4,128)}, u32[]{:S(2)}) copy-start(f32[4,8]{1,0:T(4,128)} %param.26) | copy-start | bytes 388
  9.4 30.6 %all-to-all-start = ((f32[32,1,128]{2,1,0:T(1,128)}), f32[32,1,128]{2,1,0:T(1,128)S(1)}, u32[]{:S(2)}, u32[]{:S(2)}) async-start(f32[32,1,128]{2,1,0:T(1,128)} %reshape.290), calls=%async_computation | async-start | bytes 32768 | tf_op jit(solution)/shard_map/all_to_all | solution.py:108
  26.4 18.3 %collective-permute-start = (f32[2,1,4,2048]{3,2,1,0:T(4,128)S(1)}, f32[2,1,4,2048]{3,2,1,0:T(4,128)S(1)}, u32[]{:S(2)}, u32[]{:S(2)}) collective-permute-start(f32[2,1,4,2048]{3,2,1,0:T(4,128)S(1)} %slice.248), channel_id=1, source_target_pairs={{32,0},{64,32},{96,64},{128,96},{160,128},{192,160},{224,192},{256... | collective-permute-start | bytes 196616 | tf_op jit(solution)/shard_map/ppermute | solution.py:15
  31.3 13.4 %collective-permute-start.1 = (f32[2,4,1,2048]{3,2,1,0:T(1,128)S(1)}, f32[2,4,1,2048]{3,2,1,0:T(1,128)S(1)}, u32[]{:S(2)}, u32[]{:S(2)}) collective-permute-start(f32[2,4,1,2048]{3,2,1,0:T(1,128)S(1)} %slice.252), channel_id=1, source_target_pairs={{1,0},{2,1},{3,2},{4,3},{5,4},{6,5},{7,6},{8,7},{9,8},{10,9},{11,1... | collective-permute-start | bytes 196616 | tf_op jit(solution)/shard_map/ppermute | solution.py:15
  35.4 1.4 copy-start.1
  35.4 1.5 %copy-start.2 = (f32[4,3,4,4,2048]{4,3,2,1,0:T(4,128)S(1)}, f32[4,3,4,4,2048]{4,3,2,1,0:T(4,128)}, u32[]{:S(2)}) copy-start(f32[4,3,4,4,2048]{4,3,2,1,0:T(4,128)} %param.22) | copy-start | bytes 4718596
  37.0 1.6 %copy-start.3 = (f32[4,4,4,2048]{3,2,1,0:T(4,128)}, f32[4,4,4,2048]{3,2,1,0:T(4,128)S(1)}, u32[]{:S(2)}) copy-start(f32[4,4,4,2048]{3,2,1,0:T(4,128)S(1)} %copy.36) | copy-start | bytes 1572868
  37.0 1.6 %copy-start.35 = (f32[8]{0:T(128)S(1)}, f32[8]{0:T(128)}, u32[]{:S(2)}) copy-start(f32[8]{0:T(128)} %param.24) | copy-start | bytes 100
  48.2 4.8 %copy-start.15 = (f32[256,128]{1,0:T(8,128)S(1)}, f32[256,128]{1,0:T(8,128)}, u32[]{:S(2)}) copy-start(f32[256,128]{1,0:T(8,128)} %reshape_squeeze.17) | copy-start | bytes 393220
  48.2 4.8 %copy-start.27 = (s32[1024]{0:T(1024)S(1)}, s32[1024]{0:T(1024)}, u32[]{:S(2)}) copy-start(s32[1024]{0:T(1024)} %get-tuple-element.56) | copy-start | bytes 12292
  48.2 4.8 %copy-start.29 = (s32[1024]{0:T(1024)S(1)}, s32[1024]{0:T(1024)}, u32[]{:S(2)}) copy-start(s32[1024]{0:T(1024)} %get-tuple-element.57) | copy-start | bytes 12292
  48.2 4.8 %copy-start.31 = (f32[1024]{0:T(1024)S(1)}, f32[1024]{0:T(1024)}, u32[]{:S(2)}) copy-start(f32[1024]{0:T(1024)} %compare_convert_fusion) | copy-start | bytes 12292
  49.6 4.9 %copy-start.21 = (f32[1024]{0:T(1024)S(1)}, f32[1024]{0:T(1024)}, u32[]{:S(2)}) copy-start(f32[1024]{0:T(1024)} %reshape_squeeze.18) | copy-start | bytes 12292
  49.6 4.9 %copy-start.22 = (f32[1024]{0:T(1024)S(1)}, f32[1024]{0:T(1024)}, u32[]{:S(2)}) copy-start(f32[1024]{0:T(1024)} %reshape_squeeze.16) | copy-start | bytes 12292
  49.6 4.9 %copy-start.23 = (f32[1024]{0:T(1024)S(1)}, f32[1024]{0:T(1024)}, u32[]{:S(2)}) copy-start(f32[1024]{0:T(1024)} %reshape_squeeze.15) | copy-start | bytes 12292
  50.3 18.7 %collective-permute-start.3 = (f32[2,1,4,2048]{3,2,1,0:T(4,128)}, f32[2,1,4,2048]{3,2,1,0:T(4,128)S(1)}, u32[]{:S(2)}, u32[]{:S(2)}) collective-permute-start(f32[2,1,4,2048]{3,2,1,0:T(4,128)} %pad_maximum_fusion.11), channel_id=1, source_target_pairs={{0,32},{32,64},{64,96},{96,128},{128,160},{160,192},{192,224},{224... | collective-permute-start | bytes 196616 | tf_op jit(solution)/shard_map/ppermute | solution.py:15
  54.5 0.6 copy-start.24
  64.2 6.8 %collective-permute-start.2 = (f32[2,4,1,2048]{3,2,1,0:T(1,128)}, f32[2,4,1,2048]{3,2,1,0:T(1,128)S(1)}, u32[]{:S(2)}, u32[]{:S(2)}) collective-permute-start(f32[2,4,1,2048]{3,2,1,0:T(1,128)} %slice.262), channel_id=1, source_target_pairs={{0,1},{1,2},{2,3},{3,4},{4,5},{5,6},{6,7},{7,8},{8,9},{9,10},{10,1... | collective-permute-start | bytes 196616 | tf_op jit(solution)/shard_map/ppermute | solution.py:15
  69.1 3.5 %copy-start.5 = (f32[3,4,4,2048]{3,2,1,0:T(4,128)S(1)}, f32[3,4,4,2048]{3,2,1,0:T(4,128)}, u32[]{:S(2)}) copy-start(f32[3,4,4,2048]{3,2,1,0:T(4,128)} %subtract_reduce_fusion.1) | copy-start | bytes 1179652
  69.1 3.5 %copy-start.11 = (f32[4,4,2048]{2,1,0:T(4,128)S(1)}, f32[4,4,2048]{2,1,0:T(4,128)}, u32[]{:S(2)}) copy-start(f32[4,4,2048]{2,1,0:T(4,128)} %bitcast_multiply_fusion) | copy-start | bytes 393220
  72.4 1.0 copy-start.8
  72.4 1.0 copy-start.14
  72.4 1.0 copy-start.10
  72.6 8.1 %copy-start.4 = (f32[4,4,4,2048]{3,2,1,0:T(4,128)S(1)}, f32[4,4,4,2048]{3,2,1,0:T(4,128)}, u32[]{:S(2)}) copy-start(f32[4,4,4,2048]{3,2,1,0:T(4,128)} %copy-done.3) | copy-start | bytes 1572868
  73.6 10.2 %collective-permute-start.4 = (f32[2,1,4,2048]{3,2,1,0:T(4,128)S(1)}, f32[2,1,4,2048]{3,2,1,0:T(4,128)S(1)}, u32[]{:S(2)}, u32[]{:S(2)}) collective-permute-start(f32[2,1,4,2048]{3,2,1,0:T(4,128)S(1)} %slice.329), channel_id=1, source_target_pairs={{32,0},{64,32},{96,64},{128,96},{160,128},{192,160},{224,192},{256... | collective-permute-start | bytes 196616 | tf_op jit(solution)/shard_map/ppermute | solution.py:15
  79.4 8.3 %collective-permute-start.5 = (f32[2,4,1,2048]{3,2,1,0:T(1,128)S(1)}, f32[2,4,1,2048]{3,2,1,0:T(1,128)S(1)}, u32[]{:S(2)}, u32[]{:S(2)}) collective-permute-start(f32[2,4,1,2048]{3,2,1,0:T(1,128)S(1)} %slice.285), channel_id=1, source_target_pairs={{1,0},{2,1},{3,2},{4,3},{5,4},{6,5},{7,6},{8,7},{9,8},{10,9},{11,1... | collective-permute-start | bytes 196616 | tf_op jit(solution)/shard_map/ppermute | solution.py:15
  83.6 4.2 %copy-start.28 = (s32[1024]{0:T(1024)S(1)}, s32[1024]{0:T(1024)}, u32[]{:S(2)}) copy-start(s32[1024]{0:T(1024)} %get-tuple-element.56) | copy-start | bytes 12292
  83.6 4.2 %copy-start.30 = (s32[1024]{0:T(1024)S(1)}, s32[1024]{0:T(1024)}, u32[]{:S(2)}) copy-start(s32[1024]{0:T(1024)} %get-tuple-element.57) | copy-start | bytes 12292
  83.6 4.3 %copy-start.32 = (f32[1024]{0:T(1024)S(1)}, f32[1024]{0:T(1024)}, u32[]{:S(2)}) copy-start(f32[1024]{0:T(1024)} %compare_convert_fusion) | copy-start | bytes 12292
  83.7 5.7 %copy-start.16 = (f32[1,32,32]{2,0,1:T(1,128)S(1)}, f32[1,32,32]{2,0,1:T(1,128)}, u32[]{:S(2)}) copy-start(f32[1,32,32]{2,0,1:T(1,128)} %stack.79) | copy-start | bytes 12292
  90.1 28.4 %all-to-all-start.1 = ((f32[32,2,32]{2,1,0:T(2,128)}), f32[32,2,32]{2,1,0:T(2,128)S(1)}, u32[]{:S(2)}, u32[]{:S(2)}) async-start(f32[32,2,32]{2,1,0:T(2,128)} %maximum_bitcast_fusion), calls=%async_computation.1 | async-start | bytes 65536 | tf_op jit(solution)/shard_map/all_to_all | solution.py:108
  105.1 13.5 %copy-start.26 = (s32[512]{0:T(512)S(1)}, s32[512]{0:T(512)}, u32[]{:S(2)}) copy-start(s32[512]{0:T(512)} %copy-done.25) | copy-start | bytes 6148
  105.4 13.9 %copy-start.17 = (f32[1,512]{1,0:T(1,128)S(1)}, f32[1,512]{1,0:T(1,128)}, u32[]{:S(2)}) copy-start(f32[1,512]{1,0:T(1,128)} %param.31) | copy-start | bytes 6148
  105.4 13.9 %copy-start.18 = (f32[1,512]{1,0:T(1,128)S(1)}, f32[1,512]{1,0:T(1,128)}, u32[]{:S(2)}) copy-start(f32[1,512]{1,0:T(1,128)} %param.32) | copy-start | bytes 6148
  105.4 13.9 %copy-start.19 = (f32[1,512]{1,0:T(1,128)S(1)}, f32[1,512]{1,0:T(1,128)}, u32[]{:S(2)}) copy-start(f32[1,512]{1,0:T(1,128)} %param.30) | copy-start | bytes 6148
  105.5 14.0 %copy-start.20 = (f32[1,512]{1,0:T(1,128)S(1)}, f32[1,512]{1,0:T(1,128)}, u32[]{:S(2)}) copy-start(f32[1,512]{1,0:T(1,128)} %param.33) | copy-start | bytes 6148
  105.8 36.8 %copy-start.7 = (f32[3,4,4,2048]{3,2,1,0:T(4,128)}, f32[3,4,4,2048]{3,2,1,0:T(4,128)S(1)}, u32[]{:S(2)}) copy-start(f32[3,4,4,2048]{3,2,1,0:T(4,128)S(1)} %pad_maximum_fusion.1) | copy-start | bytes 1179652
  120.5 22.2 %copy-start.34 = (f32[1,512]{1,0:T(1,128)}, f32[1,512]{1,0:T(1,128)S(1)}, u32[]{:S(2)}) copy-start(f32[1,512]{1,0:T(1,128)S(1)} %get-tuple-element.33) | copy-start | bytes 6148
  122.2 17.0 %all-to-all-start.2 = ((f32[32,1,32]{2,1,0:T(1,128)}), f32[32,1,32]{2,1,0:T(1,128)S(1)}, u32[]{:S(2)}, u32[]{:S(2)}) async-start(f32[32,1,32]{2,1,0:T(1,128)} %transpose_reshape.3), calls=%async_computation.2 | async-start | bytes 32768 | tf_op jit(solution)/shard_map/all_to_all | solution.py:108
  126.0 16.8 %copy-start.9 = (f32[4,4,2048]{2,1,0:T(4,128)S(1)}, f32[4,4,2048]{2,1,0:T(4,128)}, u32[]{:S(2)}) copy-start(f32[4,4,2048]{2,1,0:T(4,128)} %copy-done.8) | copy-start | bytes 393220
  126.1 16.5 %collective-permute-start.7 = (f32[2,1,4,2048]{3,2,1,0:T(4,128)S(1)}, f32[2,1,4,2048]{3,2,1,0:T(4,128)S(1)}, u32[]{:S(2)}, u32[]{:S(2)}) collective-permute-start(f32[2,1,4,2048]{3,2,1,0:T(4,128)S(1)} %pad_maximum_fusion.10), channel_id=1, source_target_pairs={{0,32},{32,64},{64,96},{96,128},{128,160},{160,192},{192,224},{224... | collective-permute-start | bytes 196616 | tf_op jit(solution)/shard_map/ppermute | solution.py:15
  128.0 14.7 %collective-permute-start.6 = (f32[2,4,1,2048]{3,2,1,0:T(1,128)S(1)}, f32[2,4,1,2048]{3,2,1,0:T(1,128)S(1)}, u32[]{:S(2)}, u32[]{:S(2)}) collective-permute-start(f32[2,4,1,2048]{3,2,1,0:T(1,128)S(1)} %slice.293), channel_id=1, source_target_pairs={{0,1},{1,2},{2,3},{3,4},{4,5},{5,6},{6,7},{7,8},{8,9},{9,10},{10,1... | collective-permute-start | bytes 196616 | tf_op jit(solution)/shard_map/ppermute | solution.py:15
  142.7 1.0 copy-start.6
  142.7 1.0 copy-start.12

commit v3 on v2

--- a/solution.py
+++ b/solution.py
@@ -48,7 +48,7 @@
     return jnp.stack([magn_x, magn_y, magn_z])
 
 
-def electric_update(e_field, h_field, polarization, wire_term, cells):
+def electric_base(e_field, h_field, polarization, cells):
     eps_cell, sigma_cell, strength_cell, decay_cell = cells
     magn_x, magn_y, magn_z = (h_field[0], h_field[1], h_field[2])
     minus_x, minus_y = magnetic_rims(h_field)
@@ -62,8 +62,12 @@
     )
     change = jnp.sum(polar_new - polarization, axis=0)
     drive = TIME_STEP * curl_all - TIME_STEP * sigma_cell[None] * e_field - change
+    return (drive, polar_new)
+
+
+def electric_finish(e_field, drive, wire_term, cells):
     drive = drive.at[2].add(-TIME_STEP * wire_term)
-    return (e_field + drive / eps_cell[None], polar_new)
+    return e_field + drive / cells[0][None]
 
 
 def on_device(
@@ -118,6 +122,20 @@
     drop_0 = jnp.concatenate([volt_0[1:], single_zero]) - volt_0
     outgoing = to_slots(jnp.stack([cell_ids.astype(jnp.float32), curr_0, gain_row, drop_0]), [-1.0, 0.0, 0.0, 0.0])
     incoming = exchange(outgoing)
+
+    material_hot = (
+        material[None] == jnp.arange(eps_inf.shape[0], dtype=jnp.int32)[:, None, None, None]
+    ).astype(jnp.float32)
+    eps_cell = jnp.einsum("m,mxyz->xyz", eps_inf, material_hot, precision=highest)
+    sigma_cell = jnp.einsum("m,mxyz->xyz", conductivity, material_hot, precision=highest)
+    strength_cell = jnp.einsum("pm,mxyz->pxyz", pole_strength, material_hot, precision=highest)
+    decay_cell = jnp.einsum("pm,mxyz->pxyz", pole_decay, material_hot, precision=highest)
+    cells = (eps_cell, sigma_cell, strength_cell, decay_cell)
+
+    h_field = magnetic_update(e_field, h_field)
+    drive, polar_next = electric_base(e_field, h_field, polarization, cells)
+    incoming, drive = lax.optimization_barrier((incoming, drive))
+
     recv_cells = incoming[:, 0, :].astype(jnp.int32)
     is_valid = recv_cells >= 0
     safe_cells = jnp.where(is_valid, recv_cells, 0).reshape(-1)
@@ -131,15 +149,6 @@
     row_hot = row_hot * valid_flat.astype(jnp.float32)[:, None]
     lane_hot = (safe_cells % lanes)[:, None] == jnp.arange(lanes, dtype=jnp.int32)[None, :]
 
-    material_hot = (
-        material[None] == jnp.arange(eps_inf.shape[0], dtype=jnp.int32)[:, None, None, None]
-    ).astype(jnp.float32)
-    eps_cell = jnp.einsum("m,mxyz->xyz", eps_inf, material_hot, precision=highest)
-    sigma_cell = jnp.einsum("m,mxyz->xyz", conductivity, material_hot, precision=highest)
-    strength_cell = jnp.einsum("pm,mxyz->pxyz", pole_strength, material_hot, precision=highest)
-    decay_cell = jnp.einsum("pm,mxyz->pxyz", pole_decay, material_hot, precision=highest)
-    cells = (eps_cell, sigma_cell, strength_cell, decay_cell)
-
     def sample(e_now):
         picked = jnp.dot(row_hot, e_now[2].reshape(plane_rows, lanes), precision=highest)
         return jnp.sum(jnp.where(lane_hot, picked, 0.0), axis=1)
@@ -149,12 +158,14 @@
         return jnp.einsum("kr,kl->rl", row_hot, spread, precision=highest).reshape(grid_shape)
 
     sample_0 = sample(e_field)
-    h_field = magnetic_update(e_field, h_field)
     curr_cell_1 = recv_curr + recv_gain * (sample_0 - recv_drop)
-    e_field, polarization = electric_update(e_field, h_field, polarization, wire_of(curr_cell_1), cells)
+    e_field = electric_finish(e_field, drive, wire_of(curr_cell_1), cells)
+    polarization = polar_next
     sample_1 = sample(e_field)
 
-    returned = from_slots(exchange(jnp.stack([sample_0, sample_1]).reshape(2, n_gy, capacity).transpose(1, 0, 2)))
+    returned = exchange(jnp.stack([sample_0, sample_1]).reshape(2, n_gy, capacity).transpose(1, 0, 2))
+    returned, e_field, h_field, polarization = lax.optimization_barrier((returned, e_field, h_field, polarization))
+    returned = from_slots(returned)
     seg_sample_0, seg_sample_1 = returned[0], returned[1]
     curr_1 = curr_0 + gain_row * (seg_sample_0 - drop_0)
     curr_prev = jnp.concatenate([single_zero, curr_1[:-1]])
@@ -163,10 +174,12 @@
     curr_2 = curr_1 + gain_row * (seg_sample_1 - drop_1)
     curr_prev = jnp.concatenate([single_zero, curr_2[:-1]])
     volt_2 = volt_1 - cap_row * (curr_2 - curr_prev)
+    recv_curr_2 = exchange(to_slots(curr_2[None], [0.0]))
 
     h_field = magnetic_update(e_field, h_field)
-    recv_curr_2 = exchange(to_slots(curr_2[None], [0.0])).transpose(1, 0, 2).reshape(-1)
-    e_field, polarization = electric_update(e_field, h_field, polarization, wire_of(recv_curr_2), cells)
+    drive, polarization = electric_base(e_field, h_field, polarization, cells)
+    recv_curr_2, drive = lax.optimization_barrier((recv_curr_2, drive))
+    e_field = electric_finish(e_field, drive, wire_of(recv_curr_2.transpose(1, 0, 2).reshape(-1)), cells)
     return (e_field, h_field, polarization, curr_2[None], volt_2[None])
 
 

time: 146 us -> 145 us (level)
  the two profiles are of different devices: /device:TPU:16 before, /device:TPU:38 now
where the time goes in v3:
time: 145 us; the launch traced here: 144 us
  starting transfers between devices  47.6 us (33%)
  other arithmetic  26.2 us (18%)
  blocking collectives  25.2 us (17%)
  local copies, waits for them, and re-layouts  20.8 us (14%)
  matrix products  16.5 us (11%)
  waiting for transfers between devices  6.39 us (4%)
    ppermute x8, starting transfers between devices, passed_along(): lax.ppermute(value, axis, [(source, source + steps) for source in range(f...  26.2 us
    all_to_all x1, blocking collectives, exchange(): return lax.all_to_all(blocks, 'gy', split_axis=0, concat_axis=0, tiled=True)  25.2 us
    all_to_all x2, starting transfers between devices, exchange(): return lax.all_to_all(blocks, 'gy', split_axis=0, concat_axis=0, tiled=True)  21.5 us
    ppermute x8, waiting for transfers between devices, passed_along(): lax.ppermute(value, axis, [(source, source + steps) for source in range(f...  6.38 us
    dot_general x2, matrix products, wire_of(): jnp.einsum('kr,kl->rl', row_hot, spread, precision=highest)  5.56 us
    dot_general x2, matrix products, sample(): jnp.dot(row_hot, e_now[2].reshape(plane_rows, lanes), precision=highest)  5.14 us
  transfers between devices with their start and end apart: 10, of which 2 were waited for; matrix products, arithmetic and copies ran while one was open for 14% of the time, Pallas kernels for 0%

profile of v3, /device:TPU:38, one launch (start us, length us, event | category | flops | bytes accessed | tf_op | source)
XLA Modules:
  0.0 144.2 jit_solution(12938404684486713690)
XLA Ops:
  0.7 0.7 fusion.124
  1.4 1.2 reduce-window.6
  2.8 0.8 fusion.123
  3.6 0.7 multiply_add_fusion.6
  4.3 0.8 slice.257
  5.1 0.7 convert_element_type.39
  6.0 0.8 fusion.138
  6.8 1.7 %fusion.30 = f32[4,1024]{1,0:T(4,128)S(1)} fusion(s32[512]{0:T(512)S(1)} %multiply_add_fusion.6, f32[1,512]{1,0:T(1,128)S(1)} %fusion.138, f32[1,512]{1,0:T(1,128)} %param.32, f32[1,512]{1,0:T(1,128)} %param.30, f32[1,512]{1,0:T(1,128)S(1)} %convert_element_type.39, f32[1024]{0:T(1024)S(1)} %broadcast_subtract_fusion, f32[4]{0:T(128)} %constant.114.clone), kind=kOutput, calls=%fused_computation.26 | convolution fusion | flops 25704448 | bytes 30736 | tf_op jit(solution)/shard_map/fs,ts->ft/dot_general | solution.py:107
  8.7 0.7 reshape.290
  9.4 16.4 %all-to-all-start = ((f32[32,1,128]{2,1,0:T(1,128)}), f32[32,1,128]{2,1,0:T(1,128)}, u32[]{:S(2)}, u32[]{:S(2)}) async-start(f32[32,1,128]{2,1,0:T(1,128)} %reshape.290), calls=%async_computation | async-start | bytes 32768 | tf_op jit(solution)/shard_map/all_to_all | solution.py:112
  25.8 1.6 %slice.266 = f32[2,4,1,2048]{3,2,1,0:T(1,128)} slice(f32[3,4,4,2048]{3,2,1,0:T(4,128)} %param.20), slice={[0:3:2], [0:4:1], [0:1:1], [0:2048:1]} | slice | bytes 131072 | tf_op jit(solution)/shard_map/slice | solution.py:29
  27.4 3.4 %collective-permute-start.1 = (f32[2,4,1,2048]{3,2,1,0:T(1,128)}, f32[2,4,1,2048]{3,2,1,0:T(1,128)S(1)}, u32[]{:S(2)}, u32[]{:S(2)}) collective-permute-start(f32[2,4,1,2048]{3,2,1,0:T(1,128)} %slice.266), channel_id=1, source_target_pairs={{1,0},{2,1},{3,2},{4,3},{5,4},{6,5},{7,6},{8,7},{9,8},{10,9},{11,1... | collective-permute-start | bytes 196616 | tf_op jit(solution)/shard_map/ppermute | solution.py:15
  30.8 1.5 %slice.262 = f32[2,1,4,2048]{3,2,1,0:T(4,128)} slice(f32[3,4,4,2048]{3,2,1,0:T(4,128)} %param.20), slice={[1:3], [0:1], [0:4], [0:2048]} | slice | bytes 131072 | tf_op jit(solution)/shard_map/slice | solution.py:27
  32.3 1.9 %collective-permute-start = (f32[2,1,4,2048]{3,2,1,0:T(4,128)}, f32[2,1,4,2048]{3,2,1,0:T(4,128)S(1)}, u32[]{:S(2)}, u32[]{:S(2)}) collective-permute-start(f32[2,1,4,2048]{3,2,1,0:T(4,128)} %slice.262), channel_id=1, source_target_pairs={{32,0},{64,32},{96,64},{128,96},{160,128},{192,160},{224,192},{256... | collective-permute-start | bytes 196616 | tf_op jit(solution)/shard_map/ppermute | solution.py:15
  34.2 0.6 convolution_bitcast_fusion.1
  35.2 0.6 fusion
  36.8 0.7 bitcast_multiply_fusion
  37.5 1.9 %multiply_add_fusion.1 = (f32[4,3,4,4,2048]{4,3,2,1,0:T(4,128)S(1)}, f32[3,4,4,2048]{3,2,1,0:T(4,128)}) fusion(f32[4,3,4,4,2048]{4,3,2,1,0:T(4,128)S(1)} %copy-done.7, f32[3,4,4,2048]{3,2,1,0:T(4,128)S(1)} %copy-done.1, f32[4,4,4,2048]{3,2,1,0:T(4,128)S(1)} %copy.38, f32[4,4,4,2048]{3,2,1,0:T(4,128)S(1)} %copy.37), kind=kLoop, calls=%fused_computation.19 | loop fusion | flops 1867776 | bytes 4980736 | tf_op jit(solution)/shard_map/add | solution.py:60
  40.0 0.7 slice.261
  40.7 0.7 copy.51
  41.9 1.4 reduce.26
  43.3 0.7 reshape.291
  44.1 1.9 %fusion.165 = (f32[1,4,4,2048]{3,2,1,0:T(4,128)}, f32[1,4,4,2048]{3,2,1,0:T(4,128)S(1)}, f32[4,4,2048]{2,1,0:T(4,128)S(1)}, f32[4,4,2048]{2,1,0:T(4,128)S(1)}) fusion(f32[3,4,4,2048]{3,2,1,0:T(4,128)S(1)} %copy-done.1, f32[2,4,1,2048]{3,2,1,0:T(1,128)S(1)} %collective-permute-done.1, f32[2,4,3,2048]{3,2,1,0:T(4,128)S(1)} %slice.265, ...), kind=kLoop, calls=%fused_computation.241 | loop fusion | flops 229376 | bytes 1572864 | tf_op jit(solution)/shard_map/slice | solution.py:44
  46.2 1.0 fusion.110
  47.2 0.6 pad_maximum_fusion.11
  47.9 2.4 %collective-permute-start.3 = (f32[2,1,4,2048]{3,2,1,0:T(4,128)}, f32[2,1,4,2048]{3,2,1,0:T(4,128)}, u32[]{:S(2)}, u32[]{:S(2)}) collective-permute-start(f32[2,1,4,2048]{3,2,1,0:T(4,128)} %pad_maximum_fusion.11), channel_id=1, source_target_pairs={{0,32},{32,64},{64,96},{96,128},{128,160},{160,192},{192,224},{224... | collective-permute-start | bytes 196616 | tf_op jit(solution)/shard_map/ppermute | solution.py:15
  50.4 0.7 slice.276
  51.1 0.7 slice.277
  51.9 2.6 %collective-permute-start.2 = (f32[2,4,1,2048]{3,2,1,0:T(1,128)}, f32[2,4,1,2048]{3,2,1,0:T(1,128)}, u32[]{:S(2)}, u32[]{:S(2)}) collective-permute-start(f32[2,4,1,2048]{3,2,1,0:T(1,128)} %slice.276), channel_id=1, source_target_pairs={{0,1},{1,2},{2,3},{3,4},{4,5},{5,6},{6,7},{7,8},{8,9},{9,10},{10,1... | collective-permute-start | bytes 196616 | tf_op jit(solution)/shard_map/ppermute | solution.py:15
  54.5 1.6 %reshape_squeeze.15 = f32[256,128]{1,0:T(8,128)} reshape(f32[1,4,4,2048]{3,2,1,0:T(4,128)} %get-tuple-element.67) | data formatting | bytes 262144 | tf_op jit(solution)/shard_map/reshape;squeeze | solution.py:153
  56.1 1.0 fusion.59
  57.1 2.1 %collective-permute-done.2 = f32[2,4,1,2048]{3,2,1,0:T(1,128)} collective-permute-done((f32[2,4,1,2048]{3,2,1,0:T(1,128)}, f32[2,4,1,2048]{3,2,1,0:T(1,128)}, u32[]{:S(2)}, u32[]{:S(2)}) %collective-permute-start.2) | collective-permute-done | bytes 65568 | tf_op jit(solution)/shard_map/ppermute | solution.py:15
  59.2 1.5 %fusion.77 = (f32[1,4,4,2048]{3,2,1,0:T(4,128)S(1)}, f32[4,4,2048]{2,1,0:T(4,128)S(1)}, f32[1,4,4,2048]{3,2,1,0:T(4,128)S(1)}) fusion(f32[2,4,1,2048]{3,2,1,0:T(1,128)} %collective-permute-done.2, f32[2,4,3,2048]{3,2,1,0:T(4,128)} %slice.277, f32[4,4,2048]{2,1,0:T(4,128)S(1)} %get-tuple-element.60, f32[4,4,2047]{2,1,0:T(4,128)S(1)} %bitcast.278, ...), kind=kLoop, calls=%fused_computation.96 | loop fusion | flops 491520 | bytes 2097088 | tf_op jit(solution)/shard_map/stack | solution.py:58
  61.1 0.9 convert_reduce_fusion.1
  62.1 0.6 compare_convert_fusion
  62.7 0.6 add_select_fusion.1
  63.3 1.1 slice_reduce_fusion.1
  64.4 0.7 reshape_squeeze.16
  65.1 0.7 reshape_squeeze.17
  65.7 0.7 reshape_squeeze.18
  66.4 3.0 %fusion.21 = f32[1024]{0:T(1024)} fusion(f32[256,128]{1,0:T(8,128)} %reshape_squeeze.15, f32[1024]{0:T(1024)} %compare_convert_fusion, s32[1024]{0:T(1024)} %get-tuple-element.74, s32[1024]{0:T(1024)} %get-tuple-element.73), kind=kOutput, calls=%fused_computation.23 | convolution fusion | flops 403569664 | bytes 147456 | tf_op jit(solution)/shard_map/dot_general | solution.py:153
  69.4 1.4 stack.71
  70.8 0.7 multiply_add_fusion.3
  71.5 3.5 %fusion.24 = f32[256,128]{1,0:T(8,128)} fusion(f32[1024]{0:T(1024)} %compare_convert_fusion, s32[1024]{0:T(1024)} %get-tuple-element.74, f32[1024]{0:T(1024)S(1)} %multiply_add_fusion.3, s32[1024]{0:T(1024)} %get-tuple-element.73), kind=kOutput, calls=%fused_computation.24 | convolution fusion | flops 403472384 | bytes 147456 | tf_op jit(solution)/shard_map/kr,kl->rl/dot_general | solution.py:158
  74.9 1.6 %mul.215 = f32[1,4,4,2048]{3,2,1,0:T(4,128)} reshape(f32[256,128]{1,0:T(8,128)} %fusion.24) | data formatting | bytes 262144 | tf_op jit(solution)/shard_map/mul | solution.py:69
  76.5 1.0 add_dynamic-update-slice_fusion.1
  77.5 0.7 copy-done.5
  78.3 1.1 divide_add_fusion.1
  79.5 2.1 %fusion.18 = f32[1024]{0:T(1024)S(1)} fusion(f32[256,128]{1,0:T(8,128)S(1)} %reshape_squeeze.19, f32[1024]{0:T(1024)} %compare_convert_fusion, s32[1024]{0:T(1024)} %get-tuple-element.74, s32[1024]{0:T(1024)} %get-tuple-element.73), kind=kOutput, calls=%fused_computation.22 | convolution fusion | flops 403569664 | bytes 147456 | tf_op jit(solution)/shard_map/dot_general | solution.py:153
  81.8 25.2 %all_to_all.15 = f32[32,2,32]{2,1,0:T(2,128)S(1)} all-to-all(f32[32,2,32]{2,1,0:T(2,128)S(1)} %maximum_bitcast_fusion), channel_id=1, replica_groups=mesh['gx'=16,'gy'=32] {'gy'}, dimensions={0} | all-to-all | bytes 16384 | tf_op jit(solution)/shard_map/all_to_all | solution.py:112
  107.2 0.7 fusion.2
  108.4 0.7 fusion.154
  109.0 1.0 fusion.1
  110.1 0.7 transpose_reshape.3
  110.8 5.0 %all-to-all-start.2 = ((f32[32,1,32]{2,1,0:T(1,128)}), f32[32,1,32]{2,1,0:T(1,128)S(1)}, u32[]{:S(2)}, u32[]{:S(2)}) async-start(f32[32,1,32]{2,1,0:T(1,128)} %transpose_reshape.3), calls=%async_computation.2 | async-start | bytes 32768 | tf_op jit(solution)/shard_map/all_to_all | solution.py:112
  115.8 3.5 %collective-permute-start.5 = (f32[2,4,1,2048]{3,2,1,0:T(1,128)S(1)}, f32[2,4,1,2048]{3,2,1,0:T(1,128)S(1)}, u32[]{:S(2)}, u32[]{:S(2)}) collective-permute-start(f32[2,4,1,2048]{3,2,1,0:T(1,128)S(1)} %slice.303), channel_id=1, source_target_pairs={{1,0},{2,1},{3,2},{4,3},{5,4},{6,5},{7,6},{8,7},{9,8},{10,9},{11,1... | collective-permute-start | bytes 196616 | tf_op jit(solution)/shard_map/ppermute | solution.py:15
  119.3 1.9 %collective-permute-start.4 = (f32[2,1,4,2048]{3,2,1,0:T(4,128)S(1)}, f32[2,1,4,2048]{3,2,1,0:T(4,128)S(1)}, u32[]{:S(2)}, u32[]{:S(2)}) collective-permute-start(f32[2,1,4,2048]{3,2,1,0:T(4,128)S(1)} %slice.299), channel_id=1, source_target_pairs={{32,0},{64,32},{96,64},{128,96},{160,128},{192,160},{224,192},{256... | collective-permute-start | bytes 196616 | tf_op jit(solution)/shard_map/ppermute | solution.py:15
  121.3 2.0 %subtract_reduce_fusion = (f32[3,4,4,2048]{3,2,1,0:T(4,128)S(1)}, f32[4,3,4,4,2048]{4,3,2,1,0:T(4,128)}) fusion(f32[4,3,4,4,2048]{4,3,2,1,0:T(4,128)S(1)} %get-tuple-element.42, f32[3,4,4,2048]{3,2,1,0:T(4,128)S(1)} %bitcast.267, f32[4,4,4,2048]{3,2,1,0:T(4,128)S(1)} %copy.38, f32[4,4,4,2048]{3,2,1,0:T(4,128)S(1)} %copy.37), kind=kLoop, calls=%fused_computation.16 | loop fusion | flops 1867776 | bytes 4980736 | tf_op jit(solution)/shard_map/reduce_sum | solution.py:63
  124.1 7.8 %collective-permute-start.7 = (f32[2,1,4,2048]{3,2,1,0:T(4,128)S(1)}, f32[2,1,4,2048]{3,2,1,0:T(4,128)S(1)}, u32[]{:S(2)}, u32[]{:S(2)}) collective-permute-start(f32[2,1,4,2048]{3,2,1,0:T(4,128)S(1)} %pad_maximum_fusion.10), channel_id=1, source_target_pairs={{0,32},{32,64},{64,96},{96,128},{128,160},{160,192},{192,224},{224... | collective-permute-start | bytes 196616 | tf_op jit(solution)/shard_map/ppermute | solution.py:15
  132.1 2.7 %collective-permute-start.6 = (f32[2,4,1,2048]{3,2,1,0:T(1,128)S(1)}, f32[2,4,1,2048]{3,2,1,0:T(1,128)S(1)}, u32[]{:S(2)}, u32[]{:S(2)}) collective-permute-start(f32[2,4,1,2048]{3,2,1,0:T(1,128)S(1)} %slice.313), channel_id=1, source_target_pairs={{0,1},{1,2},{2,3},{3,4},{4,5},{5,6},{6,7},{7,8},{8,9},{9,10},{10,1... | collective-permute-start | bytes 196616 | tf_op jit(solution)/shard_map/ppermute | solution.py:15
  134.8 4.3 %collective-permute-done.6 = f32[2,4,1,2048]{3,2,1,0:T(1,128)S(1)} collective-permute-done((f32[2,4,1,2048]{3,2,1,0:T(1,128)S(1)}, f32[2,4,1,2048]{3,2,1,0:T(1,128)S(1)}, u32[]{:S(2)}, u32[]{:S(2)}) %collective-permute-start.6) | collective-permute-done | bytes 65568 | tf_op jit(solution)/shard_map/ppermute | solution.py:15
  140.4 0.7 reduce.25
  141.2 2.1 %fusion.27 = f32[256,128]{1,0:T(8,128)S(1)} fusion(f32[1024]{0:T(1024)S(1)} %copy-done.26, s32[1024]{0:T(1024)S(1)} %copy-done.25, f32[1024]{0:T(1024)S(1)} %broadcast_in_dim.23, s32[1024]{0:T(1024)S(1)} %copy-done.24), kind=kOutput, calls=%fused_computation.25 | convolution fusion | flops 403472384 | bytes 147456 | tf_op jit(solution)/shard_map/kr,kl->rl/dot_general | solution.py:158
  143.4 0.8 divide_add_fusion
  (121 shorter events, 7.1 us)
Async XLA Ops:
  0.6 33.6 %copy-start = (f32[4,8]{1,0:T(4,128)S(1)}, f32[4,8]{1,0:T(4,128)}, u32[]{:S(2)}) copy-start(f32[4,8]{1,0:T(4,128)} %param.27) | copy-start | bytes 388
  0.6 33.6 %copy-start.16 = (s32[4,4,2048]{2,1,0:T(4,128)S(1)}, s32[4,4,2048]{2,1,0:T(4,128)}, u32[]{:S(2)}) copy-start(s32[4,4,2048]{2,1,0:T(4,128)} %param.23) | copy-start | bytes 393220
  1.4 33.8 %copy-start.27 = (f32[4,8]{1,0:T(4,128)S(1)}, f32[4,8]{1,0:T(4,128)}, u32[]{:S(2)}) copy-start(f32[4,8]{1,0:T(4,128)} %param.26) | copy-start | bytes 388
  4.3 30.5 %copy-start.22 = (s32[512]{0:T(512)}, s32[512]{0:T(512)S(1)}, u32[]{:S(2)}) copy-start(s32[512]{0:T(512)S(1)} %multiply_add_fusion.6) | copy-start | bytes 6148
  9.4 32.0 %all-to-all-start = ((f32[32,1,128]{2,1,0:T(1,128)}), f32[32,1,128]{2,1,0:T(1,128)}, u32[]{:S(2)}, u32[]{:S(2)}) async-start(f32[32,1,128]{2,1,0:T(1,128)} %reshape.290), calls=%async_computation | async-start | bytes 32768 | tf_op jit(solution)/shard_map/all_to_all | solution.py:112
  27.4 16.6 %collective-permute-start.1 = (f32[2,4,1,2048]{3,2,1,0:T(1,128)}, f32[2,4,1,2048]{3,2,1,0:T(1,128)S(1)}, u32[]{:S(2)}, u32[]{:S(2)}) collective-permute-start(f32[2,4,1,2048]{3,2,1,0:T(1,128)} %slice.266), channel_id=1, source_target_pairs={{1,0},{2,1},{3,2},{4,3},{5,4},{6,5},{7,6},{8,7},{9,8},{10,9},{11,1... | collective-permute-start | bytes 196616 | tf_op jit(solution)/shard_map/ppermute | solution.py:15
  32.3 11.8 %collective-permute-start = (f32[2,1,4,2048]{3,2,1,0:T(4,128)}, f32[2,1,4,2048]{3,2,1,0:T(4,128)S(1)}, u32[]{:S(2)}, u32[]{:S(2)}) collective-permute-start(f32[2,1,4,2048]{3,2,1,0:T(4,128)} %slice.262), channel_id=1, source_target_pairs={{32,0},{64,32},{96,64},{128,96},{160,128},{192,160},{224,192},{256... | collective-permute-start | bytes 196616 | tf_op jit(solution)/shard_map/ppermute | solution.py:15
  34.8 1.4 copy-start.29
  35.2 2.3 %copy-start.1 = (f32[3,4,4,2048]{3,2,1,0:T(4,128)S(1)}, f32[3,4,4,2048]{3,2,1,0:T(4,128)}, u32[]{:S(2)}) copy-start(f32[3,4,4,2048]{3,2,1,0:T(4,128)} %param.20) | copy-start | bytes 1179652
  35.2 2.3 %copy-start.7 = (f32[4,3,4,4,2048]{4,3,2,1,0:T(4,128)S(1)}, f32[4,3,4,4,2048]{4,3,2,1,0:T(4,128)}, u32[]{:S(2)}) copy-start(f32[4,3,4,4,2048]{4,3,2,1,0:T(4,128)} %param.22) | copy-start | bytes 4718596
  37.5 1.9 %copy-start.30 = (f32[8]{0:T(128)S(1)}, f32[8]{0:T(128)}, u32[]{:S(2)}) copy-start(f32[8]{0:T(128)} %param.24) | copy-start | bytes 100
  44.0 2.2 %copy-start.4 = (f32[2,3,4,2048]{3,2,1,0:T(4,128)S(1)}, f32[2,3,4,2048]{3,2,1,0:T(4,128)}, u32[]{:S(2)}) copy-start(f32[2,3,4,2048]{3,2,1,0:T(4,128)} %slice.261) | copy-start | bytes 589828
  44.1 2.2 %copy-start.13 = (f32[3,4,4,2048]{3,2,1,0:T(4,128)S(1)}, f32[3,4,4,2048]{3,2,1,0:T(4,128)}, u32[]{:S(2)}) copy-start(f32[3,4,4,2048]{3,2,1,0:T(4,128)} %param.21) | copy-start | bytes 1179652
  44.1 2.0 %copy-start.14 = (f32[2,4,1,2048]{3,2,1,0:T(1,128)}, f32[2,4,1,2048]{3,2,1,0:T(1,128)S(1)}, u32[]{:S(2)}) copy-start(f32[2,4,1,2048]{3,2,1,0:T(1,128)S(1)} %collective-permute-done.1) | copy-start | bytes 196612
  44.1 2.0 %copy-start.15 = (f32[2,1,4,2048]{3,2,1,0:T(4,128)}, f32[2,1,4,2048]{3,2,1,0:T(4,128)S(1)}, u32[]{:S(2)}) copy-start(f32[2,1,4,2048]{3,2,1,0:T(4,128)S(1)} %collective-permute-done) | copy-start | bytes 196612
  45.9 4.4 %copy-start.6 = (f32[1,4,4,2048]{3,2,1,0:T(4,128)}, f32[1,4,4,2048]{3,2,1,0:T(4,128)S(1)}, u32[]{:S(2)}) copy-start(f32[1,4,4,2048]{3,2,1,0:T(4,128)S(1)} %get-tuple-element.68) | copy-start | bytes 393220
  47.9 8.3 %collective-permute-start.3 = (f32[2,1,4,2048]{3,2,1,0:T(4,128)}, f32[2,1,4,2048]{3,2,1,0:T(4,128)}, u32[]{:S(2)}, u32[]{:S(2)}) collective-permute-start(f32[2,1,4,2048]{3,2,1,0:T(4,128)} %pad_maximum_fusion.11), channel_id=1, source_target_pairs={{0,32},{32,64},{64,96},{96,128},{128,160},{160,192},{192,224},{224... | collective-permute-start | bytes 196616 | tf_op jit(solution)/shard_map/ppermute | solution.py:15
  50.4 0.7 copy-start.2
  51.9 7.4 %collective-permute-start.2 = (f32[2,4,1,2048]{3,2,1,0:T(1,128)}, f32[2,4,1,2048]{3,2,1,0:T(1,128)}, u32[]{:S(2)}, u32[]{:S(2)}) collective-permute-start(f32[2,4,1,2048]{3,2,1,0:T(1,128)} %slice.276), channel_id=1, source_target_pairs={{0,1},{1,2},{2,3},{3,4},{4,5},{5,6},{6,7},{7,8},{8,9},{9,10},{10,1... | collective-permute-start | bytes 196616 | tf_op jit(solution)/shard_map/ppermute | solution.py:15
  57.1 3.8 %copy-start.8 = (f32[3,4,4,2048]{3,2,1,0:T(4,128)S(1)}, f32[3,4,4,2048]{3,2,1,0:T(4,128)}, u32[]{:S(2)}) copy-start(f32[3,4,4,2048]{3,2,1,0:T(4,128)} %get-tuple-element.57) | copy-start | bytes 1179652
  57.1 3.8 %copy-start.11 = (f32[4,4,2048]{2,1,0:T(4,128)S(1)}, f32[4,4,2048]{2,1,0:T(4,128)}, u32[]{:S(2)}) copy-start(f32[4,4,2048]{2,1,0:T(4,128)} %bitcast_multiply_fusion) | copy-start | bytes 393220
  66.4 11.9 %copy-start.10 = (f32[1,4,4,2048]{3,2,1,0:T(4,128)S(1)}, f32[1,4,4,2048]{3,2,1,0:T(4,128)}, u32[]{:S(2)}) copy-start(f32[1,4,4,2048]{3,2,1,0:T(4,128)} %copy.51) | copy-start | bytes 393220
  77.5 0.7 copy-start.5
  79.4 2.4 %copy-start.17 = (f32[1,32,32]{2,0,1:T(1,128)S(1)}, f32[1,32,32]{2,0,1:T(1,128)}, u32[]{:S(2)}) copy-start(f32[1,32,32]{2,0,1:T(1,128)} %stack.71) | copy-start | bytes 12292
  79.4 27.8 %copy-start.23 = (s32[512]{0:T(512)S(1)}, s32[512]{0:T(512)}, u32[]{:S(2)}) copy-start(s32[512]{0:T(512)} %copy-done.22) | copy-start | bytes 6148
  79.4 28.6 %copy-start.18 = (f32[1,512]{1,0:T(1,128)S(1)}, f32[1,512]{1,0:T(1,128)}, u32[]{:S(2)}) copy-start(f32[1,512]{1,0:T(1,128)} %param.31) | copy-start | bytes 6148
  79.4 28.6 %copy-start.19 = (f32[1,512]{1,0:T(1,128)S(1)}, f32[1,512]{1,0:T(1,128)}, u32[]{:S(2)}) copy-start(f32[1,512]{1,0:T(1,128)} %param.32) | copy-start | bytes 6148
  79.4 28.6 %copy-start.20 = (f32[1,512]{1,0:T(1,128)S(1)}, f32[1,512]{1,0:T(1,128)}, u32[]{:S(2)}) copy-start(f32[1,512]{1,0:T(1,128)} %param.30) | copy-start | bytes 6148
  79.4 28.6 %copy-start.21 = (f32[1,512]{1,0:T(1,128)S(1)}, f32[1,512]{1,0:T(1,128)}, u32[]{:S(2)}) copy-start(f32[1,512]{1,0:T(1,128)} %param.33) | copy-start | bytes 6148
  109.0 14.2 %copy-start.28 = (f32[1,512]{1,0:T(1,128)}, f32[1,512]{1,0:T(1,128)S(1)}, u32[]{:S(2)}) copy-start(f32[1,512]{1,0:T(1,128)S(1)} %get-tuple-element.49) | copy-start | bytes 6148
  110.8 29.1 %all-to-all-start.2 = ((f32[32,1,32]{2,1,0:T(1,128)}), f32[32,1,32]{2,1,0:T(1,128)S(1)}, u32[]{:S(2)}, u32[]{:S(2)}) async-start(f32[32,1,32]{2,1,0:T(1,128)} %transpose_reshape.3), calls=%async_computation.2 | async-start | bytes 32768 | tf_op jit(solution)/shard_map/all_to_all | solution.py:112
  115.8 7.6 %copy-start.3 = (f32[3,4,4,2048]{3,2,1,0:T(4,128)S(1)}, f32[3,4,4,2048]{3,2,1,0:T(4,128)}, u32[]{:S(2)}) copy-start(f32[3,4,4,2048]{3,2,1,0:T(4,128)} %copy-done.2) | copy-start | bytes 1179652
  115.8 7.6 %collective-permute-start.5 = (f32[2,4,1,2048]{3,2,1,0:T(1,128)S(1)}, f32[2,4,1,2048]{3,2,1,0:T(1,128)S(1)}, u32[]{:S(2)}, u32[]{:S(2)}) collective-permute-start(f32[2,4,1,2048]{3,2,1,0:T(1,128)S(1)} %slice.303), channel_id=1, source_target_pairs={{1,0},{2,1},{3,2},{4,3},{5,4},{6,5},{7,6},{8,7},{9,8},{10,9},{11,1... | collective-permute-start | bytes 196616 | tf_op jit(solution)/shard_map/ppermute | solution.py:15
  119.3 4.1 %collective-permute-start.4 = (f32[2,1,4,2048]{3,2,1,0:T(4,128)S(1)}, f32[2,1,4,2048]{3,2,1,0:T(4,128)S(1)}, u32[]{:S(2)}, u32[]{:S(2)}) collective-permute-start(f32[2,1,4,2048]{3,2,1,0:T(4,128)S(1)} %slice.299), channel_id=1, source_target_pairs={{32,0},{64,32},{96,64},{128,96},{160,128},{192,160},{224,192},{256... | collective-permute-start | bytes 196616 | tf_op jit(solution)/shard_map/ppermute | solution.py:15
  124.1 10.7 %collective-permute-start.7 = (f32[2,1,4,2048]{3,2,1,0:T(4,128)S(1)}, f32[2,1,4,2048]{3,2,1,0:T(4,128)S(1)}, u32[]{:S(2)}, u32[]{:S(2)}) collective-permute-start(f32[2,1,4,2048]{3,2,1,0:T(4,128)S(1)} %pad_maximum_fusion.10), channel_id=1, source_target_pairs={{0,32},{32,64},{64,96},{96,128},{128,160},{160,192},{192,224},{224... | collective-permute-start | bytes 196616 | tf_op jit(solution)/shard_map/ppermute | solution.py:15
  131.9 7.5 %copy-start.9 = (f32[3,4,4,2048]{3,2,1,0:T(4,128)}, f32[3,4,4,2048]{3,2,1,0:T(4,128)S(1)}, u32[]{:S(2)}) copy-start(f32[3,4,4,2048]{3,2,1,0:T(4,128)S(1)} %pad_maximum_fusion.1) | copy-start | bytes 1179652
  132.1 7.1 %collective-permute-start.6 = (f32[2,4,1,2048]{3,2,1,0:T(1,128)S(1)}, f32[2,4,1,2048]{3,2,1,0:T(1,128)S(1)}, u32[]{:S(2)}, u32[]{:S(2)}) collective-permute-start(f32[2,4,1,2048]{3,2,1,0:T(1,128)S(1)} %slice.313), channel_id=1, source_target_pairs={{0,1},{1,2},{2,3},{3,4},{4,5},{5,6},{6,7},{7,8},{8,9},{9,10},{10,1... | collective-permute-start | bytes 196616 | tf_op jit(solution)/shard_map/ppermute | solution.py:15
  134.8 4.8 %copy-start.12 = (f32[4,4,2048]{2,1,0:T(4,128)S(1)}, f32[4,4,2048]{2,1,0:T(4,128)}, u32[]{:S(2)}) copy-start(f32[4,4,2048]{2,1,0:T(4,128)} %bitcast_multiply_fusion) | copy-start | bytes 393220
  139.5 1.7 %copy-start.24 = (s32[1024]{0:T(1024)S(1)}, s32[1024]{0:T(1024)}, u32[]{:S(2)}) copy-start(s32[1024]{0:T(1024)} %get-tuple-element.73) | copy-start | bytes 12292
  139.5 1.7 %copy-start.25 = (s32[1024]{0:T(1024)S(1)}, s32[1024]{0:T(1024)}, u32[]{:S(2)}) copy-start(s32[1024]{0:T(1024)} %get-tuple-element.74) | copy-start | bytes 12292
  139.5 1.7 %copy-start.26 = (f32[1024]{0:T(1024)S(1)}, f32[1024]{0:T(1024)}, u32[]{:S(2)}) copy-start(f32[1024]{0:T(1024)} %compare_convert_fusion) | copy-start | bytes 12292

commit v4 on v3

--- a/solution.py
+++ b/solution.py
@@ -163,9 +163,9 @@
     polarization = polar_next
     sample_1 = sample(e_field)
 
-    returned = exchange(jnp.stack([sample_0, sample_1]).reshape(2, n_gy, capacity).transpose(1, 0, 2))
-    returned, e_field, h_field, polarization = lax.optimization_barrier((returned, e_field, h_field, polarization))
-    returned = from_slots(returned)
+    back = jnp.stack([sample_0, sample_1]).reshape(2, n_gy, capacity).transpose(1, 0, 2)
+    back, e_field, h_field, polarization = lax.optimization_barrier((back, e_field, h_field, polarization))
+    returned = from_slots(exchange(back))
     seg_sample_0, seg_sample_1 = returned[0], returned[1]
     curr_1 = curr_0 + gain_row * (seg_sample_0 - drop_0)
     curr_prev = jnp.concatenate([single_zero, curr_1[:-1]])
@@ -174,9 +174,9 @@
     curr_2 = curr_1 + gain_row * (seg_sample_1 - drop_1)
     curr_prev = jnp.concatenate([single_zero, curr_2[:-1]])
     volt_2 = volt_1 - cap_row * (curr_2 - curr_prev)
+    h_field = magnetic_update(e_field, h_field)
     recv_curr_2 = exchange(to_slots(curr_2[None], [0.0]))
 
-    h_field = magnetic_update(e_field, h_field)
     drive, polarization = electric_base(e_field, h_field, polarization, cells)
     recv_curr_2, drive = lax.optimization_barrier((recv_curr_2, drive))
     e_field = electric_finish(e_field, drive, wire_of(recv_curr_2.transpose(1, 0, 2).reshape(-1)), cells)

time: 145 us -> 145 us (level)
  the two profiles are of different devices: /device:TPU:38 before, /device:TPU:16 now
where the time goes in v4:
time: 145 us; the launch traced here: 144 us
  starting transfers between devices  66.3 us (46%)
  other arithmetic  27.6 us (19%)
  local copies, waits for them, and re-layouts  21.9 us (15%)
  matrix products  17.1 us (12%)
  waiting for transfers between devices  9.26 us (6%)
    all_to_all x3, starting transfers between devices, exchange(): return lax.all_to_all(blocks, 'gy', split_axis=0, concat_axis=0, tiled=True)  40.8 us
    ppermute x8, starting transfers between devices, passed_along(): lax.ppermute(value, axis, [(source, source + steps) for source in range(f...  25.4 us
    all_to_all x3, waiting for transfers between devices, exchange(): return lax.all_to_all(blocks, 'gy', split_axis=0, concat_axis=0, tiled=True)  6.04 us
    dot_general x2, matrix products, wire_of(): jnp.einsum('kr,kl->rl', row_hot, spread, precision=highest)  5.57 us
    dot_general x2, matrix products, sample(): jnp.dot(row_hot, e_now[2].reshape(plane_rows, lanes), precision=highest)  5.15 us
    ppermute x8, waiting for transfers between devices, passed_along(): lax.ppermute(value, axis, [(source, source + steps) for source in range(f...  3.22 us
  transfers between devices with their start and end apart: 11, of which 3 were waited for; matrix products, arithmetic and copies ran while one was open for 18% of the time, Pallas kernels for 0%

profile of v4, /device:TPU:16, one launch (start us, length us, event | category | flops | bytes accessed | tf_op | source)
XLA Modules:
  0.0 143.6 jit_solution(4910154404904609942)
XLA Ops:
  0.7 0.7 fusion.124
  1.4 1.2 reduce-window.6
  2.8 0.8 fusion.123
  3.6 0.7 multiply_add_fusion.6
  4.3 0.8 slice.257
  5.1 0.7 convert_element_type.39
  6.0 0.8 fusion.138
  6.8 1.7 %fusion.30 = f32[4,1024]{1,0:T(4,128)S(1)} fusion(s32[512]{0:T(512)S(1)} %multiply_add_fusion.6, f32[1,512]{1,0:T(1,128)S(1)} %fusion.138, f32[1,512]{1,0:T(1,128)} %param.32, f32[1,512]{1,0:T(1,128)} %param.30, f32[1,512]{1,0:T(1,128)S(1)} %convert_element_type.39, f32[1024]{0:T(1024)S(1)} %broadcast_subtract_fusion, f32[4]{0:T(128)} %constant.114.clone), kind=kOutput, calls=%fused_computation.26 | convolution fusion | flops 25704448 | bytes 30736 | tf_op jit(solution)/shard_map/fs,ts->ft/dot_general | solution.py:107
  8.7 0.7 reshape.290
  9.4 16.3 %all-to-all-start = ((f32[32,1,128]{2,1,0:T(1,128)}), f32[32,1,128]{2,1,0:T(1,128)}, u32[]{:S(2)}, u32[]{:S(2)}) async-start(f32[32,1,128]{2,1,0:T(1,128)} %reshape.290), calls=%async_computation | async-start | bytes 32768 | tf_op jit(solution)/shard_map/all_to_all | solution.py:112
  25.7 1.6 %slice.266 = f32[2,4,1,2048]{3,2,1,0:T(1,128)} slice(f32[3,4,4,2048]{3,2,1,0:T(4,128)} %param.20), slice={[0:3:2], [0:4:1], [0:1:1], [0:2048:1]} | slice | bytes 131072 | tf_op jit(solution)/shard_map/slice | solution.py:29
  27.4 1.3 collective-permute-start.1
  28.6 1.5 %slice.262 = f32[2,1,4,2048]{3,2,1,0:T(4,128)} slice(f32[3,4,4,2048]{3,2,1,0:T(4,128)} %param.20), slice={[1:3], [0:1], [0:4], [0:2048]} | slice | bytes 131072 | tf_op jit(solution)/shard_map/slice | solution.py:27
  30.1 3.9 %collective-permute-start = (f32[2,1,4,2048]{3,2,1,0:T(4,128)}, f32[2,1,4,2048]{3,2,1,0:T(4,128)S(1)}, u32[]{:S(2)}, u32[]{:S(2)}) collective-permute-start(f32[2,1,4,2048]{3,2,1,0:T(4,128)} %slice.262), channel_id=1, source_target_pairs={{32,0},{64,32},{96,64},{128,96},{160,128},{192,160},{224,192},{256... | collective-permute-start | bytes 196616 | tf_op jit(solution)/shard_map/ppermute | solution.py:15
  35.0 0.6 fusion
  36.6 0.7 bitcast_multiply_fusion
  37.3 1.9 %multiply_add_fusion.1 = (f32[4,3,4,4,2048]{4,3,2,1,0:T(4,128)S(1)}, f32[3,4,4,2048]{3,2,1,0:T(4,128)}) fusion(f32[4,3,4,4,2048]{4,3,2,1,0:T(4,128)S(1)} %copy-done.7, f32[3,4,4,2048]{3,2,1,0:T(4,128)S(1)} %copy-done.1, f32[4,4,4,2048]{3,2,1,0:T(4,128)S(1)} %copy.38, f32[4,4,4,2048]{3,2,1,0:T(4,128)S(1)} %copy.37), kind=kLoop, calls=%fused_computation.19 | loop fusion | flops 1867776 | bytes 4980736 | tf_op jit(solution)/shard_map/add | solution.py:60
  39.8 0.7 slice.261
  40.5 0.7 copy.51
  41.7 1.4 reduce.26
  43.1 0.7 reshape.291
  43.9 1.9 %fusion.165 = (f32[1,4,4,2048]{3,2,1,0:T(4,128)}, f32[1,4,4,2048]{3,2,1,0:T(4,128)S(1)}, f32[4,4,2048]{2,1,0:T(4,128)S(1)}, f32[4,4,2048]{2,1,0:T(4,128)S(1)}) fusion(f32[3,4,4,2048]{3,2,1,0:T(4,128)S(1)} %copy-done.1, f32[2,4,1,2048]{3,2,1,0:T(1,128)S(1)} %collective-permute-done.1, f32[2,4,3,2048]{3,2,1,0:T(4,128)S(1)} %slice.265, ...), kind=kLoop, calls=%fused_computation.241 | loop fusion | flops 229376 | bytes 1572864 | tf_op jit(solution)/shard_map/slice | solution.py:44
  46.1 1.0 fusion.110
  47.0 0.6 pad_maximum_fusion.11
  47.7 1.9 %collective-permute-start.3 = (f32[2,1,4,2048]{3,2,1,0:T(4,128)}, f32[2,1,4,2048]{3,2,1,0:T(4,128)}, u32[]{:S(2)}, u32[]{:S(2)}) collective-permute-start(f32[2,1,4,2048]{3,2,1,0:T(4,128)} %pad_maximum_fusion.11), channel_id=1, source_target_pairs={{0,32},{32,64},{64,96},{96,128},{128,160},{160,192},{192,224},{224... | collective-permute-start | bytes 196616 | tf_op jit(solution)/shard_map/ppermute | solution.py:15
  49.7 0.7 slice.276
  50.5 0.7 slice.277
  51.2 5.5 %collective-permute-start.2 = (f32[2,4,1,2048]{3,2,1,0:T(1,128)}, f32[2,4,1,2048]{3,2,1,0:T(1,128)}, u32[]{:S(2)}, u32[]{:S(2)}) collective-permute-start(f32[2,4,1,2048]{3,2,1,0:T(1,128)} %slice.276), channel_id=1, source_target_pairs={{0,1},{1,2},{2,3},{3,4},{4,5},{5,6},{6,7},{7,8},{8,9},{9,10},{10,1... | collective-permute-start | bytes 196616 | tf_op jit(solution)/shard_map/ppermute | solution.py:15
  56.7 1.6 %reshape_squeeze.15 = f32[256,128]{1,0:T(8,128)} reshape(f32[1,4,4,2048]{3,2,1,0:T(4,128)} %get-tuple-element.67) | data formatting | bytes 262144 | tf_op jit(solution)/shard_map/reshape;squeeze | solution.py:153
  58.3 1.0 fusion.59
  59.3 1.6 %fusion.77 = (f32[1,4,4,2048]{3,2,1,0:T(4,128)S(1)}, f32[4,4,2048]{2,1,0:T(4,128)S(1)}, f32[1,4,4,2048]{3,2,1,0:T(4,128)S(1)}) fusion(f32[2,4,1,2048]{3,2,1,0:T(1,128)} %collective-permute-done.2, f32[2,4,3,2048]{3,2,1,0:T(4,128)} %slice.277, f32[4,4,2048]{2,1,0:T(4,128)S(1)} %get-tuple-element.60, f32[4,4,2047]{2,1,0:T(4,128)S(1)} %bitcast.278, ...), kind=kLoop, calls=%fused_computation.96 | loop fusion | flops 491520 | bytes 2097088 | tf_op jit(solution)/shard_map/stack | solution.py:58
  61.3 0.9 convert_reduce_fusion.1
  63.4 1.1 slice_reduce_fusion.1
  64.6 0.7 reshape_squeeze.16
  65.2 0.7 reshape_squeeze.17
  65.9 0.7 reshape_squeeze.18
  66.5 3.0 %fusion.21 = f32[1024]{0:T(1024)} fusion(f32[256,128]{1,0:T(8,128)} %reshape_squeeze.15, f32[1024]{0:T(1024)} %compare_convert_fusion, s32[1024]{0:T(1024)} %get-tuple-element.74, s32[1024]{0:T(1024)} %get-tuple-element.73), kind=kOutput, calls=%fused_computation.23 | convolution fusion | flops 403569664 | bytes 147456 | tf_op jit(solution)/shard_map/dot_general | solution.py:153
  69.5 1.4 stack.71
  70.9 0.7 multiply_add_fusion.3
  71.6 3.5 %fusion.24 = f32[256,128]{1,0:T(8,128)} fusion(f32[1024]{0:T(1024)} %compare_convert_fusion, s32[1024]{0:T(1024)} %get-tuple-element.74, f32[1024]{0:T(1024)S(1)} %multiply_add_fusion.3, s32[1024]{0:T(1024)} %get-tuple-element.73), kind=kOutput, calls=%fused_computation.24 | convolution fusion | flops 403472384 | bytes 147456 | tf_op jit(solution)/shard_map/kr,kl->rl/dot_general | solution.py:158
  75.1 1.6 %mul.215 = f32[1,4,4,2048]{3,2,1,0:T(4,128)} reshape(f32[256,128]{1,0:T(8,128)} %fusion.24) | data formatting | bytes 262144 | tf_op jit(solution)/shard_map/mul | solution.py:69
  76.7 1.0 add_dynamic-update-slice_fusion.1
  77.7 0.7 copy-done.5
  78.4 1.1 divide_add_fusion.1
  79.6 2.2 %fusion.18 = f32[1024]{0:T(1024)S(1)} fusion(f32[256,128]{1,0:T(8,128)S(1)} %reshape_squeeze.19, f32[1024]{0:T(1024)} %compare_convert_fusion, s32[1024]{0:T(1024)} %get-tuple-element.74, s32[1024]{0:T(1024)} %get-tuple-element.73), kind=kOutput, calls=%fused_computation.22 | convolution fusion | flops 403569664 | bytes 147456 | tf_op jit(solution)/shard_map/dot_general | solution.py:153
  81.9 0.7 maximum_bitcast_fusion
  82.5 14.1 %all-to-all-start.1 = ((f32[32,2,32]{2,1,0:T(2,128)}), f32[32,2,32]{2,1,0:T(2,128)}, u32[]{:S(2)}, u32[]{:S(2)}) async-start(f32[32,2,32]{2,1,0:T(2,128)} %maximum_bitcast_fusion), calls=%async_computation.1 | async-start | bytes 65536 | tf_op jit(solution)/shard_map/all_to_all | solution.py:112
  96.7 2.0 %subtract_reduce_fusion = (f32[3,4,4,2048]{3,2,1,0:T(4,128)S(1)}, f32[4,3,4,4,2048]{4,3,2,1,0:T(4,128)}) fusion(f32[4,3,4,4,2048]{4,3,2,1,0:T(4,128)S(1)} %get-tuple-element.42, f32[3,4,4,2048]{3,2,1,0:T(4,128)S(1)} %bitcast.265, f32[4,4,4,2048]{3,2,1,0:T(4,128)S(1)} %copy.38, f32[4,4,4,2048]{3,2,1,0:T(4,128)S(1)} %copy.37), kind=kLoop, calls=%fused_computation.16 | loop fusion | flops 1867776 | bytes 4980736 | tf_op jit(solution)/shard_map/reduce_sum | solution.py:63
  98.9 1.3 collective-permute-start.5
  100.2 5.8 %collective-permute-start.4 = (f32[2,1,4,2048]{3,2,1,0:T(4,128)S(1)}, f32[2,1,4,2048]{3,2,1,0:T(4,128)S(1)}, u32[]{:S(2)}, u32[]{:S(2)}) collective-permute-start(f32[2,1,4,2048]{3,2,1,0:T(4,128)S(1)} %slice.299), channel_id=1, source_target_pairs={{32,0},{64,32},{96,64},{128,96},{160,128},{192,160},{224,192},{256... | collective-permute-start | bytes 196616 | tf_op jit(solution)/shard_map/ppermute | solution.py:15
  106.1 4.0 %all-to-all-done.1 = f32[32,2,32]{2,1,0:T(2,128)} async-done(((f32[32,2,32]{2,1,0:T(2,128)}), f32[32,2,32]{2,1,0:T(2,128)}, u32[]{:S(2)}, u32[]{:S(2)}) %all-to-all-start.1) | async-done | bytes 8224 | tf_op jit(solution)/shard_map/all_to_all | solution.py:112
  110.1 0.8 copy.39
  110.9 1.4 fusion.2
  112.7 0.7 fusion.154
  113.4 1.0 fusion.1
  114.4 0.7 transpose_reshape.3
  115.1 10.3 %all-to-all-start.2 = ((f32[32,1,32]{2,1,0:T(1,128)}), f32[32,1,32]{2,1,0:T(1,128)}, u32[]{:S(2)}, u32[]{:S(2)}) async-start(f32[32,1,32]{2,1,0:T(1,128)} %transpose_reshape.3), calls=%async_computation.2 | async-start | bytes 32768 | tf_op jit(solution)/shard_map/all_to_all | solution.py:112
  126.2 1.9 %collective-permute-start.7 = (f32[2,1,4,2048]{3,2,1,0:T(4,128)S(1)}, f32[2,1,4,2048]{3,2,1,0:T(4,128)S(1)}, u32[]{:S(2)}, u32[]{:S(2)}) collective-permute-start(f32[2,1,4,2048]{3,2,1,0:T(4,128)S(1)} %pad_maximum_fusion.10), channel_id=1, source_target_pairs={{0,32},{32,64},{64,96},{96,128},{128,160},{160,192},{192,224},{224... | collective-permute-start | bytes 196616 | tf_op jit(solution)/shard_map/ppermute | solution.py:15
  128.3 3.8 %collective-permute-start.6 = (f32[2,4,1,2048]{3,2,1,0:T(1,128)S(1)}, f32[2,4,1,2048]{3,2,1,0:T(1,128)S(1)}, u32[]{:S(2)}, u32[]{:S(2)}) collective-permute-start(f32[2,4,1,2048]{3,2,1,0:T(1,128)S(1)} %slice.313), channel_id=1, source_target_pairs={{0,1},{1,2},{2,3},{3,4},{4,5},{5,6},{6,7},{7,8},{8,9},{9,10},{10,1... | collective-permute-start | bytes 196616 | tf_op jit(solution)/shard_map/ppermute | solution.py:15
  132.2 3.2 %collective-permute-done.7 = f32[2,1,4,2048]{3,2,1,0:T(4,128)S(1)} collective-permute-done((f32[2,1,4,2048]{3,2,1,0:T(4,128)S(1)}, f32[2,1,4,2048]{3,2,1,0:T(4,128)S(1)}, u32[]{:S(2)}, u32[]{:S(2)}) %collective-permute-start.7) | collective-permute-done | bytes 65568 | tf_op jit(solution)/shard_map/ppermute | solution.py:15
  136.6 2.0 %all-to-all-done.2 = f32[32,1,32]{2,1,0:T(1,128)} async-done(((f32[32,1,32]{2,1,0:T(1,128)}), f32[32,1,32]{2,1,0:T(1,128)}, u32[]{:S(2)}, u32[]{:S(2)}) %all-to-all-start.2) | async-done | bytes 4128 | tf_op jit(solution)/shard_map/all_to_all | solution.py:112
  139.1 1.4 reduce.25
  140.6 2.1 %fusion.27 = f32[256,128]{1,0:T(8,128)S(1)} fusion(f32[1024]{0:T(1024)S(1)} %copy-done.26, s32[1024]{0:T(1024)S(1)} %copy-done.25, f32[1024]{0:T(1024)S(1)} %broadcast_in_dim.23, s32[1024]{0:T(1024)S(1)} %copy-done.24), kind=kOutput, calls=%fused_computation.25 | convolution fusion | flops 403472384 | bytes 147456 | tf_op jit(solution)/shard_map/kr,kl->rl/dot_general | solution.py:158
  142.8 0.8 divide_add_fusion
  (122 shorter events, 9.2 us)
Async XLA Ops:
  0.6 33.4 %copy-start = (f32[4,8]{1,0:T(4,128)S(1)}, f32[4,8]{1,0:T(4,128)}, u32[]{:S(2)}) copy-start(f32[4,8]{1,0:T(4,128)} %param.27) | copy-start | bytes 388
  0.6 33.4 %copy-start.16 = (s32[4,4,2048]{2,1,0:T(4,128)S(1)}, s32[4,4,2048]{2,1,0:T(4,128)}, u32[]{:S(2)}) copy-start(s32[4,4,2048]{2,1,0:T(4,128)} %param.23) | copy-start | bytes 393220
  1.4 33.6 %copy-start.27 = (f32[4,8]{1,0:T(4,128)S(1)}, f32[4,8]{1,0:T(4,128)}, u32[]{:S(2)}) copy-start(f32[4,8]{1,0:T(4,128)} %param.26) | copy-start | bytes 388
  4.3 4.2 %copy-start.22 = (s32[512]{0:T(512)}, s32[512]{0:T(512)S(1)}, u32[]{:S(2)}) copy-start(s32[512]{0:T(512)S(1)} %multiply_add_fusion.6) | copy-start | bytes 6148
  9.4 31.8 %all-to-all-start = ((f32[32,1,128]{2,1,0:T(1,128)}), f32[32,1,128]{2,1,0:T(1,128)}, u32[]{:S(2)}, u32[]{:S(2)}) async-start(f32[32,1,128]{2,1,0:T(1,128)} %reshape.290), calls=%async_computation | async-start | bytes 32768 | tf_op jit(solution)/shard_map/all_to_all | solution.py:112
  27.4 16.5 %collective-permute-start.1 = (f32[2,4,1,2048]{3,2,1,0:T(1,128)}, f32[2,4,1,2048]{3,2,1,0:T(1,128)S(1)}, u32[]{:S(2)}, u32[]{:S(2)}) collective-permute-start(f32[2,4,1,2048]{3,2,1,0:T(1,128)} %slice.266), channel_id=1, source_target_pairs={{1,0},{2,1},{3,2},{4,3},{5,4},{6,5},{7,6},{8,7},{9,8},{10,9},{11,1... | collective-permute-start | bytes 196616 | tf_op jit(solution)/shard_map/ppermute | solution.py:15
  30.1 13.7 %collective-permute-start = (f32[2,1,4,2048]{3,2,1,0:T(4,128)}, f32[2,1,4,2048]{3,2,1,0:T(4,128)S(1)}, u32[]{:S(2)}, u32[]{:S(2)}) collective-permute-start(f32[2,1,4,2048]{3,2,1,0:T(4,128)} %slice.262), channel_id=1, source_target_pairs={{32,0},{64,32},{96,64},{128,96},{160,128},{192,160},{224,192},{256... | collective-permute-start | bytes 196616 | tf_op jit(solution)/shard_map/ppermute | solution.py:15
  34.6 1.4 copy-start.29
  35.0 2.3 %copy-start.1 = (f32[3,4,4,2048]{3,2,1,0:T(4,128)S(1)}, f32[3,4,4,2048]{3,2,1,0:T(4,128)}, u32[]{:S(2)}) copy-start(f32[3,4,4,2048]{3,2,1,0:T(4,128)} %param.20) | copy-start | bytes 1179652
  35.0 2.3 %copy-start.7 = (f32[4,3,4,4,2048]{4,3,2,1,0:T(4,128)S(1)}, f32[4,3,4,4,2048]{4,3,2,1,0:T(4,128)}, u32[]{:S(2)}) copy-start(f32[4,3,4,4,2048]{4,3,2,1,0:T(4,128)} %param.22) | copy-start | bytes 4718596
  37.3 1.9 %copy-start.30 = (f32[8]{0:T(128)S(1)}, f32[8]{0:T(128)}, u32[]{:S(2)}) copy-start(f32[8]{0:T(128)} %param.24) | copy-start | bytes 100
  43.8 2.2 %copy-start.4 = (f32[2,3,4,2048]{3,2,1,0:T(4,128)S(1)}, f32[2,3,4,2048]{3,2,1,0:T(4,128)}, u32[]{:S(2)}) copy-start(f32[2,3,4,2048]{3,2,1,0:T(4,128)} %slice.261) | copy-start | bytes 589828
  43.9 2.2 %copy-start.13 = (f32[3,4,4,2048]{3,2,1,0:T(4,128)S(1)}, f32[3,4,4,2048]{3,2,1,0:T(4,128)}, u32[]{:S(2)}) copy-start(f32[3,4,4,2048]{3,2,1,0:T(4,128)} %param.21) | copy-start | bytes 1179652
  43.9 2.0 %copy-start.14 = (f32[2,4,1,2048]{3,2,1,0:T(1,128)}, f32[2,4,1,2048]{3,2,1,0:T(1,128)S(1)}, u32[]{:S(2)}) copy-start(f32[2,4,1,2048]{3,2,1,0:T(1,128)S(1)} %collective-permute-done.1) | copy-start | bytes 196612
  43.9 2.0 %copy-start.15 = (f32[2,1,4,2048]{3,2,1,0:T(4,128)}, f32[2,1,4,2048]{3,2,1,0:T(4,128)S(1)}, u32[]{:S(2)}) copy-start(f32[2,1,4,2048]{3,2,1,0:T(4,128)S(1)} %collective-permute-done) | copy-start | bytes 196612
  45.7 4.0 %copy-start.6 = (f32[1,4,4,2048]{3,2,1,0:T(4,128)}, f32[1,4,4,2048]{3,2,1,0:T(4,128)S(1)}, u32[]{:S(2)}) copy-start(f32[1,4,4,2048]{3,2,1,0:T(4,128)S(1)} %get-tuple-element.68) | copy-start | bytes 393220
  47.7 10.6 %collective-permute-start.3 = (f32[2,1,4,2048]{3,2,1,0:T(4,128)}, f32[2,1,4,2048]{3,2,1,0:T(4,128)}, u32[]{:S(2)}, u32[]{:S(2)}) collective-permute-start(f32[2,1,4,2048]{3,2,1,0:T(4,128)} %pad_maximum_fusion.11), channel_id=1, source_target_pairs={{0,32},{32,64},{64,96},{96,128},{128,160},{160,192},{192,224},{224... | collective-permute-start | bytes 196616 | tf_op jit(solution)/shard_map/ppermute | solution.py:15
  49.7 0.8 copy-start.2
  51.2 8.1 %collective-permute-start.2 = (f32[2,4,1,2048]{3,2,1,0:T(1,128)}, f32[2,4,1,2048]{3,2,1,0:T(1,128)}, u32[]{:S(2)}, u32[]{:S(2)}) collective-permute-start(f32[2,4,1,2048]{3,2,1,0:T(1,128)} %slice.276), channel_id=1, source_target_pairs={{0,1},{1,2},{2,3},{3,4},{4,5},{5,6},{6,7},{7,8},{8,9},{9,10},{10,1... | collective-permute-start | bytes 196616 | tf_op jit(solution)/shard_map/ppermute | solution.py:15
  59.3 1.7 %copy-start.8 = (f32[3,4,4,2048]{3,2,1,0:T(4,128)S(1)}, f32[3,4,4,2048]{3,2,1,0:T(4,128)}, u32[]{:S(2)}) copy-start(f32[3,4,4,2048]{3,2,1,0:T(4,128)} %get-tuple-element.57) | copy-start | bytes 1179652
  59.3 1.7 %copy-start.11 = (f32[4,4,2048]{2,1,0:T(4,128)S(1)}, f32[4,4,2048]{2,1,0:T(4,128)}, u32[]{:S(2)}) copy-start(f32[4,4,2048]{2,1,0:T(4,128)} %bitcast_multiply_fusion) | copy-start | bytes 393220
  66.5 11.9 %copy-start.10 = (f32[1,4,4,2048]{3,2,1,0:T(4,128)S(1)}, f32[1,4,4,2048]{3,2,1,0:T(4,128)}, u32[]{:S(2)}) copy-start(f32[1,4,4,2048]{3,2,1,0:T(4,128)} %copy.51) | copy-start | bytes 393220
  77.7 0.7 copy-start.5
  79.5 2.4 %copy-start.17 = (f32[1,32,32]{2,0,1:T(1,128)S(1)}, f32[1,32,32]{2,0,1:T(1,128)}, u32[]{:S(2)}) copy-start(f32[1,32,32]{2,0,1:T(1,128)} %stack.71) | copy-start | bytes 12292
  82.5 27.6 %all-to-all-start.1 = ((f32[32,2,32]{2,1,0:T(2,128)}), f32[32,2,32]{2,1,0:T(2,128)}, u32[]{:S(2)}, u32[]{:S(2)}) async-start(f32[32,2,32]{2,1,0:T(2,128)} %maximum_bitcast_fusion), calls=%async_computation.1 | async-start | bytes 65536 | tf_op jit(solution)/shard_map/all_to_all | solution.py:112
  98.7 13.6 %copy-start.18 = (f32[1,512]{1,0:T(1,128)S(1)}, f32[1,512]{1,0:T(1,128)}, u32[]{:S(2)}) copy-start(f32[1,512]{1,0:T(1,128)} %param.31) | copy-start | bytes 6148
  98.7 13.6 %copy-start.19 = (f32[1,512]{1,0:T(1,128)S(1)}, f32[1,512]{1,0:T(1,128)}, u32[]{:S(2)}) copy-start(f32[1,512]{1,0:T(1,128)} %param.32) | copy-start | bytes 6148
  98.7 13.6 %copy-start.20 = (f32[1,512]{1,0:T(1,128)S(1)}, f32[1,512]{1,0:T(1,128)}, u32[]{:S(2)}) copy-start(f32[1,512]{1,0:T(1,128)} %param.30) | copy-start | bytes 6148
  98.7 13.7 %copy-start.21 = (f32[1,512]{1,0:T(1,128)S(1)}, f32[1,512]{1,0:T(1,128)}, u32[]{:S(2)}) copy-start(f32[1,512]{1,0:T(1,128)} %param.33) | copy-start | bytes 6148
  98.7 14.7 %copy-start.23 = (s32[512]{0:T(512)S(1)}, s32[512]{0:T(512)}, u32[]{:S(2)}) copy-start(s32[512]{0:T(512)} %copy-done.22) | copy-start | bytes 6148
  98.7 26.8 %copy-start.3 = (f32[3,4,4,2048]{3,2,1,0:T(4,128)S(1)}, f32[3,4,4,2048]{3,2,1,0:T(4,128)}, u32[]{:S(2)}) copy-start(f32[3,4,4,2048]{3,2,1,0:T(4,128)} %copy-done.2) | copy-start | bytes 1179652
  98.9 26.6 %collective-permute-start.5 = (f32[2,4,1,2048]{3,2,1,0:T(1,128)S(1)}, f32[2,4,1,2048]{3,2,1,0:T(1,128)S(1)}, u32[]{:S(2)}, u32[]{:S(2)}) collective-permute-start(f32[2,4,1,2048]{3,2,1,0:T(1,128)S(1)} %slice.303), channel_id=1, source_target_pairs={{1,0},{2,1},{3,2},{4,3},{5,4},{6,5},{7,6},{8,7},{9,8},{10,9},{11,1... | collective-permute-start | bytes 196616 | tf_op jit(solution)/shard_map/ppermute | solution.py:15
  100.2 25.3 %collective-permute-start.4 = (f32[2,1,4,2048]{3,2,1,0:T(4,128)S(1)}, f32[2,1,4,2048]{3,2,1,0:T(4,128)S(1)}, u32[]{:S(2)}, u32[]{:S(2)}) collective-permute-start(f32[2,1,4,2048]{3,2,1,0:T(4,128)S(1)} %slice.299), channel_id=1, source_target_pairs={{32,0},{64,32},{96,64},{128,96},{160,128},{192,160},{224,192},{256... | collective-permute-start | bytes 196616 | tf_op jit(solution)/shard_map/ppermute | solution.py:15
  113.4 1.0 copy-start.28
  115.1 23.4 %all-to-all-start.2 = ((f32[32,1,32]{2,1,0:T(1,128)}), f32[32,1,32]{2,1,0:T(1,128)}, u32[]{:S(2)}, u32[]{:S(2)}) async-start(f32[32,1,32]{2,1,0:T(1,128)} %transpose_reshape.3), calls=%async_computation.2 | async-start | bytes 32768 | tf_op jit(solution)/shard_map/all_to_all | solution.py:112
  126.2 9.2 %collective-permute-start.7 = (f32[2,1,4,2048]{3,2,1,0:T(4,128)S(1)}, f32[2,1,4,2048]{3,2,1,0:T(4,128)S(1)}, u32[]{:S(2)}, u32[]{:S(2)}) collective-permute-start(f32[2,1,4,2048]{3,2,1,0:T(4,128)S(1)} %pad_maximum_fusion.10), channel_id=1, source_target_pairs={{0,32},{32,64},{64,96},{96,128},{128,160},{160,192},{192,224},{224... | collective-permute-start | bytes 196616 | tf_op jit(solution)/shard_map/ppermute | solution.py:15
  128.2 7.6 %copy-start.9 = (f32[3,4,4,2048]{3,2,1,0:T(4,128)}, f32[3,4,4,2048]{3,2,1,0:T(4,128)S(1)}, u32[]{:S(2)}) copy-start(f32[3,4,4,2048]{3,2,1,0:T(4,128)S(1)} %pad_maximum_fusion.1) | copy-start | bytes 1179652
  128.3 7.1 %collective-permute-start.6 = (f32[2,4,1,2048]{3,2,1,0:T(1,128)S(1)}, f32[2,4,1,2048]{3,2,1,0:T(1,128)S(1)}, u32[]{:S(2)}, u32[]{:S(2)}) collective-permute-start(f32[2,4,1,2048]{3,2,1,0:T(1,128)S(1)} %slice.313), channel_id=1, source_target_pairs={{0,1},{1,2},{2,3},{3,4},{4,5},{5,6},{6,7},{7,8},{8,9},{9,10},{10,1... | collective-permute-start | bytes 196616 | tf_op jit(solution)/shard_map/ppermute | solution.py:15
  135.4 0.9 copy-start.12
  135.8 4.8 %copy-start.24 = (s32[1024]{0:T(1024)S(1)}, s32[1024]{0:T(1024)}, u32[]{:S(2)}) copy-start(s32[1024]{0:T(1024)} %get-tuple-element.73) | copy-start | bytes 12292
  135.8 4.8 %copy-start.25 = (s32[1024]{0:T(1024)S(1)}, s32[1024]{0:T(1024)}, u32[]{:S(2)}) copy-start(s32[1024]{0:T(1024)} %get-tuple-element.74) | copy-start | bytes 12292
  135.8 4.7 %copy-start.26 = (f32[1024]{0:T(1024)S(1)}, f32[1024]{0:T(1024)}, u32[]{:S(2)}) copy-start(f32[1024]{0:T(1024)} %compare_convert_fusion) | copy-start | bytes 12292

commit v5 on v4

--- a/solution.py
+++ b/solution.py
@@ -157,14 +157,23 @@
         spread = jnp.where(lane_hot, values[:, None], 0.0)
         return jnp.einsum("kr,kl->rl", row_hot, spread, precision=highest).reshape(grid_shape)
 
-    sample_0 = sample(e_field)
+    def plane(field):
+        return field.reshape(plane_rows, lanes)
+
+    def pick(planes):
+        picked = jnp.dot(row_hot, jnp.concatenate(planes, axis=1), precision=highest)
+        return [jnp.sum(jnp.where(lane_hot, picked[:, i * lanes:(i + 1) * lanes], 0.0), axis=1) for i in range(len(planes))]
+
+    sample_0, drive_at, eps_at = pick([plane(e_field[2]), plane(drive[2]), plane(eps_cell)])
     curr_cell_1 = recv_curr + recv_gain * (sample_0 - recv_drop)
-    e_field = electric_finish(e_field, drive, wire_of(curr_cell_1), cells)
+    wire_plane = jnp.einsum("kr,kl->rl", row_hot, jnp.where(lane_hot, curr_cell_1[:, None], 0.0), precision=highest)
+    (wire_at,) = pick([wire_plane])
+    sample_1 = jnp.where(valid_flat, sample_0 + (drive_at + -TIME_STEP * wire_at) / eps_at, 0.0)
     polarization = polar_next
-    sample_1 = sample(e_field)
 
     back = jnp.stack([sample_0, sample_1]).reshape(2, n_gy, capacity).transpose(1, 0, 2)
-    back, e_field, h_field, polarization = lax.optimization_barrier((back, e_field, h_field, polarization))
+    back, drive, wire_plane, h_field, polarization = lax.optimization_barrier((back, drive, wire_plane, h_field, polarization))
+    e_field = electric_finish(e_field, drive, wire_plane.reshape(grid_shape), cells)
     returned = from_slots(exchange(back))
     seg_sample_0, seg_sample_1 = returned[0], returned[1]
     curr_1 = curr_0 + gain_row * (seg_sample_0 - drop_0)

time: 145 us -> 155 us (1.069)
  starting transfers between devices: 66.3 us -> 72 us
  local copies, waits for them, and re-layouts: 21.9 us -> 26.5 us
  other arithmetic: 27.6 us -> 31 us
  waiting for transfers between devices: 9.26 us -> 6.32 us
    all_to_all x3, starting transfers between devices: 40.8 us -> 47.3 us  [exchange(): return lax.all_to_all(blocks, 'gy', split_axis=0, concat_axis=0, tiled=True)]
    all_to_all x3, waiting for transfers between devices: 6.04 us -> 2.09 us  [exchange(): return lax.all_to_all(blocks, 'gy', split_axis=0, concat_axis=0, tiled=True)]
    dot_general x2 -> x1, matrix products: 5.57 us -> 2.11 us  [wire_of(): jnp.einsum('kr,kl->rl', row_hot, spread, precision=highest)]
    unnamed x63 -> x81, local copies, waits for them, and re-layouts: 1.97 us -> 3.97 us
    dot_general x2 -> x3, matrix products: 5.15 us -> 7.12 us  [the longest x2 5.01 us: pick(): jnp.dot(row_hot, jnp.concatenate(planes, axis=1), precision=highest)]
    reshape x0 -> x1, local copies, waits for them, and re-layouts: none -> 1.62 us  [plane(): return field.reshape(plane_rows, lanes)]
    mul x0 -> x1, other arithmetic: none -> 1.57 us  [electric_finish(): drive = drive.at[2].add(-TIME_STEP * wire_term)]
  transfers between devices with their start and end apart: 11 -> 11, of which waited for: 3 -> 3; matrix products, arithmetic and copies ran while one was open for 18% -> 22% of each run, Pallas kernels for 0% -> 0%
where the time goes in v5:
time: 155 us; the launch traced here: 153 us
  starting transfers between devices  72 us (46%)
  other arithmetic  31 us (20%)
  local copies, waits for them, and re-layouts  26.5 us (17%)
  matrix products  15.9 us (10%)
  waiting for transfers between devices  6.32 us (4%)
    all_to_all x3, starting transfers between devices, exchange(): return lax.all_to_all(blocks, 'gy', split_axis=0, concat_axis=0, tiled=True)  47.3 us
    ppermute x8, starting transfers between devices, passed_along(): lax.ppermute(value, axis, [(source, source + steps) for source in range(f...  24.7 us
    dot_general x2, matrix products, pick(): jnp.dot(row_hot, jnp.concatenate(planes, axis=1), precision=highest)  5.01 us
    ppermute x8, waiting for transfers between devices, passed_along(): lax.ppermute(value, axis, [(source, source + steps) for source in range(f...  4.23 us
    unnamed x81, local copies, waits for them, and re-layouts  3.97 us
  transfers between devices with their start and end apart: 11, of which 3 were waited for; matrix products, arithmetic and copies ran while one was open for 22% of the time, Pallas kernels for 0%

profile of v5, /device:TPU:16, one launch (start us, length us, event | category | flops | bytes accessed | tf_op | source)
XLA Modules:
  0.0 153.2 jit_solution(9329467353487751148)
XLA Ops:
  0.7 0.8 slice.266
  1.4 0.7 convert_element_type.48
  2.1 0.7 fusion.123
  2.8 1.2 reduce-window.6
  4.2 0.8 fusion.122
  5.0 0.7 multiply_add_fusion.6
  6.0 0.8 fusion.137
  6.8 1.7 %fusion.21 = f32[4,1024]{1,0:T(4,128)S(1)} fusion(s32[512]{0:T(512)S(1)} %multiply_add_fusion.6, f32[1,512]{1,0:T(1,128)S(1)} %fusion.137, f32[1,512]{1,0:T(1,128)} %param.32, f32[1,512]{1,0:T(1,128)} %param.30, f32[1,512]{1,0:T(1,128)S(1)} %convert_element_type.48, f32[1024]{0:T(1024)S(1)} %broadcast_subtract_fusion, f32[4]{0:T(128)} %constant.115.clone), kind=kOutput, calls=%fused_computation.23 | convolution fusion | flops 25704448 | bytes 30736 | tf_op jit(solution)/shard_map/fs,ts->ft/dot_general | solution.py:107
  8.7 0.7 reshape.354
  9.4 16.3 %all-to-all-start = ((f32[32,1,128]{2,1,0:T(1,128)}), f32[32,1,128]{2,1,0:T(1,128)}, u32[]{:S(2)}, u32[]{:S(2)}) async-start(f32[32,1,128]{2,1,0:T(1,128)} %reshape.354), calls=%async_computation | async-start | bytes 32768 | tf_op jit(solution)/shard_map/all_to_all | solution.py:112
  25.7 1.5 slice.271
  27.2 3.9 %collective-permute-start = (f32[2,1,4,2048]{3,2,1,0:T(4,128)}, f32[2,1,4,2048]{3,2,1,0:T(4,128)S(1)}, u32[]{:S(2)}, u32[]{:S(2)}) collective-permute-start(f32[2,1,4,2048]{3,2,1,0:T(4,128)} %slice.271), channel_id=1, source_target_pairs={{32,0},{64,32},{96,64},{128,96},{160,128},{192,160},{224,192},{256... | collective-permute-start | bytes 196616 | tf_op jit(solution)/shard_map/ppermute | solution.py:15
  31.1 1.6 %slice.275 = f32[2,4,1,2048]{3,2,1,0:T(1,128)} slice(f32[3,4,4,2048]{3,2,1,0:T(4,128)} %param.20), slice={[0:3:2], [0:4:1], [0:1:1], [0:2048:1]} | slice | bytes 131072 | tf_op jit(solution)/shard_map/slice | solution.py:29
  32.7 1.3 collective-permute-start.1
  34.0 1.5 fusion.23
  35.5 0.7 bitcast_multiply_fusion
  38.3 1.9 %multiply_add_fusion.1 = (f32[4,3,4,4,2048]{4,3,2,1,0:T(4,128)S(1)}, f32[3,4,4,2048]{3,2,1,0:T(4,128)}) fusion(f32[4,3,4,4,2048]{4,3,2,1,0:T(4,128)S(1)} %copy-done.8, f32[3,4,4,2048]{3,2,1,0:T(4,128)S(1)} %copy-done.1, f32[4,4,4,2048]{3,2,1,0:T(4,128)S(1)} %copy.41, f32[4,4,4,2048]{3,2,1,0:T(4,128)S(1)} %copy.40), kind=kLoop, calls=%fused_computation.19 | loop fusion | flops 1867776 | bytes 4980736 | tf_op jit(solution)/shard_map/add | solution.py:60
  40.9 0.7 copy.56
  41.6 1.6 %reshape.318 = f32[256,128]{1,0:T(8,128)} reshape(f32[4,4,2048]{2,1,0:T(4,128)} %bitcast.291) | data formatting | bytes 262144 | tf_op jit(solution)/shard_map/reshape | solution.py:161
  43.7 2.0 %reduce.22 = f32[32,128]{1,0:T(8,128)} reduce(f32[32,1,128]{2,1,0:T(1,128)} %all-to-all-done, f32[]{:T(128)} %broadcast.291), dimensions={1}, to_apply=%all_to_all.9.reduce_sub_computation | reduce | bytes 32772 | tf_op jit(solution)/shard_map/all_to_all | solution.py:112
  45.7 1.4 reshape.355
  47.1 1.8 %fusion.165 = (f32[1,4,4,2048]{3,2,1,0:T(4,128)}, f32[1,4,4,2048]{3,2,1,0:T(4,128)S(1)}, f32[4,4,2048]{2,1,0:T(4,128)S(1)}, f32[4,4,2048]{2,1,0:T(4,128)S(1)}) fusion(f32[3,4,4,2048]{3,2,1,0:T(4,128)S(1)} %copy-done.1, f32[2,4,1,2048]{3,2,1,0:T(1,128)} %collective-permute-done.1, f32[2,4,3,2048]{3,2,1,0:T(4,128)S(1)} %slice.274, ...), kind=kLoop, calls=%fused_computation.253 | loop fusion | flops 229376 | bytes 1572864 | tf_op jit(solution)/shard_map/slice | solution.py:44
  49.2 1.1 fusion.109
  51.0 1.9 %collective-permute-start.3 = (f32[2,1,4,2048]{3,2,1,0:T(4,128)}, f32[2,1,4,2048]{3,2,1,0:T(4,128)}, u32[]{:S(2)}, u32[]{:S(2)}) collective-permute-start(f32[2,1,4,2048]{3,2,1,0:T(4,128)} %pad_maximum_fusion.11), channel_id=1, source_target_pairs={{0,32},{32,64},{64,96},{96,128},{128,160},{160,192},{192,224},{224... | collective-permute-start | bytes 196616 | tf_op jit(solution)/shard_map/ppermute | solution.py:15
  53.0 0.8 slice.285
  53.8 0.7 slice.286
  54.5 1.6 %reshape_squeeze.15 = f32[256,128]{1,0:T(8,128)} reshape(f32[1,4,4,2048]{3,2,1,0:T(4,128)} %get-tuple-element.72) | data formatting | bytes 262144 | tf_op jit(solution)/shard_map/reshape;squeeze | solution.py:161
  56.1 4.7 %collective-permute-start.2 = (f32[2,4,1,2048]{3,2,1,0:T(1,128)}, f32[2,4,1,2048]{3,2,1,0:T(1,128)S(1)}, u32[]{:S(2)}, u32[]{:S(2)}) collective-permute-start(f32[2,4,1,2048]{3,2,1,0:T(1,128)} %slice.285), channel_id=1, source_target_pairs={{0,1},{1,2},{2,3},{3,4},{4,5},{5,6},{6,7},{7,8},{8,9},{9,10},{10,1... | collective-permute-start | bytes 196616 | tf_op jit(solution)/shard_map/ppermute | solution.py:15
  60.9 1.0 fusion.58
  61.9 1.0 collective-permute-done.2
  62.9 1.5 fusion.76
  68.0 0.7 reshape_squeeze.18
  68.6 0.7 reshape_squeeze.17
  69.3 0.7 reshape_squeeze.16
  70.1 2.8 %fusion.10 = f32[1024,384]{0,1:T(8,128)S(1)} fusion(f32[1024]{0:T(1024)} %compare_convert_fusion, s32[1024]{0:T(1024)} %get-tuple-element.79, f32[256,128]{1,0:T(8,128)} %reshape.318, f32[256,128]{1,0:T(8,128)} %reshape_squeeze.16, f32[256,128]{1,0:T(8,128)} %reshape_squeeze.15), kind=kOutput, calls=%fused_computation.14 | convolution fusion | flops 1208680448 | bytes 1974272 | tf_op jit(solution)/shard_map/dot_general | solution.py:164
  72.9 0.8 fusion.28
  73.7 0.7 stack.69
  74.4 2.1 %fusion.8 = f32[256,128]{1,0:T(8,128)S(1)} fusion(f32[1024]{0:T(1024)S(1)} %copy-done.28, s32[1024]{0:T(1024)S(1)} %copy-done.26, f32[1024]{0:T(1024)S(1)} %multiply_add_fusion.3, s32[1024]{0:T(1024)S(1)} %copy-done.24), kind=kOutput, calls=%fused_computation.12 | convolution fusion | flops 403439616 | bytes 147456 | tf_op jit(solution)/shard_map/kr,kl->rl/dot_general | solution.py:169
  77.2 2.2 %fusion.15 = f32[1024]{0:T(1024)S(1)} fusion(f32[256,128]{1,0:T(8,128)S(1)} %fusion.8, f32[1024]{0:T(1024)} %compare_convert_fusion, s32[1024]{0:T(1024)} %get-tuple-element.79, s32[1024]{0:T(1024)} %get-tuple-element.78), kind=kOutput, calls=%fused_computation.21 | convolution fusion | flops 403569664 | bytes 147456 | tf_op jit(solution)/shard_map/dot_general | solution.py:164
  80.0 1.3 div.45
  81.3 0.8 add_select_fusion
  82.1 0.7 maximum_bitcast_fusion
  83.4 16.3 %all-to-all-start.1 = ((f32[32,2,32]{2,1,0:T(2,128)}), f32[32,2,32]{2,1,0:T(2,128)}, u32[]{:S(2)}, u32[]{:S(2)}) async-start(f32[32,2,32]{2,1,0:T(2,128)} %copy.43), calls=%async_computation.1 | async-start | bytes 65536 | tf_op jit(solution)/shard_map/all_to_all | solution.py:112
  99.8 1.6 %broadcast_multiply_fusion = f32[256,128]{1,0:T(8,128)} fusion(f32[256,128]{1,0:T(8,128)} %copy-done.19), kind=kLoop, calls=%fused_computation.180 | loop fusion | flops 32768 | bytes 262144 | tf_op jit(solution)/shard_map/mul | solution.py:69
  101.4 1.6 %mul.232 = f32[1,4,4,2048]{3,2,1,0:T(4,128)} reshape(f32[256,128]{1,0:T(8,128)} %broadcast_multiply_fusion) | data formatting | bytes 262144 | tf_op jit(solution)/shard_map/mul | solution.py:69
  103.0 1.0 add_dynamic-update-slice_fusion.1
  103.9 0.7 copy-done.5
  104.7 1.1 divide_add_fusion.1
  105.8 2.7 %subtract_reduce_fusion = (f32[3,4,4,2048]{3,2,1,0:T(4,128)}, f32[4,3,4,4,2048]{4,3,2,1,0:T(4,128)}) fusion(f32[4,3,4,4,2048]{4,3,2,1,0:T(4,128)S(1)} %get-tuple-element.44, f32[3,4,4,2048]{3,2,1,0:T(4,128)S(1)} %bitcast.267, f32[4,4,4,2048]{3,2,1,0:T(4,128)S(1)} %copy.41, f32[4,4,4,2048]{3,2,1,0:T(4,128)S(1)} %copy.40), kind=kLoop, calls=%fused_computation.16 | loop fusion | flops 1867776 | bytes 4980736 | tf_op jit(solution)/shard_map/reduce_sum | solution.py:63
  108.7 5.8 %collective-permute-start.4 = (f32[2,1,4,2048]{3,2,1,0:T(4,128)S(1)}, f32[2,1,4,2048]{3,2,1,0:T(4,128)S(1)}, u32[]{:S(2)}, u32[]{:S(2)}) collective-permute-start(f32[2,1,4,2048]{3,2,1,0:T(4,128)S(1)} %slice.357), channel_id=1, source_target_pairs={{32,0},{64,32},{96,64},{128,96},{160,128},{192,160},{224,192},{256... | collective-permute-start | bytes 196616 | tf_op jit(solution)/shard_map/ppermute | solution.py:15
  114.5 1.3 collective-permute-start.5
  115.9 0.8 copy.44
  116.7 0.7 fusion.2
  117.9 0.7 fusion.153
  118.5 1.0 fusion.1
  119.6 0.7 transpose_reshape.3
  120.2 14.6 %all-to-all-start.2 = ((f32[32,1,32]{2,1,0:T(1,128)}), f32[32,1,32]{2,1,0:T(1,128)}, u32[]{:S(2)}, u32[]{:S(2)}) async-start(f32[32,1,32]{2,1,0:T(1,128)} %transpose_reshape.3), calls=%async_computation.2 | async-start | bytes 32768 | tf_op jit(solution)/shard_map/all_to_all | solution.py:112
  135.6 1.9 %collective-permute-start.7 = (f32[2,1,4,2048]{3,2,1,0:T(4,128)S(1)}, f32[2,1,4,2048]{3,2,1,0:T(4,128)S(1)}, u32[]{:S(2)}, u32[]{:S(2)}) collective-permute-start(f32[2,1,4,2048]{3,2,1,0:T(4,128)S(1)} %pad_maximum_fusion.10), channel_id=1, source_target_pairs={{0,32},{32,64},{64,96},{96,128},{128,160},{160,192},{192,224},{224... | collective-permute-start | bytes 196616 | tf_op jit(solution)/shard_map/ppermute | solution.py:15
  137.7 3.8 %collective-permute-start.6 = (f32[2,4,1,2048]{3,2,1,0:T(1,128)S(1)}, f32[2,4,1,2048]{3,2,1,0:T(1,128)S(1)}, u32[]{:S(2)}, u32[]{:S(2)}) collective-permute-start(f32[2,4,1,2048]{3,2,1,0:T(1,128)S(1)} %slice.325), channel_id=1, source_target_pairs={{0,1},{1,2},{2,3},{3,4},{4,5},{5,6},{6,7},{7,8},{8,9},{9,10},{10,1... | collective-permute-start | bytes 196616 | tf_op jit(solution)/shard_map/ppermute | solution.py:15
  141.6 3.2 %collective-permute-done.7 = f32[2,1,4,2048]{3,2,1,0:T(4,128)S(1)} collective-permute-done((f32[2,1,4,2048]{3,2,1,0:T(4,128)S(1)}, f32[2,1,4,2048]{3,2,1,0:T(4,128)S(1)}, u32[]{:S(2)}, u32[]{:S(2)}) %collective-permute-start.7) | collective-permute-done | bytes 65568 | tf_op jit(solution)/shard_map/ppermute | solution.py:15
  146.1 2.1 %all-to-all-done.2 = f32[32,1,32]{2,1,0:T(1,128)} async-done(((f32[32,1,32]{2,1,0:T(1,128)}), f32[32,1,32]{2,1,0:T(1,128)}, u32[]{:S(2)}, u32[]{:S(2)}) %all-to-all-start.2) | async-done | bytes 4128 | tf_op jit(solution)/shard_map/all_to_all | solution.py:112
  148.7 1.4 reduce.21
  150.2 2.1 %fusion.18 = f32[256,128]{1,0:T(8,128)S(1)} fusion(f32[1024]{0:T(1024)S(1)} %copy-done.29, s32[1024]{0:T(1024)S(1)} %copy-done.27, f32[1024]{0:T(1024)S(1)} %broadcast_in_dim.34, s32[1024]{0:T(1024)S(1)} %copy-done.25), kind=kOutput, calls=%fused_computation.22 | convolution fusion | flops 403472384 | bytes 147456 | tf_op jit(solution)/shard_map/kr,kl->rl/dot_general | solution.py:158
  152.4 0.8 divide_add_fusion
  (147 shorter events, 13.8 us)
Async XLA Ops:
  0.6 35.5 %copy-start = (f32[4,8]{1,0:T(4,128)S(1)}, f32[4,8]{1,0:T(4,128)}, u32[]{:S(2)}) copy-start(f32[4,8]{1,0:T(4,128)} %param.27) | copy-start | bytes 388
  0.6 35.5 %copy-start.16 = (s32[4,4,2048]{2,1,0:T(4,128)S(1)}, s32[4,4,2048]{2,1,0:T(4,128)}, u32[]{:S(2)}) copy-start(s32[4,4,2048]{2,1,0:T(4,128)} %param.23) | copy-start | bytes 393220
  5.7 27.0 %copy-start.35 = (s32[512]{0:T(512)}, s32[512]{0:T(512)S(1)}, u32[]{:S(2)}) copy-start(s32[512]{0:T(512)S(1)} %multiply_add_fusion.6) | copy-start | bytes 6148
  8.5 28.6 %copy-start.37 = (f32[4,8]{1,0:T(4,128)S(1)}, f32[4,8]{1,0:T(4,128)}, u32[]{:S(2)}) copy-start(f32[4,8]{1,0:T(4,128)} %param.26) | copy-start | bytes 388
  9.4 33.8 %all-to-all-start = ((f32[32,1,128]{2,1,0:T(1,128)}), f32[32,1,128]{2,1,0:T(1,128)}, u32[]{:S(2)}, u32[]{:S(2)}) async-start(f32[32,1,128]{2,1,0:T(1,128)} %reshape.354), calls=%async_computation | async-start | bytes 32768 | tf_op jit(solution)/shard_map/all_to_all | solution.py:112
  27.2 19.9 %collective-permute-start = (f32[2,1,4,2048]{3,2,1,0:T(4,128)}, f32[2,1,4,2048]{3,2,1,0:T(4,128)S(1)}, u32[]{:S(2)}, u32[]{:S(2)}) collective-permute-start(f32[2,1,4,2048]{3,2,1,0:T(4,128)} %slice.271), channel_id=1, source_target_pairs={{32,0},{64,32},{96,64},{128,96},{160,128},{192,160},{224,192},{256... | collective-permute-start | bytes 196616 | tf_op jit(solution)/shard_map/ppermute | solution.py:15
  32.7 14.4 %collective-permute-start.1 = (f32[2,4,1,2048]{3,2,1,0:T(1,128)}, f32[2,4,1,2048]{3,2,1,0:T(1,128)}, u32[]{:S(2)}, u32[]{:S(2)}) collective-permute-start(f32[2,4,1,2048]{3,2,1,0:T(1,128)} %slice.275), channel_id=1, source_target_pairs={{1,0},{2,1},{3,2},{4,3},{5,4},{6,5},{7,6},{8,7},{9,8},{10,9},{11,1... | collective-permute-start | bytes 196616 | tf_op jit(solution)/shard_map/ppermute | solution.py:15
  36.8 1.4 copy-start.1
  36.8 1.5 %copy-start.8 = (f32[4,3,4,4,2048]{4,3,2,1,0:T(4,128)S(1)}, f32[4,3,4,4,2048]{4,3,2,1,0:T(4,128)}, u32[]{:S(2)}) copy-start(f32[4,3,4,4,2048]{4,3,2,1,0:T(4,128)} %param.22) | copy-start | bytes 4718596
  38.3 1.9 %copy-start.39 = (f32[8]{0:T(128)S(1)}, f32[8]{0:T(128)}, u32[]{:S(2)}) copy-start(f32[8]{0:T(128)} %param.24) | copy-start | bytes 100
  40.8 8.3 %copy-start.4 = (f32[2,3,4,2048]{3,2,1,0:T(4,128)}, f32[2,3,4,2048]{3,2,1,0:T(4,128)S(1)}, u32[]{:S(2)}) copy-start(f32[2,3,4,2048]{3,2,1,0:T(4,128)S(1)} %slice.270) | copy-start | bytes 589828
  47.1 2.1 %copy-start.14 = (f32[3,4,4,2048]{3,2,1,0:T(4,128)S(1)}, f32[3,4,4,2048]{3,2,1,0:T(4,128)}, u32[]{:S(2)}) copy-start(f32[3,4,4,2048]{3,2,1,0:T(4,128)} %param.21) | copy-start | bytes 1179652
  47.1 1.9 %copy-start.15 = (f32[2,1,4,2048]{3,2,1,0:T(4,128)}, f32[2,1,4,2048]{3,2,1,0:T(4,128)S(1)}, u32[]{:S(2)}) copy-start(f32[2,1,4,2048]{3,2,1,0:T(4,128)S(1)} %collective-permute-done) | copy-start | bytes 196612
  48.9 5.6 %copy-start.7 = (f32[1,4,4,2048]{3,2,1,0:T(4,128)}, f32[1,4,4,2048]{3,2,1,0:T(4,128)S(1)}, u32[]{:S(2)}) copy-start(f32[1,4,4,2048]{3,2,1,0:T(4,128)S(1)} %get-tuple-element.73) | copy-start | bytes 393220
  51.0 9.9 %collective-permute-start.3 = (f32[2,1,4,2048]{3,2,1,0:T(4,128)}, f32[2,1,4,2048]{3,2,1,0:T(4,128)}, u32[]{:S(2)}, u32[]{:S(2)}) collective-permute-start(f32[2,1,4,2048]{3,2,1,0:T(4,128)} %pad_maximum_fusion.11), channel_id=1, source_target_pairs={{0,32},{32,64},{64,96},{96,128},{128,160},{160,192},{192,224},{224... | collective-permute-start | bytes 196616 | tf_op jit(solution)/shard_map/ppermute | solution.py:15
  53.0 0.8 copy-start.2
  56.1 6.8 %collective-permute-start.2 = (f32[2,4,1,2048]{3,2,1,0:T(1,128)}, f32[2,4,1,2048]{3,2,1,0:T(1,128)S(1)}, u32[]{:S(2)}, u32[]{:S(2)}) collective-permute-start(f32[2,4,1,2048]{3,2,1,0:T(1,128)} %slice.285), channel_id=1, source_target_pairs={{0,1},{1,2},{2,3},{3,4},{4,5},{5,6},{6,7},{7,8},{8,9},{9,10},{10,1... | collective-permute-start | bytes 196616 | tf_op jit(solution)/shard_map/ppermute | solution.py:15
  61.9 2.7 %copy-start.10 = (f32[3,4,4,2048]{3,2,1,0:T(4,128)S(1)}, f32[3,4,4,2048]{3,2,1,0:T(4,128)}, u32[]{:S(2)}) copy-start(f32[3,4,4,2048]{3,2,1,0:T(4,128)} %get-tuple-element.62) | copy-start | bytes 1179652
  61.9 2.7 %copy-start.12 = (f32[4,4,2048]{2,1,0:T(4,128)S(1)}, f32[4,4,2048]{2,1,0:T(4,128)}, u32[]{:S(2)}) copy-start(f32[4,4,2048]{2,1,0:T(4,128)} %bitcast_multiply_fusion) | copy-start | bytes 393220
  64.4 0.8 copy-start.17
  65.4 0.6 copy-start.18
  70.0 2.9 %copy-start.24 = (s32[1024]{0:T(1024)S(1)}, s32[1024]{0:T(1024)}, u32[]{:S(2)}) copy-start(s32[1024]{0:T(1024)} %get-tuple-element.78) | copy-start | bytes 12292
  70.0 4.3 %copy-start.32 = (f32[1024]{0:T(1024)S(1)}, f32[1024]{0:T(1024)}, u32[]{:S(2)}) copy-start(f32[1024]{0:T(1024)} %reshape_squeeze.19) | copy-start | bytes 12292
  70.0 4.3 %copy-start.33 = (f32[1024]{0:T(1024)S(1)}, f32[1024]{0:T(1024)}, u32[]{:S(2)}) copy-start(f32[1024]{0:T(1024)} %reshape_squeeze.18) | copy-start | bytes 12292
  70.0 4.3 %copy-start.34 = (f32[1024]{0:T(1024)S(1)}, f32[1024]{0:T(1024)}, u32[]{:S(2)}) copy-start(f32[1024]{0:T(1024)} %reshape_squeeze.17) | copy-start | bytes 12292
  70.0 4.3 %copy-start.26 = (s32[1024]{0:T(1024)S(1)}, s32[1024]{0:T(1024)}, u32[]{:S(2)}) copy-start(s32[1024]{0:T(1024)} %get-tuple-element.79) | copy-start | bytes 12292
  70.1 4.3 %copy-start.28 = (f32[1024]{0:T(1024)S(1)}, f32[1024]{0:T(1024)}, u32[]{:S(2)}) copy-start(f32[1024]{0:T(1024)} %compare_convert_fusion) | copy-start | bytes 12292
  74.3 5.0 %copy-start.30 = (f32[1024]{0:T(1024)S(1)}, f32[1024]{0:T(1024)}, u32[]{:S(2)}) copy-start(f32[1024]{0:T(1024)} %get-tuple-element.47) | copy-start | bytes 12292
  74.3 5.0 %copy-start.31 = (f32[1024]{0:T(1024)S(1)}, f32[1024]{0:T(1024)}, u32[]{:S(2)}) copy-start(f32[1024]{0:T(1024)} %get-tuple-element.48) | copy-start | bytes 12292
  76.5 0.7 copy-start.19
  77.2 27.5 %copy-start.6 = (f32[1,4,4,2048]{3,2,1,0:T(4,128)S(1)}, f32[1,4,4,2048]{3,2,1,0:T(4,128)}, u32[]{:S(2)}) copy-start(f32[1,4,4,2048]{3,2,1,0:T(4,128)} %copy.56) | copy-start | bytes 393220
  83.4 32.4 %all-to-all-start.1 = ((f32[32,2,32]{2,1,0:T(2,128)}), f32[32,2,32]{2,1,0:T(2,128)}, u32[]{:S(2)}, u32[]{:S(2)}) async-start(f32[32,2,32]{2,1,0:T(2,128)} %copy.43), calls=%async_computation.1 | async-start | bytes 65536 | tf_op jit(solution)/shard_map/all_to_all | solution.py:112
  103.9 0.7 copy-start.5
  105.8 10.9 %copy-start.36 = (s32[512]{0:T(512)S(1)}, s32[512]{0:T(512)}, u32[]{:S(2)}) copy-start(s32[512]{0:T(512)} %copy-done.35) | copy-start | bytes 6148
  108.5 8.9 %copy-start.20 = (f32[1,512]{1,0:T(1,128)S(1)}, f32[1,512]{1,0:T(1,128)}, u32[]{:S(2)}) copy-start(f32[1,512]{1,0:T(1,128)} %param.31) | copy-start | bytes 6148
  108.5 8.9 %copy-start.21 = (f32[1,512]{1,0:T(1,128)S(1)}, f32[1,512]{1,0:T(1,128)}, u32[]{:S(2)}) copy-start(f32[1,512]{1,0:T(1,128)} %param.32) | copy-start | bytes 6148
  108.5 8.9 %copy-start.22 = (f32[1,512]{1,0:T(1,128)S(1)}, f32[1,512]{1,0:T(1,128)}, u32[]{:S(2)}) copy-start(f32[1,512]{1,0:T(1,128)} %param.30) | copy-start | bytes 6148
  108.5 9.0 %copy-start.23 = (f32[1,512]{1,0:T(1,128)S(1)}, f32[1,512]{1,0:T(1,128)}, u32[]{:S(2)}) copy-start(f32[1,512]{1,0:T(1,128)} %param.33) | copy-start | bytes 6148
  108.5 26.4 %copy-start.3 = (f32[3,4,4,2048]{3,2,1,0:T(4,128)S(1)}, f32[3,4,4,2048]{3,2,1,0:T(4,128)}, u32[]{:S(2)}) copy-start(f32[3,4,4,2048]{3,2,1,0:T(4,128)} %copy-done.2) | copy-start | bytes 1179652
  108.7 26.2 %collective-permute-start.4 = (f32[2,1,4,2048]{3,2,1,0:T(4,128)S(1)}, f32[2,1,4,2048]{3,2,1,0:T(4,128)S(1)}, u32[]{:S(2)}, u32[]{:S(2)}) collective-permute-start(f32[2,1,4,2048]{3,2,1,0:T(4,128)S(1)} %slice.357), channel_id=1, source_target_pairs={{32,0},{64,32},{96,64},{128,96},{160,128},{192,160},{224,192},{256... | collective-permute-start | bytes 196616 | tf_op jit(solution)/shard_map/ppermute | solution.py:15
  114.5 20.4 %collective-permute-start.5 = (f32[2,4,1,2048]{3,2,1,0:T(1,128)S(1)}, f32[2,4,1,2048]{3,2,1,0:T(1,128)S(1)}, u32[]{:S(2)}, u32[]{:S(2)}) collective-permute-start(f32[2,4,1,2048]{3,2,1,0:T(1,128)S(1)} %slice.315), channel_id=1, source_target_pairs={{1,0},{2,1},{3,2},{4,3},{5,4},{6,5},{7,6},{8,7},{9,8},{10,9},{11,1... | collective-permute-start | bytes 196616 | tf_op jit(solution)/shard_map/ppermute | solution.py:15
  118.5 1.0 copy-start.38
  120.2 27.9 %all-to-all-start.2 = ((f32[32,1,32]{2,1,0:T(1,128)}), f32[32,1,32]{2,1,0:T(1,128)}, u32[]{:S(2)}, u32[]{:S(2)}) async-start(f32[32,1,32]{2,1,0:T(1,128)} %transpose_reshape.3), calls=%async_computation.2 | async-start | bytes 32768 | tf_op jit(solution)/shard_map/all_to_all | solution.py:112
  135.6 9.2 %collective-permute-start.7 = (f32[2,1,4,2048]{3,2,1,0:T(4,128)S(1)}, f32[2,1,4,2048]{3,2,1,0:T(4,128)S(1)}, u32[]{:S(2)}, u32[]{:S(2)}) collective-permute-start(f32[2,1,4,2048]{3,2,1,0:T(4,128)S(1)} %pad_maximum_fusion.10), channel_id=1, source_target_pairs={{0,32},{32,64},{64,96},{96,128},{128,160},{160,192},{192,224},{224... | collective-permute-start | bytes 196616 | tf_op jit(solution)/shard_map/ppermute | solution.py:15
  137.6 7.6 %copy-start.11 = (f32[3,4,4,2048]{3,2,1,0:T(4,128)}, f32[3,4,4,2048]{3,2,1,0:T(4,128)S(1)}, u32[]{:S(2)}) copy-start(f32[3,4,4,2048]{3,2,1,0:T(4,128)S(1)} %pad_maximum_fusion.1) | copy-start | bytes 1179652
  137.7 7.1 %collective-permute-start.6 = (f32[2,4,1,2048]{3,2,1,0:T(1,128)S(1)}, f32[2,4,1,2048]{3,2,1,0:T(1,128)S(1)}, u32[]{:S(2)}, u32[]{:S(2)}) collective-permute-start(f32[2,4,1,2048]{3,2,1,0:T(1,128)S(1)} %slice.325), channel_id=1, source_target_pairs={{0,1},{1,2},{2,3},{3,4},{4,5},{5,6},{6,7},{7,8},{8,9},{9,10},{10,1... | collective-permute-start | bytes 196616 | tf_op jit(solution)/shard_map/ppermute | solution.py:15
  144.9 1.0 copy-start.9
  144.9 1.0 copy-start.13
  145.2 4.9 %copy-start.25 = (s32[1024]{0:T(1024)S(1)}, s32[1024]{0:T(1024)}, u32[]{:S(2)}) copy-start(s32[1024]{0:T(1024)} %get-tuple-element.78) | copy-start | bytes 12292
  145.2 4.9 %copy-start.27 = (s32[1024]{0:T(1024)S(1)}, s32[1024]{0:T(1024)}, u32[]{:S(2)}) copy-start(s32[1024]{0:T(1024)} %get-tuple-element.79) | copy-start | bytes 12292
  145.2 4.9 %copy-start.29 = (f32[1024]{0:T(1024)S(1)}, f32[1024]{0:T(1024)}, u32[]{:S(2)}) copy-start(f32[1024]{0:T(1024)} %compare_convert_fusion) | copy-start | bytes 12292

commit v6 on v4

--- a/solution.py
+++ b/solution.py
@@ -121,6 +121,8 @@
     curr_0 = current[0]
     drop_0 = jnp.concatenate([volt_0[1:], single_zero]) - volt_0
     outgoing = to_slots(jnp.stack([cell_ids.astype(jnp.float32), curr_0, gain_row, drop_0]), [-1.0, 0.0, 0.0, 0.0])
+    h_field = magnetic_update(e_field, h_field)
+    outgoing, h_field = lax.optimization_barrier((outgoing, h_field))
     incoming = exchange(outgoing)
 
     material_hot = (
@@ -132,7 +134,6 @@
     decay_cell = jnp.einsum("pm,mxyz->pxyz", pole_decay, material_hot, precision=highest)
     cells = (eps_cell, sigma_cell, strength_cell, decay_cell)
 
-    h_field = magnetic_update(e_field, h_field)
     drive, polar_next = electric_base(e_field, h_field, polarization, cells)
     incoming, drive = lax.optimization_barrier((incoming, drive))
 

time: 145 us -> 139 us (0.959)
  starting transfers between devices: 66.3 us -> 60.9 us
  waiting for transfers between devices: 9.26 us -> 13.5 us
  local copies, waits for them, and re-layouts: 21.9 us -> 18.9 us
  other arithmetic: 27.6 us -> 25.6 us
    all_to_all x3, waiting for transfers between devices: 6.04 us -> 10.4 us  [exchange(): return lax.all_to_all(blocks, 'gy', split_axis=0, concat_axis=0, tiled=True)]
    all_to_all x3, starting transfers between devices: 40.8 us -> 37.4 us  [exchange(): return lax.all_to_all(blocks, 'gy', split_axis=0, concat_axis=0, tiled=True)]
    ppermute x8, starting transfers between devices: 25.4 us -> 23.4 us  [passed_along(): lax.ppermute(value, axis, [(source, source + steps) for source in range(f...]
    another operation x2, local copies, waits for them, and re-layouts: 1.69 us -> 3.25 us  [sample(): e_now[2].reshape(plane_rows, lanes)]
  transfers between devices with their start and end apart: 11 -> 11, of which waited for: 3 -> 4; matrix products, arithmetic and copies ran while one was open for 18% -> 21% of each run, Pallas kernels for 0% -> 0%
where the time goes in v6:
time: 139 us; the launch traced here: 138 us
  starting transfers between devices  60.9 us (44%)
  other arithmetic  25.6 us (18%)
  local copies, waits for them, and re-layouts  18.9 us (14%)
  matrix products  17.6 us (13%)
  waiting for transfers between devices  13.5 us (10%)
    all_to_all x3, starting transfers between devices, exchange(): return lax.all_to_all(blocks, 'gy', split_axis=0, concat_axis=0, tiled=True)  37.4 us
    ppermute x8, starting transfers between devices, passed_along(): lax.ppermute(value, axis, [(source, source + steps) for source in range(f...  23.4 us
    all_to_all x3, waiting for transfers between devices, exchange(): return lax.all_to_all(blocks, 'gy', split_axis=0, concat_axis=0, tiled=True)  10.4 us
    dot_general x2, matrix products, wire_of(): jnp.einsum('kr,kl->rl', row_hot, spread, precision=highest)  5.56 us
    dot_general x2, matrix products, sample(): jnp.dot(row_hot, e_now[2].reshape(plane_rows, lanes), precision=highest)  5.37 us
    another operation x2, local copies, waits for them, and re-layouts, sample(): e_now[2].reshape(plane_rows, lanes)  3.25 us
    ppermute x8, waiting for transfers between devices, passed_along(): lax.ppermute(value, axis, [(source, source + steps) for source in range(f...  3.14 us
  transfers between devices with their start and end apart: 11, of which 4 were waited for; matrix products, arithmetic and copies ran while one was open for 21% of the time, Pallas kernels for 0%

profile of v6, /device:TPU:16, one launch (start us, length us, event | category | flops | bytes accessed | tf_op | source)
XLA Modules:
  0.0 137.8 jit_solution(13097937457203853372)
XLA Ops:
  0.7 1.0 slice.269
  1.7 1.3 collective-permute-start
  3.0 0.8 slice.278
  3.9 3.9 %collective-permute-start.1 = (f32[2,1,4,2048]{3,2,1,0:T(4,128)S(1)}, f32[2,1,4,2048]{3,2,1,0:T(4,128)S(1)}, u32[]{:S(2)}, u32[]{:S(2)}) collective-permute-start(f32[2,1,4,2048]{3,2,1,0:T(4,128)S(1)} %slice.278), channel_id=1, source_target_pairs={{32,0},{64,32},{96,64},{128,96},{160,128},{192,160},{224,192},{256... | collective-permute-start | bytes 196616 | tf_op jit(solution)/shard_map/ppermute | solution.py:15
  7.7 0.7 fusion.127
  8.4 1.2 reduce-window.6
  9.8 0.8 fusion.126
  10.6 0.7 multiply_add_fusion.6
  11.3 0.8 slice.264
  12.1 0.7 convert_element_type.39
  13.1 1.5 %convolution_bitcast_fusion.1 = f32[4,4,4,2048]{3,0,2,1:T(4,128)S(1)} fusion(s32[4,4,2048]{2,1,0:T(4,128)} %param.23, f32[4,8]{1,0:T(4,128)S(1)} %copy-done), kind=kOutput, calls=%fused_computation.2 | convolution fusion | flops 12845056 | bytes 655488 | tf_op jit(solution)/shard_map/pm,mxyz->pxyz/dot_general | solution.py:134
  15.0 0.6 fusion
  16.0 0.6 fusion.32
  16.6 0.7 bitcast_multiply_fusion
  17.4 1.9 %multiply_add_fusion.1 = (f32[4,3,4,4,2048]{4,3,2,1,0:T(4,128)S(1)}, f32[3,4,4,2048]{3,2,1,0:T(4,128)}) fusion(f32[4,3,4,4,2048]{4,3,2,1,0:T(4,128)S(1)} %copy-done.5, f32[3,4,4,2048]{3,2,1,0:T(4,128)S(1)} %copy-done.1, f32[4,4,4,2048]{3,2,1,0:T(4,128)S(1)} %copy.38, f32[4,4,4,2048]{3,2,1,0:T(4,128)S(1)} %copy.37), kind=kLoop, calls=%fused_computation.19 | loop fusion | flops 1867776 | bytes 4980736 | tf_op jit(solution)/shard_map/add | solution.py:60
  19.3 1.0 fusion.30
  20.6 1.7 %fusion.167 = (f32[1,4,4,2048]{3,2,1,0:T(4,128)}, f32[1,4,4,2048]{3,2,1,0:T(4,128)S(1)}, f32[4,4,2048]{2,1,0:T(4,128)S(1)}, f32[4,4,2048]{2,1,0:T(4,128)S(1)}) fusion(f32[3,4,4,2048]{3,2,1,0:T(4,128)S(1)} %copy-done.1, f32[2,4,1,2048]{3,2,1,0:T(1,128)S(1)} %collective-permute-done, f32[2,4,3,2048]{3,2,1,0:T(4,128)S(1)} %slice.268, ...), kind=kLoop, calls=%fused_computation.242 | loop fusion | flops 229376 | bytes 1572864 | tf_op jit(solution)/shard_map/slice | solution.py:44
  22.6 1.2 fusion.95
  23.9 0.7 slice.284
  24.6 0.7 reshape.292
  25.3 18.0 %all-to-all-start = ((f32[32,1,128]{2,1,0:T(1,128)}), f32[32,1,128]{2,1,0:T(1,128)}, u32[]{:S(2)}, u32[]{:S(2)}) async-start(f32[32,1,128]{2,1,0:T(1,128)} %reshape.292), calls=%async_computation | async-start | bytes 32768 | tf_op jit(solution)/shard_map/all_to_all | solution.py:112
  43.4 3.6 %collective-permute-start.2 = (f32[2,4,1,2048]{3,2,1,0:T(1,128)}, f32[2,4,1,2048]{3,2,1,0:T(1,128)S(1)}, u32[]{:S(2)}, u32[]{:S(2)}) collective-permute-start(f32[2,4,1,2048]{3,2,1,0:T(1,128)} %slice.284), channel_id=1, source_target_pairs={{0,1},{1,2},{2,3},{3,4},{4,5},{5,6},{6,7},{7,8},{8,9},{9,10},{10,1... | collective-permute-start | bytes 196616 | tf_op jit(solution)/shard_map/ppermute | solution.py:15
  47.0 2.1 %collective-permute-start.3 = (f32[2,1,4,2048]{3,2,1,0:T(4,128)S(1)}, f32[2,1,4,2048]{3,2,1,0:T(4,128)}, u32[]{:S(2)}, u32[]{:S(2)}) collective-permute-start(f32[2,1,4,2048]{3,2,1,0:T(4,128)S(1)} %slice.291), channel_id=1, source_target_pairs={{0,32},{32,64},{64,96},{96,128},{128,160},{160,192},{192,224},{224... | collective-permute-start | bytes 196616 | tf_op jit(solution)/shard_map/ppermute | solution.py:15
  49.1 0.6 fusion.31
  49.7 0.7 copy.51
  50.4 1.6 %reshape_squeeze.15 = f32[256,128]{1,0:T(8,128)} reshape(f32[1,4,4,2048]{3,2,1,0:T(4,128)} %get-tuple-element.68) | data formatting | bytes 262144 | tf_op jit(solution)/shard_map/reshape;squeeze | solution.py:154
  52.1 4.6 %all-to-all-done = f32[32,1,128]{2,1,0:T(1,128)} async-done(((f32[32,1,128]{2,1,0:T(1,128)}), f32[32,1,128]{2,1,0:T(1,128)}, u32[]{:S(2)}, u32[]{:S(2)}) %all-to-all-start) | async-done | bytes 16416 | tf_op jit(solution)/shard_map/all_to_all | solution.py:112
  57.2 1.4 %reduce.26 = f32[32,128]{1,0:T(8,128)S(1)} reduce(f32[32,1,128]{2,1,0:T(1,128)} %all-to-all-done, f32[]{:T(128)} %broadcast.264), dimensions={1}, to_apply=%all_to_all.9.reduce_sub_computation | reduce | bytes 32772 | tf_op jit(solution)/shard_map/all_to_all | solution.py:112
  58.6 0.7 reshape.293
  59.3 0.9 slice_bitcast_fusion.5
  60.3 1.0 fusion.81
  61.3 1.2 fusion.55
  62.5 0.9 convert_reduce_fusion.1
  63.4 0.6 compare_convert_fusion
  64.0 0.6 add_select_fusion.1
  65.0 2.4 %fusion.21 = f32[1024]{0:T(1024)S(1)} fusion(f32[256,128]{1,0:T(8,128)} %reshape_squeeze.15, f32[1024]{0:T(1024)} %compare_convert_fusion, s32[1024]{0:T(1024)} %get-tuple-element.80, s32[1024]{0:T(1024)} %get-tuple-element.79), kind=kOutput, calls=%fused_computation.23 | convolution fusion | flops 403569664 | bytes 147456 | tf_op jit(solution)/shard_map/dot_general | solution.py:154
  67.4 0.7 stack.65
  68.1 3.5 %fusion.24 = f32[256,128]{1,0:T(8,128)} fusion(f32[1024]{0:T(1024)} %compare_convert_fusion, s32[1024]{0:T(1024)} %get-tuple-element.80, f32[1024]{0:T(1024)S(1)} %multiply_add_fusion.3, s32[1024]{0:T(1024)} %get-tuple-element.79), kind=kOutput, calls=%fused_computation.24 | convolution fusion | flops 403472384 | bytes 147456 | tf_op jit(solution)/shard_map/kr,kl->rl/dot_general | solution.py:159
  71.6 0.9 mul.212
  72.6 0.7 copy-done.4
  73.3 1.1 divide_add_fusion.1
  74.4 0.7 slice.348
  75.1 1.6 %reshape_squeeze.19 = f32[256,128]{1,0:T(8,128)} reshape(f32[1,4,4,2048]{3,2,1,0:T(4,128)} %slice.348) | data formatting | bytes 262144 | tf_op jit(solution)/shard_map/reshape;squeeze | solution.py:154
  76.7 3.0 %fusion.18 = f32[1024]{0:T(1024)} fusion(f32[256,128]{1,0:T(8,128)} %reshape_squeeze.19, f32[1024]{0:T(1024)} %compare_convert_fusion, s32[1024]{0:T(1024)} %get-tuple-element.80, s32[1024]{0:T(1024)} %get-tuple-element.79), kind=kOutput, calls=%fused_computation.22 | convolution fusion | flops 403569664 | bytes 147456 | tf_op jit(solution)/shard_map/dot_general | solution.py:154
  79.7 1.4 stack.66
  81.0 1.4 %maximum_bitcast_fusion = f32[32,2,32]{2,1,0:T(2,128)} fusion(f32[1,32,32]{2,0,1:T(1,128)} %stack.66, f32[1,32,32]{2,0,1:T(1,128)} %stack.65), kind=kLoop, calls=%fused_computation.177 | loop fusion | flops 2048 | bytes 16384 | tf_op jit(solution)/shard_map/transpose | solution.py:167
  82.4 8.9 %all-to-all-start.1 = ((f32[32,2,32]{2,1,0:T(2,128)}), f32[32,2,32]{2,1,0:T(2,128)}, u32[]{:S(2)}, u32[]{:S(2)}) async-start(f32[32,2,32]{2,1,0:T(2,128)} %maximum_bitcast_fusion), calls=%async_computation.1 | async-start | bytes 65536 | tf_op jit(solution)/shard_map/all_to_all | solution.py:112
  91.3 2.7 %subtract_reduce_fusion = (f32[3,4,4,2048]{3,2,1,0:T(4,128)}, f32[4,3,4,4,2048]{4,3,2,1,0:T(4,128)}) fusion(f32[4,3,4,4,2048]{4,3,2,1,0:T(4,128)S(1)} %get-tuple-element.46, f32[3,4,4,2048]{3,2,1,0:T(4,128)S(1)} %bitcast.236, f32[4,4,4,2048]{3,2,1,0:T(4,128)S(1)} %copy-done.3, f32[4,4,4,2048]{3,2,1,0:T(4,128)S(1)} %copy.37), kind=kLoop, calls=%fused_computation.16 | loop fusion | flops 1867776 | bytes 4980736 | tf_op jit(solution)/shard_map/reduce_sum | solution.py:63
  94.3 1.3 collective-permute-start.5
  95.6 5.4 %collective-permute-start.4 = (f32[2,1,4,2048]{3,2,1,0:T(4,128)S(1)}, f32[2,1,4,2048]{3,2,1,0:T(4,128)S(1)}, u32[]{:S(2)}, u32[]{:S(2)}) collective-permute-start(f32[2,1,4,2048]{3,2,1,0:T(4,128)S(1)} %slice.309), channel_id=1, source_target_pairs={{32,0},{64,32},{96,64},{128,96},{160,128},{192,160},{224,192},{256... | collective-permute-start | bytes 196616 | tf_op jit(solution)/shard_map/ppermute | solution.py:15
  101.0 3.7 %all-to-all-done.1 = f32[32,2,32]{2,1,0:T(2,128)} async-done(((f32[32,2,32]{2,1,0:T(2,128)}), f32[32,2,32]{2,1,0:T(2,128)}, u32[]{:S(2)}, u32[]{:S(2)}) %all-to-all-start.1) | async-done | bytes 8224 | tf_op jit(solution)/shard_map/all_to_all | solution.py:112
  104.7 0.8 copy.39
  105.5 1.4 %fusion.2 = f32[2,512]{1,0:T(2,128)S(1)} fusion(f32[2,1024]{1,0:T(2,128)S(1)} %reshape.250, s32[512]{0:T(512)} %copy-done.22), kind=kOutput, calls=%fused_computation.6 | convolution fusion | flops 13107200 | bytes 14336 | tf_op jit(solution)/shard_map/ft,ts->fs/dot_general | solution.py:116
  107.4 0.7 fusion.157
  108.0 1.0 fusion.1
  109.1 0.7 transpose_reshape.3
  109.8 10.5 %all-to-all-start.2 = ((f32[32,1,32]{2,1,0:T(1,128)}), f32[32,1,32]{2,1,0:T(1,128)S(1)}, u32[]{:S(2)}, u32[]{:S(2)}) async-start(f32[32,1,32]{2,1,0:T(1,128)} %transpose_reshape.3), calls=%async_computation.2 | async-start | bytes 32768 | tf_op jit(solution)/shard_map/all_to_all | solution.py:112
  121.0 1.9 %collective-permute-start.7 = (f32[2,1,4,2048]{3,2,1,0:T(4,128)S(1)}, f32[2,1,4,2048]{3,2,1,0:T(4,128)S(1)}, u32[]{:S(2)}, u32[]{:S(2)}) collective-permute-start(f32[2,1,4,2048]{3,2,1,0:T(4,128)S(1)} %pad_maximum_fusion.10), channel_id=1, source_target_pairs={{0,32},{32,64},{64,96},{96,128},{128,160},{160,192},{192,224},{224... | collective-permute-start | bytes 196616 | tf_op jit(solution)/shard_map/ppermute | solution.py:15
  123.1 3.9 %collective-permute-start.6 = (f32[2,4,1,2048]{3,2,1,0:T(1,128)S(1)}, f32[2,4,1,2048]{3,2,1,0:T(1,128)S(1)}, u32[]{:S(2)}, u32[]{:S(2)}) collective-permute-start(f32[2,4,1,2048]{3,2,1,0:T(1,128)S(1)} %slice.323), channel_id=1, source_target_pairs={{0,1},{1,2},{2,3},{3,4},{4,5},{5,6},{6,7},{7,8},{8,9},{9,10},{10,1... | collective-permute-start | bytes 196616 | tf_op jit(solution)/shard_map/ppermute | solution.py:15
  127.1 3.1 %collective-permute-done.7 = f32[2,1,4,2048]{3,2,1,0:T(4,128)S(1)} collective-permute-done((f32[2,1,4,2048]{3,2,1,0:T(4,128)S(1)}, f32[2,1,4,2048]{3,2,1,0:T(4,128)S(1)}, u32[]{:S(2)}, u32[]{:S(2)}) %collective-permute-start.7) | collective-permute-done | bytes 65568 | tf_op jit(solution)/shard_map/ppermute | solution.py:15
  131.5 2.0 %all-to-all-done.2 = f32[32,1,32]{2,1,0:T(1,128)S(1)} async-done(((f32[32,1,32]{2,1,0:T(1,128)}), f32[32,1,32]{2,1,0:T(1,128)S(1)}, u32[]{:S(2)}, u32[]{:S(2)}) %all-to-all-start.2) | async-done | bytes 4128 | tf_op jit(solution)/shard_map/all_to_all | solution.py:112
  134.0 0.7 reduce.25
  134.8 2.1 %fusion.27 = f32[256,128]{1,0:T(8,128)S(1)} fusion(f32[1024]{0:T(1024)S(1)} %copy-done.26, s32[1024]{0:T(1024)S(1)} %copy-done.25, f32[1024]{0:T(1024)S(1)} %broadcast_in_dim.23, s32[1024]{0:T(1024)S(1)} %copy-done.24), kind=kOutput, calls=%fused_computation.25 | convolution fusion | flops 403472384 | bytes 147456 | tf_op jit(solution)/shard_map/kr,kl->rl/dot_general | solution.py:159
  137.1 0.8 divide_add_fusion
  (124 shorter events, 6.4 us)
Async XLA Ops:
  0.6 12.4 %copy-start = (f32[4,8]{1,0:T(4,128)S(1)}, f32[4,8]{1,0:T(4,128)}, u32[]{:S(2)}) copy-start(f32[4,8]{1,0:T(4,128)} %param.27) | copy-start | bytes 388
  0.6 14.3 %copy-start.11 = (s32[4,4,2048]{2,1,0:T(4,128)S(1)}, s32[4,4,2048]{2,1,0:T(4,128)}, u32[]{:S(2)}) copy-start(s32[4,4,2048]{2,1,0:T(4,128)} %param.23) | copy-start | bytes 393220
  0.7 14.3 %copy-start.27 = (f32[4,8]{1,0:T(4,128)S(1)}, f32[4,8]{1,0:T(4,128)}, u32[]{:S(2)}) copy-start(f32[4,8]{1,0:T(4,128)} %param.26) | copy-start | bytes 388
  1.7 18.9 %collective-permute-start = (f32[2,4,1,2048]{3,2,1,0:T(1,128)S(1)}, f32[2,4,1,2048]{3,2,1,0:T(1,128)S(1)}, u32[]{:S(2)}, u32[]{:S(2)}) collective-permute-start(f32[2,4,1,2048]{3,2,1,0:T(1,128)S(1)} %slice.269), channel_id=1, source_target_pairs={{1,0},{2,1},{3,2},{4,3},{5,4},{6,5},{7,6},{8,7},{9,8},{10,9},{11,1... | collective-permute-start | bytes 196616 | tf_op jit(solution)/shard_map/ppermute | solution.py:15
  3.9 16.7 %collective-permute-start.1 = (f32[2,1,4,2048]{3,2,1,0:T(4,128)S(1)}, f32[2,1,4,2048]{3,2,1,0:T(4,128)S(1)}, u32[]{:S(2)}, u32[]{:S(2)}) collective-permute-start(f32[2,1,4,2048]{3,2,1,0:T(4,128)S(1)} %slice.278), channel_id=1, source_target_pairs={{32,0},{64,32},{96,64},{128,96},{160,128},{192,160},{224,192},{256... | collective-permute-start | bytes 196616 | tf_op jit(solution)/shard_map/ppermute | solution.py:15
  11.3 8.0 %copy-start.22 = (s32[512]{0:T(512)}, s32[512]{0:T(512)S(1)}, u32[]{:S(2)}) copy-start(s32[512]{0:T(512)S(1)} %multiply_add_fusion.6) | copy-start | bytes 6148
  12.1 5.2 %copy-start.15 = (f32[1,511]{1,0:T(1,128)}, f32[1,511]{1,0:T(1,128)S(1)}, u32[]{:S(2)}) copy-start(f32[1,511]{1,0:T(1,128)S(1)} %slice.264) | copy-start | bytes 6136
  14.6 1.4 %copy-start.29 = (f32[8]{0:T(128)S(1)}, f32[8]{0:T(128)}, u32[]{:S(2)}) copy-start(f32[8]{0:T(128)} %param.25) | copy-start | bytes 100
  15.0 2.3 %copy-start.13 = (f32[1,512]{1,0:T(1,128)S(1)}, f32[1,512]{1,0:T(1,128)}, u32[]{:S(2)}) copy-start(f32[1,512]{1,0:T(1,128)} %param.31) | copy-start | bytes 6148
  15.0 2.4 %copy-start.1 = (f32[3,4,4,2048]{3,2,1,0:T(4,128)S(1)}, f32[3,4,4,2048]{3,2,1,0:T(4,128)}, u32[]{:S(2)}) copy-start(f32[3,4,4,2048]{3,2,1,0:T(4,128)} %param.20) | copy-start | bytes 1179652
  15.0 2.4 %copy-start.5 = (f32[4,3,4,4,2048]{4,3,2,1,0:T(4,128)S(1)}, f32[4,3,4,4,2048]{4,3,2,1,0:T(4,128)}, u32[]{:S(2)}) copy-start(f32[4,3,4,4,2048]{4,3,2,1,0:T(4,128)} %param.22) | copy-start | bytes 4718596
  16.0 3.3 %copy-start.2 = (f32[4,4,4,2048]{3,2,1,0:T(4,128)}, f32[4,4,4,2048]{3,2,1,0:T(4,128)S(1)}, u32[]{:S(2)}) copy-start(f32[4,4,4,2048]{3,2,1,0:T(4,128)S(1)} %copy.38) | copy-start | bytes 1572868
  17.4 1.9 %copy-start.19 = (f32[1,512]{1,0:T(1,128)}, f32[1,512]{1,0:T(1,128)S(1)}, u32[]{:S(2)}) copy-start(f32[1,512]{1,0:T(1,128)S(1)} %fusion.141) | copy-start | bytes 6148
  17.4 1.9 %copy-start.14 = (f32[1,512]{1,0:T(1,128)S(1)}, f32[1,512]{1,0:T(1,128)}, u32[]{:S(2)}) copy-start(f32[1,512]{1,0:T(1,128)} %param.32) | copy-start | bytes 6148
  17.4 1.9 %copy-start.17 = (f32[1,512]{1,0:T(1,128)S(1)}, f32[1,512]{1,0:T(1,128)}, u32[]{:S(2)}) copy-start(f32[1,512]{1,0:T(1,128)} %param.30) | copy-start | bytes 6148
  17.4 1.9 %copy-start.31 = (f32[4]{0:T(128)S(1)}, f32[4]{0:T(128)}, u32[]{:S(2)}) copy-start(f32[4]{0:T(128)} %constant.114.clone) | copy-start | bytes 52
  22.5 26.7 %copy-start.30 = (f32[8]{0:T(128)S(1)}, f32[8]{0:T(128)}, u32[]{:S(2)}) copy-start(f32[8]{0:T(128)} %param.24) | copy-start | bytes 100
  25.3 31.3 %all-to-all-start = ((f32[32,1,128]{2,1,0:T(1,128)}), f32[32,1,128]{2,1,0:T(1,128)}, u32[]{:S(2)}, u32[]{:S(2)}) async-start(f32[32,1,128]{2,1,0:T(1,128)} %reshape.292), calls=%async_computation | async-start | bytes 32768 | tf_op jit(solution)/shard_map/all_to_all | solution.py:112
  43.4 16.0 %collective-permute-start.2 = (f32[2,4,1,2048]{3,2,1,0:T(1,128)}, f32[2,4,1,2048]{3,2,1,0:T(1,128)S(1)}, u32[]{:S(2)}, u32[]{:S(2)}) collective-permute-start(f32[2,4,1,2048]{3,2,1,0:T(1,128)} %slice.284), channel_id=1, source_target_pairs={{0,1},{1,2},{2,3},{3,4},{4,5},{5,6},{6,7},{7,8},{8,9},{9,10},{10,1... | collective-permute-start | bytes 196616 | tf_op jit(solution)/shard_map/ppermute | solution.py:15
  47.0 12.3 %collective-permute-start.3 = (f32[2,1,4,2048]{3,2,1,0:T(4,128)S(1)}, f32[2,1,4,2048]{3,2,1,0:T(4,128)}, u32[]{:S(2)}, u32[]{:S(2)}) collective-permute-start(f32[2,1,4,2048]{3,2,1,0:T(4,128)S(1)} %slice.291), channel_id=1, source_target_pairs={{0,32},{32,64},{64,96},{96,128},{128,160},{160,192},{192,224},{224... | collective-permute-start | bytes 196616 | tf_op jit(solution)/shard_map/ppermute | solution.py:15
  59.3 1.9 %copy-start.7 = (f32[3,4,4,2048]{3,2,1,0:T(4,128)S(1)}, f32[3,4,4,2048]{3,2,1,0:T(4,128)}, u32[]{:S(2)}) copy-start(f32[3,4,4,2048]{3,2,1,0:T(4,128)} %get-tuple-element.59) | copy-start | bytes 1179652
  61.3 3.4 %copy-start.12 = (f32[32,4,32]{2,1,0:T(4,128)S(1)}, f32[32,4,32]{2,1,0:T(4,128)}, u32[]{:S(2)}) copy-start(f32[32,4,32]{2,1,0:T(4,128)} %reshape.293) | copy-start | bytes 49156
  65.0 8.3 %copy-start.9 = (f32[1,4,4,2048]{3,2,1,0:T(4,128)S(1)}, f32[1,4,4,2048]{3,2,1,0:T(4,128)}, u32[]{:S(2)}) copy-start(f32[1,4,4,2048]{3,2,1,0:T(4,128)} %copy.51) | copy-start | bytes 393220
  72.6 0.7 copy-start.4
  74.4 16.9 %copy-start.3 = (f32[4,4,4,2048]{3,2,1,0:T(4,128)S(1)}, f32[4,4,4,2048]{3,2,1,0:T(4,128)}, u32[]{:S(2)}) copy-start(f32[4,4,4,2048]{3,2,1,0:T(4,128)} %copy-done.2) | copy-start | bytes 1572868
  82.4 22.3 %all-to-all-start.1 = ((f32[32,2,32]{2,1,0:T(2,128)}), f32[32,2,32]{2,1,0:T(2,128)}, u32[]{:S(2)}, u32[]{:S(2)}) async-start(f32[32,2,32]{2,1,0:T(2,128)} %maximum_bitcast_fusion), calls=%async_computation.1 | async-start | bytes 65536 | tf_op jit(solution)/shard_map/all_to_all | solution.py:112
  94.1 12.9 %copy-start.16 = (f32[1,511]{1,0:T(1,128)S(1)}, f32[1,511]{1,0:T(1,128)}, u32[]{:S(2)}) copy-start(f32[1,511]{1,0:T(1,128)} %copy-done.15) | copy-start | bytes 6136
  94.1 12.9 %copy-start.18 = (f32[1,512]{1,0:T(1,128)S(1)}, f32[1,512]{1,0:T(1,128)}, u32[]{:S(2)}) copy-start(f32[1,512]{1,0:T(1,128)} %param.30) | copy-start | bytes 6148
  94.1 13.0 %copy-start.20 = (f32[1,512]{1,0:T(1,128)S(1)}, f32[1,512]{1,0:T(1,128)}, u32[]{:S(2)}) copy-start(f32[1,512]{1,0:T(1,128)} %copy-done.19) | copy-start | bytes 6148
  94.1 13.0 %copy-start.21 = (f32[1,512]{1,0:T(1,128)S(1)}, f32[1,512]{1,0:T(1,128)}, u32[]{:S(2)}) copy-start(f32[1,512]{1,0:T(1,128)} %param.33) | copy-start | bytes 6148
  94.1 13.9 %copy-start.23 = (s32[512]{0:T(512)S(1)}, s32[512]{0:T(512)}, u32[]{:S(2)}) copy-start(s32[512]{0:T(512)} %copy-done.22) | copy-start | bytes 6148
  94.3 26.0 %collective-permute-start.5 = (f32[2,4,1,2048]{3,2,1,0:T(1,128)S(1)}, f32[2,4,1,2048]{3,2,1,0:T(1,128)S(1)}, u32[]{:S(2)}, u32[]{:S(2)}) collective-permute-start(f32[2,4,1,2048]{3,2,1,0:T(1,128)S(1)} %slice.313), channel_id=1, source_target_pairs={{1,0},{2,1},{3,2},{4,3},{5,4},{6,5},{7,6},{8,7},{9,8},{10,9},{11,1... | collective-permute-start | bytes 196616 | tf_op jit(solution)/shard_map/ppermute | solution.py:15
  95.6 24.8 %collective-permute-start.4 = (f32[2,1,4,2048]{3,2,1,0:T(4,128)S(1)}, f32[2,1,4,2048]{3,2,1,0:T(4,128)S(1)}, u32[]{:S(2)}, u32[]{:S(2)}) collective-permute-start(f32[2,1,4,2048]{3,2,1,0:T(4,128)S(1)} %slice.309), channel_id=1, source_target_pairs={{32,0},{64,32},{96,64},{128,96},{160,128},{192,160},{224,192},{256... | collective-permute-start | bytes 196616 | tf_op jit(solution)/shard_map/ppermute | solution.py:15
  108.0 12.9 %copy-start.28 = (f32[1,512]{1,0:T(1,128)}, f32[1,512]{1,0:T(1,128)S(1)}, u32[]{:S(2)}) copy-start(f32[1,512]{1,0:T(1,128)S(1)} %get-tuple-element.53) | copy-start | bytes 6148
  109.8 23.8 %all-to-all-start.2 = ((f32[32,1,32]{2,1,0:T(1,128)}), f32[32,1,32]{2,1,0:T(1,128)S(1)}, u32[]{:S(2)}, u32[]{:S(2)}) async-start(f32[32,1,32]{2,1,0:T(1,128)} %transpose_reshape.3), calls=%async_computation.2 | async-start | bytes 32768 | tf_op jit(solution)/shard_map/all_to_all | solution.py:112
  121.0 9.2 %collective-permute-start.7 = (f32[2,1,4,2048]{3,2,1,0:T(4,128)S(1)}, f32[2,1,4,2048]{3,2,1,0:T(4,128)S(1)}, u32[]{:S(2)}, u32[]{:S(2)}) collective-permute-start(f32[2,1,4,2048]{3,2,1,0:T(4,128)S(1)} %pad_maximum_fusion.10), channel_id=1, source_target_pairs={{0,32},{32,64},{64,96},{96,128},{128,160},{160,192},{192,224},{224... | collective-permute-start | bytes 196616 | tf_op jit(solution)/shard_map/ppermute | solution.py:15
  123.0 7.6 %copy-start.8 = (f32[3,4,4,2048]{3,2,1,0:T(4,128)}, f32[3,4,4,2048]{3,2,1,0:T(4,128)S(1)}, u32[]{:S(2)}) copy-start(f32[3,4,4,2048]{3,2,1,0:T(4,128)S(1)} %pad_maximum_fusion.1) | copy-start | bytes 1179652
  123.1 7.1 %collective-permute-start.6 = (f32[2,4,1,2048]{3,2,1,0:T(1,128)S(1)}, f32[2,4,1,2048]{3,2,1,0:T(1,128)S(1)}, u32[]{:S(2)}, u32[]{:S(2)}) collective-permute-start(f32[2,4,1,2048]{3,2,1,0:T(1,128)S(1)} %slice.323), channel_id=1, source_target_pairs={{0,1},{1,2},{2,3},{3,4},{4,5},{5,6},{6,7},{7,8},{8,9},{9,10},{10,1... | collective-permute-start | bytes 196616 | tf_op jit(solution)/shard_map/ppermute | solution.py:15
  130.3 1.0 copy-start.6
  130.3 1.0 copy-start.10
  130.6 4.2 %copy-start.24 = (s32[1024]{0:T(1024)S(1)}, s32[1024]{0:T(1024)}, u32[]{:S(2)}) copy-start(s32[1024]{0:T(1024)} %get-tuple-element.79) | copy-start | bytes 12292
  130.7 4.2 %copy-start.25 = (s32[1024]{0:T(1024)S(1)}, s32[1024]{0:T(1024)}, u32[]{:S(2)}) copy-start(s32[1024]{0:T(1024)} %get-tuple-element.80) | copy-start | bytes 12292
  130.7 4.2 %copy-start.26 = (f32[1024]{0:T(1024)S(1)}, f32[1024]{0:T(1024)}, u32[]{:S(2)}) copy-start(f32[1024]{0:T(1024)} %compare_convert_fusion) | copy-start | bytes 12292

commit v7 on v6

--- a/solution.py
+++ b/solution.py
@@ -68,6 +68,19 @@
 def electric_finish(e_field, drive, wire_term, cells):
     drive = drive.at[2].add(-TIME_STEP * wire_term)
     return e_field + drive / cells[0][None]
+
+
+def split_parts(values):
+    high = lax.reduce_precision(values, exponent_bits=8, mantissa_bits=7)
+    rest = values - high
+    middle = lax.reduce_precision(rest, exponent_bits=8, mantissa_bits=7)
+    low = rest - middle
+    return [part.astype(jnp.bfloat16) for part in (high, middle, low)]
+
+
+def hot_dot(spec, hot, values):
+    parts = [jnp.einsum(spec, hot, part, preferred_element_type=jnp.float32) for part in split_parts(values)]
+    return (parts[0] + parts[1]) + parts[2]
 
 
 def on_device(
@@ -100,11 +113,12 @@
 
     slot_total = n_gy * capacity
     highest = lax.Precision.HIGHEST
-    slot_hot = (jnp.arange(slot_total, dtype=jnp.int32)[:, None] == slot_at[None, :]).astype(jnp.float32)
-    slot_used = jnp.sum(slot_hot, axis=1)
+    slot_match = jnp.arange(slot_total, dtype=jnp.int32)[:, None] == slot_at[None, :]
+    slot_hot = slot_match.astype(jnp.bfloat16)
+    slot_used = jnp.sum(slot_match.astype(jnp.float32), axis=1)
 
     def to_slots(rows, fill):
-        placed = jnp.einsum("fs,ts->ft", rows, slot_hot, precision=highest)
+        placed = hot_dot("ts,fs->ft", slot_hot, rows)
         buffer = placed + jnp.asarray(fill, jnp.float32)[:, None] * (1.0 - slot_used)[None, :]
         return buffer.reshape(rows.shape[0], n_gy, capacity).transpose(1, 0, 2)
 
@@ -113,7 +127,7 @@
 
     def from_slots(blocks):
         flat = blocks.transpose(1, 0, 2).reshape(blocks.shape[1], slot_total)
-        return jnp.einsum("ft,ts->fs", flat, slot_hot, precision=highest)
+        return hot_dot("ts,ft->fs", slot_hot, flat)
 
     gain_row = wire_gain[0]
     cap_row = wire_cap[0]
@@ -146,17 +160,17 @@
     valid_flat = is_valid.reshape(-1)
     lanes = 128
     plane_rows = cell_total // lanes
-    row_hot = ((safe_cells // lanes)[:, None] == jnp.arange(plane_rows, dtype=jnp.int32)[None, :]).astype(jnp.float32)
-    row_hot = row_hot * valid_flat.astype(jnp.float32)[:, None]
+    row_match = (safe_cells // lanes)[:, None] == jnp.arange(plane_rows, dtype=jnp.int32)[None, :]
+    row_hot = (row_match & valid_flat[:, None]).astype(jnp.bfloat16)
     lane_hot = (safe_cells % lanes)[:, None] == jnp.arange(lanes, dtype=jnp.int32)[None, :]
 
     def sample(e_now):
-        picked = jnp.dot(row_hot, e_now[2].reshape(plane_rows, lanes), precision=highest)
+        picked = hot_dot("kr,rl->kl", row_hot, e_now[2].reshape(plane_rows, lanes))
         return jnp.sum(jnp.where(lane_hot, picked, 0.0), axis=1)
 
     def wire_of(values):
         spread = jnp.where(lane_hot, values[:, None], 0.0)
-        return jnp.einsum("kr,kl->rl", row_hot, spread, precision=highest).reshape(grid_shape)
+        return hot_dot("kr,kl->rl", row_hot, spread).reshape(grid_shape)
 
     sample_0 = sample(e_field)
     curr_cell_1 = recv_curr + recv_gain * (sample_0 - recv_drop)

time: 139 us -> 146 us (1.050)
  matrix products: 17.6 us -> 24.6 us
    dot_general x7 -> x21, matrix products: 14.4 us -> 22.2 us  [hot_dot(): jnp.einsum(spec, hot, part, preferred_element_type=jnp.float32)]
where the time goes in v7:
time: 146 us; the launch traced here: 144 us
  starting transfers between devices  61.1 us (42%)
  other arithmetic  25.7 us (18%)
  matrix products  24.6 us (17%)
  local copies, waits for them, and re-layouts  17.9 us (12%)
  waiting for transfers between devices  13.3 us (9%)
  between operations  1.47 us (1%)
    all_to_all x3, starting transfers between devices, exchange(): return lax.all_to_all(blocks, 'gy', split_axis=0, concat_axis=0, tiled=True)  37.7 us
    ppermute x8, starting transfers between devices, passed_along(): lax.ppermute(value, axis, [(source, source + steps) for source in range(f...  23.4 us
    dot_general x21, matrix products, hot_dot(): jnp.einsum(spec, hot, part, preferred_element_type=jnp.float32)  22.2 us
    all_to_all x3, waiting for transfers between devices, exchange(): return lax.all_to_all(blocks, 'gy', split_axis=0, concat_axis=0, tiled=True)  10.2 us
    ppermute x8, waiting for transfers between devices, passed_along(): lax.ppermute(value, axis, [(source, source + steps) for source in range(f...  3.14 us
  transfers between devices with their start and end apart: 11, of which 4 were waited for; matrix products, arithmetic and copies ran while one was open for 21% of the time, Pallas kernels for 0%

profile of v7, /device:TPU:16, one launch (start us, length us, event | category | flops | bytes accessed | tf_op | source)
XLA Modules:
  0.0 144.1 jit_solution(15701435601081551742)
XLA Ops:
  0.7 1.0 slice.269
  1.7 1.3 collective-permute-start
  3.0 0.8 slice.278
  3.8 3.9 %collective-permute-start.1 = (f32[2,1,4,2048]{3,2,1,0:T(4,128)S(1)}, f32[2,1,4,2048]{3,2,1,0:T(4,128)S(1)}, u32[]{:S(2)}, u32[]{:S(2)}) collective-permute-start(f32[2,1,4,2048]{3,2,1,0:T(4,128)S(1)} %slice.278), channel_id=1, source_target_pairs={{32,0},{64,32},{96,64},{128,96},{160,128},{192,160},{224,192},{256... | collective-permute-start | bytes 196616 | tf_op jit(solution)/shard_map/ppermute | solution.py:15
  7.7 0.7 fusion.196
  8.4 1.2 reduce-window.6
  9.8 0.8 fusion.195
  10.6 0.7 multiply_add_fusion.6
  11.3 0.8 slice.264
  12.1 0.7 convert_element_type.101
  12.8 0.8 fusion.214
  13.5 1.2 fusion.7
  14.7 1.2 fusion.8
  18.8 0.7 bitcast_multiply_fusion
  19.5 1.9 %multiply_add_fusion.1 = (f32[4,3,4,4,2048]{4,3,2,1,0:T(4,128)S(1)}, f32[3,4,4,2048]{3,2,1,0:T(4,128)}) fusion(f32[4,3,4,4,2048]{4,3,2,1,0:T(4,128)S(1)} %copy-done.5, f32[3,4,4,2048]{3,2,1,0:T(4,128)S(1)} %copy-done.1, f32[4,4,4,2048]{3,2,1,0:T(4,128)S(1)} %copy.38, f32[4,4,4,2048]{3,2,1,0:T(4,128)S(1)} %copy.37), kind=kLoop, calls=%fused_computation.17 | loop fusion | flops 1867776 | bytes 4980736 | tf_op jit(solution)/shard_map/add | solution.py:60
  22.1 1.7 %fusion.240 = (f32[1,4,4,2048]{3,2,1,0:T(4,128)}, f32[1,4,4,2048]{3,2,1,0:T(4,128)S(1)}, f32[4,4,2048]{2,1,0:T(4,128)S(1)}, f32[4,4,2048]{2,1,0:T(4,128)S(1)}) fusion(f32[3,4,4,2048]{3,2,1,0:T(4,128)S(1)} %copy-done.1, f32[2,4,1,2048]{3,2,1,0:T(1,128)S(1)} %collective-permute-done, f32[2,4,3,2048]{3,2,1,0:T(4,128)S(1)} %slice.268, ...), kind=kLoop, calls=%fused_computation.325 | loop fusion | flops 229376 | bytes 1572864 | tf_op jit(solution)/shard_map/slice | solution.py:44
  24.1 1.2 fusion.162
  25.5 0.7 slice.284
  26.2 0.7 reshape.336
  26.9 18.0 %all-to-all-start = ((f32[32,1,128]{2,1,0:T(1,128)}), f32[32,1,128]{2,1,0:T(1,128)}, u32[]{:S(2)}, u32[]{:S(2)}) async-start(f32[32,1,128]{2,1,0:T(1,128)} %reshape.336), calls=%async_computation | async-start | bytes 32768 | tf_op jit(solution)/shard_map/all_to_all | solution.py:126
  44.9 3.6 %collective-permute-start.2 = (f32[2,4,1,2048]{3,2,1,0:T(1,128)}, f32[2,4,1,2048]{3,2,1,0:T(1,128)S(1)}, u32[]{:S(2)}, u32[]{:S(2)}) collective-permute-start(f32[2,4,1,2048]{3,2,1,0:T(1,128)} %slice.284), channel_id=1, source_target_pairs={{0,1},{1,2},{2,3},{3,4},{4,5},{5,6},{6,7},{7,8},{8,9},{9,10},{10,1... | collective-permute-start | bytes 196616 | tf_op jit(solution)/shard_map/ppermute | solution.py:15
  48.5 2.1 %collective-permute-start.3 = (f32[2,1,4,2048]{3,2,1,0:T(4,128)S(1)}, f32[2,1,4,2048]{3,2,1,0:T(4,128)}, u32[]{:S(2)}, u32[]{:S(2)}) collective-permute-start(f32[2,1,4,2048]{3,2,1,0:T(4,128)S(1)} %slice.291), channel_id=1, source_target_pairs={{0,32},{32,64},{64,96},{96,128},{128,160},{160,192},{192,224},{224... | collective-permute-start | bytes 196616 | tf_op jit(solution)/shard_map/ppermute | solution.py:15
  51.2 0.7 copy.51
  52.0 1.6 %reshape_squeeze.15 = f32[256,128]{1,0:T(8,128)} reshape(f32[1,4,4,2048]{3,2,1,0:T(4,128)} %get-tuple-element.68) | data formatting | bytes 262144 | tf_op jit(solution)/shard_map/reshape;squeeze | solution.py:168
  53.6 4.4 %all-to-all-done = f32[32,1,128]{2,1,0:T(1,128)} async-done(((f32[32,1,128]{2,1,0:T(1,128)}), f32[32,1,128]{2,1,0:T(1,128)}, u32[]{:S(2)}, u32[]{:S(2)}) %all-to-all-start) | async-done | bytes 16416 | tf_op jit(solution)/shard_map/all_to_all | solution.py:126
  58.5 1.4 reduce.26
  59.9 0.7 reshape.337
  60.7 0.9 slice_bitcast_fusion.5
  61.6 1.0 fusion.148
  62.6 1.2 fusion.106
  63.8 0.9 convert_reduce_fusion.1
  66.3 1.3 convolution_add_fusion.3
  67.7 1.6 %fusion.24 = f32[1024]{0:T(1024)S(1)} fusion(f32[1024,128]{0,1:T(8,128)} %convolution_add_fusion.3, s32[1024]{0:T(1024)S(1)} %get-tuple-element.80, pred[1024]{0:T(1024)(128)(4,1)} %copy-done.26, s32[1024]{0:T(1024)S(1)} %copy-done.32, f32[256,128]{1,0:T(8,128)S(1)} %copy-done.12), kind=kOutput, calls=%fused_computation.36 | convolution fusion | flops 68320256 | bytes 668672 | tf_op jit(solution)/shard_map/kr,rl->kl/dot_general | solution.py:82
  69.9 2.1 %fusion.18 = f32[256,128]{1,0:T(8,128)} fusion(s32[1024]{0:T(1024)S(1)} %get-tuple-element.80, pred[1024]{0:T(1024)(128)(4,1)} %copy-done.26, f32[1024]{0:T(1024)S(1)} %multiply_add_fusion.3, s32[1024]{0:T(1024)S(1)} %copy-done.32), kind=kOutput, calls=%fused_computation.30 | convolution fusion | flops 68812800 | bytes 144384 | tf_op jit(solution)/shard_map/kr,kl->rl/dot_general | solution.py:82
  72.0 1.3 fusion.20
  73.4 0.7 stack.65
  74.0 2.3 %fusion.32 = f32[256,128]{1,0:T(8,128)} fusion(f32[256,128]{1,0:T(8,128)} %fusion.18, f32[256,128]{1,0:T(8,128)} %fusion.20, s32[1024]{0:T(1024)S(1)} %get-tuple-element.80, pred[1024]{0:T(1024)(128)(4,1)S(1)} %copy-done.28, f32[1024]{0:T(1024)S(1)} %multiply_add_fusion.3, s32[1024]{0:T(1024)S(1)} %copy-done.34), kind=kOutput, calls=%fused_computation.40 | convolution fusion | flops 68517888 | bytes 406528 | tf_op jit(solution)/shard_map/kr,kl->rl/dot_general | solution.py:82
  76.3 0.9 mul.211
  77.4 0.7 copy-done.4
  78.1 1.1 divide_add_fusion.1
  79.2 0.7 reshape_squeeze.19
  79.9 1.5 %fusion.66 = f32[1024,128]{0,1:T(8,128)S(1)} fusion(s32[1024]{0:T(1024)S(1)} %get-tuple-element.80, pred[1024]{0:T(1024)(128)(4,1)} %copy-done.26, f32[256,128]{1,0:T(8,128)} %reshape_squeeze.19), kind=kOutput, calls=%fused_computation.63 | convolution fusion | flops 67698688 | bytes 660480 | tf_op jit(solution)/shard_map/kr,rl->kl/dot_general | solution.py:82
  81.5 1.5 %convolution_add_fusion.1 = f32[1024,128]{0,1:T(8,128)S(1)} fusion(f32[1024,128]{0,1:T(8,128)S(1)} %fusion.66, s32[1024]{0:T(1024)S(1)} %get-tuple-element.80, pred[1024]{0:T(1024)(128)(4,1)} %copy-done.26, f32[256,128]{1,0:T(8,128)} %reshape_squeeze.19), kind=kOutput, calls=%fused_computation.20 | convolution fusion | flops 67895296 | bytes 1184768 | tf_op jit(solution)/shard_map/kr,rl->kl/dot_general | solution.py:82
  82.9 1.8 %fusion.25 = f32[1024]{0:T(1024)} fusion(f32[1024,128]{0,1:T(8,128)S(1)} %convolution_add_fusion.1, s32[1024]{0:T(1024)S(1)} %get-tuple-element.80, pred[1024]{0:T(1024)(128)(4,1)} %copy-done.26, s32[1024]{0:T(1024)} %get-tuple-element.79, f32[256,128]{1,0:T(8,128)S(1)} %copy-done.13), kind=kOutput, calls=%fused_computation.37 | convolution fusion | flops 68320256 | bytes 668672 | tf_op jit(solution)/shard_map/kr,rl->kl/dot_general | solution.py:82
  84.8 1.4 stack.66
  86.2 1.4 maximum_bitcast_fusion
  87.5 9.1 %all-to-all-start.1 = ((f32[32,2,32]{2,1,0:T(2,128)}), f32[32,2,32]{2,1,0:T(2,128)}, u32[]{:S(2)}, u32[]{:S(2)}) async-start(f32[32,2,32]{2,1,0:T(2,128)} %maximum_bitcast_fusion), calls=%async_computation.1 | async-start | bytes 65536 | tf_op jit(solution)/shard_map/all_to_all | solution.py:126
  96.6 2.7 %subtract_reduce_fusion = (f32[3,4,4,2048]{3,2,1,0:T(4,128)}, f32[4,3,4,4,2048]{4,3,2,1,0:T(4,128)}) fusion(f32[4,3,4,4,2048]{4,3,2,1,0:T(4,128)S(1)} %get-tuple-element.46, f32[3,4,4,2048]{3,2,1,0:T(4,128)S(1)} %bitcast.240, f32[4,4,4,2048]{3,2,1,0:T(4,128)S(1)} %copy-done.3, f32[4,4,4,2048]{3,2,1,0:T(4,128)S(1)} %copy.37), kind=kLoop, calls=%fused_computation.14 | loop fusion | flops 1867776 | bytes 4980736 | tf_op jit(solution)/shard_map/reduce_sum | solution.py:63
  99.6 1.3 collective-permute-start.5
  100.9 5.4 %collective-permute-start.4 = (f32[2,1,4,2048]{3,2,1,0:T(4,128)S(1)}, f32[2,1,4,2048]{3,2,1,0:T(4,128)S(1)}, u32[]{:S(2)}, u32[]{:S(2)}) collective-permute-start(f32[2,1,4,2048]{3,2,1,0:T(4,128)S(1)} %slice.309), channel_id=1, source_target_pairs={{32,0},{64,32},{96,64},{128,96},{160,128},{192,160},{224,192},{256... | collective-permute-start | bytes 196616 | tf_op jit(solution)/shard_map/ppermute | solution.py:15
  106.3 3.7 %all-to-all-done.1 = f32[32,2,32]{2,1,0:T(2,128)} async-done(((f32[32,2,32]{2,1,0:T(2,128)}), f32[32,2,32]{2,1,0:T(2,128)}, u32[]{:S(2)}, u32[]{:S(2)}) %all-to-all-start.1) | async-done | bytes 8224 | tf_op jit(solution)/shard_map/all_to_all | solution.py:126
  110.0 0.8 copy.39
  110.9 1.1 fusion.4
  115.3 0.7 transpose_reshape.3
  116.0 10.6 %all-to-all-start.2 = ((f32[32,1,32]{2,1,0:T(1,128)}), f32[32,1,32]{2,1,0:T(1,128)S(1)}, u32[]{:S(2)}, u32[]{:S(2)}) async-start(f32[32,1,32]{2,1,0:T(1,128)} %transpose_reshape.3), calls=%async_computation.2 | async-start | bytes 32768 | tf_op jit(solution)/shard_map/all_to_all | solution.py:126
  127.3 1.9 %collective-permute-start.7 = (f32[2,1,4,2048]{3,2,1,0:T(4,128)S(1)}, f32[2,1,4,2048]{3,2,1,0:T(4,128)S(1)}, u32[]{:S(2)}, u32[]{:S(2)}) collective-permute-start(f32[2,1,4,2048]{3,2,1,0:T(4,128)S(1)} %pad_maximum_fusion.10), channel_id=1, source_target_pairs={{0,32},{32,64},{64,96},{96,128},{128,160},{160,192},{192,224},{224... | collective-permute-start | bytes 196616 | tf_op jit(solution)/shard_map/ppermute | solution.py:15
  129.4 3.9 %collective-permute-start.6 = (f32[2,4,1,2048]{3,2,1,0:T(1,128)S(1)}, f32[2,4,1,2048]{3,2,1,0:T(1,128)S(1)}, u32[]{:S(2)}, u32[]{:S(2)}) collective-permute-start(f32[2,4,1,2048]{3,2,1,0:T(1,128)S(1)} %slice.323), channel_id=1, source_target_pairs={{0,1},{1,2},{2,3},{3,4},{4,5},{5,6},{6,7},{7,8},{8,9},{9,10},{10,1... | collective-permute-start | bytes 196616 | tf_op jit(solution)/shard_map/ppermute | solution.py:15
  133.4 3.1 %collective-permute-done.7 = f32[2,1,4,2048]{3,2,1,0:T(4,128)S(1)} collective-permute-done((f32[2,1,4,2048]{3,2,1,0:T(4,128)S(1)}, f32[2,1,4,2048]{3,2,1,0:T(4,128)S(1)}, u32[]{:S(2)}, u32[]{:S(2)}) %collective-permute-start.7) | collective-permute-done | bytes 65568 | tf_op jit(solution)/shard_map/ppermute | solution.py:15
  137.8 2.0 %all-to-all-done.2 = f32[32,1,32]{2,1,0:T(1,128)S(1)} async-done(((f32[32,1,32]{2,1,0:T(1,128)}), f32[32,1,32]{2,1,0:T(1,128)S(1)}, u32[]{:S(2)}, u32[]{:S(2)}) %all-to-all-start.2) | async-done | bytes 4128 | tf_op jit(solution)/shard_map/all_to_all | solution.py:126
  140.3 0.7 reduce.25
  141.1 0.7 fusion.12
  141.8 0.7 fusion.14
  142.5 0.7 fusion.41
  143.3 0.8 divide_add_fusion
  (156 shorter events, 13.8 us)
Async XLA Ops:
  0.6 15.5 %copy-start = (f32[4,8]{1,0:T(4,128)S(1)}, f32[4,8]{1,0:T(4,128)}, u32[]{:S(2)}) copy-start(f32[4,8]{1,0:T(4,128)} %param.27) | copy-start | bytes 388
  0.6 15.5 %copy-start.11 = (s32[4,4,2048]{2,1,0:T(4,128)S(1)}, s32[4,4,2048]{2,1,0:T(4,128)}, u32[]{:S(2)}) copy-start(s32[4,4,2048]{2,1,0:T(4,128)} %param.23) | copy-start | bytes 393220
  1.7 20.4 %collective-permute-start = (f32[2,4,1,2048]{3,2,1,0:T(1,128)S(1)}, f32[2,4,1,2048]{3,2,1,0:T(1,128)S(1)}, u32[]{:S(2)}, u32[]{:S(2)}) collective-permute-start(f32[2,4,1,2048]{3,2,1,0:T(1,128)S(1)} %slice.269), channel_id=1, source_target_pairs={{1,0},{2,1},{3,2},{4,3},{5,4},{6,5},{7,6},{8,7},{9,8},{10,9},{11,1... | collective-permute-start | bytes 196616 | tf_op jit(solution)/shard_map/ppermute | solution.py:15
  3.8 18.3 %collective-permute-start.1 = (f32[2,1,4,2048]{3,2,1,0:T(4,128)S(1)}, f32[2,1,4,2048]{3,2,1,0:T(4,128)S(1)}, u32[]{:S(2)}, u32[]{:S(2)}) collective-permute-start(f32[2,1,4,2048]{3,2,1,0:T(4,128)S(1)} %slice.278), channel_id=1, source_target_pairs={{32,0},{64,32},{96,64},{128,96},{160,128},{192,160},{224,192},{256... | collective-permute-start | bytes 196616 | tf_op jit(solution)/shard_map/ppermute | solution.py:15
  8.4 8.7 %copy-start.36 = (f32[4,8]{1,0:T(4,128)S(1)}, f32[4,8]{1,0:T(4,128)}, u32[]{:S(2)}) copy-start(f32[4,8]{1,0:T(4,128)} %param.26) | copy-start | bytes 388
  11.3 10.1 %copy-start.30 = (s32[512]{0:T(512)}, s32[512]{0:T(512)S(1)}, u32[]{:S(2)}) copy-start(s32[512]{0:T(512)S(1)} %multiply_add_fusion.6) | copy-start | bytes 6148
  12.1 5.7 %copy-start.17 = (f32[1,511]{1,0:T(1,128)}, f32[1,511]{1,0:T(1,128)S(1)}, u32[]{:S(2)}) copy-start(f32[1,511]{1,0:T(1,128)S(1)} %slice.264) | copy-start | bytes 6136
  13.5 7.8 %copy-start.21 = (f32[1,512]{1,0:T(1,128)}, f32[1,512]{1,0:T(1,128)S(1)}, u32[]{:S(2)}) copy-start(f32[1,512]{1,0:T(1,128)S(1)} %fusion.214) | copy-start | bytes 6148
  16.8 1.4 copy-start.38
  17.1 2.3 %copy-start.1 = (f32[3,4,4,2048]{3,2,1,0:T(4,128)S(1)}, f32[3,4,4,2048]{3,2,1,0:T(4,128)}, u32[]{:S(2)}) copy-start(f32[3,4,4,2048]{3,2,1,0:T(4,128)} %param.20) | copy-start | bytes 1179652
  17.2 2.3 %copy-start.5 = (f32[4,3,4,4,2048]{4,3,2,1,0:T(4,128)S(1)}, f32[4,3,4,4,2048]{4,3,2,1,0:T(4,128)}, u32[]{:S(2)}) copy-start(f32[4,3,4,4,2048]{4,3,2,1,0:T(4,128)} %param.22) | copy-start | bytes 4718596
  18.2 3.2 %copy-start.2 = (f32[4,4,4,2048]{3,2,1,0:T(4,128)}, f32[4,4,4,2048]{3,2,1,0:T(4,128)S(1)}, u32[]{:S(2)}) copy-start(f32[4,4,4,2048]{3,2,1,0:T(4,128)S(1)} %copy.38) | copy-start | bytes 1572868
  19.5 1.9 %copy-start.16 = (f32[1,512]{1,0:T(1,128)S(1)}, f32[1,512]{1,0:T(1,128)}, u32[]{:S(2)}) copy-start(f32[1,512]{1,0:T(1,128)} %param.32) | copy-start | bytes 6148
  19.5 1.9 %copy-start.19 = (f32[1,512]{1,0:T(1,128)S(1)}, f32[1,512]{1,0:T(1,128)}, u32[]{:S(2)}) copy-start(f32[1,512]{1,0:T(1,128)} %param.30) | copy-start | bytes 6148
  19.5 1.9 %copy-start.40 = (f32[4]{0:T(128)S(1)}, f32[4]{0:T(128)}, u32[]{:S(2)}) copy-start(f32[4]{0:T(128)} %constant.122.clone) | copy-start | bytes 52
  24.0 26.6 %copy-start.39 = (f32[8]{0:T(128)S(1)}, f32[8]{0:T(128)}, u32[]{:S(2)}) copy-start(f32[8]{0:T(128)} %param.24) | copy-start | bytes 100
  26.9 31.2 %all-to-all-start = ((f32[32,1,128]{2,1,0:T(1,128)}), f32[32,1,128]{2,1,0:T(1,128)}, u32[]{:S(2)}, u32[]{:S(2)}) async-start(f32[32,1,128]{2,1,0:T(1,128)} %reshape.336), calls=%async_computation | async-start | bytes 32768 | tf_op jit(solution)/shard_map/all_to_all | solution.py:126
  44.9 15.8 %collective-permute-start.2 = (f32[2,4,1,2048]{3,2,1,0:T(1,128)}, f32[2,4,1,2048]{3,2,1,0:T(1,128)S(1)}, u32[]{:S(2)}, u32[]{:S(2)}) collective-permute-start(f32[2,4,1,2048]{3,2,1,0:T(1,128)} %slice.284), channel_id=1, source_target_pairs={{0,1},{1,2},{2,3},{3,4},{4,5},{5,6},{6,7},{7,8},{8,9},{9,10},{10,1... | collective-permute-start | bytes 196616 | tf_op jit(solution)/shard_map/ppermute | solution.py:15
  48.5 12.1 %collective-permute-start.3 = (f32[2,1,4,2048]{3,2,1,0:T(4,128)S(1)}, f32[2,1,4,2048]{3,2,1,0:T(4,128)}, u32[]{:S(2)}, u32[]{:S(2)}) collective-permute-start(f32[2,1,4,2048]{3,2,1,0:T(4,128)S(1)} %slice.291), channel_id=1, source_target_pairs={{0,32},{32,64},{64,96},{96,128},{128,160},{160,192},{192,224},{224... | collective-permute-start | bytes 196616 | tf_op jit(solution)/shard_map/ppermute | solution.py:15
  60.7 2.0 %copy-start.7 = (f32[3,4,4,2048]{3,2,1,0:T(4,128)S(1)}, f32[3,4,4,2048]{3,2,1,0:T(4,128)}, u32[]{:S(2)}) copy-start(f32[3,4,4,2048]{3,2,1,0:T(4,128)} %get-tuple-element.59) | copy-start | bytes 1179652
  62.6 2.8 %copy-start.14 = (f32[32,4,32]{2,1,0:T(4,128)S(1)}, f32[32,4,32]{2,1,0:T(4,128)}, u32[]{:S(2)}) copy-start(f32[32,4,32]{2,1,0:T(4,128)} %reshape.337) | copy-start | bytes 49156
  62.6 3.1 %copy-start.12 = (f32[256,128]{1,0:T(8,128)S(1)}, f32[256,128]{1,0:T(8,128)}, u32[]{:S(2)}) copy-start(f32[256,128]{1,0:T(8,128)} %reshape_squeeze.15) | copy-start | bytes 393220
  65.4 2.3 %copy-start.26 = (pred[1024]{0:T(1024)(128)(4,1)}, pred[1024]{0:T(1024)(128)(4,1)S(1)}, u32[]{:S(2)}) copy-start(pred[1024]{0:T(1024)(128)(4,1)S(1)} %broadcast_compare_fusion) | copy-start | bytes 3076
  65.6 2.1 %copy-start.32 = (s32[1024]{0:T(1024)S(1)}, s32[1024]{0:T(1024)}, u32[]{:S(2)}) copy-start(s32[1024]{0:T(1024)} %get-tuple-element.79) | copy-start | bytes 12292
  67.7 4.3 %copy-start.27 = (pred[1024]{0:T(1024)(128)(4,1)S(1)}, pred[1024]{0:T(1024)(128)(4,1)}, u32[]{:S(2)}) copy-start(pred[1024]{0:T(1024)(128)(4,1)} %copy-done.26) | copy-start | bytes 3076
  67.7 4.3 %copy-start.33 = (s32[1024]{0:T(1024)S(1)}, s32[1024]{0:T(1024)}, u32[]{:S(2)}) copy-start(s32[1024]{0:T(1024)} %get-tuple-element.79) | copy-start | bytes 12292
  69.3 0.6 copy-start.24
  69.9 4.1 %copy-start.28 = (pred[1024]{0:T(1024)(128)(4,1)S(1)}, pred[1024]{0:T(1024)(128)(4,1)}, u32[]{:S(2)}) copy-start(pred[1024]{0:T(1024)(128)(4,1)} %copy-done.26) | copy-start | bytes 3076
  69.9 4.1 %copy-start.34 = (s32[1024]{0:T(1024)S(1)}, s32[1024]{0:T(1024)}, u32[]{:S(2)}) copy-start(s32[1024]{0:T(1024)} %get-tuple-element.79) | copy-start | bytes 12292
  72.0 1.3 copy-start.25
  72.0 6.1 %copy-start.9 = (f32[1,4,4,2048]{3,2,1,0:T(4,128)S(1)}, f32[1,4,4,2048]{3,2,1,0:T(4,128)}, u32[]{:S(2)}) copy-start(f32[1,4,4,2048]{3,2,1,0:T(4,128)} %copy.51) | copy-start | bytes 393220
  77.3 0.7 copy-start.4
  79.9 3.0 %copy-start.13 = (f32[256,128]{1,0:T(8,128)S(1)}, f32[256,128]{1,0:T(8,128)}, u32[]{:S(2)}) copy-start(f32[256,128]{1,0:T(8,128)} %reshape_squeeze.19) | copy-start | bytes 393220
  79.9 16.7 %copy-start.3 = (f32[4,4,4,2048]{3,2,1,0:T(4,128)S(1)}, f32[4,4,4,2048]{3,2,1,0:T(4,128)}, u32[]{:S(2)}) copy-start(f32[4,4,4,2048]{3,2,1,0:T(4,128)} %copy-done.2) | copy-start | bytes 1572868
  87.5 22.5 %all-to-all-start.1 = ((f32[32,2,32]{2,1,0:T(2,128)}), f32[32,2,32]{2,1,0:T(2,128)}, u32[]{:S(2)}, u32[]{:S(2)}) async-start(f32[32,2,32]{2,1,0:T(2,128)} %maximum_bitcast_fusion), calls=%async_computation.1 | async-start | bytes 65536 | tf_op jit(solution)/shard_map/all_to_all | solution.py:126
  99.4 12.6 %copy-start.31 = (s32[512]{0:T(512)S(1)}, s32[512]{0:T(512)}, u32[]{:S(2)}) copy-start(s32[512]{0:T(512)} %copy-done.30) | copy-start | bytes 6148
  99.4 13.5 %copy-start.15 = (f32[1,512]{1,0:T(1,128)S(1)}, f32[1,512]{1,0:T(1,128)}, u32[]{:S(2)}) copy-start(f32[1,512]{1,0:T(1,128)} %param.31) | copy-start | bytes 6148
  99.4 13.5 %copy-start.18 = (f32[1,511]{1,0:T(1,128)S(1)}, f32[1,511]{1,0:T(1,128)}, u32[]{:S(2)}) copy-start(f32[1,511]{1,0:T(1,128)} %copy-done.17) | copy-start | bytes 6136
  99.4 13.5 %copy-start.20 = (f32[1,512]{1,0:T(1,128)S(1)}, f32[1,512]{1,0:T(1,128)}, u32[]{:S(2)}) copy-start(f32[1,512]{1,0:T(1,128)} %param.30) | copy-start | bytes 6148
  99.4 13.6 %copy-start.22 = (f32[1,512]{1,0:T(1,128)S(1)}, f32[1,512]{1,0:T(1,128)}, u32[]{:S(2)}) copy-start(f32[1,512]{1,0:T(1,128)} %copy-done.21) | copy-start | bytes 6148
  99.4 13.6 %copy-start.23 = (f32[1,512]{1,0:T(1,128)S(1)}, f32[1,512]{1,0:T(1,128)}, u32[]{:S(2)}) copy-start(f32[1,512]{1,0:T(1,128)} %param.33) | copy-start | bytes 6148
  99.6 27.0 %collective-permute-start.5 = (f32[2,4,1,2048]{3,2,1,0:T(1,128)S(1)}, f32[2,4,1,2048]{3,2,1,0:T(1,128)S(1)}, u32[]{:S(2)}, u32[]{:S(2)}) collective-permute-start(f32[2,4,1,2048]{3,2,1,0:T(1,128)S(1)} %slice.313), channel_id=1, source_target_pairs={{1,0},{2,1},{3,2},{4,3},{5,4},{6,5},{7,6},{8,7},{9,8},{10,9},{11,1... | collective-permute-start | bytes 196616 | tf_op jit(solution)/shard_map/ppermute | solution.py:15
  100.9 25.7 %collective-permute-start.4 = (f32[2,1,4,2048]{3,2,1,0:T(4,128)S(1)}, f32[2,1,4,2048]{3,2,1,0:T(4,128)S(1)}, u32[]{:S(2)}, u32[]{:S(2)}) collective-permute-start(f32[2,1,4,2048]{3,2,1,0:T(4,128)S(1)} %slice.309), channel_id=1, source_target_pairs={{32,0},{64,32},{96,64},{128,96},{160,128},{192,160},{224,192},{256... | collective-permute-start | bytes 196616 | tf_op jit(solution)/shard_map/ppermute | solution.py:15
  114.0 12.9 %copy-start.37 = (f32[1,512]{1,0:T(1,128)}, f32[1,512]{1,0:T(1,128)S(1)}, u32[]{:S(2)}) copy-start(f32[1,512]{1,0:T(1,128)S(1)} %get-tuple-element.53) | copy-start | bytes 6148
  116.0 23.8 %all-to-all-start.2 = ((f32[32,1,32]{2,1,0:T(1,128)}), f32[32,1,32]{2,1,0:T(1,128)S(1)}, u32[]{:S(2)}, u32[]{:S(2)}) async-start(f32[32,1,32]{2,1,0:T(1,128)} %transpose_reshape.3), calls=%async_computation.2 | async-start | bytes 32768 | tf_op jit(solution)/shard_map/all_to_all | solution.py:126
  127.3 9.2 %collective-permute-start.7 = (f32[2,1,4,2048]{3,2,1,0:T(4,128)S(1)}, f32[2,1,4,2048]{3,2,1,0:T(4,128)S(1)}, u32[]{:S(2)}, u32[]{:S(2)}) collective-permute-start(f32[2,1,4,2048]{3,2,1,0:T(4,128)S(1)} %pad_maximum_fusion.10), channel_id=1, source_target_pairs={{0,32},{32,64},{64,96},{96,128},{128,160},{160,192},{192,224},{224... | collective-permute-start | bytes 196616 | tf_op jit(solution)/shard_map/ppermute | solution.py:15
  129.3 7.6 %copy-start.8 = (f32[3,4,4,2048]{3,2,1,0:T(4,128)}, f32[3,4,4,2048]{3,2,1,0:T(4,128)S(1)}, u32[]{:S(2)}) copy-start(f32[3,4,4,2048]{3,2,1,0:T(4,128)S(1)} %pad_maximum_fusion.1) | copy-start | bytes 1179652
  129.4 7.1 %collective-permute-start.6 = (f32[2,4,1,2048]{3,2,1,0:T(1,128)S(1)}, f32[2,4,1,2048]{3,2,1,0:T(1,128)S(1)}, u32[]{:S(2)}, u32[]{:S(2)}) collective-permute-start(f32[2,4,1,2048]{3,2,1,0:T(1,128)S(1)} %slice.323), channel_id=1, source_target_pairs={{0,1},{1,2},{2,3},{3,4},{4,5},{5,6},{6,7},{7,8},{8,9},{9,10},{10,1... | collective-permute-start | bytes 196616 | tf_op jit(solution)/shard_map/ppermute | solution.py:15
  136.6 1.0 copy-start.6
  136.6 1.0 copy-start.10
  136.9 4.2 %copy-start.29 = (pred[1024]{0:T(1024)(128)(4,1)S(1)}, pred[1024]{0:T(1024)(128)(4,1)}, u32[]{:S(2)}) copy-start(pred[1024]{0:T(1024)(128)(4,1)} %copy-done.26) | copy-start | bytes 3076
  136.9 4.2 %copy-start.35 = (s32[1024]{0:T(1024)S(1)}, s32[1024]{0:T(1024)}, u32[]{:S(2)}) copy-start(s32[1024]{0:T(1024)} %get-tuple-element.79) | copy-start | bytes 12292

commit v8 on v6

--- a/solution.py
+++ b/solution.py
@@ -48,10 +48,10 @@
     return jnp.stack([magn_x, magn_y, magn_z])
 
 
-def electric_base(e_field, h_field, polarization, cells):
+def electric_base(e_field, h_field, polarization, cells, rims=None):
     eps_cell, sigma_cell, strength_cell, decay_cell = cells
     magn_x, magn_y, magn_z = (h_field[0], h_field[1], h_field[2])
-    minus_x, minus_y = magnetic_rims(h_field)
+    minus_x, minus_y = magnetic_rims(h_field) if rims is None else rims
     curl_x = magn_z - minus_y[1] - (magn_y - prev_vertical(magn_y))
     curl_y = magn_x - prev_vertical(magn_x) - (magn_z - minus_x[1])
     curl_z = magn_y - minus_x[0] - (magn_x - minus_y[0])
@@ -91,8 +91,9 @@
     capacity = max(2 * seg_count // n_gy, 16)
     owner_col = seg_owner[0, :, 0]
     cell_ids = seg_cell[0]
-    owner_hot = (owner_col[:, None] == jnp.arange(n_gy, dtype=jnp.int32)[None, :]).astype(jnp.int32)
-    rank_in = jnp.sum((jnp.cumsum(owner_hot, axis=0) - 1) * owner_hot, axis=1)
+    order = jnp.arange(seg_count, dtype=jnp.int32)
+    earlier_same = (owner_col[None, :] == owner_col[:, None]) & (order[None, :] < order[:, None])
+    rank_in = jnp.sum(earlier_same.astype(jnp.int32), axis=1)
     slot_at = owner_col * capacity + rank_in
     grid_shape = material.shape
     cell_total = grid_shape[0] * grid_shape[1] * grid_shape[2]
@@ -166,7 +167,11 @@
 
     back = jnp.stack([sample_0, sample_1]).reshape(2, n_gy, capacity).transpose(1, 0, 2)
     back, e_field, h_field, polarization = lax.optimization_barrier((back, e_field, h_field, polarization))
-    returned = from_slots(exchange(back))
+    returned = exchange(back)
+    h_field = magnetic_update(e_field, h_field)
+    rims = magnetic_rims(h_field)
+    returned, rims = lax.optimization_barrier((returned, rims))
+    returned = from_slots(returned)
     seg_sample_0, seg_sample_1 = returned[0], returned[1]
     curr_1 = curr_0 + gain_row * (seg_sample_0 - drop_0)
     curr_prev = jnp.concatenate([single_zero, curr_1[:-1]])
@@ -175,10 +180,9 @@
     curr_2 = curr_1 + gain_row * (seg_sample_1 - drop_1)
     curr_prev = jnp.concatenate([single_zero, curr_2[:-1]])
     volt_2 = volt_1 - cap_row * (curr_2 - curr_prev)
-    h_field = magnetic_update(e_field, h_field)
     recv_curr_2 = exchange(to_slots(curr_2[None], [0.0]))
 
-    drive, polarization = electric_base(e_field, h_field, polarization, cells)
+    drive, polarization = electric_base(e_field, h_field, polarization, cells, rims)
     recv_curr_2, drive = lax.optimization_barrier((recv_curr_2, drive))
     e_field = electric_finish(e_field, drive, wire_of(recv_curr_2.transpose(1, 0, 2).reshape(-1)), cells)
     return (e_field, h_field, polarization, curr_2[None], volt_2[None])

time: 139 us -> 152 us (1.094)
  the two profiles are of different devices: /device:TPU:16 before, /device:TPU:7 now
where the time goes in v8:
time: 152 us; the launch traced here: 151 us
  starting transfers between devices  66.4 us (44%)
  other arithmetic  26.3 us (17%)
  waiting for transfers between devices  20.4 us (13%)
  local copies, waits for them, and re-layouts  19.4 us (13%)
  matrix products  16.9 us (11%)
    all_to_all x3, starting transfers between devices, exchange(): return lax.all_to_all(blocks, 'gy', split_axis=0, concat_axis=0, tiled=True)  36.7 us
    ppermute x8, starting transfers between devices, passed_along(): lax.ppermute(value, axis, [(source, source + steps) for source in range(f...  29.7 us
    all_to_all x3, waiting for transfers between devices, exchange(): return lax.all_to_all(blocks, 'gy', split_axis=0, concat_axis=0, tiled=True)  19.2 us
    dot_general x2, matrix products, wire_of(): jnp.einsum('kr,kl->rl', row_hot, spread, precision=highest)  5.56 us
    dot_general x2, matrix products, sample(): jnp.dot(row_hot, e_now[2].reshape(plane_rows, lanes), precision=highest)  5.36 us
    another operation x2, local copies, waits for them, and re-layouts, sample(): e_now[2].reshape(plane_rows, lanes)  3.25 us
  transfers between devices with their start and end apart: 11, of which 3 were waited for; matrix products, arithmetic and copies ran while one was open for 16% of the time, Pallas kernels for 0%

profile of v8, /device:TPU:7, one launch (start us, length us, event | category | flops | bytes accessed | tf_op | source)
XLA Modules:
  0.0 150.8 jit_solution(10910141962269790224)
XLA Ops:
  0.7 1.0 slice.261
  1.7 1.3 collective-permute-start
  3.0 0.8 slice.270
  3.9 2.6 %collective-permute-start.1 = (f32[2,1,4,2048]{3,2,1,0:T(4,128)S(1)}, f32[2,1,4,2048]{3,2,1,0:T(4,128)S(1)}, u32[]{:S(2)}, u32[]{:S(2)}) collective-permute-start(f32[2,1,4,2048]{3,2,1,0:T(4,128)S(1)} %slice.270), channel_id=1, source_target_pairs={{32,0},{64,32},{96,64},{128,96},{160,128},{192,160},{224,192},{256... | collective-permute-start | bytes 196616 | tf_op jit(solution)/shard_map/ppermute | solution.py:15
  6.4 1.0 convert_reduce_fusion.1
  7.4 0.7 multiply_add_fusion.6
  8.4 0.8 slice.258
  9.2 0.7 convert_element_type.37
  9.9 1.5 convolution_bitcast_fusion.1
  11.8 0.6 fusion
  13.4 0.7 bitcast_multiply_fusion
  14.2 1.9 %multiply_add_fusion.1 = (f32[4,3,4,4,2048]{4,3,2,1,0:T(4,128)S(1)}, f32[3,4,4,2048]{3,2,1,0:T(4,128)}) fusion(f32[4,3,4,4,2048]{4,3,2,1,0:T(4,128)S(1)} %copy-done.5, f32[3,4,4,2048]{3,2,1,0:T(4,128)S(1)} %copy-done.1, f32[4,4,4,2048]{3,2,1,0:T(4,128)S(1)} %copy.32, f32[4,4,4,2048]{3,2,1,0:T(4,128)S(1)} %copy.31), kind=kLoop, calls=%fused_computation.19 | loop fusion | flops 1867776 | bytes 4980736 | tf_op jit(solution)/shard_map/add | solution.py:60
  16.1 1.0 fusion.30
  17.4 1.7 %fusion.158 = (f32[1,4,4,2048]{3,2,1,0:T(4,128)}, f32[1,4,4,2048]{3,2,1,0:T(4,128)S(1)}, f32[4,4,2048]{2,1,0:T(4,128)S(1)}, f32[4,4,2048]{2,1,0:T(4,128)S(1)}) fusion(f32[3,4,4,2048]{3,2,1,0:T(4,128)S(1)} %copy-done.1, f32[2,4,1,2048]{3,2,1,0:T(1,128)S(1)} %collective-permute-done, f32[2,4,3,2048]{3,2,1,0:T(4,128)S(1)} %slice.260, ...), kind=kLoop, calls=%fused_computation.230 | loop fusion | flops 229376 | bytes 1572864 | tf_op jit(solution)/shard_map/slice | solution.py:44
  19.4 1.2 fusion.96
  20.7 0.7 slice.276
  21.4 4.3 %collective-permute-start.2 = (f32[2,4,1,2048]{3,2,1,0:T(1,128)}, f32[2,4,1,2048]{3,2,1,0:T(1,128)S(1)}, u32[]{:S(2)}, u32[]{:S(2)}) collective-permute-start(f32[2,4,1,2048]{3,2,1,0:T(1,128)} %slice.276), channel_id=1, source_target_pairs={{0,1},{1,2},{2,3},{3,4},{4,5},{5,6},{6,7},{7,8},{8,9},{9,10},{10,1... | collective-permute-start | bytes 196616 | tf_op jit(solution)/shard_map/ppermute | solution.py:15
  25.7 7.2 %collective-permute-start.3 = (f32[2,1,4,2048]{3,2,1,0:T(4,128)S(1)}, f32[2,1,4,2048]{3,2,1,0:T(4,128)}, u32[]{:S(2)}, u32[]{:S(2)}) collective-permute-start(f32[2,1,4,2048]{3,2,1,0:T(4,128)S(1)} %slice.283), channel_id=1, source_target_pairs={{0,32},{32,64},{64,96},{96,128},{128,160},{160,192},{192,224},{224... | collective-permute-start | bytes 196616 | tf_op jit(solution)/shard_map/ppermute | solution.py:15
  32.9 0.7 reshape.273
  33.6 16.2 %all-to-all-start = ((f32[32,1,128]{2,1,0:T(1,128)}), f32[32,1,128]{2,1,0:T(1,128)}, u32[]{:S(2)}, u32[]{:S(2)}) async-start(f32[32,1,128]{2,1,0:T(1,128)} %reshape.273), calls=%async_computation | async-start | bytes 32768 | tf_op jit(solution)/shard_map/all_to_all | solution.py:113
  50.4 0.7 copy.43
  51.2 1.6 %reshape_squeeze.15 = f32[256,128]{1,0:T(8,128)} reshape(f32[1,4,4,2048]{3,2,1,0:T(4,128)} %get-tuple-element.75) | data formatting | bytes 262144 | tf_op jit(solution)/shard_map/reshape;squeeze | solution.py:155
  52.8 8.8 %all-to-all-done = f32[32,1,128]{2,1,0:T(1,128)} async-done(((f32[32,1,128]{2,1,0:T(1,128)}), f32[32,1,128]{2,1,0:T(1,128)}, u32[]{:S(2)}, u32[]{:S(2)}) %all-to-all-start) | async-done | bytes 16416 | tf_op jit(solution)/shard_map/all_to_all | solution.py:113
  62.0 1.4 reduce.24
  63.5 0.7 reshape.274
  64.2 0.9 slice_bitcast_fusion.3
  65.1 1.0 fusion.82
  66.1 1.2 fusion.56
  67.3 0.9 convert_reduce_fusion.2
  68.3 0.6 add_select_fusion.1
  68.9 0.6 compare_convert_fusion
  69.8 2.4 %fusion.21 = f32[1024]{0:T(1024)S(1)} fusion(f32[256,128]{1,0:T(8,128)} %reshape_squeeze.15, f32[1024]{0:T(1024)} %compare_convert_fusion, s32[1024]{0:T(1024)} %get-tuple-element.87, s32[1024]{0:T(1024)} %get-tuple-element.86), kind=kOutput, calls=%fused_computation.23 | convolution fusion | flops 403569664 | bytes 147456 | tf_op jit(solution)/shard_map/dot_general | solution.py:155
  72.2 0.7 stack.65
  72.9 3.5 %fusion.24 = f32[256,128]{1,0:T(8,128)} fusion(f32[1024]{0:T(1024)} %compare_convert_fusion, s32[1024]{0:T(1024)} %get-tuple-element.87, f32[1024]{0:T(1024)S(1)} %multiply_add_fusion.3, s32[1024]{0:T(1024)} %get-tuple-element.86), kind=kOutput, calls=%fused_computation.24 | convolution fusion | flops 403472384 | bytes 147456 | tf_op jit(solution)/shard_map/kr,kl->rl/dot_general | solution.py:160
  76.4 0.9 mul.208
  77.4 0.7 copy-done.4
  78.1 1.1 divide_add_fusion.1
  79.2 0.7 slice.339
  79.9 1.6 %reshape_squeeze.19 = f32[256,128]{1,0:T(8,128)} reshape(f32[1,4,4,2048]{3,2,1,0:T(4,128)} %slice.339) | data formatting | bytes 262144 | tf_op jit(solution)/shard_map/reshape;squeeze | solution.py:155
  81.5 3.0 %fusion.18 = f32[1024]{0:T(1024)} fusion(f32[256,128]{1,0:T(8,128)} %reshape_squeeze.19, f32[1024]{0:T(1024)} %compare_convert_fusion, s32[1024]{0:T(1024)} %get-tuple-element.87, s32[1024]{0:T(1024)} %get-tuple-element.86), kind=kOutput, calls=%fused_computation.22 | convolution fusion | flops 403569664 | bytes 147456 | tf_op jit(solution)/shard_map/dot_general | solution.py:155
  84.5 1.4 stack.66
  85.8 1.4 maximum_bitcast_fusion
  87.2 0.6 slice.298
  87.8 0.7 slice.305
  88.5 1.9 %collective-permute-start.4 = (f32[2,1,4,2048]{3,2,1,0:T(4,128)}, f32[2,1,4,2048]{3,2,1,0:T(4,128)}, u32[]{:S(2)}, u32[]{:S(2)}) collective-permute-start(f32[2,1,4,2048]{3,2,1,0:T(4,128)} %slice.298), channel_id=1, source_target_pairs={{32,0},{64,32},{96,64},{128,96},{160,128},{192,160},{224,192},{256... | collective-permute-start | bytes 196616 | tf_op jit(solution)/shard_map/ppermute | solution.py:15
  90.4 1.3 collective-permute-start.5
  91.7 5.4 %all-to-all-start.1 = ((f32[32,2,32]{2,1,0:T(2,128)}), f32[32,2,32]{2,1,0:T(2,128)}, u32[]{:S(2)}, u32[]{:S(2)}) async-start(f32[32,2,32]{2,1,0:T(2,128)} %maximum_bitcast_fusion), calls=%async_computation.1 | async-start | bytes 65536 | tf_op jit(solution)/shard_map/all_to_all | solution.py:113
  97.2 2.7 %subtract_reduce_fusion = (f32[3,4,4,2048]{3,2,1,0:T(4,128)}, f32[4,3,4,4,2048]{4,3,2,1,0:T(4,128)}) fusion(f32[4,3,4,4,2048]{4,3,2,1,0:T(4,128)S(1)} %get-tuple-element.52, f32[3,4,4,2048]{3,2,1,0:T(4,128)S(1)} %bitcast.214, f32[4,4,4,2048]{3,2,1,0:T(4,128)S(1)} %copy-done.3, f32[4,4,4,2048]{3,2,1,0:T(4,128)S(1)} %copy.31), kind=kLoop, calls=%fused_computation.16 | loop fusion | flops 1867776 | bytes 4980736 | tf_op jit(solution)/shard_map/reduce_sum | solution.py:63
  100.0 0.9 slice_bitcast_fusion
  101.2 1.0 fusion.101
  102.3 8.4 %collective-permute-start.6 = (f32[2,1,4,2048]{3,2,1,0:T(4,128)S(1)}, f32[2,1,4,2048]{3,2,1,0:T(4,128)S(1)}, u32[]{:S(2)}, u32[]{:S(2)}) collective-permute-start(f32[2,1,4,2048]{3,2,1,0:T(4,128)S(1)} %pad_maximum_fusion.10), channel_id=1, source_target_pairs={{0,32},{32,64},{64,96},{96,128},{128,160},{160,192},{192,224},{224... | collective-permute-start | bytes 196616 | tf_op jit(solution)/shard_map/ppermute | solution.py:15
  111.0 2.7 %collective-permute-start.7 = (f32[2,4,1,2048]{3,2,1,0:T(1,128)S(1)}, f32[2,4,1,2048]{3,2,1,0:T(1,128)S(1)}, u32[]{:S(2)}, u32[]{:S(2)}) collective-permute-start(f32[2,4,1,2048]{3,2,1,0:T(1,128)S(1)} %slice.312), channel_id=1, source_target_pairs={{0,1},{1,2},{2,3},{3,4},{4,5},{5,6},{6,7},{7,8},{8,9},{9,10},{10,1... | collective-permute-start | bytes 196616 | tf_op jit(solution)/shard_map/ppermute | solution.py:15
  113.8 1.2 collective-permute-done.7
  115.1 0.8 copy.33
  116.0 0.7 fusion.2
  117.1 0.7 fusion.148
  117.8 1.0 fusion.1
  118.8 0.7 transpose_reshape.3
  119.5 15.1 %all-to-all-start.2 = ((f32[32,1,32]{2,1,0:T(1,128)}), f32[32,1,32]{2,1,0:T(1,128)S(1)}, u32[]{:S(2)}, u32[]{:S(2)}) async-start(f32[32,1,32]{2,1,0:T(1,128)} %transpose_reshape.3), calls=%async_computation.2 | async-start | bytes 32768 | tf_op jit(solution)/shard_map/all_to_all | solution.py:113
  134.7 1.0 fusion.115
  136.1 10.4 %all-to-all-done.2 = f32[32,1,32]{2,1,0:T(1,128)S(1)} async-done(((f32[32,1,32]{2,1,0:T(1,128)}), f32[32,1,32]{2,1,0:T(1,128)S(1)}, u32[]{:S(2)}, u32[]{:S(2)}) %all-to-all-start.2) | async-done | bytes 4128 | tf_op jit(solution)/shard_map/all_to_all | solution.py:113
  147.0 0.7 reduce.23
  147.8 2.1 %fusion.27 = f32[256,128]{1,0:T(8,128)S(1)} fusion(f32[1024]{0:T(1024)S(1)} %copy-done.26, s32[1024]{0:T(1024)S(1)} %copy-done.25, f32[1024]{0:T(1024)S(1)} %broadcast_in_dim.23, s32[1024]{0:T(1024)S(1)} %copy-done.24), kind=kOutput, calls=%fused_computation.25 | convolution fusion | flops 403472384 | bytes 147456 | tf_op jit(solution)/shard_map/kr,kl->rl/dot_general | solution.py:160
  150.0 0.8 divide_add_fusion
  (120 shorter events, 6.3 us)
Async XLA Ops:
  0.6 9.3 %copy-start = (f32[4,8]{1,0:T(4,128)S(1)}, f32[4,8]{1,0:T(4,128)}, u32[]{:S(2)}) copy-start(f32[4,8]{1,0:T(4,128)} %param.27) | copy-start | bytes 388
  0.6 11.1 %copy-start.11 = (s32[4,4,2048]{2,1,0:T(4,128)S(1)}, s32[4,4,2048]{2,1,0:T(4,128)}, u32[]{:S(2)}) copy-start(s32[4,4,2048]{2,1,0:T(4,128)} %param.23) | copy-start | bytes 393220
  0.7 11.1 %copy-start.27 = (f32[4,8]{1,0:T(4,128)S(1)}, f32[4,8]{1,0:T(4,128)}, u32[]{:S(2)}) copy-start(f32[4,8]{1,0:T(4,128)} %param.26) | copy-start | bytes 388
  1.7 15.7 %collective-permute-start = (f32[2,4,1,2048]{3,2,1,0:T(1,128)S(1)}, f32[2,4,1,2048]{3,2,1,0:T(1,128)S(1)}, u32[]{:S(2)}, u32[]{:S(2)}) collective-permute-start(f32[2,4,1,2048]{3,2,1,0:T(1,128)S(1)} %slice.261), channel_id=1, source_target_pairs={{1,0},{2,1},{3,2},{4,3},{5,4},{6,5},{7,6},{8,7},{9,8},{10,9},{11,1... | collective-permute-start | bytes 196616 | tf_op jit(solution)/shard_map/ppermute | solution.py:15
  3.9 13.5 %collective-permute-start.1 = (f32[2,1,4,2048]{3,2,1,0:T(4,128)S(1)}, f32[2,1,4,2048]{3,2,1,0:T(4,128)S(1)}, u32[]{:S(2)}, u32[]{:S(2)}) collective-permute-start(f32[2,1,4,2048]{3,2,1,0:T(4,128)S(1)} %slice.270), channel_id=1, source_target_pairs={{32,0},{64,32},{96,64},{128,96},{160,128},{192,160},{224,192},{256... | collective-permute-start | bytes 196616 | tf_op jit(solution)/shard_map/ppermute | solution.py:15
  8.1 7.9 %copy-start.22 = (s32[512]{0:T(512)}, s32[512]{0:T(512)S(1)}, u32[]{:S(2)}) copy-start(s32[512]{0:T(512)S(1)} %multiply_add_fusion.6) | copy-start | bytes 6148
  9.2 4.9 %copy-start.15 = (f32[1,511]{1,0:T(1,128)}, f32[1,511]{1,0:T(1,128)S(1)}, u32[]{:S(2)}) copy-start(f32[1,511]{1,0:T(1,128)S(1)} %slice.258) | copy-start | bytes 6136
  11.4 1.4 copy-start.29
  11.8 2.3 %copy-start.13 = (f32[1,512]{1,0:T(1,128)S(1)}, f32[1,512]{1,0:T(1,128)}, u32[]{:S(2)}) copy-start(f32[1,512]{1,0:T(1,128)} %param.31) | copy-start | bytes 6148
  11.8 2.4 %copy-start.1 = (f32[3,4,4,2048]{3,2,1,0:T(4,128)S(1)}, f32[3,4,4,2048]{3,2,1,0:T(4,128)}, u32[]{:S(2)}) copy-start(f32[3,4,4,2048]{3,2,1,0:T(4,128)} %param.20) | copy-start | bytes 1179652
  11.8 2.4 %copy-start.5 = (f32[4,3,4,4,2048]{4,3,2,1,0:T(4,128)S(1)}, f32[4,3,4,4,2048]{4,3,2,1,0:T(4,128)}, u32[]{:S(2)}) copy-start(f32[4,3,4,4,2048]{4,3,2,1,0:T(4,128)} %param.22) | copy-start | bytes 4718596
  12.8 3.3 %copy-start.2 = (f32[4,4,4,2048]{3,2,1,0:T(4,128)}, f32[4,4,4,2048]{3,2,1,0:T(4,128)S(1)}, u32[]{:S(2)}) copy-start(f32[4,4,4,2048]{3,2,1,0:T(4,128)S(1)} %copy.32) | copy-start | bytes 1572868
  14.2 1.9 %copy-start.19 = (f32[1,512]{1,0:T(1,128)}, f32[1,512]{1,0:T(1,128)S(1)}, u32[]{:S(2)}) copy-start(f32[1,512]{1,0:T(1,128)S(1)} %fusion.132) | copy-start | bytes 6148
  14.2 1.9 %copy-start.14 = (f32[1,512]{1,0:T(1,128)S(1)}, f32[1,512]{1,0:T(1,128)}, u32[]{:S(2)}) copy-start(f32[1,512]{1,0:T(1,128)} %param.32) | copy-start | bytes 6148
  14.2 1.9 %copy-start.17 = (f32[1,512]{1,0:T(1,128)S(1)}, f32[1,512]{1,0:T(1,128)}, u32[]{:S(2)}) copy-start(f32[1,512]{1,0:T(1,128)} %param.30) | copy-start | bytes 6148
  14.2 1.9 %copy-start.31 = (f32[4]{0:T(128)S(1)}, f32[4]{0:T(128)}, u32[]{:S(2)}) copy-start(f32[4]{0:T(128)} %constant.108.clone) | copy-start | bytes 52
  19.2 30.6 %copy-start.30 = (f32[8]{0:T(128)S(1)}, f32[8]{0:T(128)}, u32[]{:S(2)}) copy-start(f32[8]{0:T(128)} %param.24) | copy-start | bytes 100
  21.4 42.8 %collective-permute-start.2 = (f32[2,4,1,2048]{3,2,1,0:T(1,128)}, f32[2,4,1,2048]{3,2,1,0:T(1,128)S(1)}, u32[]{:S(2)}, u32[]{:S(2)}) collective-permute-start(f32[2,4,1,2048]{3,2,1,0:T(1,128)} %slice.276), channel_id=1, source_target_pairs={{0,1},{1,2},{2,3},{3,4},{4,5},{5,6},{6,7},{7,8},{8,9},{9,10},{10,1... | collective-permute-start | bytes 196616 | tf_op jit(solution)/shard_map/ppermute | solution.py:15
  25.7 38.5 %collective-permute-start.3 = (f32[2,1,4,2048]{3,2,1,0:T(4,128)S(1)}, f32[2,1,4,2048]{3,2,1,0:T(4,128)}, u32[]{:S(2)}, u32[]{:S(2)}) collective-permute-start(f32[2,1,4,2048]{3,2,1,0:T(4,128)S(1)} %slice.283), channel_id=1, source_target_pairs={{0,32},{32,64},{64,96},{96,128},{128,160},{160,192},{192,224},{224... | collective-permute-start | bytes 196616 | tf_op jit(solution)/shard_map/ppermute | solution.py:15
  33.6 27.9 %all-to-all-start = ((f32[32,1,128]{2,1,0:T(1,128)}), f32[32,1,128]{2,1,0:T(1,128)}, u32[]{:S(2)}, u32[]{:S(2)}) async-start(f32[32,1,128]{2,1,0:T(1,128)} %reshape.273), calls=%async_computation | async-start | bytes 32768 | tf_op jit(solution)/shard_map/all_to_all | solution.py:113
  64.2 1.9 %copy-start.7 = (f32[3,4,4,2048]{3,2,1,0:T(4,128)S(1)}, f32[3,4,4,2048]{3,2,1,0:T(4,128)}, u32[]{:S(2)}) copy-start(f32[3,4,4,2048]{3,2,1,0:T(4,128)} %get-tuple-element.65) | copy-start | bytes 1179652
  66.1 3.4 %copy-start.12 = (f32[32,4,32]{2,1,0:T(4,128)S(1)}, f32[32,4,32]{2,1,0:T(4,128)}, u32[]{:S(2)}) copy-start(f32[32,4,32]{2,1,0:T(4,128)} %reshape.274) | copy-start | bytes 49156
  69.8 8.3 %copy-start.9 = (f32[1,4,4,2048]{3,2,1,0:T(4,128)S(1)}, f32[1,4,4,2048]{3,2,1,0:T(4,128)}, u32[]{:S(2)}) copy-start(f32[1,4,4,2048]{3,2,1,0:T(4,128)} %copy.43) | copy-start | bytes 393220
  77.4 0.7 copy-start.4
  79.2 17.9 %copy-start.3 = (f32[4,4,4,2048]{3,2,1,0:T(4,128)S(1)}, f32[4,4,4,2048]{3,2,1,0:T(4,128)}, u32[]{:S(2)}) copy-start(f32[4,4,4,2048]{3,2,1,0:T(4,128)} %copy-done.2) | copy-start | bytes 1572868
  88.5 11.5 %collective-permute-start.4 = (f32[2,1,4,2048]{3,2,1,0:T(4,128)}, f32[2,1,4,2048]{3,2,1,0:T(4,128)}, u32[]{:S(2)}, u32[]{:S(2)}) collective-permute-start(f32[2,1,4,2048]{3,2,1,0:T(4,128)} %slice.298), channel_id=1, source_target_pairs={{32,0},{64,32},{96,64},{128,96},{160,128},{192,160},{224,192},{256... | collective-permute-start | bytes 196616 | tf_op jit(solution)/shard_map/ppermute | solution.py:15
  90.4 9.6 %collective-permute-start.5 = (f32[2,4,1,2048]{3,2,1,0:T(1,128)}, f32[2,4,1,2048]{3,2,1,0:T(1,128)}, u32[]{:S(2)}, u32[]{:S(2)}) collective-permute-start(f32[2,4,1,2048]{3,2,1,0:T(1,128)} %slice.305), channel_id=1, source_target_pairs={{1,0},{2,1},{3,2},{4,3},{5,4},{6,5},{7,6},{8,7},{9,8},{10,9},{11,1... | collective-permute-start | bytes 196616 | tf_op jit(solution)/shard_map/ppermute | solution.py:15
  91.7 23.4 %all-to-all-start.1 = ((f32[32,2,32]{2,1,0:T(2,128)}), f32[32,2,32]{2,1,0:T(2,128)}, u32[]{:S(2)}, u32[]{:S(2)}) async-start(f32[32,2,32]{2,1,0:T(2,128)} %maximum_bitcast_fusion), calls=%async_computation.1 | async-start | bytes 65536 | tf_op jit(solution)/shard_map/all_to_all | solution.py:113
  102.2 13.8 %copy-start.23 = (s32[512]{0:T(512)S(1)}, s32[512]{0:T(512)}, u32[]{:S(2)}) copy-start(s32[512]{0:T(512)} %copy-done.22) | copy-start | bytes 6148
  102.3 11.4 %collective-permute-start.6 = (f32[2,1,4,2048]{3,2,1,0:T(4,128)S(1)}, f32[2,1,4,2048]{3,2,1,0:T(4,128)S(1)}, u32[]{:S(2)}, u32[]{:S(2)}) collective-permute-start(f32[2,1,4,2048]{3,2,1,0:T(4,128)S(1)} %pad_maximum_fusion.10), channel_id=1, source_target_pairs={{0,32},{32,64},{64,96},{96,128},{128,160},{160,192},{192,224},{224... | collective-permute-start | bytes 196616 | tf_op jit(solution)/shard_map/ppermute | solution.py:15
  110.7 6.0 %copy-start.16 = (f32[1,511]{1,0:T(1,128)S(1)}, f32[1,511]{1,0:T(1,128)}, u32[]{:S(2)}) copy-start(f32[1,511]{1,0:T(1,128)} %copy-done.15) | copy-start | bytes 6136
  110.7 6.0 %copy-start.18 = (f32[1,512]{1,0:T(1,128)S(1)}, f32[1,512]{1,0:T(1,128)}, u32[]{:S(2)}) copy-start(f32[1,512]{1,0:T(1,128)} %param.30) | copy-start | bytes 6148
  110.7 6.1 %copy-start.21 = (f32[1,512]{1,0:T(1,128)S(1)}, f32[1,512]{1,0:T(1,128)}, u32[]{:S(2)}) copy-start(f32[1,512]{1,0:T(1,128)} %param.33) | copy-start | bytes 6148
  110.7 6.3 %copy-start.20 = (f32[1,512]{1,0:T(1,128)S(1)}, f32[1,512]{1,0:T(1,128)}, u32[]{:S(2)}) copy-start(f32[1,512]{1,0:T(1,128)} %copy-done.19) | copy-start | bytes 6148
  110.8 8.7 %copy-start.8 = (f32[3,4,4,2048]{3,2,1,0:T(4,128)}, f32[3,4,4,2048]{3,2,1,0:T(4,128)S(1)}, u32[]{:S(2)}) copy-start(f32[3,4,4,2048]{3,2,1,0:T(4,128)S(1)} %pad_maximum_fusion.1) | copy-start | bytes 1179652
  111.0 4.1 %collective-permute-start.7 = (f32[2,4,1,2048]{3,2,1,0:T(1,128)S(1)}, f32[2,4,1,2048]{3,2,1,0:T(1,128)S(1)}, u32[]{:S(2)}, u32[]{:S(2)}) collective-permute-start(f32[2,4,1,2048]{3,2,1,0:T(1,128)S(1)} %slice.312), channel_id=1, source_target_pairs={{0,1},{1,2},{2,3},{3,4},{4,5},{5,6},{6,7},{7,8},{8,9},{9,10},{10,1... | collective-permute-start | bytes 196616 | tf_op jit(solution)/shard_map/ppermute | solution.py:15
  117.8 18.1 %copy-start.28 = (f32[1,512]{1,0:T(1,128)}, f32[1,512]{1,0:T(1,128)S(1)}, u32[]{:S(2)}) copy-start(f32[1,512]{1,0:T(1,128)S(1)} %get-tuple-element.59) | copy-start | bytes 6148
  118.8 17.1 %copy-start.6 = (f32[3,4,4,2048]{3,2,1,0:T(4,128)S(1)}, f32[3,4,4,2048]{3,2,1,0:T(4,128)}, u32[]{:S(2)}) copy-start(f32[3,4,4,2048]{3,2,1,0:T(4,128)} %get-tuple-element.62) | copy-start | bytes 1179652
  118.8 17.1 %copy-start.10 = (f32[4,4,2048]{2,1,0:T(4,128)S(1)}, f32[4,4,2048]{2,1,0:T(4,128)}, u32[]{:S(2)}) copy-start(f32[4,4,2048]{2,1,0:T(4,128)} %bitcast_multiply_fusion) | copy-start | bytes 393220
  119.5 27.0 %all-to-all-start.2 = ((f32[32,1,32]{2,1,0:T(1,128)}), f32[32,1,32]{2,1,0:T(1,128)S(1)}, u32[]{:S(2)}, u32[]{:S(2)}) async-start(f32[32,1,32]{2,1,0:T(1,128)} %transpose_reshape.3), calls=%async_computation.2 | async-start | bytes 32768 | tf_op jit(solution)/shard_map/all_to_all | solution.py:113
  135.6 12.2 %copy-start.24 = (s32[1024]{0:T(1024)S(1)}, s32[1024]{0:T(1024)}, u32[]{:S(2)}) copy-start(s32[1024]{0:T(1024)} %get-tuple-element.86) | copy-start | bytes 12292
  135.6 12.2 %copy-start.25 = (s32[1024]{0:T(1024)S(1)}, s32[1024]{0:T(1024)}, u32[]{:S(2)}) copy-start(s32[1024]{0:T(1024)} %get-tuple-element.87) | copy-start | bytes 12292
  135.6 12.2 %copy-start.26 = (f32[1024]{0:T(1024)S(1)}, f32[1024]{0:T(1024)}, u32[]{:S(2)}) copy-start(f32[1024]{0:T(1024)} %compare_convert_fusion) | copy-start | bytes 12292

commit v9 on v6

--- a/solution.py
+++ b/solution.py
@@ -91,8 +91,9 @@
     capacity = max(2 * seg_count // n_gy, 16)
     owner_col = seg_owner[0, :, 0]
     cell_ids = seg_cell[0]
-    owner_hot = (owner_col[:, None] == jnp.arange(n_gy, dtype=jnp.int32)[None, :]).astype(jnp.int32)
-    rank_in = jnp.sum((jnp.cumsum(owner_hot, axis=0) - 1) * owner_hot, axis=1)
+    order = jnp.arange(seg_count, dtype=jnp.int32)
+    earlier_same = (owner_col[None, :] == owner_col[:, None]) & (order[None, :] < order[:, None])
+    rank_in = jnp.sum(earlier_same.astype(jnp.int32), axis=1)
     slot_at = owner_col * capacity + rank_in
     grid_shape = material.shape
     cell_total = grid_shape[0] * grid_shape[1] * grid_shape[2]

time: 139 us -> 137 us (0.986)
  other arithmetic: 25.6 us -> 23.9 us
  transfers between devices with their start and end apart: 11 -> 11, of which waited for: 4 -> 4; matrix products, arithmetic and copies ran while one was open for 21% -> 20% of each run, Pallas kernels for 0% -> 0%
where the time goes in v9:
time: 137 us; the launch traced here: 136 us
  starting transfers between devices  61.1 us (45%)
  other arithmetic  23.9 us (17%)
  local copies, waits for them, and re-layouts  18.6 us (14%)
  matrix products  17.6 us (13%)
  waiting for transfers between devices  13.4 us (10%)
  between operations  1.37 us (1%)
    all_to_all x3, starting transfers between devices, exchange(): return lax.all_to_all(blocks, 'gy', split_axis=0, concat_axis=0, tiled=True)  37.6 us
    ppermute x8, starting transfers between devices, passed_along(): lax.ppermute(value, axis, [(source, source + steps) for source in range(f...  23.4 us
    all_to_all x3, waiting for transfers between devices, exchange(): return lax.all_to_all(blocks, 'gy', split_axis=0, concat_axis=0, tiled=True)  10.3 us
    dot_general x2, matrix products, wire_of(): jnp.einsum('kr,kl->rl', row_hot, spread, precision=highest)  5.56 us
    dot_general x2, matrix products, sample(): jnp.dot(row_hot, e_now[2].reshape(plane_rows, lanes), precision=highest)  5.37 us
    another operation x2, local copies, waits for them, and re-layouts, sample(): e_now[2].reshape(plane_rows, lanes)  3.24 us
    ppermute x8, waiting for transfers between devices, passed_along(): lax.ppermute(value, axis, [(source, source + steps) for source in range(f...  3.14 us
    reduce_sum x1, other arithmetic, electric_base(): change = jnp.sum(polar_new - polarization, axis=0)  2.75 us
  transfers between devices with their start and end apart: 11, of which 4 were waited for; matrix products, arithmetic and copies ran while one was open for 20% of the time, Pallas kernels for 0%

profile of v9, /device:TPU:16, one launch (start us, length us, event | category | flops | bytes accessed | tf_op | source)
XLA Modules:
  0.0 136.0 jit_solution(6733378146530898177)
XLA Ops:
  0.7 1.0 slice.261
  1.7 1.3 collective-permute-start
  3.0 0.8 slice.270
  3.9 3.9 %collective-permute-start.1 = (f32[2,1,4,2048]{3,2,1,0:T(4,128)S(1)}, f32[2,1,4,2048]{3,2,1,0:T(4,128)S(1)}, u32[]{:S(2)}, u32[]{:S(2)}) collective-permute-start(f32[2,1,4,2048]{3,2,1,0:T(4,128)S(1)} %slice.270), channel_id=1, source_target_pairs={{32,0},{64,32},{96,64},{128,96},{160,128},{192,160},{224,192},{256... | collective-permute-start | bytes 196616 | tf_op jit(solution)/shard_map/ppermute | solution.py:15
  7.7 1.0 convert_reduce_fusion.1
  8.7 0.7 multiply_add_fusion.6
  9.4 0.8 slice.258
  10.2 0.7 convert_element_type.37
  11.2 1.5 %convolution_bitcast_fusion.1 = f32[4,4,4,2048]{3,0,2,1:T(4,128)S(1)} fusion(s32[4,4,2048]{2,1,0:T(4,128)} %param.23, f32[4,8]{1,0:T(4,128)S(1)} %copy-done), kind=kOutput, calls=%fused_computation.2 | convolution fusion | flops 12845056 | bytes 655488 | tf_op jit(solution)/shard_map/pm,mxyz->pxyz/dot_general | solution.py:135
  13.1 0.6 fusion
  14.1 0.6 fusion.32
  14.7 0.7 bitcast_multiply_fusion
  15.5 1.9 %multiply_add_fusion.1 = (f32[4,3,4,4,2048]{4,3,2,1,0:T(4,128)S(1)}, f32[3,4,4,2048]{3,2,1,0:T(4,128)}) fusion(f32[4,3,4,4,2048]{4,3,2,1,0:T(4,128)S(1)} %copy-done.5, f32[3,4,4,2048]{3,2,1,0:T(4,128)S(1)} %copy-done.1, f32[4,4,4,2048]{3,2,1,0:T(4,128)S(1)} %copy.32, f32[4,4,4,2048]{3,2,1,0:T(4,128)S(1)} %copy.31), kind=kLoop, calls=%fused_computation.19 | loop fusion | flops 1867776 | bytes 4980736 | tf_op jit(solution)/shard_map/add | solution.py:60
  17.4 1.0 fusion.30
  18.7 1.7 %fusion.165 = (f32[1,4,4,2048]{3,2,1,0:T(4,128)}, f32[1,4,4,2048]{3,2,1,0:T(4,128)S(1)}, f32[4,4,2048]{2,1,0:T(4,128)S(1)}, f32[4,4,2048]{2,1,0:T(4,128)S(1)}) fusion(f32[3,4,4,2048]{3,2,1,0:T(4,128)S(1)} %copy-done.1, f32[2,4,1,2048]{3,2,1,0:T(1,128)S(1)} %collective-permute-done, f32[2,4,3,2048]{3,2,1,0:T(4,128)S(1)} %slice.260, ...), kind=kLoop, calls=%fused_computation.237 | loop fusion | flops 229376 | bytes 1572864 | tf_op jit(solution)/shard_map/slice | solution.py:44
  20.7 1.2 fusion.96
  22.0 0.7 slice.276
  22.7 0.7 reshape.273
  23.4 18.0 %all-to-all-start = ((f32[32,1,128]{2,1,0:T(1,128)}), f32[32,1,128]{2,1,0:T(1,128)}, u32[]{:S(2)}, u32[]{:S(2)}) async-start(f32[32,1,128]{2,1,0:T(1,128)} %reshape.273), calls=%async_computation | async-start | bytes 32768 | tf_op jit(solution)/shard_map/all_to_all | solution.py:113
  41.5 3.6 %collective-permute-start.2 = (f32[2,4,1,2048]{3,2,1,0:T(1,128)}, f32[2,4,1,2048]{3,2,1,0:T(1,128)S(1)}, u32[]{:S(2)}, u32[]{:S(2)}) collective-permute-start(f32[2,4,1,2048]{3,2,1,0:T(1,128)} %slice.276), channel_id=1, source_target_pairs={{0,1},{1,2},{2,3},{3,4},{4,5},{5,6},{6,7},{7,8},{8,9},{9,10},{10,1... | collective-permute-start | bytes 196616 | tf_op jit(solution)/shard_map/ppermute | solution.py:15
  45.1 2.1 %collective-permute-start.3 = (f32[2,1,4,2048]{3,2,1,0:T(4,128)S(1)}, f32[2,1,4,2048]{3,2,1,0:T(4,128)}, u32[]{:S(2)}, u32[]{:S(2)}) collective-permute-start(f32[2,1,4,2048]{3,2,1,0:T(4,128)S(1)} %slice.283), channel_id=1, source_target_pairs={{0,32},{32,64},{64,96},{96,128},{128,160},{160,192},{192,224},{224... | collective-permute-start | bytes 196616 | tf_op jit(solution)/shard_map/ppermute | solution.py:15
  47.2 0.6 fusion.31
  47.8 0.7 copy.43
  48.5 1.6 %reshape_squeeze.15 = f32[256,128]{1,0:T(8,128)} reshape(f32[1,4,4,2048]{3,2,1,0:T(4,128)} %get-tuple-element.68) | data formatting | bytes 262144 | tf_op jit(solution)/shard_map/reshape;squeeze | solution.py:155
  50.1 4.5 %all-to-all-done = f32[32,1,128]{2,1,0:T(1,128)} async-done(((f32[32,1,128]{2,1,0:T(1,128)}), f32[32,1,128]{2,1,0:T(1,128)}, u32[]{:S(2)}, u32[]{:S(2)}) %all-to-all-start) | async-done | bytes 16416 | tf_op jit(solution)/shard_map/all_to_all | solution.py:113
  54.6 0.5 broadcast.230
  55.1 1.4 %reduce.24 = f32[32,128]{1,0:T(8,128)S(1)} reduce(f32[32,1,128]{2,1,0:T(1,128)} %all-to-all-done, f32[]{:T(128)} %broadcast.230), dimensions={1}, to_apply=%all_to_all.9.reduce_sub_computation | reduce | bytes 32772 | tf_op jit(solution)/shard_map/all_to_all | solution.py:113
  56.5 0.7 reshape.274
  57.2 0.9 slice_bitcast_fusion.5
  58.2 1.0 fusion.82
  59.2 1.2 fusion.56
  60.4 0.9 convert_reduce_fusion.2
  61.3 0.6 compare_convert_fusion
  61.9 0.6 add_select_fusion.1
  62.9 2.4 %fusion.21 = f32[1024]{0:T(1024)S(1)} fusion(f32[256,128]{1,0:T(8,128)} %reshape_squeeze.15, f32[1024]{0:T(1024)} %compare_convert_fusion, s32[1024]{0:T(1024)} %get-tuple-element.80, s32[1024]{0:T(1024)} %get-tuple-element.79), kind=kOutput, calls=%fused_computation.23 | convolution fusion | flops 403569664 | bytes 147456 | tf_op jit(solution)/shard_map/dot_general | solution.py:155
  65.3 0.7 stack.65
  66.0 3.5 %fusion.24 = f32[256,128]{1,0:T(8,128)} fusion(f32[1024]{0:T(1024)} %compare_convert_fusion, s32[1024]{0:T(1024)} %get-tuple-element.80, f32[1024]{0:T(1024)S(1)} %multiply_add_fusion.3, s32[1024]{0:T(1024)} %get-tuple-element.79), kind=kOutput, calls=%fused_computation.24 | convolution fusion | flops 403472384 | bytes 147456 | tf_op jit(solution)/shard_map/kr,kl->rl/dot_general | solution.py:160
  69.5 0.9 mul.208
  70.5 0.7 copy-done.4
  71.2 1.1 divide_add_fusion.1
  72.3 0.7 slice.339
  73.0 1.6 %reshape_squeeze.19 = f32[256,128]{1,0:T(8,128)} reshape(f32[1,4,4,2048]{3,2,1,0:T(4,128)} %slice.339) | data formatting | bytes 262144 | tf_op jit(solution)/shard_map/reshape;squeeze | solution.py:155
  74.6 3.0 %fusion.18 = f32[1024]{0:T(1024)} fusion(f32[256,128]{1,0:T(8,128)} %reshape_squeeze.19, f32[1024]{0:T(1024)} %compare_convert_fusion, s32[1024]{0:T(1024)} %get-tuple-element.80, s32[1024]{0:T(1024)} %get-tuple-element.79), kind=kOutput, calls=%fused_computation.22 | convolution fusion | flops 403569664 | bytes 147456 | tf_op jit(solution)/shard_map/dot_general | solution.py:155
  77.6 1.4 %stack.66 = f32[1,32,32]{2,0,1:T(1,128)} reshape(f32[1024]{0:T(1024)} %fusion.18) | data formatting | bytes 8192 | tf_op jit(solution)/shard_map/stack | solution.py:168
  78.9 1.4 %maximum_bitcast_fusion = f32[32,2,32]{2,1,0:T(2,128)} fusion(f32[1,32,32]{2,0,1:T(1,128)} %stack.66, f32[1,32,32]{2,0,1:T(1,128)} %stack.65), kind=kLoop, calls=%fused_computation.172 | loop fusion | flops 2048 | bytes 16384 | tf_op jit(solution)/shard_map/transpose | solution.py:168
  80.3 9.1 %all-to-all-start.1 = ((f32[32,2,32]{2,1,0:T(2,128)}), f32[32,2,32]{2,1,0:T(2,128)}, u32[]{:S(2)}, u32[]{:S(2)}) async-start(f32[32,2,32]{2,1,0:T(2,128)} %maximum_bitcast_fusion), calls=%async_computation.1 | async-start | bytes 65536 | tf_op jit(solution)/shard_map/all_to_all | solution.py:113
  89.4 2.7 %subtract_reduce_fusion = (f32[3,4,4,2048]{3,2,1,0:T(4,128)}, f32[4,3,4,4,2048]{4,3,2,1,0:T(4,128)}) fusion(f32[4,3,4,4,2048]{4,3,2,1,0:T(4,128)S(1)} %get-tuple-element.46, f32[3,4,4,2048]{3,2,1,0:T(4,128)S(1)} %bitcast.220, f32[4,4,4,2048]{3,2,1,0:T(4,128)S(1)} %copy-done.3, f32[4,4,4,2048]{3,2,1,0:T(4,128)S(1)} %copy.31), kind=kLoop, calls=%fused_computation.16 | loop fusion | flops 1867776 | bytes 4980736 | tf_op jit(solution)/shard_map/reduce_sum | solution.py:63
  92.4 1.3 collective-permute-start.5
  93.7 5.4 %collective-permute-start.4 = (f32[2,1,4,2048]{3,2,1,0:T(4,128)S(1)}, f32[2,1,4,2048]{3,2,1,0:T(4,128)S(1)}, u32[]{:S(2)}, u32[]{:S(2)}) collective-permute-start(f32[2,1,4,2048]{3,2,1,0:T(4,128)S(1)} %slice.301), channel_id=1, source_target_pairs={{32,0},{64,32},{96,64},{128,96},{160,128},{192,160},{224,192},{256... | collective-permute-start | bytes 196616 | tf_op jit(solution)/shard_map/ppermute | solution.py:15
  99.1 3.7 %all-to-all-done.1 = f32[32,2,32]{2,1,0:T(2,128)} async-done(((f32[32,2,32]{2,1,0:T(2,128)}), f32[32,2,32]{2,1,0:T(2,128)}, u32[]{:S(2)}, u32[]{:S(2)}) %all-to-all-start.1) | async-done | bytes 8224 | tf_op jit(solution)/shard_map/all_to_all | solution.py:113
  102.8 0.8 copy.33
  103.6 1.4 %fusion.2 = f32[2,512]{1,0:T(2,128)S(1)} fusion(f32[2,1024]{1,0:T(2,128)S(1)} %reshape.232, s32[512]{0:T(512)} %copy-done.22), kind=kOutput, calls=%fused_computation.6 | convolution fusion | flops 13107200 | bytes 14336 | tf_op jit(solution)/shard_map/ft,ts->fs/dot_general | solution.py:117
  105.4 0.7 fusion.155
  106.1 1.0 fusion.1
  107.1 0.7 transpose_reshape.3
  107.8 10.5 %all-to-all-start.2 = ((f32[32,1,32]{2,1,0:T(1,128)}), f32[32,1,32]{2,1,0:T(1,128)S(1)}, u32[]{:S(2)}, u32[]{:S(2)}) async-start(f32[32,1,32]{2,1,0:T(1,128)} %transpose_reshape.3), calls=%async_computation.2 | async-start | bytes 32768 | tf_op jit(solution)/shard_map/all_to_all | solution.py:113
  119.1 1.9 %collective-permute-start.7 = (f32[2,1,4,2048]{3,2,1,0:T(4,128)S(1)}, f32[2,1,4,2048]{3,2,1,0:T(4,128)S(1)}, u32[]{:S(2)}, u32[]{:S(2)}) collective-permute-start(f32[2,1,4,2048]{3,2,1,0:T(4,128)S(1)} %pad_maximum_fusion.10), channel_id=1, source_target_pairs={{0,32},{32,64},{64,96},{96,128},{128,160},{160,192},{192,224},{224... | collective-permute-start | bytes 196616 | tf_op jit(solution)/shard_map/ppermute | solution.py:15
  121.2 3.9 %collective-permute-start.6 = (f32[2,4,1,2048]{3,2,1,0:T(1,128)S(1)}, f32[2,4,1,2048]{3,2,1,0:T(1,128)S(1)}, u32[]{:S(2)}, u32[]{:S(2)}) collective-permute-start(f32[2,4,1,2048]{3,2,1,0:T(1,128)S(1)} %slice.315), channel_id=1, source_target_pairs={{0,1},{1,2},{2,3},{3,4},{4,5},{5,6},{6,7},{7,8},{8,9},{9,10},{10,1... | collective-permute-start | bytes 196616 | tf_op jit(solution)/shard_map/ppermute | solution.py:15
  125.1 3.1 %collective-permute-done.7 = f32[2,1,4,2048]{3,2,1,0:T(4,128)S(1)} collective-permute-done((f32[2,1,4,2048]{3,2,1,0:T(4,128)S(1)}, f32[2,1,4,2048]{3,2,1,0:T(4,128)S(1)}, u32[]{:S(2)}, u32[]{:S(2)}) %collective-permute-start.7) | collective-permute-done | bytes 65568 | tf_op jit(solution)/shard_map/ppermute | solution.py:15
  129.6 2.1 %all-to-all-done.2 = f32[32,1,32]{2,1,0:T(1,128)S(1)} async-done(((f32[32,1,32]{2,1,0:T(1,128)}), f32[32,1,32]{2,1,0:T(1,128)S(1)}, u32[]{:S(2)}, u32[]{:S(2)}) %all-to-all-start.2) | async-done | bytes 4128 | tf_op jit(solution)/shard_map/all_to_all | solution.py:113
  131.7 0.5 broadcast.228
  132.2 0.7 reduce.23
  133.0 2.1 %fusion.27 = f32[256,128]{1,0:T(8,128)S(1)} fusion(f32[1024]{0:T(1024)S(1)} %copy-done.26, s32[1024]{0:T(1024)S(1)} %copy-done.25, f32[1024]{0:T(1024)S(1)} %broadcast_in_dim.23, s32[1024]{0:T(1024)S(1)} %copy-done.24), kind=kOutput, calls=%fused_computation.25 | convolution fusion | flops 403472384 | bytes 147456 | tf_op jit(solution)/shard_map/kr,kl->rl/dot_general | solution.py:160
  135.2 0.8 divide_add_fusion
  (119 shorter events, 5.1 us)
Async XLA Ops:
  0.6 10.6 %copy-start = (f32[4,8]{1,0:T(4,128)S(1)}, f32[4,8]{1,0:T(4,128)}, u32[]{:S(2)}) copy-start(f32[4,8]{1,0:T(4,128)} %param.27) | copy-start | bytes 388
  0.6 12.4 %copy-start.11 = (s32[4,4,2048]{2,1,0:T(4,128)S(1)}, s32[4,4,2048]{2,1,0:T(4,128)}, u32[]{:S(2)}) copy-start(s32[4,4,2048]{2,1,0:T(4,128)} %param.23) | copy-start | bytes 393220
  0.7 12.4 %copy-start.27 = (f32[4,8]{1,0:T(4,128)S(1)}, f32[4,8]{1,0:T(4,128)}, u32[]{:S(2)}) copy-start(f32[4,8]{1,0:T(4,128)} %param.26) | copy-start | bytes 388
  1.7 17.0 %collective-permute-start = (f32[2,4,1,2048]{3,2,1,0:T(1,128)S(1)}, f32[2,4,1,2048]{3,2,1,0:T(1,128)S(1)}, u32[]{:S(2)}, u32[]{:S(2)}) collective-permute-start(f32[2,4,1,2048]{3,2,1,0:T(1,128)S(1)} %slice.261), channel_id=1, source_target_pairs={{1,0},{2,1},{3,2},{4,3},{5,4},{6,5},{7,6},{8,7},{9,8},{10,9},{11,1... | collective-permute-start | bytes 196616 | tf_op jit(solution)/shard_map/ppermute | solution.py:15
  3.9 14.8 %collective-permute-start.1 = (f32[2,1,4,2048]{3,2,1,0:T(4,128)S(1)}, f32[2,1,4,2048]{3,2,1,0:T(4,128)S(1)}, u32[]{:S(2)}, u32[]{:S(2)}) collective-permute-start(f32[2,1,4,2048]{3,2,1,0:T(4,128)S(1)} %slice.270), channel_id=1, source_target_pairs={{32,0},{64,32},{96,64},{128,96},{160,128},{192,160},{224,192},{256... | collective-permute-start | bytes 196616 | tf_op jit(solution)/shard_map/ppermute | solution.py:15
  9.4 8.0 %copy-start.22 = (s32[512]{0:T(512)}, s32[512]{0:T(512)S(1)}, u32[]{:S(2)}) copy-start(s32[512]{0:T(512)S(1)} %multiply_add_fusion.6) | copy-start | bytes 6148
  10.2 5.2 %copy-start.15 = (f32[1,511]{1,0:T(1,128)}, f32[1,511]{1,0:T(1,128)S(1)}, u32[]{:S(2)}) copy-start(f32[1,511]{1,0:T(1,128)S(1)} %slice.258) | copy-start | bytes 6136
  12.7 1.4 %copy-start.29 = (f32[8]{0:T(128)S(1)}, f32[8]{0:T(128)}, u32[]{:S(2)}) copy-start(f32[8]{0:T(128)} %param.25) | copy-start | bytes 100
  13.1 2.3 %copy-start.13 = (f32[1,512]{1,0:T(1,128)S(1)}, f32[1,512]{1,0:T(1,128)}, u32[]{:S(2)}) copy-start(f32[1,512]{1,0:T(1,128)} %param.31) | copy-start | bytes 6148
  13.1 2.4 %copy-start.1 = (f32[3,4,4,2048]{3,2,1,0:T(4,128)S(1)}, f32[3,4,4,2048]{3,2,1,0:T(4,128)}, u32[]{:S(2)}) copy-start(f32[3,4,4,2048]{3,2,1,0:T(4,128)} %param.20) | copy-start | bytes 1179652
  13.1 2.4 %copy-start.5 = (f32[4,3,4,4,2048]{4,3,2,1,0:T(4,128)S(1)}, f32[4,3,4,4,2048]{4,3,2,1,0:T(4,128)}, u32[]{:S(2)}) copy-start(f32[4,3,4,4,2048]{4,3,2,1,0:T(4,128)} %param.22) | copy-start | bytes 4718596
  14.1 3.3 %copy-start.2 = (f32[4,4,4,2048]{3,2,1,0:T(4,128)}, f32[4,4,4,2048]{3,2,1,0:T(4,128)S(1)}, u32[]{:S(2)}) copy-start(f32[4,4,4,2048]{3,2,1,0:T(4,128)S(1)} %copy.32) | copy-start | bytes 1572868
  15.5 1.9 %copy-start.19 = (f32[1,512]{1,0:T(1,128)}, f32[1,512]{1,0:T(1,128)S(1)}, u32[]{:S(2)}) copy-start(f32[1,512]{1,0:T(1,128)S(1)} %fusion.139) | copy-start | bytes 6148
  15.5 1.9 %copy-start.14 = (f32[1,512]{1,0:T(1,128)S(1)}, f32[1,512]{1,0:T(1,128)}, u32[]{:S(2)}) copy-start(f32[1,512]{1,0:T(1,128)} %param.32) | copy-start | bytes 6148
  15.5 1.9 %copy-start.17 = (f32[1,512]{1,0:T(1,128)S(1)}, f32[1,512]{1,0:T(1,128)}, u32[]{:S(2)}) copy-start(f32[1,512]{1,0:T(1,128)} %param.30) | copy-start | bytes 6148
  15.5 1.9 %copy-start.31 = (f32[4]{0:T(128)S(1)}, f32[4]{0:T(128)}, u32[]{:S(2)}) copy-start(f32[4]{0:T(128)} %constant.108.clone) | copy-start | bytes 52
  20.6 26.6 %copy-start.30 = (f32[8]{0:T(128)S(1)}, f32[8]{0:T(128)}, u32[]{:S(2)}) copy-start(f32[8]{0:T(128)} %param.24) | copy-start | bytes 100
  23.4 31.2 %all-to-all-start = ((f32[32,1,128]{2,1,0:T(1,128)}), f32[32,1,128]{2,1,0:T(1,128)}, u32[]{:S(2)}, u32[]{:S(2)}) async-start(f32[32,1,128]{2,1,0:T(1,128)} %reshape.273), calls=%async_computation | async-start | bytes 32768 | tf_op jit(solution)/shard_map/all_to_all | solution.py:113
  41.5 15.8 %collective-permute-start.2 = (f32[2,4,1,2048]{3,2,1,0:T(1,128)}, f32[2,4,1,2048]{3,2,1,0:T(1,128)S(1)}, u32[]{:S(2)}, u32[]{:S(2)}) collective-permute-start(f32[2,4,1,2048]{3,2,1,0:T(1,128)} %slice.276), channel_id=1, source_target_pairs={{0,1},{1,2},{2,3},{3,4},{4,5},{5,6},{6,7},{7,8},{8,9},{9,10},{10,1... | collective-permute-start | bytes 196616 | tf_op jit(solution)/shard_map/ppermute | solution.py:15
  45.1 12.1 %collective-permute-start.3 = (f32[2,1,4,2048]{3,2,1,0:T(4,128)S(1)}, f32[2,1,4,2048]{3,2,1,0:T(4,128)}, u32[]{:S(2)}, u32[]{:S(2)}) collective-permute-start(f32[2,1,4,2048]{3,2,1,0:T(4,128)S(1)} %slice.283), channel_id=1, source_target_pairs={{0,32},{32,64},{64,96},{96,128},{128,160},{160,192},{192,224},{224... | collective-permute-start | bytes 196616 | tf_op jit(solution)/shard_map/ppermute | solution.py:15
  57.2 1.9 %copy-start.7 = (f32[3,4,4,2048]{3,2,1,0:T(4,128)S(1)}, f32[3,4,4,2048]{3,2,1,0:T(4,128)}, u32[]{:S(2)}) copy-start(f32[3,4,4,2048]{3,2,1,0:T(4,128)} %get-tuple-element.59) | copy-start | bytes 1179652
  59.2 3.4 %copy-start.12 = (f32[32,4,32]{2,1,0:T(4,128)S(1)}, f32[32,4,32]{2,1,0:T(4,128)}, u32[]{:S(2)}) copy-start(f32[32,4,32]{2,1,0:T(4,128)} %reshape.274) | copy-start | bytes 49156
  62.9 8.3 %copy-start.9 = (f32[1,4,4,2048]{3,2,1,0:T(4,128)S(1)}, f32[1,4,4,2048]{3,2,1,0:T(4,128)}, u32[]{:S(2)}) copy-start(f32[1,4,4,2048]{3,2,1,0:T(4,128)} %copy.43) | copy-start | bytes 393220
  70.5 0.7 copy-start.4
  72.3 17.1 %copy-start.3 = (f32[4,4,4,2048]{3,2,1,0:T(4,128)S(1)}, f32[4,4,4,2048]{3,2,1,0:T(4,128)}, u32[]{:S(2)}) copy-start(f32[4,4,4,2048]{3,2,1,0:T(4,128)} %copy-done.2) | copy-start | bytes 1572868
  80.3 22.5 %all-to-all-start.1 = ((f32[32,2,32]{2,1,0:T(2,128)}), f32[32,2,32]{2,1,0:T(2,128)}, u32[]{:S(2)}, u32[]{:S(2)}) async-start(f32[32,2,32]{2,1,0:T(2,128)} %maximum_bitcast_fusion), calls=%async_computation.1 | async-start | bytes 65536 | tf_op jit(solution)/shard_map/all_to_all | solution.py:113
  92.2 12.9 %copy-start.16 = (f32[1,511]{1,0:T(1,128)S(1)}, f32[1,511]{1,0:T(1,128)}, u32[]{:S(2)}) copy-start(f32[1,511]{1,0:T(1,128)} %copy-done.15) | copy-start | bytes 6136
  92.2 12.9 %copy-start.18 = (f32[1,512]{1,0:T(1,128)S(1)}, f32[1,512]{1,0:T(1,128)}, u32[]{:S(2)}) copy-start(f32[1,512]{1,0:T(1,128)} %param.30) | copy-start | bytes 6148
  92.2 13.0 %copy-start.20 = (f32[1,512]{1,0:T(1,128)S(1)}, f32[1,512]{1,0:T(1,128)}, u32[]{:S(2)}) copy-start(f32[1,512]{1,0:T(1,128)} %copy-done.19) | copy-start | bytes 6148
  92.2 13.0 %copy-start.21 = (f32[1,512]{1,0:T(1,128)S(1)}, f32[1,512]{1,0:T(1,128)}, u32[]{:S(2)}) copy-start(f32[1,512]{1,0:T(1,128)} %param.33) | copy-start | bytes 6148
  92.2 13.9 %copy-start.23 = (s32[512]{0:T(512)S(1)}, s32[512]{0:T(512)}, u32[]{:S(2)}) copy-start(s32[512]{0:T(512)} %copy-done.22) | copy-start | bytes 6148
  92.4 26.0 %collective-permute-start.5 = (f32[2,4,1,2048]{3,2,1,0:T(1,128)S(1)}, f32[2,4,1,2048]{3,2,1,0:T(1,128)S(1)}, u32[]{:S(2)}, u32[]{:S(2)}) collective-permute-start(f32[2,4,1,2048]{3,2,1,0:T(1,128)S(1)} %slice.305), channel_id=1, source_target_pairs={{1,0},{2,1},{3,2},{4,3},{5,4},{6,5},{7,6},{8,7},{9,8},{10,9},{11,1... | collective-permute-start | bytes 196616 | tf_op jit(solution)/shard_map/ppermute | solution.py:15
  93.7 24.7 %collective-permute-start.4 = (f32[2,1,4,2048]{3,2,1,0:T(4,128)S(1)}, f32[2,1,4,2048]{3,2,1,0:T(4,128)S(1)}, u32[]{:S(2)}, u32[]{:S(2)}) collective-permute-start(f32[2,1,4,2048]{3,2,1,0:T(4,128)S(1)} %slice.301), channel_id=1, source_target_pairs={{32,0},{64,32},{96,64},{128,96},{160,128},{192,160},{224,192},{256... | collective-permute-start | bytes 196616 | tf_op jit(solution)/shard_map/ppermute | solution.py:15
  106.1 12.9 %copy-start.28 = (f32[1,512]{1,0:T(1,128)}, f32[1,512]{1,0:T(1,128)S(1)}, u32[]{:S(2)}) copy-start(f32[1,512]{1,0:T(1,128)S(1)} %get-tuple-element.53) | copy-start | bytes 6148
  107.8 23.9 %all-to-all-start.2 = ((f32[32,1,32]{2,1,0:T(1,128)}), f32[32,1,32]{2,1,0:T(1,128)S(1)}, u32[]{:S(2)}, u32[]{:S(2)}) async-start(f32[32,1,32]{2,1,0:T(1,128)} %transpose_reshape.3), calls=%async_computation.2 | async-start | bytes 32768 | tf_op jit(solution)/shard_map/all_to_all | solution.py:113
  119.1 9.2 %collective-permute-start.7 = (f32[2,1,4,2048]{3,2,1,0:T(4,128)S(1)}, f32[2,1,4,2048]{3,2,1,0:T(4,128)S(1)}, u32[]{:S(2)}, u32[]{:S(2)}) collective-permute-start(f32[2,1,4,2048]{3,2,1,0:T(4,128)S(1)} %pad_maximum_fusion.10), channel_id=1, source_target_pairs={{0,32},{32,64},{64,96},{96,128},{128,160},{160,192},{192,224},{224... | collective-permute-start | bytes 196616 | tf_op jit(solution)/shard_map/ppermute | solution.py:15
  121.1 7.6 %copy-start.8 = (f32[3,4,4,2048]{3,2,1,0:T(4,128)}, f32[3,4,4,2048]{3,2,1,0:T(4,128)S(1)}, u32[]{:S(2)}) copy-start(f32[3,4,4,2048]{3,2,1,0:T(4,128)S(1)} %pad_maximum_fusion.1) | copy-start | bytes 1179652
  121.2 7.1 %collective-permute-start.6 = (f32[2,4,1,2048]{3,2,1,0:T(1,128)S(1)}, f32[2,4,1,2048]{3,2,1,0:T(1,128)S(1)}, u32[]{:S(2)}, u32[]{:S(2)}) collective-permute-start(f32[2,4,1,2048]{3,2,1,0:T(1,128)S(1)} %slice.315), channel_id=1, source_target_pairs={{0,1},{1,2},{2,3},{3,4},{4,5},{5,6},{6,7},{7,8},{8,9},{9,10},{10,1... | collective-permute-start | bytes 196616 | tf_op jit(solution)/shard_map/ppermute | solution.py:15
  128.3 1.0 copy-start.6
  128.3 1.0 copy-start.10
  128.7 4.3 %copy-start.24 = (s32[1024]{0:T(1024)S(1)}, s32[1024]{0:T(1024)}, u32[]{:S(2)}) copy-start(s32[1024]{0:T(1024)} %get-tuple-element.79) | copy-start | bytes 12292
  128.7 4.3 %copy-start.25 = (s32[1024]{0:T(1024)S(1)}, s32[1024]{0:T(1024)}, u32[]{:S(2)}) copy-start(s32[1024]{0:T(1024)} %get-tuple-element.80) | copy-start | bytes 12292
  128.7 4.3 %copy-start.26 = (f32[1024]{0:T(1024)S(1)}, f32[1024]{0:T(1024)}, u32[]{:S(2)}) copy-start(f32[1024]{0:T(1024)} %compare_convert_fusion) | copy-start | bytes 12292

commit v10 on v9

--- a/solution.py
+++ b/solution.py
@@ -140,24 +140,23 @@
 
     recv_cells = incoming[:, 0, :].astype(jnp.int32)
     is_valid = recv_cells >= 0
-    safe_cells = jnp.where(is_valid, recv_cells, 0).reshape(-1)
-    recv_curr = incoming[:, 1, :].reshape(-1)
-    recv_gain = incoming[:, 2, :].reshape(-1)
-    recv_drop = incoming[:, 3, :].reshape(-1)
-    valid_flat = is_valid.reshape(-1)
+    safe_cells = jnp.where(is_valid, recv_cells, 0)
+    recv_curr = incoming[:, 1, :]
+    recv_gain = incoming[:, 2, :]
+    recv_drop = incoming[:, 3, :]
     lanes = 128
     plane_rows = cell_total // lanes
-    row_hot = ((safe_cells // lanes)[:, None] == jnp.arange(plane_rows, dtype=jnp.int32)[None, :]).astype(jnp.float32)
-    row_hot = row_hot * valid_flat.astype(jnp.float32)[:, None]
-    lane_hot = (safe_cells % lanes)[:, None] == jnp.arange(lanes, dtype=jnp.int32)[None, :]
+    row_hot = ((safe_cells // lanes)[:, :, None] == jnp.arange(plane_rows, dtype=jnp.int32)).astype(jnp.float32)
+    row_hot = row_hot * is_valid.astype(jnp.float32)[:, :, None]
+    lane_hot = (safe_cells % lanes)[:, :, None] == jnp.arange(lanes, dtype=jnp.int32)
 
     def sample(e_now):
-        picked = jnp.dot(row_hot, e_now[2].reshape(plane_rows, lanes), precision=highest)
-        return jnp.sum(jnp.where(lane_hot, picked, 0.0), axis=1)
+        picked = jnp.einsum("scr,rl->scl", row_hot, e_now[2].reshape(plane_rows, lanes), precision=highest)
+        return jnp.sum(jnp.where(lane_hot, picked, 0.0), axis=2)
 
     def wire_of(values):
-        spread = jnp.where(lane_hot, values[:, None], 0.0)
-        return jnp.einsum("kr,kl->rl", row_hot, spread, precision=highest).reshape(grid_shape)
+        spread = jnp.where(lane_hot, values[:, :, None], 0.0)
+        return jnp.einsum("scr,scl->rl", row_hot, spread, precision=highest).reshape(grid_shape)
 
     sample_0 = sample(e_field)
     curr_cell_1 = recv_curr + recv_gain * (sample_0 - recv_drop)
@@ -165,7 +164,7 @@
     polarization = polar_next
     sample_1 = sample(e_field)
 
-    back = jnp.stack([sample_0, sample_1]).reshape(2, n_gy, capacity).transpose(1, 0, 2)
+    back = jnp.stack([sample_0, sample_1], axis=1)
     back, e_field, h_field, polarization = lax.optimization_barrier((back, e_field, h_field, polarization))
     returned = from_slots(exchange(back))
     seg_sample_0, seg_sample_1 = returned[0], returned[1]
@@ -181,7 +180,7 @@
 
     drive, polarization = electric_base(e_field, h_field, polarization, cells)
     recv_curr_2, drive = lax.optimization_barrier((recv_curr_2, drive))
-    e_field = electric_finish(e_field, drive, wire_of(recv_curr_2.transpose(1, 0, 2).reshape(-1)), cells)
+    e_field = electric_finish(e_field, drive, wire_of(recv_curr_2[:, 0, :]), cells)
     return (e_field, h_field, polarization, curr_2[None], volt_2[None])
 
 

time: 137 us -> 131 us (0.956)
  local copies, waits for them, and re-layouts: 18.6 us -> 14.3 us
  waiting for transfers between devices: 13.4 us -> 15.9 us
  starting transfers between devices: 61.1 us -> 58.8 us
  other arithmetic: 23.9 us -> 22.2 us
    another operation x2, local copies, waits for them, and re-layouts: 3.24 us -> 0.79 us  [sample(): e_now[2].reshape(plane_rows, lanes)]
    another operation x5 -> x0, local copies, waits for them, and re-layouts: 2.27 us -> none  [the longest x2 2.06 us: on_device(): jnp.stack([sample_0, sample_1]).reshape(2, n_gy, capacity)]
    ppermute x8, starting transfers between devices: 23.4 us -> 21.2 us  [passed_along(): lax.ppermute(value, axis, [(source, source + steps) for source in range(f...]
    all_to_all x3, waiting for transfers between devices: 10.3 us -> 12.5 us  [exchange(): return lax.all_to_all(blocks, 'gy', split_axis=0, concat_axis=0, tiled=True)]
    convert_element_type x2 -> x1, other arithmetic: 1.49 us -> 0.01 us  [on_device(): row_hot = row_hot * is_valid.astype(jnp.float32)[:, :, None]]
    select_n x0 -> x2, other arithmetic: none -> 1.39 us  [wire_of(): spread = jnp.where(lane_hot, values[:, :, None], 0.0)]
    transpose x1 -> x0, other arithmetic: 1.39 us -> none  [on_device(): jnp.stack([sample_0, sample_1]).reshape(2, n_gy, capacity)]
  transfers between devices with their start and end apart: 11 -> 11, of which waited for: 4 -> 4; matrix products, arithmetic and copies ran while one was open for 20% -> 18% of each run, Pallas kernels for 0% -> 0%
where the time goes in v10:
time: 131 us; the launch traced here: 129 us
  starting transfers between devices  58.8 us (45%)
  other arithmetic  22.2 us (17%)
  matrix products  16.6 us (13%)
  waiting for transfers between devices  15.9 us (12%)
  local copies, waits for them, and re-layouts  14.3 us (11%)
  between operations  1.52 us (1%)
    all_to_all x3, starting transfers between devices, exchange(): return lax.all_to_all(blocks, 'gy', split_axis=0, concat_axis=0, tiled=True)  37.6 us
    ppermute x8, starting transfers between devices, passed_along(): lax.ppermute(value, axis, [(source, source + steps) for source in range(f...  21.2 us
    all_to_all x3, waiting for transfers between devices, exchange(): return lax.all_to_all(blocks, 'gy', split_axis=0, concat_axis=0, tiled=True)  12.5 us
    dot_general x2, matrix products, wire_of(): jnp.einsum('scr,scl->rl', row_hot, spread, precision=highest)  5.25 us
    dot_general x2, matrix products, sample(): jnp.einsum('scr,rl->scl', row_hot, e_now[2].reshape(plane_rows, lanes), p...  4.72 us
    reduce_sum x1, other arithmetic, electric_base(): change = jnp.sum(polar_new - polarization, axis=0)  3.49 us
    ppermute x8, waiting for transfers between devices, passed_along(): lax.ppermute(value, axis, [(source, source + steps) for source in range(f...  3.44 us
    unnamed x65, local copies, waits for them, and re-layouts  2.68 us
  transfers between devices with their start and end apart: 11, of which 4 were waited for; matrix products, arithmetic and copies ran while one was open for 18% of the time, Pallas kernels for 0%

profile of v10, /device:TPU:16, one launch (start us, length us, event | category | flops | bytes accessed | tf_op | source)
XLA Modules:
  0.0 129.3 jit_solution(11882225423377924342)
XLA Ops:
  0.7 1.0 slice.261
  1.7 1.3 collective-permute-start
  3.0 0.8 slice.270
  3.9 3.9 %collective-permute-start.1 = (f32[2,1,4,2048]{3,2,1,0:T(4,128)S(1)}, f32[2,1,4,2048]{3,2,1,0:T(4,128)S(1)}, u32[]{:S(2)}, u32[]{:S(2)}) collective-permute-start(f32[2,1,4,2048]{3,2,1,0:T(4,128)S(1)} %slice.270), channel_id=1, source_target_pairs={{32,0},{64,32},{96,64},{128,96},{160,128},{192,160},{224,192},{256... | collective-permute-start | bytes 196616 | tf_op jit(solution)/shard_map/ppermute | solution.py:15
  7.7 1.0 convert_reduce_fusion.1
  8.7 0.7 multiply_add_fusion.5
  9.4 0.8 slice.258
  10.2 0.7 convert_element_type.35
  11.2 1.5 %convolution_bitcast_fusion.1 = f32[4,4,4,2048]{3,0,2,1:T(4,128)S(1)} fusion(s32[4,4,2048]{2,1,0:T(4,128)} %param.23, f32[4,8]{1,0:T(4,128)S(1)} %copy-done), kind=kOutput, calls=%fused_computation.2 | convolution fusion | flops 12845056 | bytes 655488 | tf_op jit(solution)/shard_map/pm,mxyz->pxyz/dot_general | solution.py:135
  12.7 0.3 copy.55
  13.1 0.6 fusion
  13.7 0.3 copy.56
  14.1 0.6 fusion.10
  14.9 2.0 %multiply_add_fusion.1 = (f32[4,3,4,4,2048]{4,3,2,1,0:T(4,128)}, f32[3,4,4,2048]{3,2,1,0:T(4,128)S(1)}) fusion(f32[4,3,4,4,2048]{4,3,2,1,0:T(4,128)S(1)} %copy-done.3, f32[3,4,4,2048]{3,2,1,0:T(4,128)S(1)} %copy-done.1, f32[4,4,4,2048]{3,2,1,0:T(4,128)S(1)} %copy.56, f32[4,4,4,2048]{3,2,1,0:T(4,128)S(1)} %copy.55), kind=kLoop, calls=%fused_computation.11 | loop fusion | flops 1867776 | bytes 4980736 | tf_op jit(solution)/shard_map/add | solution.py:60
  16.9 1.0 fusion.8
  18.2 1.1 fusion.138
  19.6 1.2 fusion.69
  20.9 0.7 slice.276
  21.6 0.7 reshape.239
  22.3 17.9 %all-to-all-start = ((f32[32,1,128]{2,1,0:T(1,128)}), f32[32,1,128]{2,1,0:T(1,128)S(1)}, u32[]{:S(2)}, u32[]{:S(2)}) async-start(f32[32,1,128]{2,1,0:T(1,128)} %reshape.239), calls=%async_computation | async-start | bytes 32768 | tf_op jit(solution)/shard_map/all_to_all | solution.py:113
  40.2 3.7 %collective-permute-start.2 = (f32[2,4,1,2048]{3,2,1,0:T(1,128)}, f32[2,4,1,2048]{3,2,1,0:T(1,128)S(1)}, u32[]{:S(2)}, u32[]{:S(2)}) collective-permute-start(f32[2,4,1,2048]{3,2,1,0:T(1,128)} %slice.276), channel_id=1, source_target_pairs={{0,1},{1,2},{2,3},{3,4},{4,5},{5,6},{6,7},{7,8},{8,9},{9,10},{10,1... | collective-permute-start | bytes 196616 | tf_op jit(solution)/shard_map/ppermute | solution.py:15
  43.9 2.1 %collective-permute-start.3 = (f32[2,1,4,2048]{3,2,1,0:T(4,128)S(1)}, f32[2,1,4,2048]{3,2,1,0:T(4,128)S(1)}, u32[]{:S(2)}, u32[]{:S(2)}) collective-permute-start(f32[2,1,4,2048]{3,2,1,0:T(4,128)S(1)} %slice.283), channel_id=1, source_target_pairs={{0,32},{32,64},{64,96},{96,128},{128,160},{160,192},{192,224},{224... | collective-permute-start | bytes 196616 | tf_op jit(solution)/shard_map/ppermute | solution.py:15
  46.0 1.2 fusion.9
  47.3 0.7 reshape.229
  48.1 5.2 %all-to-all-done = f32[32,1,128]{2,1,0:T(1,128)S(1)} async-done(((f32[32,1,128]{2,1,0:T(1,128)}), f32[32,1,128]{2,1,0:T(1,128)S(1)}, u32[]{:S(2)}, u32[]{:S(2)}) %all-to-all-start) | async-done | bytes 16416 | tf_op jit(solution)/shard_map/all_to_all | solution.py:113
  53.3 0.5 broadcast.204
  53.8 0.6 reduce.4
  54.7 0.5 copy-done.8
  55.2 1.0 fusion.55
  56.4 0.6 copy.60
  57.0 0.6 fusion.139
  57.6 0.6 add_select_fusion.1
  58.3 0.7 copy.58
  58.9 0.7 copy.57
  59.6 1.1 fusion.15
  60.8 2.5 %fusion.4 = f32[32,32]{1,0:T(8,128)S(1)} fusion(f32[256,128,1]{1,0,2:T(8,128)} %reshape.229, f32[32,32,256]{2,0,1:T(8,128)S(1)} %fusion.15, s32[32,32]{1,0:T(8,128)} %get-tuple-element.76), kind=kOutput, calls=%fused_computation.14 | convolution fusion | flops 403045376 | bytes 1187840 | tf_op jit(solution)/shard_map/scr,rl->scl/dot_general | solution.py:154
  63.2 0.6 copy-done.10
  63.9 0.3 fusion.29
  64.2 3.0 %fusion.7 = f32[256,128]{1,0:T(8,128)} fusion(f32[32,32,128]{2,1,0:T(8,128)S(1)} %fusion.29, f32[32,32]{0,1:T(8,128)S(1)} %copy-done.12, s32[32,32]{0,1:T(8,128)S(1)} %copy-done.14), kind=kOutput, calls=%fused_computation.19 | convolution fusion | flops 403210240 | bytes 663552 | tf_op jit(solution)/shard_map/scr,scl->rl/dot_general | solution.py:159
  67.2 1.6 %mul.208 = f32[1,4,4,2048]{3,2,1,0:T(4,128)} reshape(f32[256,128]{1,0:T(8,128)} %fusion.7) | data formatting | bytes 262144 | tf_op jit(solution)/shard_map/mul | solution.py:69
  68.8 1.0 add_dynamic-update-slice_fusion.1
  69.8 0.7 copy-done.2
  70.5 1.1 divide_add_fusion.1
  71.7 2.3 %fusion.5 = f32[32,32]{1,0:T(8,128)S(1)} fusion(f32[256,128,1]{1,0,2:T(8,128)S(1)} %reshape.233, f32[32,32,256]{2,0,1:T(8,128)S(1)} %fusion.15, s32[32,32]{1,0:T(8,128)} %get-tuple-element.76), kind=kOutput, calls=%fused_computation.15 | convolution fusion | flops 403045376 | bytes 1187840 | tf_op jit(solution)/shard_map/scr,rl->scl/dot_general | solution.py:154
  74.0 0.7 pad_maximum_fusion.11
  74.7 0.6 copy.64
  75.3 10.4 %all-to-all-start.1 = ((f32[32,2,32]{2,1,0:T(2,128)}), f32[32,2,32]{2,1,0:T(2,128)S(1)}, u32[]{:S(2)}, u32[]{:S(2)}) async-start(f32[32,2,32]{2,1,0:T(2,128)} %copy.64), calls=%async_computation.1 | async-start | bytes 65536 | tf_op jit(solution)/shard_map/all_to_all | solution.py:113
  85.7 3.5 %subtract_reduce_fusion = (f32[3,4,4,2048]{3,2,1,0:T(4,128)S(1)}, f32[4,3,4,4,2048]{4,3,2,1,0:T(4,128)}) fusion(f32[4,3,4,4,2048]{4,3,2,1,0:T(4,128)} %get-tuple-element.46, f32[3,4,4,2048]{3,2,1,0:T(4,128)S(1)} %bitcast.241, f32[4,4,4,2048]{3,2,1,0:T(4,128)S(1)} %copy.56, f32[4,4,4,2048]{3,2,1,0:T(4,128)S(1)} %copy.55), kind=kLoop, calls=%fused_computation.8 | loop fusion | flops 1867776 | bytes 4980736 | tf_op jit(solution)/shard_map/reduce_sum | solution.py:63
  89.5 1.3 collective-permute-start.5
  90.8 3.2 %collective-permute-start.4 = (f32[2,1,4,2048]{3,2,1,0:T(4,128)S(1)}, f32[2,1,4,2048]{3,2,1,0:T(4,128)S(1)}, u32[]{:S(2)}, u32[]{:S(2)}) collective-permute-start(f32[2,1,4,2048]{3,2,1,0:T(4,128)S(1)} %slice.301), channel_id=1, source_target_pairs={{32,0},{64,32},{96,64},{128,96},{160,128},{192,160},{224,192},{256... | collective-permute-start | bytes 196616 | tf_op jit(solution)/shard_map/ppermute | solution.py:15
  94.0 5.2 %all-to-all-done.1 = f32[32,2,32]{2,1,0:T(2,128)S(1)} async-done(((f32[32,2,32]{2,1,0:T(2,128)}), f32[32,2,32]{2,1,0:T(2,128)S(1)}, u32[]{:S(2)}, u32[]{:S(2)}) %all-to-all-start.1) | async-done | bytes 8224 | tf_op jit(solution)/shard_map/all_to_all | solution.py:113
  99.2 0.7 fusion.2
  100.4 0.7 fusion.130
  101.0 1.0 fusion.1
  102.1 0.7 transpose_reshape.3
  102.8 9.3 %all-to-all-start.2 = ((f32[32,1,32]{2,1,0:T(1,128)}), f32[32,1,32]{2,1,0:T(1,128)}, u32[]{:S(2)}, u32[]{:S(2)}) async-start(f32[32,1,32]{2,1,0:T(1,128)} %transpose_reshape.3), calls=%async_computation.2 | async-start | bytes 32768 | tf_op jit(solution)/shard_map/all_to_all | solution.py:113
  112.7 2.1 %collective-permute-start.7 = (f32[2,1,4,2048]{3,2,1,0:T(4,128)S(1)}, f32[2,1,4,2048]{3,2,1,0:T(4,128)S(1)}, u32[]{:S(2)}, u32[]{:S(2)}) collective-permute-start(f32[2,1,4,2048]{3,2,1,0:T(4,128)S(1)} %pad_maximum_fusion.10), channel_id=1, source_target_pairs={{0,32},{32,64},{64,96},{96,128},{128,160},{160,192},{192,224},{224... | collective-permute-start | bytes 196616 | tf_op jit(solution)/shard_map/ppermute | solution.py:15
  115.1 3.6 %collective-permute-start.6 = (f32[2,4,1,2048]{3,2,1,0:T(1,128)S(1)}, f32[2,4,1,2048]{3,2,1,0:T(1,128)S(1)}, u32[]{:S(2)}, u32[]{:S(2)}) collective-permute-start(f32[2,4,1,2048]{3,2,1,0:T(1,128)S(1)} %slice.315), channel_id=1, source_target_pairs={{0,1},{1,2},{2,3},{3,4},{4,5},{5,6},{6,7},{7,8},{8,9},{9,10},{10,1... | collective-permute-start | bytes 196616 | tf_op jit(solution)/shard_map/ppermute | solution.py:15
  118.7 3.4 %collective-permute-done.7 = f32[2,1,4,2048]{3,2,1,0:T(4,128)S(1)} collective-permute-done((f32[2,1,4,2048]{3,2,1,0:T(4,128)S(1)}, f32[2,1,4,2048]{3,2,1,0:T(4,128)S(1)}, u32[]{:S(2)}, u32[]{:S(2)}) %collective-permute-start.7) | collective-permute-done | bytes 65568 | tf_op jit(solution)/shard_map/ppermute | solution.py:15
  122.2 0.3 fusion.43
  123.0 2.1 %all-to-all-done.2 = f32[32,1,32]{2,1,0:T(1,128)} async-done(((f32[32,1,32]{2,1,0:T(1,128)}), f32[32,1,32]{2,1,0:T(1,128)}, u32[]{:S(2)}, u32[]{:S(2)}) %all-to-all-start.2) | async-done | bytes 4128 | tf_op jit(solution)/shard_map/all_to_all | solution.py:113
  125.0 1.1 fusion.28
  126.1 2.3 %fusion.6 = f32[256,128]{1,0:T(8,128)S(1)} fusion(f32[32,32,128]{2,1,0:T(8,128)S(1)} %fusion.28, f32[32,32]{0,1:T(8,128)S(1)} %copy-done.13, s32[32,32]{0,1:T(8,128)S(1)} %copy-done.15), kind=kOutput, calls=%fused_computation.17 | convolution fusion | flops 403210240 | bytes 663552 | tf_op jit(solution)/shard_map/scr,scl->rl/dot_general | solution.py:159
  128.5 0.8 divide_add_fusion
  (116 shorter events, 3.8 us)
Async XLA Ops:
  0.6 10.6 %copy-start = (f32[4,8]{1,0:T(4,128)S(1)}, f32[4,8]{1,0:T(4,128)}, u32[]{:S(2)}) copy-start(f32[4,8]{1,0:T(4,128)} %param.27) | copy-start | bytes 388
  0.6 12.4 %copy-start.5 = (s32[4,4,2048]{2,1,0:T(4,128)S(1)}, s32[4,4,2048]{2,1,0:T(4,128)}, u32[]{:S(2)}) copy-start(s32[4,4,2048]{2,1,0:T(4,128)} %param.23) | copy-start | bytes 393220
  0.7 12.4 %copy-start.28 = (f32[4,8]{1,0:T(4,128)S(1)}, f32[4,8]{1,0:T(4,128)}, u32[]{:S(2)}) copy-start(f32[4,8]{1,0:T(4,128)} %param.26) | copy-start | bytes 388
  1.7 16.5 %collective-permute-start = (f32[2,4,1,2048]{3,2,1,0:T(1,128)S(1)}, f32[2,4,1,2048]{3,2,1,0:T(1,128)S(1)}, u32[]{:S(2)}, u32[]{:S(2)}) collective-permute-start(f32[2,4,1,2048]{3,2,1,0:T(1,128)S(1)} %slice.261), channel_id=1, source_target_pairs={{1,0},{2,1},{3,2},{4,3},{5,4},{6,5},{7,6},{8,7},{9,8},{10,9},{11,1... | collective-permute-start | bytes 196616 | tf_op jit(solution)/shard_map/ppermute | solution.py:15
  3.9 14.3 %collective-permute-start.1 = (f32[2,1,4,2048]{3,2,1,0:T(4,128)S(1)}, f32[2,1,4,2048]{3,2,1,0:T(4,128)S(1)}, u32[]{:S(2)}, u32[]{:S(2)}) collective-permute-start(f32[2,1,4,2048]{3,2,1,0:T(4,128)S(1)} %slice.270), channel_id=1, source_target_pairs={{32,0},{64,32},{96,64},{128,96},{160,128},{192,160},{224,192},{256... | collective-permute-start | bytes 196616 | tf_op jit(solution)/shard_map/ppermute | solution.py:15
  9.4 7.4 %copy-start.26 = (s32[512]{0:T(512)}, s32[512]{0:T(512)S(1)}, u32[]{:S(2)}) copy-start(s32[512]{0:T(512)S(1)} %multiply_add_fusion.5) | copy-start | bytes 6148
  10.2 4.5 %copy-start.19 = (f32[1,511]{1,0:T(1,128)}, f32[1,511]{1,0:T(1,128)S(1)}, u32[]{:S(2)}) copy-start(f32[1,511]{1,0:T(1,128)S(1)} %slice.258) | copy-start | bytes 6136
  12.7 1.4 %copy-start.30 = (f32[8]{0:T(128)S(1)}, f32[8]{0:T(128)}, u32[]{:S(2)}) copy-start(f32[8]{0:T(128)} %param.25) | copy-start | bytes 100
  13.1 1.7 %copy-start.17 = (f32[1,512]{1,0:T(1,128)S(1)}, f32[1,512]{1,0:T(1,128)}, u32[]{:S(2)}) copy-start(f32[1,512]{1,0:T(1,128)} %param.31) | copy-start | bytes 6148
  13.1 1.8 %copy-start.1 = (f32[3,4,4,2048]{3,2,1,0:T(4,128)S(1)}, f32[3,4,4,2048]{3,2,1,0:T(4,128)}, u32[]{:S(2)}) copy-start(f32[3,4,4,2048]{3,2,1,0:T(4,128)} %param.20) | copy-start | bytes 1179652
  13.1 1.7 %copy-start.3 = (f32[4,3,4,4,2048]{4,3,2,1,0:T(4,128)S(1)}, f32[4,3,4,4,2048]{4,3,2,1,0:T(4,128)}, u32[]{:S(2)}) copy-start(f32[4,3,4,4,2048]{4,3,2,1,0:T(4,128)} %param.22) | copy-start | bytes 4718596
  14.8 2.1 %copy-start.23 = (f32[1,512]{1,0:T(1,128)}, f32[1,512]{1,0:T(1,128)S(1)}, u32[]{:S(2)}) copy-start(f32[1,512]{1,0:T(1,128)S(1)} %fusion.114) | copy-start | bytes 6148
  14.8 2.1 %copy-start.18 = (f32[1,512]{1,0:T(1,128)S(1)}, f32[1,512]{1,0:T(1,128)}, u32[]{:S(2)}) copy-start(f32[1,512]{1,0:T(1,128)} %param.32) | copy-start | bytes 6148
  14.8 2.1 %copy-start.21 = (f32[1,512]{1,0:T(1,128)S(1)}, f32[1,512]{1,0:T(1,128)}, u32[]{:S(2)}) copy-start(f32[1,512]{1,0:T(1,128)} %param.30) | copy-start | bytes 6148
  14.9 2.1 %copy-start.31 = (f32[4]{0:T(128)S(1)}, f32[4]{0:T(128)}, u32[]{:S(2)}) copy-start(f32[4]{0:T(128)} %constant.108.clone) | copy-start | bytes 52
  22.3 31.0 %all-to-all-start = ((f32[32,1,128]{2,1,0:T(1,128)}), f32[32,1,128]{2,1,0:T(1,128)S(1)}, u32[]{:S(2)}, u32[]{:S(2)}) async-start(f32[32,1,128]{2,1,0:T(1,128)} %reshape.239), calls=%async_computation | async-start | bytes 32768 | tf_op jit(solution)/shard_map/all_to_all | solution.py:113
  40.2 14.3 %collective-permute-start.2 = (f32[2,4,1,2048]{3,2,1,0:T(1,128)}, f32[2,4,1,2048]{3,2,1,0:T(1,128)S(1)}, u32[]{:S(2)}, u32[]{:S(2)}) collective-permute-start(f32[2,4,1,2048]{3,2,1,0:T(1,128)} %slice.276), channel_id=1, source_target_pairs={{0,1},{1,2},{2,3},{3,4},{4,5},{5,6},{6,7},{7,8},{8,9},{9,10},{10,1... | collective-permute-start | bytes 196616 | tf_op jit(solution)/shard_map/ppermute | solution.py:15
  43.9 10.6 %collective-permute-start.3 = (f32[2,1,4,2048]{3,2,1,0:T(4,128)S(1)}, f32[2,1,4,2048]{3,2,1,0:T(4,128)S(1)}, u32[]{:S(2)}, u32[]{:S(2)}) collective-permute-start(f32[2,1,4,2048]{3,2,1,0:T(4,128)S(1)} %slice.283), channel_id=1, source_target_pairs={{0,32},{32,64},{64,96},{96,128},{128,160},{160,192},{192,224},{224... | collective-permute-start | bytes 196616 | tf_op jit(solution)/shard_map/ppermute | solution.py:15
  54.5 0.6 copy-start.8
  54.6 0.6 copy-start.9
  59.6 4.2 %copy-start.11 = (f32[32,4,32]{2,0,1:T(8,128)S(1)}, f32[32,4,32]{2,0,1:T(8,128)}, u32[]{:S(2)}) copy-start(f32[32,4,32]{2,0,1:T(8,128)} %copy.60) | copy-start | bytes 49156
  59.6 4.2 %copy-start.16 = (f32[32,1,32]{2,1,0:T(1,128)S(1)}, f32[32,1,32]{2,1,0:T(1,128)}, u32[]{:S(2)}) copy-start(f32[32,1,32]{2,1,0:T(1,128)} %get-tuple-element.74) | copy-start | bytes 12292
  59.6 4.3 %copy-start.6 = (s32[32,32]{1,0:T(8,128)S(1)}, s32[32,32]{1,0:T(8,128)}, u32[]{:S(2)}) copy-start(s32[32,32]{1,0:T(8,128)} %get-tuple-element.76) | copy-start | bytes 12292
  59.6 4.6 %copy-start.12 = (f32[32,32]{0,1:T(8,128)S(1)}, f32[32,32]{0,1:T(8,128)}, u32[]{:S(2)}) copy-start(f32[32,32]{0,1:T(8,128)} %copy.58) | copy-start | bytes 12292
  59.6 4.6 %copy-start.14 = (s32[32,32]{0,1:T(8,128)S(1)}, s32[32,32]{0,1:T(8,128)}, u32[]{:S(2)}) copy-start(s32[32,32]{0,1:T(8,128)} %copy.57) | copy-start | bytes 12292
  63.2 0.6 copy-start.10
  69.8 0.7 copy-start.2
  75.3 23.8 %all-to-all-start.1 = ((f32[32,2,32]{2,1,0:T(2,128)}), f32[32,2,32]{2,1,0:T(2,128)S(1)}, u32[]{:S(2)}, u32[]{:S(2)}) async-start(f32[32,2,32]{2,1,0:T(2,128)} %copy.64), calls=%async_computation.1 | async-start | bytes 65536 | tf_op jit(solution)/shard_map/all_to_all | solution.py:113
  85.7 13.5 %copy-start.27 = (s32[512]{0:T(512)S(1)}, s32[512]{0:T(512)}, u32[]{:S(2)}) copy-start(s32[512]{0:T(512)} %copy-done.26) | copy-start | bytes 6148
  89.2 10.7 %copy-start.20 = (f32[1,511]{1,0:T(1,128)S(1)}, f32[1,511]{1,0:T(1,128)}, u32[]{:S(2)}) copy-start(f32[1,511]{1,0:T(1,128)} %copy-done.19) | copy-start | bytes 6136
  89.2 10.7 %copy-start.22 = (f32[1,512]{1,0:T(1,128)S(1)}, f32[1,512]{1,0:T(1,128)}, u32[]{:S(2)}) copy-start(f32[1,512]{1,0:T(1,128)} %param.30) | copy-start | bytes 6148
  89.3 10.8 %copy-start.24 = (f32[1,512]{1,0:T(1,128)S(1)}, f32[1,512]{1,0:T(1,128)}, u32[]{:S(2)}) copy-start(f32[1,512]{1,0:T(1,128)} %copy-done.23) | copy-start | bytes 6148
  89.3 10.8 %copy-start.25 = (f32[1,512]{1,0:T(1,128)S(1)}, f32[1,512]{1,0:T(1,128)}, u32[]{:S(2)}) copy-start(f32[1,512]{1,0:T(1,128)} %param.33) | copy-start | bytes 6148
  89.5 22.6 %collective-permute-start.5 = (f32[2,4,1,2048]{3,2,1,0:T(1,128)S(1)}, f32[2,4,1,2048]{3,2,1,0:T(1,128)S(1)}, u32[]{:S(2)}, u32[]{:S(2)}) collective-permute-start(f32[2,4,1,2048]{3,2,1,0:T(1,128)S(1)} %slice.305), channel_id=1, source_target_pairs={{1,0},{2,1},{3,2},{4,3},{5,4},{6,5},{7,6},{8,7},{9,8},{10,9},{11,1... | collective-permute-start | bytes 196616 | tf_op jit(solution)/shard_map/ppermute | solution.py:15
  90.8 21.3 %collective-permute-start.4 = (f32[2,1,4,2048]{3,2,1,0:T(4,128)S(1)}, f32[2,1,4,2048]{3,2,1,0:T(4,128)S(1)}, u32[]{:S(2)}, u32[]{:S(2)}) collective-permute-start(f32[2,1,4,2048]{3,2,1,0:T(4,128)S(1)} %slice.301), channel_id=1, source_target_pairs={{32,0},{64,32},{96,64},{128,96},{160,128},{192,160},{224,192},{256... | collective-permute-start | bytes 196616 | tf_op jit(solution)/shard_map/ppermute | solution.py:15
  101.0 11.7 %copy-start.29 = (f32[1,512]{1,0:T(1,128)}, f32[1,512]{1,0:T(1,128)S(1)}, u32[]{:S(2)}) copy-start(f32[1,512]{1,0:T(1,128)S(1)} %get-tuple-element.50) | copy-start | bytes 6148
  102.8 22.3 %all-to-all-start.2 = ((f32[32,1,32]{2,1,0:T(1,128)}), f32[32,1,32]{2,1,0:T(1,128)}, u32[]{:S(2)}, u32[]{:S(2)}) async-start(f32[32,1,32]{2,1,0:T(1,128)} %transpose_reshape.3), calls=%async_computation.2 | async-start | bytes 32768 | tf_op jit(solution)/shard_map/all_to_all | solution.py:113
  112.7 9.4 %collective-permute-start.7 = (f32[2,1,4,2048]{3,2,1,0:T(4,128)S(1)}, f32[2,1,4,2048]{3,2,1,0:T(4,128)S(1)}, u32[]{:S(2)}, u32[]{:S(2)}) collective-permute-start(f32[2,1,4,2048]{3,2,1,0:T(4,128)S(1)} %pad_maximum_fusion.10), channel_id=1, source_target_pairs={{0,32},{32,64},{64,96},{96,128},{128,160},{160,192},{192,224},{224... | collective-permute-start | bytes 196616 | tf_op jit(solution)/shard_map/ppermute | solution.py:15
  115.0 7.6 %copy-start.4 = (f32[3,4,4,2048]{3,2,1,0:T(4,128)}, f32[3,4,4,2048]{3,2,1,0:T(4,128)S(1)}, u32[]{:S(2)}) copy-start(f32[3,4,4,2048]{3,2,1,0:T(4,128)S(1)} %pad_maximum_fusion.1) | copy-start | bytes 1179652
  115.1 7.1 %collective-permute-start.6 = (f32[2,4,1,2048]{3,2,1,0:T(1,128)S(1)}, f32[2,4,1,2048]{3,2,1,0:T(1,128)S(1)}, u32[]{:S(2)}, u32[]{:S(2)}) collective-permute-start(f32[2,4,1,2048]{3,2,1,0:T(1,128)S(1)} %slice.315), channel_id=1, source_target_pairs={{0,1},{1,2},{2,3},{3,4},{4,5},{5,6},{6,7},{7,8},{8,9},{9,10},{10,1... | collective-permute-start | bytes 196616 | tf_op jit(solution)/shard_map/ppermute | solution.py:15
  122.6 2.4 %copy-start.7 = (s32[32,32]{1,0:T(8,128)S(1)}, s32[32,32]{1,0:T(8,128)}, u32[]{:S(2)}) copy-start(s32[32,32]{1,0:T(8,128)} %get-tuple-element.76) | copy-start | bytes 12292
  122.6 3.5 %copy-start.13 = (f32[32,32]{0,1:T(8,128)S(1)}, f32[32,32]{0,1:T(8,128)}, u32[]{:S(2)}) copy-start(f32[32,32]{0,1:T(8,128)} %copy.58) | copy-start | bytes 12292
  122.6 3.5 %copy-start.15 = (s32[32,32]{0,1:T(8,128)S(1)}, s32[32,32]{0,1:T(8,128)}, u32[]{:S(2)}) copy-start(s32[32,32]{0,1:T(8,128)} %copy.57) | copy-start | bytes 12292

commit v11 on v10

--- a/solution.py
+++ b/solution.py
@@ -99,22 +99,21 @@
     cell_total = grid_shape[0] * grid_shape[1] * grid_shape[2]
     single_zero = jnp.zeros((1,), jnp.float32)
 
-    slot_total = n_gy * capacity
     highest = lax.Precision.HIGHEST
-    slot_hot = (jnp.arange(slot_total, dtype=jnp.int32)[:, None] == slot_at[None, :]).astype(jnp.float32)
-    slot_used = jnp.sum(slot_hot, axis=1)
+    slot_index = jnp.arange(n_gy, dtype=jnp.int32)[:, None] * capacity + jnp.arange(capacity, dtype=jnp.int32)[None, :]
+    slot_match = slot_index[:, :, None] == slot_at[None, None, :]
+    slot_hot = slot_match.astype(jnp.float32)
+    slot_used = jnp.sum(slot_hot, axis=2)
 
     def to_slots(rows, fill):
-        placed = jnp.einsum("fs,ts->ft", rows, slot_hot, precision=highest)
-        buffer = placed + jnp.asarray(fill, jnp.float32)[:, None] * (1.0 - slot_used)[None, :]
-        return buffer.reshape(rows.shape[0], n_gy, capacity).transpose(1, 0, 2)
+        placed = jnp.einsum("dcs,fs->dfc", slot_hot, rows, precision=highest)
+        return placed + jnp.asarray(fill, jnp.float32)[None, :, None] * (1.0 - slot_used)[:, None, :]
 
     def exchange(blocks):
         return lax.all_to_all(blocks, "gy", split_axis=0, concat_axis=0, tiled=True)
 
     def from_slots(blocks):
-        flat = blocks.transpose(1, 0, 2).reshape(blocks.shape[1], slot_total)
-        return jnp.einsum("ft,ts->fs", flat, slot_hot, precision=highest)
+        return jnp.einsum("dfc,dcs->fs", blocks, slot_hot, precision=highest)
 
     gain_row = wire_gain[0]
     cap_row = wire_cap[0]

time: 131 us -> 131 us (level)
  matrix products: 16.6 us -> 18.9 us
  waiting for transfers between devices: 15.9 us -> 17.3 us
    dot_general x3, matrix products: 2.75 us -> 5.71 us  [the longest x2 4.39 us: to_slots(): placed = jnp.einsum('dcs,fs->dfc', slot_hot, rows, precision=highest)]
    all_to_all x3, waiting for transfers between devices: 12.5 us -> 13.8 us  [exchange(): return lax.all_to_all(blocks, 'gy', split_axis=0, concat_axis=0, tiled=True)]
    unnamed x65 -> x77, local copies, waits for them, and re-layouts: 2.68 us -> 2.71 us
  transfers between devices with their start and end apart: 11 -> 11, of which waited for: 4 -> 4; matrix products, arithmetic and copies ran while one was open for 18% -> 20% of each run, Pallas kernels for 0% -> 0%
where the time goes in v11:
time: 131 us; the launch traced here: 130 us
  starting transfers between devices  57.8 us (44%)
  other arithmetic  20.9 us (16%)
  matrix products  18.9 us (14%)
  waiting for transfers between devices  17.3 us (13%)
  local copies, waits for them, and re-layouts  13.5 us (10%)
  between operations  1.63 us (1%)
    all_to_all x3, starting transfers between devices, exchange(): return lax.all_to_all(blocks, 'gy', split_axis=0, concat_axis=0, tiled=True)  37.1 us
    ppermute x8, starting transfers between devices, passed_along(): lax.ppermute(value, axis, [(source, source + steps) for source in range(f...  20.6 us
    all_to_all x3, waiting for transfers between devices, exchange(): return lax.all_to_all(blocks, 'gy', split_axis=0, concat_axis=0, tiled=True)  13.8 us
    dot_general x2, matrix products, wire_of(): jnp.einsum('scr,scl->rl', row_hot, spread, precision=highest)  5.25 us
    dot_general x2, matrix products, sample(): jnp.einsum('scr,rl->scl', row_hot, e_now[2].reshape(plane_rows, lanes), p...  4.72 us
    dot_general x2, matrix products, to_slots(): placed = jnp.einsum('dcs,fs->dfc', slot_hot, rows, precision=highest)  4.39 us
    reduce_sum x1, other arithmetic, electric_base(): change = jnp.sum(polar_new - polarization, axis=0)  3.54 us
    ppermute x8, waiting for transfers between devices, passed_along(): lax.ppermute(value, axis, [(source, source + steps) for source in range(f...  3.44 us
  transfers between devices with their start and end apart: 11, of which 4 were waited for; matrix products, arithmetic and copies ran while one was open for 20% of the time, Pallas kernels for 0%

profile of v11, /device:TPU:16, one launch (start us, length us, event | category | flops | bytes accessed | tf_op | source)
XLA Modules:
  0.0 130.0 jit_solution(2614454326361594949)
XLA Ops:
  0.7 1.0 slice.261
  1.7 1.3 collective-permute-start
  3.0 0.8 slice.270
  3.9 3.9 %collective-permute-start.1 = (f32[2,1,4,2048]{3,2,1,0:T(4,128)S(1)}, f32[2,1,4,2048]{3,2,1,0:T(4,128)S(1)}, u32[]{:S(2)}, u32[]{:S(2)}) collective-permute-start(f32[2,1,4,2048]{3,2,1,0:T(4,128)S(1)} %slice.270), channel_id=1, source_target_pairs={{32,0},{64,32},{96,64},{128,96},{160,128},{192,160},{224,192},{256... | collective-permute-start | bytes 196616 | tf_op jit(solution)/shard_map/ppermute | solution.py:15
  7.7 1.0 convert_reduce_fusion.1
  8.7 0.7 multiply_add_fusion.4
  9.4 0.4 broadcast_compare_fusion
  9.8 0.4 convert_reduce_fusion
  10.3 0.8 slice.258
  11.1 0.7 convert_element_type.35
  11.8 1.5 %convolution_bitcast_fusion.1 = f32[4,4,4,2048]{3,0,2,1:T(4,128)S(1)} fusion(s32[4,4,2048]{2,1,0:T(4,128)} %param.23, f32[4,8]{1,0:T(4,128)S(1)} %copy-done), kind=kOutput, calls=%fused_computation.2 | convolution fusion | flops 12845056 | bytes 655488 | tf_op jit(solution)/shard_map/pm,mxyz->pxyz/dot_general | solution.py:134
  13.3 0.3 copy.50
  13.7 0.6 fusion
  14.3 0.3 copy.51
  14.7 0.6 fusion.21
  15.5 2.0 %multiply_add_fusion.1 = (f32[4,3,4,4,2048]{4,3,2,1,0:T(4,128)}, f32[3,4,4,2048]{3,2,1,0:T(4,128)S(1)}) fusion(f32[4,3,4,4,2048]{4,3,2,1,0:T(4,128)S(1)} %copy-done.3, f32[3,4,4,2048]{3,2,1,0:T(4,128)S(1)} %copy-done.1, f32[4,4,4,2048]{3,2,1,0:T(4,128)S(1)} %copy.51, f32[4,4,4,2048]{3,2,1,0:T(4,128)S(1)} %copy.50), kind=kLoop, calls=%fused_computation.11 | loop fusion | flops 1867776 | bytes 4980736 | tf_op jit(solution)/shard_map/add | solution.py:60
  17.5 2.2 %fusion.12 = f32[32,4,32]{2,1,0:T(4,128)S(1)} fusion(pred[32,32,512]{2,0,1:T(32,128)(4,1)S(1)} %broadcast_compare_fusion, f32[32,32]{1,0:T(8,128)S(1)} %copy.49, f32[4]{0:T(128)S(1)} %copy-done.37, f32[1,512]{1,0:T(1,128)S(1)} %fusion.123, f32[1,512]{1,0:T(1,128)S(1)} %copy-done.25, f32[1,512]{1,0:T(1,128)S(1)} %copy-done.28, ...), kind=kOutput, calls=%fused_computation.21 | convolution fusion | flops 25180160 | bytes 552976 | tf_op jit(solution)/shard_map/dcs,fs->dfc/dot_general | solution.py:109
  20.7 0.7 reshape.258
  21.4 17.9 %all-to-all-start = ((f32[32,1,128]{2,1,0:T(1,128)}), f32[32,1,128]{2,1,0:T(1,128)S(1)}, u32[]{:S(2)}, u32[]{:S(2)}) async-start(f32[32,1,128]{2,1,0:T(1,128)} %reshape.258), calls=%async_computation | async-start | bytes 32768 | tf_op jit(solution)/shard_map/all_to_all | solution.py:113
  39.3 3.7 %collective-permute-start.2 = (f32[2,4,1,2048]{3,2,1,0:T(1,128)S(1)}, f32[2,4,1,2048]{3,2,1,0:T(1,128)S(1)}, u32[]{:S(2)}, u32[]{:S(2)}) collective-permute-start(f32[2,4,1,2048]{3,2,1,0:T(1,128)S(1)} %slice.276), channel_id=1, source_target_pairs={{0,1},{1,2},{2,3},{3,4},{4,5},{5,6},{6,7},{7,8},{8,9},{9,10},{10,1... | collective-permute-start | bytes 196616 | tf_op jit(solution)/shard_map/ppermute | solution.py:15
  43.0 2.1 %collective-permute-start.3 = (f32[2,1,4,2048]{3,2,1,0:T(4,128)S(1)}, f32[2,1,4,2048]{3,2,1,0:T(4,128)S(1)}, u32[]{:S(2)}, u32[]{:S(2)}) collective-permute-start(f32[2,1,4,2048]{3,2,1,0:T(4,128)S(1)} %slice.283), channel_id=1, source_target_pairs={{0,32},{32,64},{64,96},{96,128},{128,160},{160,192},{192,224},{224... | collective-permute-start | bytes 196616 | tf_op jit(solution)/shard_map/ppermute | solution.py:15
  45.1 0.6 fusion.20
  45.8 0.7 reshape.247
  46.5 5.9 %all-to-all-done = f32[32,1,128]{2,1,0:T(1,128)S(1)} async-done(((f32[32,1,128]{2,1,0:T(1,128)}), f32[32,1,128]{2,1,0:T(1,128)S(1)}, u32[]{:S(2)}, u32[]{:S(2)}) %all-to-all-start) | async-done | bytes 16416 | tf_op jit(solution)/shard_map/all_to_all | solution.py:113
  52.5 0.5 broadcast.222
  53.0 0.7 reduce.4
  54.0 0.5 copy-done.11
  54.4 1.0 fusion.65
  55.4 0.2 fusion.45
  55.7 0.6 copy.55
  56.3 0.6 fusion.148
  56.9 0.6 add_select_fusion.1
  57.5 0.7 copy.53
  58.2 0.7 copy.52
  58.9 1.1 fusion.25
  60.0 2.5 %fusion.5 = f32[32,32]{1,0:T(8,128)S(1)} fusion(f32[256,128,1]{1,0,2:T(8,128)} %reshape.247, f32[32,32,256]{2,0,1:T(8,128)S(1)} %fusion.25, s32[32,32]{1,0:T(8,128)} %get-tuple-element.76), kind=kOutput, calls=%fused_computation.14 | convolution fusion | flops 403045376 | bytes 1187840 | tf_op jit(solution)/shard_map/scr,rl->scl/dot_general | solution.py:153
  62.5 0.6 copy-done.13
  63.1 0.3 fusion.39
  63.5 3.0 %fusion.8 = f32[256,128]{1,0:T(8,128)} fusion(f32[32,32,128]{2,1,0:T(8,128)S(1)} %fusion.39, f32[32,32]{0,1:T(8,128)S(1)} %copy-done.19, s32[32,32]{0,1:T(8,128)S(1)} %copy-done.21), kind=kOutput, calls=%fused_computation.19 | convolution fusion | flops 403210240 | bytes 663552 | tf_op jit(solution)/shard_map/scr,scl->rl/dot_general | solution.py:158
  66.5 1.6 %mul.221 = f32[1,4,4,2048]{3,2,1,0:T(4,128)} reshape(f32[256,128]{1,0:T(8,128)} %fusion.8) | data formatting | bytes 262144 | tf_op jit(solution)/shard_map/mul | solution.py:69
  68.1 1.0 add_dynamic-update-slice_fusion.1
  69.1 0.7 copy-done.2
  69.8 1.1 divide_add_fusion.1
  71.0 2.3 %fusion.6 = f32[32,32]{1,0:T(8,128)S(1)} fusion(f32[256,128,1]{1,0,2:T(8,128)S(1)} %reshape.251, f32[32,32,256]{2,0,1:T(8,128)S(1)} %fusion.25, s32[32,32]{1,0:T(8,128)} %get-tuple-element.76), kind=kOutput, calls=%fused_computation.15 | convolution fusion | flops 403045376 | bytes 1187840 | tf_op jit(solution)/shard_map/scr,rl->scl/dot_general | solution.py:153
  73.2 0.7 pad_maximum_fusion.11
  74.0 0.6 copy.59
  74.6 10.3 %all-to-all-start.1 = ((f32[32,2,32]{2,1,0:T(2,128)}), f32[32,2,32]{2,1,0:T(2,128)S(1)}, u32[]{:S(2)}, u32[]{:S(2)}) async-start(f32[32,2,32]{2,1,0:T(2,128)} %copy.59), calls=%async_computation.1 | async-start | bytes 65536 | tf_op jit(solution)/shard_map/all_to_all | solution.py:113
  84.9 3.5 %subtract_reduce_fusion = (f32[3,4,4,2048]{3,2,1,0:T(4,128)S(1)}, f32[4,3,4,4,2048]{4,3,2,1,0:T(4,128)}) fusion(f32[4,3,4,4,2048]{4,3,2,1,0:T(4,128)} %get-tuple-element.46, f32[3,4,4,2048]{3,2,1,0:T(4,128)S(1)} %bitcast.251, f32[4,4,4,2048]{3,2,1,0:T(4,128)S(1)} %copy.51, f32[4,4,4,2048]{3,2,1,0:T(4,128)S(1)} %copy.50), kind=kLoop, calls=%fused_computation.8 | loop fusion | flops 1867776 | bytes 4980736 | tf_op jit(solution)/shard_map/reduce_sum | solution.py:63
  88.6 1.3 collective-permute-start.5
  89.9 2.9 %collective-permute-start.4 = (f32[2,1,4,2048]{3,2,1,0:T(4,128)S(1)}, f32[2,1,4,2048]{3,2,1,0:T(4,128)S(1)}, u32[]{:S(2)}, u32[]{:S(2)}) collective-permute-start(f32[2,1,4,2048]{3,2,1,0:T(4,128)S(1)} %slice.301), channel_id=1, source_target_pairs={{32,0},{64,32},{96,64},{128,96},{160,128},{192,160},{224,192},{256... | collective-permute-start | bytes 196616 | tf_op jit(solution)/shard_map/ppermute | solution.py:15
  92.8 5.5 %all-to-all-done.1 = f32[32,2,32]{2,1,0:T(2,128)S(1)} async-done(((f32[32,2,32]{2,1,0:T(2,128)}), f32[32,2,32]{2,1,0:T(2,128)S(1)}, u32[]{:S(2)}, u32[]{:S(2)}) %all-to-all-start.1) | async-done | bytes 8224 | tf_op jit(solution)/shard_map/all_to_all | solution.py:113
  98.3 1.3 %fusion.15 = f32[2,512]{1,0:T(2,128)S(1)} fusion(f32[32,2,32]{2,1,0:T(2,128)S(1)} %all-to-all-done.1, pred[32,32,512]{2,0,1:T(32,128)(4,1)S(1)} %copy-done.7), kind=kOutput, calls=%fused_computation.22 | convolution fusion | flops 12582912 | bytes 536576 | tf_op jit(solution)/shard_map/dfc,dcs->fs/dot_general | solution.py:116
  100.0 0.7 fusion.139
  100.7 2.2 %fusion.18 = f32[1,32,32]{1,0,2:T(1,128)S(1)} fusion(s32[512]{0:T(512)S(1)} %multiply_add_fusion.4, s32[32,32]{0,1:T(8,128)S(1)} %copy-done.15, f32[1,512]{1,0:T(1,128)S(1)} %get-tuple-element.50), kind=kOutput, calls=%fused_computation.23 | convolution fusion | flops 6815744 | bytes 12288 | tf_op jit(solution)/shard_map/dcs,fs->dfc/dot_general | solution.py:109
  102.9 0.7 copy.61
  103.6 9.0 %all-to-all-start.2 = ((f32[32,1,32]{2,1,0:T(1,128)}), f32[32,1,32]{2,1,0:T(1,128)}, u32[]{:S(2)}, u32[]{:S(2)}) async-start(f32[32,1,32]{2,1,0:T(1,128)} %copy.61), calls=%async_computation.2 | async-start | bytes 32768 | tf_op jit(solution)/shard_map/all_to_all | solution.py:113
  113.3 1.9 %collective-permute-start.7 = (f32[2,1,4,2048]{3,2,1,0:T(4,128)S(1)}, f32[2,1,4,2048]{3,2,1,0:T(4,128)S(1)}, u32[]{:S(2)}, u32[]{:S(2)}) collective-permute-start(f32[2,1,4,2048]{3,2,1,0:T(4,128)S(1)} %pad_maximum_fusion.10), channel_id=1, source_target_pairs={{0,32},{32,64},{64,96},{96,128},{128,160},{160,192},{192,224},{224... | collective-permute-start | bytes 196616 | tf_op jit(solution)/shard_map/ppermute | solution.py:15
  115.4 3.6 %collective-permute-start.6 = (f32[2,4,1,2048]{3,2,1,0:T(1,128)S(1)}, f32[2,4,1,2048]{3,2,1,0:T(1,128)S(1)}, u32[]{:S(2)}, u32[]{:S(2)}) collective-permute-start(f32[2,4,1,2048]{3,2,1,0:T(1,128)S(1)} %slice.315), channel_id=1, source_target_pairs={{0,1},{1,2},{2,3},{3,4},{4,5},{5,6},{6,7},{7,8},{8,9},{9,10},{10,1... | collective-permute-start | bytes 196616 | tf_op jit(solution)/shard_map/ppermute | solution.py:15
  119.1 3.4 %collective-permute-done.7 = f32[2,1,4,2048]{3,2,1,0:T(4,128)S(1)} collective-permute-done((f32[2,1,4,2048]{3,2,1,0:T(4,128)S(1)}, f32[2,1,4,2048]{3,2,1,0:T(4,128)S(1)}, u32[]{:S(2)}, u32[]{:S(2)}) %collective-permute-start.7) | collective-permute-done | bytes 65568 | tf_op jit(solution)/shard_map/ppermute | solution.py:15
  122.6 0.3 fusion.53
  123.3 2.4 %all-to-all-done.2 = f32[32,1,32]{2,1,0:T(1,128)} async-done(((f32[32,1,32]{2,1,0:T(1,128)}), f32[32,1,32]{2,1,0:T(1,128)}, u32[]{:S(2)}, u32[]{:S(2)}) %all-to-all-start.2) | async-done | bytes 4128 | tf_op jit(solution)/shard_map/all_to_all | solution.py:113
  125.7 1.1 fusion.38
  126.8 2.3 %fusion.7 = f32[256,128]{1,0:T(8,128)S(1)} fusion(f32[32,32,128]{2,1,0:T(8,128)S(1)} %fusion.38, f32[32,32]{0,1:T(8,128)S(1)} %copy-done.20, s32[32,32]{0,1:T(8,128)S(1)} %copy-done.22), kind=kOutput, calls=%fused_computation.17 | convolution fusion | flops 403210240 | bytes 663552 | tf_op jit(solution)/shard_map/scr,scl->rl/dot_general | solution.py:158
  129.2 0.8 divide_add_fusion
  (128 shorter events, 3.6 us)
Async XLA Ops:
  0.6 11.1 %copy-start = (f32[4,8]{1,0:T(4,128)S(1)}, f32[4,8]{1,0:T(4,128)}, u32[]{:S(2)}) copy-start(f32[4,8]{1,0:T(4,128)} %param.27) | copy-start | bytes 388
  0.6 13.0 %copy-start.5 = (s32[4,4,2048]{2,1,0:T(4,128)S(1)}, s32[4,4,2048]{2,1,0:T(4,128)}, u32[]{:S(2)}) copy-start(s32[4,4,2048]{2,1,0:T(4,128)} %param.23) | copy-start | bytes 393220
  0.7 13.0 %copy-start.33 = (f32[4,8]{1,0:T(4,128)S(1)}, f32[4,8]{1,0:T(4,128)}, u32[]{:S(2)}) copy-start(f32[4,8]{1,0:T(4,128)} %param.26) | copy-start | bytes 388
  1.7 18.1 %collective-permute-start = (f32[2,4,1,2048]{3,2,1,0:T(1,128)S(1)}, f32[2,4,1,2048]{3,2,1,0:T(1,128)S(1)}, u32[]{:S(2)}, u32[]{:S(2)}) collective-permute-start(f32[2,4,1,2048]{3,2,1,0:T(1,128)S(1)} %slice.261), channel_id=1, source_target_pairs={{1,0},{2,1},{3,2},{4,3},{5,4},{6,5},{7,6},{8,7},{9,8},{10,9},{11,1... | collective-permute-start | bytes 196616 | tf_op jit(solution)/shard_map/ppermute | solution.py:15
  3.9 16.0 %collective-permute-start.1 = (f32[2,1,4,2048]{3,2,1,0:T(4,128)S(1)}, f32[2,1,4,2048]{3,2,1,0:T(4,128)S(1)}, u32[]{:S(2)}, u32[]{:S(2)}) collective-permute-start(f32[2,1,4,2048]{3,2,1,0:T(4,128)S(1)} %slice.270), channel_id=1, source_target_pairs={{32,0},{64,32},{96,64},{128,96},{160,128},{192,160},{224,192},{256... | collective-permute-start | bytes 196616 | tf_op jit(solution)/shard_map/ppermute | solution.py:15
  9.4 4.9 %copy-start.14 = (s32[32,32]{0,1:T(8,128)}, s32[32,32]{0,1:T(8,128)S(1)}, u32[]{:S(2)}) copy-start(s32[32,32]{0,1:T(8,128)S(1)} %iota_add_fusion) | copy-start | bytes 12292
  9.8 7.7 %copy-start.6 = (pred[32,32,512]{2,0,1:T(32,128)(4,1)}, pred[32,32,512]{2,0,1:T(32,128)(4,1)S(1)}, u32[]{:S(2)}) copy-start(pred[32,32,512]{2,0,1:T(32,128)(4,1)S(1)} %broadcast_compare_fusion) | copy-start | bytes 1572868
  10.2 4.5 %copy-start.16 = (f32[32,32]{0,1:T(8,128)}, f32[32,32]{0,1:T(8,128)S(1)}, u32[]{:S(2)}) copy-start(f32[32,32]{0,1:T(8,128)S(1)} %convert_reduce_fusion) | copy-start | bytes 12292
  11.1 4.3 %copy-start.26 = (f32[1,511]{1,0:T(1,128)}, f32[1,511]{1,0:T(1,128)S(1)}, u32[]{:S(2)}) copy-start(f32[1,511]{1,0:T(1,128)S(1)} %slice.258) | copy-start | bytes 6136
  13.2 1.4 %copy-start.35 = (f32[8]{0:T(128)S(1)}, f32[8]{0:T(128)}, u32[]{:S(2)}) copy-start(f32[8]{0:T(128)} %param.25) | copy-start | bytes 100
  13.6 1.7 %copy-start.24 = (f32[1,512]{1,0:T(1,128)S(1)}, f32[1,512]{1,0:T(1,128)}, u32[]{:S(2)}) copy-start(f32[1,512]{1,0:T(1,128)} %param.31) | copy-start | bytes 6148
  13.6 1.8 %copy-start.1 = (f32[3,4,4,2048]{3,2,1,0:T(4,128)S(1)}, f32[3,4,4,2048]{3,2,1,0:T(4,128)}, u32[]{:S(2)}) copy-start(f32[3,4,4,2048]{3,2,1,0:T(4,128)} %param.20) | copy-start | bytes 1179652
  13.7 1.8 %copy-start.3 = (f32[4,3,4,4,2048]{4,3,2,1,0:T(4,128)S(1)}, f32[4,3,4,4,2048]{4,3,2,1,0:T(4,128)}, u32[]{:S(2)}) copy-start(f32[4,3,4,4,2048]{4,3,2,1,0:T(4,128)} %param.22) | copy-start | bytes 4718596
  15.4 2.1 %copy-start.30 = (f32[1,512]{1,0:T(1,128)}, f32[1,512]{1,0:T(1,128)S(1)}, u32[]{:S(2)}) copy-start(f32[1,512]{1,0:T(1,128)S(1)} %fusion.123) | copy-start | bytes 6148
  15.4 2.1 %copy-start.25 = (f32[1,512]{1,0:T(1,128)S(1)}, f32[1,512]{1,0:T(1,128)}, u32[]{:S(2)}) copy-start(f32[1,512]{1,0:T(1,128)} %param.32) | copy-start | bytes 6148
  15.4 2.1 %copy-start.28 = (f32[1,512]{1,0:T(1,128)S(1)}, f32[1,512]{1,0:T(1,128)}, u32[]{:S(2)}) copy-start(f32[1,512]{1,0:T(1,128)} %param.30) | copy-start | bytes 6148
  15.4 2.1 %copy-start.37 = (f32[4]{0:T(128)S(1)}, f32[4]{0:T(128)}, u32[]{:S(2)}) copy-start(f32[4]{0:T(128)} %constant.109.clone) | copy-start | bytes 52
  17.5 2.3 %copy-start.10 = (f32[3,4,4,2048]{3,2,1,0:T(4,128)S(1)}, f32[3,4,4,2048]{3,2,1,0:T(4,128)}, u32[]{:S(2)}) copy-start(f32[3,4,4,2048]{3,2,1,0:T(4,128)} %param.21) | copy-start | bytes 1179652
  20.2 25.0 %copy-start.36 = (f32[8]{0:T(128)S(1)}, f32[8]{0:T(128)}, u32[]{:S(2)}) copy-start(f32[8]{0:T(128)} %param.24) | copy-start | bytes 100
  21.4 31.1 %all-to-all-start = ((f32[32,1,128]{2,1,0:T(1,128)}), f32[32,1,128]{2,1,0:T(1,128)S(1)}, u32[]{:S(2)}, u32[]{:S(2)}) async-start(f32[32,1,128]{2,1,0:T(1,128)} %reshape.258), calls=%async_computation | async-start | bytes 32768 | tf_op jit(solution)/shard_map/all_to_all | solution.py:113
  39.3 14.5 %collective-permute-start.2 = (f32[2,4,1,2048]{3,2,1,0:T(1,128)S(1)}, f32[2,4,1,2048]{3,2,1,0:T(1,128)S(1)}, u32[]{:S(2)}, u32[]{:S(2)}) collective-permute-start(f32[2,4,1,2048]{3,2,1,0:T(1,128)S(1)} %slice.276), channel_id=1, source_target_pairs={{0,1},{1,2},{2,3},{3,4},{4,5},{5,6},{6,7},{7,8},{8,9},{9,10},{10,1... | collective-permute-start | bytes 196616 | tf_op jit(solution)/shard_map/ppermute | solution.py:15
  43.0 10.8 %collective-permute-start.3 = (f32[2,1,4,2048]{3,2,1,0:T(4,128)S(1)}, f32[2,1,4,2048]{3,2,1,0:T(4,128)S(1)}, u32[]{:S(2)}, u32[]{:S(2)}) collective-permute-start(f32[2,1,4,2048]{3,2,1,0:T(4,128)S(1)} %slice.283), channel_id=1, source_target_pairs={{0,32},{32,64},{64,96},{96,128},{128,160},{160,192},{192,224},{224... | collective-permute-start | bytes 196616 | tf_op jit(solution)/shard_map/ppermute | solution.py:15
  53.8 0.6 copy-start.11
  53.8 0.6 copy-start.12
  58.9 4.2 %copy-start.18 = (f32[32,4,32]{2,0,1:T(8,128)S(1)}, f32[32,4,32]{2,0,1:T(8,128)}, u32[]{:S(2)}) copy-start(f32[32,4,32]{2,0,1:T(8,128)} %copy.55) | copy-start | bytes 49156
  58.9 4.2 %copy-start.23 = (f32[32,1,32]{2,1,0:T(1,128)S(1)}, f32[32,1,32]{2,1,0:T(1,128)}, u32[]{:S(2)}) copy-start(f32[32,1,32]{2,1,0:T(1,128)} %get-tuple-element.74) | copy-start | bytes 12292
  58.9 4.2 %copy-start.8 = (s32[32,32]{1,0:T(8,128)S(1)}, s32[32,32]{1,0:T(8,128)}, u32[]{:S(2)}) copy-start(s32[32,32]{1,0:T(8,128)} %get-tuple-element.76) | copy-start | bytes 12292
  58.9 4.6 %copy-start.19 = (f32[32,32]{0,1:T(8,128)S(1)}, f32[32,32]{0,1:T(8,128)}, u32[]{:S(2)}) copy-start(f32[32,32]{0,1:T(8,128)} %copy.53) | copy-start | bytes 12292
  58.9 4.6 %copy-start.21 = (s32[32,32]{0,1:T(8,128)S(1)}, s32[32,32]{0,1:T(8,128)}, u32[]{:S(2)}) copy-start(s32[32,32]{0,1:T(8,128)} %copy.52) | copy-start | bytes 12292
  62.5 0.6 copy-start.13
  69.0 0.7 copy-start.2
  74.6 23.7 %all-to-all-start.1 = ((f32[32,2,32]{2,1,0:T(2,128)}), f32[32,2,32]{2,1,0:T(2,128)S(1)}, u32[]{:S(2)}, u32[]{:S(2)}) async-start(f32[32,2,32]{2,1,0:T(2,128)} %copy.59), calls=%async_computation.1 | async-start | bytes 65536 | tf_op jit(solution)/shard_map/all_to_all | solution.py:113
  84.9 13.4 %copy-start.7 = (pred[32,32,512]{2,0,1:T(32,128)(4,1)S(1)}, pred[32,32,512]{2,0,1:T(32,128)(4,1)}, u32[]{:S(2)}) copy-start(pred[32,32,512]{2,0,1:T(32,128)(4,1)} %copy-done.6) | copy-start | bytes 1572868
  88.4 11.2 %copy-start.27 = (f32[1,511]{1,0:T(1,128)S(1)}, f32[1,511]{1,0:T(1,128)}, u32[]{:S(2)}) copy-start(f32[1,511]{1,0:T(1,128)} %copy-done.26) | copy-start | bytes 6136
  88.4 11.2 %copy-start.29 = (f32[1,512]{1,0:T(1,128)S(1)}, f32[1,512]{1,0:T(1,128)}, u32[]{:S(2)}) copy-start(f32[1,512]{1,0:T(1,128)} %param.30) | copy-start | bytes 6148
  88.4 11.3 %copy-start.31 = (f32[1,512]{1,0:T(1,128)S(1)}, f32[1,512]{1,0:T(1,128)}, u32[]{:S(2)}) copy-start(f32[1,512]{1,0:T(1,128)} %copy-done.30) | copy-start | bytes 6148
  88.4 11.3 %copy-start.32 = (f32[1,512]{1,0:T(1,128)S(1)}, f32[1,512]{1,0:T(1,128)}, u32[]{:S(2)}) copy-start(f32[1,512]{1,0:T(1,128)} %param.33) | copy-start | bytes 6148
  88.5 12.2 %copy-start.15 = (s32[32,32]{0,1:T(8,128)S(1)}, s32[32,32]{0,1:T(8,128)}, u32[]{:S(2)}) copy-start(s32[32,32]{0,1:T(8,128)} %copy-done.14) | copy-start | bytes 12292
  88.6 14.3 %copy-start.17 = (f32[32,32]{0,1:T(8,128)S(1)}, f32[32,32]{0,1:T(8,128)}, u32[]{:S(2)}) copy-start(f32[32,32]{0,1:T(8,128)} %copy-done.16) | copy-start | bytes 12292
  88.6 23.9 %collective-permute-start.5 = (f32[2,4,1,2048]{3,2,1,0:T(1,128)S(1)}, f32[2,4,1,2048]{3,2,1,0:T(1,128)S(1)}, u32[]{:S(2)}, u32[]{:S(2)}) collective-permute-start(f32[2,4,1,2048]{3,2,1,0:T(1,128)S(1)} %slice.305), channel_id=1, source_target_pairs={{1,0},{2,1},{3,2},{4,3},{5,4},{6,5},{7,6},{8,7},{9,8},{10,9},{11,1... | collective-permute-start | bytes 196616 | tf_op jit(solution)/shard_map/ppermute | solution.py:15
  89.9 22.7 %collective-permute-start.4 = (f32[2,1,4,2048]{3,2,1,0:T(4,128)S(1)}, f32[2,1,4,2048]{3,2,1,0:T(4,128)S(1)}, u32[]{:S(2)}, u32[]{:S(2)}) collective-permute-start(f32[2,1,4,2048]{3,2,1,0:T(4,128)S(1)} %slice.301), channel_id=1, source_target_pairs={{32,0},{64,32},{96,64},{128,96},{160,128},{192,160},{224,192},{256... | collective-permute-start | bytes 196616 | tf_op jit(solution)/shard_map/ppermute | solution.py:15
  100.7 11.9 %copy-start.34 = (f32[1,512]{1,0:T(1,128)}, f32[1,512]{1,0:T(1,128)S(1)}, u32[]{:S(2)}) copy-start(f32[1,512]{1,0:T(1,128)S(1)} %get-tuple-element.50) | copy-start | bytes 6148
  103.6 22.1 %all-to-all-start.2 = ((f32[32,1,32]{2,1,0:T(1,128)}), f32[32,1,32]{2,1,0:T(1,128)}, u32[]{:S(2)}, u32[]{:S(2)}) async-start(f32[32,1,32]{2,1,0:T(1,128)} %copy.61), calls=%async_computation.2 | async-start | bytes 32768 | tf_op jit(solution)/shard_map/all_to_all | solution.py:113
  113.3 9.2 %collective-permute-start.7 = (f32[2,1,4,2048]{3,2,1,0:T(4,128)S(1)}, f32[2,1,4,2048]{3,2,1,0:T(4,128)S(1)}, u32[]{:S(2)}, u32[]{:S(2)}) collective-permute-start(f32[2,1,4,2048]{3,2,1,0:T(4,128)S(1)} %pad_maximum_fusion.10), channel_id=1, source_target_pairs={{0,32},{32,64},{64,96},{96,128},{128,160},{160,192},{192,224},{224... | collective-permute-start | bytes 196616 | tf_op jit(solution)/shard_map/ppermute | solution.py:15
  115.3 7.6 %copy-start.4 = (f32[3,4,4,2048]{3,2,1,0:T(4,128)}, f32[3,4,4,2048]{3,2,1,0:T(4,128)S(1)}, u32[]{:S(2)}) copy-start(f32[3,4,4,2048]{3,2,1,0:T(4,128)S(1)} %pad_maximum_fusion.1) | copy-start | bytes 1179652
  115.4 7.1 %collective-permute-start.6 = (f32[2,4,1,2048]{3,2,1,0:T(1,128)S(1)}, f32[2,4,1,2048]{3,2,1,0:T(1,128)S(1)}, u32[]{:S(2)}, u32[]{:S(2)}) collective-permute-start(f32[2,4,1,2048]{3,2,1,0:T(1,128)S(1)} %slice.315), channel_id=1, source_target_pairs={{0,1},{1,2},{2,3},{3,4},{4,5},{5,6},{6,7},{7,8},{8,9},{9,10},{10,1... | collective-permute-start | bytes 196616 | tf_op jit(solution)/shard_map/ppermute | solution.py:15
  122.9 2.8 %copy-start.9 = (s32[32,32]{1,0:T(8,128)S(1)}, s32[32,32]{1,0:T(8,128)}, u32[]{:S(2)}) copy-start(s32[32,32]{1,0:T(8,128)} %get-tuple-element.76) | copy-start | bytes 12292
  122.9 3.9 %copy-start.20 = (f32[32,32]{0,1:T(8,128)S(1)}, f32[32,32]{0,1:T(8,128)}, u32[]{:S(2)}) copy-start(f32[32,32]{0,1:T(8,128)} %copy.53) | copy-start | bytes 12292
  122.9 3.9 %copy-start.22 = (s32[32,32]{0,1:T(8,128)S(1)}, s32[32,32]{0,1:T(8,128)}, u32[]{:S(2)}) copy-start(s32[32,32]{0,1:T(8,128)} %copy.52) | copy-start | bytes 12292

commit v12 on v10

--- a/solution.py
+++ b/solution.py
@@ -126,13 +126,16 @@
     outgoing, h_field = lax.optimization_barrier((outgoing, h_field))
     incoming = exchange(outgoing)
 
-    material_hot = (
-        material[None] == jnp.arange(eps_inf.shape[0], dtype=jnp.int32)[:, None, None, None]
-    ).astype(jnp.float32)
-    eps_cell = jnp.einsum("m,mxyz->xyz", eps_inf, material_hot, precision=highest)
-    sigma_cell = jnp.einsum("m,mxyz->xyz", conductivity, material_hot, precision=highest)
-    strength_cell = jnp.einsum("pm,mxyz->pxyz", pole_strength, material_hot, precision=highest)
-    decay_cell = jnp.einsum("pm,mxyz->pxyz", pole_decay, material_hot, precision=highest)
+    def per_cell(table):
+        picked = jnp.broadcast_to(table[..., 0][..., None, None, None], table.shape[:-1] + grid_shape)
+        for index in range(1, table.shape[-1]):
+            picked = jnp.where(material == index, table[..., index][..., None, None, None], picked)
+        return picked
+
+    eps_cell = per_cell(eps_inf)
+    sigma_cell = per_cell(conductivity)
+    strength_cell = per_cell(pole_strength)
+    decay_cell = per_cell(pole_decay)
     cells = (eps_cell, sigma_cell, strength_cell, decay_cell)
 
     drive, polar_next = electric_base(e_field, h_field, polarization, cells)

time: 131 us -> 139 us (1.061)
  other arithmetic: 22.2 us -> 32.6 us
  matrix products: 16.6 us -> 11.9 us
  starting transfers between devices: 58.8 us -> 62.8 us
  waiting for transfers between devices: 15.9 us -> 12 us
  local copies, waits for them, and re-layouts: 14.3 us -> 17.1 us
    select_n x0 -> x1, other arithmetic: none -> 6.22 us  [per_cell(): jnp.where(material == index, table[..., index][..., None, None, None], pi...]
    mul x1, other arithmetic: 0.06 us -> 5.2 us  [electric_base(): TIME_STEP * sigma_cell[None] * e_field]
    slice x0 -> x3, local copies, waits for them, and re-layouts: none -> 4.69 us  [per_cell(): table[..., index][..., None, None, None]]
    all_to_all x3, waiting for transfers between devices: 12.5 us -> 8.47 us  [exchange(): return lax.all_to_all(blocks, 'gy', split_axis=0, concat_axis=0, tiled=True)]
    dot_general x4 -> x0, matrix products: 3.89 us -> none  [the longest x1 1.48 us: on_device(): jnp.einsum('pm,mxyz->pxyz', pole_decay, material_hot, precision=highest)]
    all_to_all x3, starting transfers between devices: 37.6 us -> 39.7 us  [exchange(): return lax.all_to_all(blocks, 'gy', split_axis=0, concat_axis=0, tiled=True)]
    ppermute x8, starting transfers between devices: 21.2 us -> 23.1 us  [passed_along(): lax.ppermute(value, axis, [(source, source + steps) for source in range(f...]
    add x1, other arithmetic: 2.01 us -> 3.42 us  [electric_base(): decay_cell[:, None] * polarization]
  transfers between devices with their start and end apart: 11 -> 11, of which waited for: 4 -> 4; matrix products, arithmetic and copies ran while one was open for 18% -> 27% of each run, Pallas kernels for 0% -> 0%
where the time goes in v12:
time: 139 us; the launch traced here: 138 us
  starting transfers between devices  62.8 us (45%)
  other arithmetic  32.6 us (23%)
  local copies, waits for them, and re-layouts  17.1 us (12%)
  waiting for transfers between devices  12 us (9%)
  matrix products  11.9 us (9%)
  between operations  1.46 us (1%)
    all_to_all x3, starting transfers between devices, exchange(): return lax.all_to_all(blocks, 'gy', split_axis=0, concat_axis=0, tiled=True)  39.7 us
    ppermute x8, starting transfers between devices, passed_along(): lax.ppermute(value, axis, [(source, source + steps) for source in range(f...  23.1 us
    all_to_all x3, waiting for transfers between devices, exchange(): return lax.all_to_all(blocks, 'gy', split_axis=0, concat_axis=0, tiled=True)  8.47 us
    select_n x1, other arithmetic, per_cell(): jnp.where(material == index, table[..., index][..., None, None, None], pi...  6.22 us
    mul x1, other arithmetic, electric_base(): TIME_STEP * sigma_cell[None] * e_field  5.2 us
    dot_general x2, matrix products, wire_of(): jnp.einsum('scr,scl->rl', row_hot, spread, precision=highest)  5.18 us
    slice x3, local copies, waits for them, and re-layouts, per_cell(): table[..., index][..., None, None, None]  4.69 us
    dot_general x2, matrix products, sample(): jnp.einsum('scr,rl->scl', row_hot, e_now[2].reshape(plane_rows, lanes), p...  3.99 us
  transfers between devices with their start and end apart: 11, of which 4 were waited for; matrix products, arithmetic and copies ran while one was open for 27% of the time, Pallas kernels for 0%

profile of v12, /device:TPU:16, one launch (start us, length us, event | category | flops | bytes accessed | tf_op | source)
XLA Modules:
  0.0 137.9 jit_solution(6356527324031181907)
XLA Ops:
  0.7 1.0 slice.357
  1.7 1.3 collective-permute-start
  3.0 0.8 slice.366
  3.9 3.9 %collective-permute-start.1 = (f32[2,1,4,2048]{3,2,1,0:T(4,128)S(1)}, f32[2,1,4,2048]{3,2,1,0:T(4,128)S(1)}, u32[]{:S(2)}, u32[]{:S(2)}) collective-permute-start(f32[2,1,4,2048]{3,2,1,0:T(4,128)S(1)} %slice.366), channel_id=1, source_target_pairs={{32,0},{64,32},{96,64},{128,96},{160,128},{192,160},{224,192},{256... | collective-permute-start | bytes 196616 | tf_op jit(solution)/shard_map/ppermute | solution.py:15
  7.8 1.0 convert_reduce_fusion.1
  8.8 0.7 multiply_add_fusion.5
  9.4 0.8 slice.354
  10.2 0.7 convert_element_type.34
  10.9 0.3 convert_reduce_fusion
  11.2 1.6 %fusion.131 = (f32[1]{0:T(128)}, f32[1]{0:T(128)}, f32[1]{0:T(128)}, f32[1]{0:T(128)}, f32[1]{0:T(128)}, /*index=5*/f32[1]{0:T(128)}, f32[1]{0:T(128)}, f32[1]{0:T(128)}) fusion(f32[8]{0:T(128)} %param.24), kind=kLoop, calls=%fused_computation.237 | loop fusion | bytes 64 | tf_op jit(solution)/shard_map/slice | solution.py:132
  12.8 1.6 %fusion.130 = (f32[1]{0:T(128)}, f32[1]{0:T(128)}, f32[1]{0:T(128)}, f32[1]{0:T(128)}, f32[1]{0:T(128)}, /*index=5*/f32[1]{0:T(128)}, f32[1]{0:T(128)}, f32[1]{0:T(128)}) fusion(f32[8]{0:T(128)} %param.25), kind=kLoop, calls=%fused_computation.236 | loop fusion | bytes 64 | tf_op jit(solution)/shard_map/slice | solution.py:132
  14.5 0.8 fusion.107
  15.2 1.4 %slice_reduce_fusion.7 = (f32[4]{0:T(128)S(1)}, f32[4]{0:T(128)S(1)}, f32[4]{0:T(128)S(1)}, f32[4]{0:T(128)S(1)}, f32[4]{0:T(128)S(1)}, /*index=5*/f32[4]{0:T(12...) fusion(f32[4,8]{1,0:T(4,128)} %param.26, ...), kind=kLoop, calls=%fused_computation.217 | loop fusion | bytes 512 | tf_op jit(solution)/shard_map/slice | solution.py:132
  16.7 6.2 %select_select_fusion.1 = (f32[4,4,2048]{2,1,0:T(4,128)S(1)}, pred[4,4,2048]{2,1,0:T(4,128)(4,1)S(1)}, pred[4,4,2048]{2,1,0:T(4,128)(4,1)S(1)}, pred[4,4,2048]{2...) fusion(f32[]{:T(128)} %bitcast.37, f32[]{:T(128)} %bitcast.36, ...), kind=kLoop, calls=%fused_computation.140 | loop fusion | flops 458752 | bytes 491552 | tf_op jit(solution)/shard_map/jit(_where)/select_n | solution.py:132
  22.9 5.2 %select_multiply_fusion.1 = f32[4,4,2048]{2,1,0:T(4,128)S(1)} fusion(pred[4,4,2048]{2,1,0:T(4,128)(4,1)S(1)} %get-tuple-element.72, pred[4,4,2048]{2,1,0:T(4,128)(4,1)S(1)} %get-tuple-element.73, pred[4,4,2048]{2,1,0:T(4,128)(4,1)S(1)} %get-tuple-element.74, pred[4,4,2048]{2,1,0:T(4,128)(4,1)S(1)} %get-tuple-element.75, ...), kind=kLoop, calls=%fused_computation.142 | loop fusion | flops 262144 | bytes 360480 | tf_op jit(solution)/shard_map/mul | solution.py:64
  28.1 1.0 select_multiply_fusion
  29.1 1.0 fusion.7
  30.9 0.2 fusion.62
  31.3 0.7 reshape.294
  32.0 17.9 %all-to-all-start = ((f32[32,1,128]{2,1,0:T(1,128)}), f32[32,1,128]{2,1,0:T(1,128)S(1)}, u32[]{:S(2)}, u32[]{:S(2)}) async-start(f32[32,1,128]{2,1,0:T(1,128)} %reshape.294), calls=%async_computation | async-start | bytes 32768 | tf_op jit(solution)/shard_map/all_to_all | solution.py:113
  49.9 3.7 %collective-permute-start.2 = (f32[2,4,1,2048]{3,2,1,0:T(1,128)S(1)}, f32[2,4,1,2048]{3,2,1,0:T(1,128)S(1)}, u32[]{:S(2)}, u32[]{:S(2)}) collective-permute-start(f32[2,4,1,2048]{3,2,1,0:T(1,128)S(1)} %slice.372), channel_id=1, source_target_pairs={{0,1},{1,2},{2,3},{3,4},{4,5},{5,6},{6,7},{7,8},{8,9},{9,10},{10,1... | collective-permute-start | bytes 196616 | tf_op jit(solution)/shard_map/ppermute | solution.py:15
  53.6 2.1 %collective-permute-start.3 = (f32[2,1,4,2048]{3,2,1,0:T(4,128)S(1)}, f32[2,1,4,2048]{3,2,1,0:T(4,128)S(1)}, u32[]{:S(2)}, u32[]{:S(2)}) collective-permute-start(f32[2,1,4,2048]{3,2,1,0:T(4,128)S(1)} %slice.379), channel_id=1, source_target_pairs={{0,32},{32,64},{64,96},{96,128},{128,160},{160,192},{192,224},{224... | collective-permute-start | bytes 196616 | tf_op jit(solution)/shard_map/ppermute | solution.py:15
  55.7 3.4 %multiply_add_fusion.1 = (f32[4,3,4,4,2048]{4,3,2,1,0:T(4,128)}, f32[3,4,4,2048]{3,2,1,0:T(4,128)S(1)}) fusion(f32[4,3,4,4,2048]{4,3,2,1,0:T(4,128)} %param.22, f32[3,4,4,2048]{3,2,1,0:T(4,128)S(1)} %copy-done, f32[4,4,4,2048]{3,2,1,0:T(4,128)S(1)} %get-tuple-element.79, f32[4,4,4,2048]{3,2,1,0:T(4,128)S(1)} %get-tuple-element.80), kind=kLoop, calls=%fused_computation.8 | loop fusion | flops 1867776 | bytes 4980736 | tf_op jit(solution)/shard_map/add | solution.py:60
  59.2 0.7 reshape.270
  59.9 3.2 %all-to-all-done = f32[32,1,128]{2,1,0:T(1,128)S(1)} async-done(((f32[32,1,128]{2,1,0:T(1,128)}), f32[32,1,128]{2,1,0:T(1,128)S(1)}, u32[]{:S(2)}, u32[]{:S(2)}) %all-to-all-start) | async-done | bytes 16416 | tf_op jit(solution)/shard_map/all_to_all | solution.py:113
  63.1 0.5 broadcast.432
  63.6 0.7 reduce.36
  64.5 0.2 fusion.48
  64.8 0.2 fusion.28
  65.0 0.6 copy.52
  65.6 0.6 fusion.128
  66.3 0.7 copy.50
  66.9 0.7 copy.49
  67.6 1.1 fusion.12
  68.7 2.5 %fusion.3 = f32[32,32]{1,0:T(8,128)S(1)} fusion(f32[256,128,1]{1,0,2:T(8,128)} %reshape.270, f32[32,32,256]{2,0,1:T(8,128)S(1)} %fusion.12, s32[32,32]{1,0:T(8,128)S(1)} %get-tuple-element.102), kind=kOutput, calls=%fused_computation.11 | convolution fusion | flops 403045376 | bytes 1187840 | tf_op jit(solution)/shard_map/scr,rl->scl/dot_general | solution.py:157
  71.2 0.6 copy-done.4
  71.8 0.3 fusion.26
  72.2 2.9 %fusion.6 = f32[256,128]{1,0:T(8,128)} fusion(f32[32,32,128]{2,1,0:T(8,128)S(1)} %fusion.26, f32[32,32]{0,1:T(8,128)S(1)} %copy-done.6, s32[32,32]{0,1:T(8,128)S(1)} %copy-done.8), kind=kOutput, calls=%fused_computation.16 | convolution fusion | flops 403210240 | bytes 663552 | tf_op jit(solution)/shard_map/scr,scl->rl/dot_general | solution.py:162
  75.1 1.6 %mul.212 = f32[1,4,4,2048]{3,2,1,0:T(4,128)} reshape(f32[256,128]{1,0:T(8,128)} %fusion.6) | data formatting | bytes 262144 | tf_op jit(solution)/shard_map/mul | solution.py:69
  76.7 0.9 add_dynamic-update-slice_fusion.1
  77.7 0.7 copy-done.1
  78.4 1.0 divide_add_fusion.1
  79.6 1.5 %fusion.4 = f32[32,32]{1,0:T(8,128)S(1)} fusion(f32[256,128,1]{1,0,2:T(8,128)S(1)} %reshape.272, f32[32,32,256]{2,0,1:T(8,128)S(1)} %fusion.12, s32[32,32]{1,0:T(8,128)S(1)} %get-tuple-element.102), kind=kOutput, calls=%fused_computation.12 | convolution fusion | flops 403045376 | bytes 1187840 | tf_op jit(solution)/shard_map/scr,rl->scl/dot_general | solution.py:157
  81.1 0.7 pad_maximum_fusion.11
  81.8 0.6 copy.56
  82.5 10.3 %all-to-all-start.1 = ((f32[32,2,32]{2,1,0:T(2,128)}), f32[32,2,32]{2,1,0:T(2,128)S(1)}, u32[]{:S(2)}, u32[]{:S(2)}) async-start(f32[32,2,32]{2,1,0:T(2,128)} %copy.56), calls=%async_computation.1 | async-start | bytes 65536 | tf_op jit(solution)/shard_map/all_to_all | solution.py:113
  92.7 3.4 %subtract_reduce_fusion = (f32[3,4,4,2048]{3,2,1,0:T(4,128)S(1)}, f32[4,3,4,4,2048]{4,3,2,1,0:T(4,128)}) fusion(f32[4,3,4,4,2048]{4,3,2,1,0:T(4,128)} %get-tuple-element.46, f32[3,4,4,2048]{3,2,1,0:T(4,128)S(1)} %bitcast.226, f32[4,4,4,2048]{3,2,1,0:T(4,128)S(1)} %get-tuple-element.79, f32[4,4,4,2048]{3,2,1,0:T(4,128)S(1)} %get-tuple-element.80), kind=kLoop, calls=%fused_computation.5 | loop fusion | flops 1867776 | bytes 4980736 | tf_op jit(solution)/shard_map/reduce_sum | solution.py:63
  96.4 1.3 collective-permute-start.5
  97.7 5.4 %collective-permute-start.4 = (f32[2,1,4,2048]{3,2,1,0:T(4,128)S(1)}, f32[2,1,4,2048]{3,2,1,0:T(4,128)S(1)}, u32[]{:S(2)}, u32[]{:S(2)}) collective-permute-start(f32[2,1,4,2048]{3,2,1,0:T(4,128)S(1)} %slice.429), channel_id=1, source_target_pairs={{32,0},{64,32},{96,64},{128,96},{160,128},{192,160},{224,192},{256... | collective-permute-start | bytes 196616 | tf_op jit(solution)/shard_map/ppermute | solution.py:15
  103.1 3.0 %all-to-all-done.1 = f32[32,2,32]{2,1,0:T(2,128)S(1)} async-done(((f32[32,2,32]{2,1,0:T(2,128)}), f32[32,2,32]{2,1,0:T(2,128)S(1)}, u32[]{:S(2)}, u32[]{:S(2)}) %all-to-all-start.1) | async-done | bytes 8224 | tf_op jit(solution)/shard_map/all_to_all | solution.py:113
  106.2 0.7 fusion.1
  107.4 0.7 fusion.121
  108.1 1.0 fusion
  109.1 0.7 transpose_reshape.3
  109.8 11.5 %all-to-all-start.2 = ((f32[32,1,32]{2,1,0:T(1,128)}), f32[32,1,32]{2,1,0:T(1,128)S(1)}, u32[]{:S(2)}, u32[]{:S(2)}) async-start(f32[32,1,32]{2,1,0:T(1,128)} %transpose_reshape.3), calls=%async_computation.2 | async-start | bytes 32768 | tf_op jit(solution)/shard_map/all_to_all | solution.py:113
  122.0 1.9 %collective-permute-start.7 = (f32[2,1,4,2048]{3,2,1,0:T(4,128)S(1)}, f32[2,1,4,2048]{3,2,1,0:T(4,128)S(1)}, u32[]{:S(2)}, u32[]{:S(2)}) collective-permute-start(f32[2,1,4,2048]{3,2,1,0:T(4,128)S(1)} %pad_maximum_fusion.10), channel_id=1, source_target_pairs={{0,32},{32,64},{64,96},{96,128},{128,160},{160,192},{192,224},{224... | collective-permute-start | bytes 196616 | tf_op jit(solution)/shard_map/ppermute | solution.py:15
  124.2 3.5 %collective-permute-start.6 = (f32[2,4,1,2048]{3,2,1,0:T(1,128)S(1)}, f32[2,4,1,2048]{3,2,1,0:T(1,128)S(1)}, u32[]{:S(2)}, u32[]{:S(2)}) collective-permute-start(f32[2,4,1,2048]{3,2,1,0:T(1,128)S(1)} %slice.443), channel_id=1, source_target_pairs={{0,1},{1,2},{2,3},{3,4},{4,5},{5,6},{6,7},{7,8},{8,9},{9,10},{10,1... | collective-permute-start | bytes 196616 | tf_op jit(solution)/shard_map/ppermute | solution.py:15
  127.7 3.6 %collective-permute-done.7 = f32[2,1,4,2048]{3,2,1,0:T(4,128)S(1)} collective-permute-done((f32[2,1,4,2048]{3,2,1,0:T(4,128)S(1)}, f32[2,1,4,2048]{3,2,1,0:T(4,128)S(1)}, u32[]{:S(2)}, u32[]{:S(2)}) %collective-permute-start.7) | collective-permute-done | bytes 65568 | tf_op jit(solution)/shard_map/ppermute | solution.py:15
  131.3 0.3 fusion.36
  131.8 0.2 fusion.30
  132.0 2.3 %all-to-all-done.2 = f32[32,1,32]{2,1,0:T(1,128)S(1)} async-done(((f32[32,1,32]{2,1,0:T(1,128)}), f32[32,1,32]{2,1,0:T(1,128)S(1)}, u32[]{:S(2)}, u32[]{:S(2)}) %all-to-all-start.2) | async-done | bytes 4128 | tf_op jit(solution)/shard_map/all_to_all | solution.py:113
  134.4 0.3 fusion.25
  134.7 2.3 %fusion.5 = f32[256,128]{1,0:T(8,128)S(1)} fusion(f32[32,32,128]{2,1,0:T(8,128)S(1)} %fusion.25, f32[32,32]{0,1:T(8,128)S(1)} %copy-done.7, s32[32,32]{0,1:T(8,128)S(1)} %copy-done.9), kind=kOutput, calls=%fused_computation.14 | convolution fusion | flops 403210240 | bytes 663552 | tf_op jit(solution)/shard_map/scr,scl->rl/dot_general | solution.py:162
  137.1 0.8 divide_add_fusion
  (104 shorter events, 3.1 us)
Async XLA Ops:
  0.6 28.5 %copy-start.26 = (f32[4]{0:T(128)S(1)}, f32[4]{0:T(128)}, u32[]{:S(2)}) copy-start(f32[4]{0:T(128)} %constant.119.clone) | copy-start | bytes 52
  0.6 29.5 %copy-start = (f32[3,4,4,2048]{3,2,1,0:T(4,128)S(1)}, f32[3,4,4,2048]{3,2,1,0:T(4,128)}, u32[]{:S(2)}) copy-start(f32[3,4,4,2048]{3,2,1,0:T(4,128)} %param.20) | copy-start | bytes 1179652
  0.7 28.4 %copy-start.14 = (f32[1,512]{1,0:T(1,128)S(1)}, f32[1,512]{1,0:T(1,128)}, u32[]{:S(2)}) copy-start(f32[1,512]{1,0:T(1,128)} %param.32) | copy-start | bytes 6148
  0.7 28.4 %copy-start.18 = (f32[1,512]{1,0:T(1,128)S(1)}, f32[1,512]{1,0:T(1,128)}, u32[]{:S(2)}) copy-start(f32[1,512]{1,0:T(1,128)} %param.30) | copy-start | bytes 6148
  1.7 28.7 %collective-permute-start = (f32[2,4,1,2048]{3,2,1,0:T(1,128)S(1)}, f32[2,4,1,2048]{3,2,1,0:T(1,128)S(1)}, u32[]{:S(2)}, u32[]{:S(2)}) collective-permute-start(f32[2,4,1,2048]{3,2,1,0:T(1,128)S(1)} %slice.357), channel_id=1, source_target_pairs={{1,0},{2,1},{3,2},{4,3},{5,4},{6,5},{7,6},{8,7},{9,8},{10,9},{11,1... | collective-permute-start | bytes 196616 | tf_op jit(solution)/shard_map/ppermute | solution.py:15
  3.9 26.6 %collective-permute-start.1 = (f32[2,1,4,2048]{3,2,1,0:T(4,128)S(1)}, f32[2,1,4,2048]{3,2,1,0:T(4,128)S(1)}, u32[]{:S(2)}, u32[]{:S(2)}) collective-permute-start(f32[2,1,4,2048]{3,2,1,0:T(4,128)S(1)} %slice.366), channel_id=1, source_target_pairs={{32,0},{64,32},{96,64},{128,96},{160,128},{192,160},{224,192},{256... | collective-permute-start | bytes 196616 | tf_op jit(solution)/shard_map/ppermute | solution.py:15
  9.4 20.8 %copy-start.23 = (s32[512]{0:T(512)}, s32[512]{0:T(512)S(1)}, u32[]{:S(2)}) copy-start(s32[512]{0:T(512)S(1)} %multiply_add_fusion.5) | copy-start | bytes 6148
  10.2 6.5 %copy-start.16 = (f32[1,511]{1,0:T(1,128)}, f32[1,511]{1,0:T(1,128)S(1)}, u32[]{:S(2)}) copy-start(f32[1,511]{1,0:T(1,128)S(1)} %slice.354) | copy-start | bytes 6136
  11.2 5.5 %copy-start.12 = (f32[1024]{0:T(1024)}, f32[1024]{0:T(1024)S(1)}, u32[]{:S(2)}) copy-start(f32[1024]{0:T(1024)S(1)} %convert_reduce_fusion) | copy-start | bytes 12292
  15.2 15.0 %copy-start.20 = (f32[1,512]{1,0:T(1,128)}, f32[1,512]{1,0:T(1,128)S(1)}, u32[]{:S(2)}) copy-start(f32[1,512]{1,0:T(1,128)S(1)} %fusion.107) | copy-start | bytes 6148
  28.1 2.3 %copy-start.3 = (f32[3,4,4,2048]{3,2,1,0:T(4,128)S(1)}, f32[3,4,4,2048]{3,2,1,0:T(4,128)}, u32[]{:S(2)}) copy-start(f32[3,4,4,2048]{3,2,1,0:T(4,128)} %param.21) | copy-start | bytes 1179652
  32.0 31.1 %all-to-all-start = ((f32[32,1,128]{2,1,0:T(1,128)}), f32[32,1,128]{2,1,0:T(1,128)S(1)}, u32[]{:S(2)}, u32[]{:S(2)}) async-start(f32[32,1,128]{2,1,0:T(1,128)} %reshape.294), calls=%async_computation | async-start | bytes 32768 | tf_op jit(solution)/shard_map/all_to_all | solution.py:113
  49.9 14.5 %collective-permute-start.2 = (f32[2,4,1,2048]{3,2,1,0:T(1,128)S(1)}, f32[2,4,1,2048]{3,2,1,0:T(1,128)S(1)}, u32[]{:S(2)}, u32[]{:S(2)}) collective-permute-start(f32[2,4,1,2048]{3,2,1,0:T(1,128)S(1)} %slice.372), channel_id=1, source_target_pairs={{0,1},{1,2},{2,3},{3,4},{4,5},{5,6},{6,7},{7,8},{8,9},{9,10},{10,1... | collective-permute-start | bytes 196616 | tf_op jit(solution)/shard_map/ppermute | solution.py:15
  53.6 10.8 %collective-permute-start.3 = (f32[2,1,4,2048]{3,2,1,0:T(4,128)S(1)}, f32[2,1,4,2048]{3,2,1,0:T(4,128)S(1)}, u32[]{:S(2)}, u32[]{:S(2)}) collective-permute-start(f32[2,1,4,2048]{3,2,1,0:T(4,128)S(1)} %slice.379), channel_id=1, source_target_pairs={{0,32},{32,64},{64,96},{96,128},{128,160},{160,192},{192,224},{224... | collective-permute-start | bytes 196616 | tf_op jit(solution)/shard_map/ppermute | solution.py:15
  67.6 4.2 %copy-start.5 = (f32[32,4,32]{2,0,1:T(8,128)S(1)}, f32[32,4,32]{2,0,1:T(8,128)}, u32[]{:S(2)}) copy-start(f32[32,4,32]{2,0,1:T(8,128)} %copy.52) | copy-start | bytes 49156
  67.6 4.2 %copy-start.10 = (f32[32,1,32]{2,1,0:T(1,128)S(1)}, f32[32,1,32]{2,1,0:T(1,128)}, u32[]{:S(2)}) copy-start(f32[32,1,32]{2,1,0:T(1,128)} %get-tuple-element.100) | copy-start | bytes 12292
  67.6 4.6 %copy-start.6 = (f32[32,32]{0,1:T(8,128)S(1)}, f32[32,32]{0,1:T(8,128)}, u32[]{:S(2)}) copy-start(f32[32,32]{0,1:T(8,128)} %copy.50) | copy-start | bytes 12292
  67.6 4.6 %copy-start.8 = (s32[32,32]{0,1:T(8,128)S(1)}, s32[32,32]{0,1:T(8,128)}, u32[]{:S(2)}) copy-start(s32[32,32]{0,1:T(8,128)} %copy.49) | copy-start | bytes 12292
  71.2 0.6 copy-start.4
  77.7 0.7 copy-start.1
  82.5 23.7 %all-to-all-start.1 = ((f32[32,2,32]{2,1,0:T(2,128)}), f32[32,2,32]{2,1,0:T(2,128)S(1)}, u32[]{:S(2)}, u32[]{:S(2)}) async-start(f32[32,2,32]{2,1,0:T(2,128)} %copy.56), calls=%async_computation.1 | async-start | bytes 65536 | tf_op jit(solution)/shard_map/all_to_all | solution.py:113
  92.7 13.5 %copy-start.24 = (s32[512]{0:T(512)S(1)}, s32[512]{0:T(512)}, u32[]{:S(2)}) copy-start(s32[512]{0:T(512)} %copy-done.23) | copy-start | bytes 6148
  96.2 10.8 %copy-start.11 = (f32[1,512]{1,0:T(1,128)S(1)}, f32[1,512]{1,0:T(1,128)}, u32[]{:S(2)}) copy-start(f32[1,512]{1,0:T(1,128)} %param.31) | copy-start | bytes 6148
  96.2 10.8 %copy-start.15 = (f32[1,512]{1,0:T(1,128)S(1)}, f32[1,512]{1,0:T(1,128)}, u32[]{:S(2)}) copy-start(f32[1,512]{1,0:T(1,128)} %param.32) | copy-start | bytes 6148
  96.2 10.8 %copy-start.17 = (f32[1,511]{1,0:T(1,128)S(1)}, f32[1,511]{1,0:T(1,128)}, u32[]{:S(2)}) copy-start(f32[1,511]{1,0:T(1,128)} %copy-done.16) | copy-start | bytes 6136
  96.2 10.8 %copy-start.19 = (f32[1,512]{1,0:T(1,128)S(1)}, f32[1,512]{1,0:T(1,128)}, u32[]{:S(2)}) copy-start(f32[1,512]{1,0:T(1,128)} %param.30) | copy-start | bytes 6148
  96.2 10.9 %copy-start.21 = (f32[1,512]{1,0:T(1,128)S(1)}, f32[1,512]{1,0:T(1,128)}, u32[]{:S(2)}) copy-start(f32[1,512]{1,0:T(1,128)} %copy-done.20) | copy-start | bytes 6148
  96.2 10.9 %copy-start.22 = (f32[1,512]{1,0:T(1,128)S(1)}, f32[1,512]{1,0:T(1,128)}, u32[]{:S(2)}) copy-start(f32[1,512]{1,0:T(1,128)} %param.33) | copy-start | bytes 6148
  96.2 12.8 %copy-start.13 = (f32[1024]{0:T(1024)S(1)}, f32[1024]{0:T(1024)}, u32[]{:S(2)}) copy-start(f32[1024]{0:T(1024)} %copy-done.12) | copy-start | bytes 12292
  96.4 24.9 %collective-permute-start.5 = (f32[2,4,1,2048]{3,2,1,0:T(1,128)S(1)}, f32[2,4,1,2048]{3,2,1,0:T(1,128)S(1)}, u32[]{:S(2)}, u32[]{:S(2)}) collective-permute-start(f32[2,4,1,2048]{3,2,1,0:T(1,128)S(1)} %slice.433), channel_id=1, source_target_pairs={{1,0},{2,1},{3,2},{4,3},{5,4},{6,5},{7,6},{8,7},{9,8},{10,9},{11,1... | collective-permute-start | bytes 196616 | tf_op jit(solution)/shard_map/ppermute | solution.py:15
  97.7 23.6 %collective-permute-start.4 = (f32[2,1,4,2048]{3,2,1,0:T(4,128)S(1)}, f32[2,1,4,2048]{3,2,1,0:T(4,128)S(1)}, u32[]{:S(2)}, u32[]{:S(2)}) collective-permute-start(f32[2,1,4,2048]{3,2,1,0:T(4,128)S(1)} %slice.429), channel_id=1, source_target_pairs={{32,0},{64,32},{96,64},{128,96},{160,128},{192,160},{224,192},{256... | collective-permute-start | bytes 196616 | tf_op jit(solution)/shard_map/ppermute | solution.py:15
  108.1 13.9 %copy-start.25 = (f32[1,512]{1,0:T(1,128)}, f32[1,512]{1,0:T(1,128)S(1)}, u32[]{:S(2)}) copy-start(f32[1,512]{1,0:T(1,128)S(1)} %get-tuple-element.66) | copy-start | bytes 6148
  109.8 24.6 %all-to-all-start.2 = ((f32[32,1,32]{2,1,0:T(1,128)}), f32[32,1,32]{2,1,0:T(1,128)S(1)}, u32[]{:S(2)}, u32[]{:S(2)}) async-start(f32[32,1,32]{2,1,0:T(1,128)} %transpose_reshape.3), calls=%async_computation.2 | async-start | bytes 32768 | tf_op jit(solution)/shard_map/all_to_all | solution.py:113
  122.0 9.2 %collective-permute-start.7 = (f32[2,1,4,2048]{3,2,1,0:T(4,128)S(1)}, f32[2,1,4,2048]{3,2,1,0:T(4,128)S(1)}, u32[]{:S(2)}, u32[]{:S(2)}) collective-permute-start(f32[2,1,4,2048]{3,2,1,0:T(4,128)S(1)} %pad_maximum_fusion.10), channel_id=1, source_target_pairs={{0,32},{32,64},{64,96},{96,128},{128,160},{160,192},{192,224},{224... | collective-permute-start | bytes 196616 | tf_op jit(solution)/shard_map/ppermute | solution.py:15
  124.1 7.6 %copy-start.2 = (f32[3,4,4,2048]{3,2,1,0:T(4,128)}, f32[3,4,4,2048]{3,2,1,0:T(4,128)S(1)}, u32[]{:S(2)}) copy-start(f32[3,4,4,2048]{3,2,1,0:T(4,128)S(1)} %pad_maximum_fusion.1) | copy-start | bytes 1179652
  124.2 7.1 %collective-permute-start.6 = (f32[2,4,1,2048]{3,2,1,0:T(1,128)S(1)}, f32[2,4,1,2048]{3,2,1,0:T(1,128)S(1)}, u32[]{:S(2)}, u32[]{:S(2)}) collective-permute-start(f32[2,4,1,2048]{3,2,1,0:T(1,128)S(1)} %slice.443), channel_id=1, source_target_pairs={{0,1},{1,2},{2,3},{3,4},{4,5},{5,6},{6,7},{7,8},{8,9},{9,10},{10,1... | collective-permute-start | bytes 196616 | tf_op jit(solution)/shard_map/ppermute | solution.py:15
  131.7 3.0 %copy-start.7 = (f32[32,32]{0,1:T(8,128)S(1)}, f32[32,32]{0,1:T(8,128)}, u32[]{:S(2)}) copy-start(f32[32,32]{0,1:T(8,128)} %copy.50) | copy-start | bytes 12292
  131.7 3.0 %copy-start.9 = (s32[32,32]{0,1:T(8,128)S(1)}, s32[32,32]{0,1:T(8,128)}, u32[]{:S(2)}) copy-start(s32[32,32]{0,1:T(8,128)} %copy.49) | copy-start | bytes 12292

commit v13 on v10

--- a/solution.py
+++ b/solution.py
@@ -160,12 +160,18 @@
 
     sample_0 = sample(e_field)
     curr_cell_1 = recv_curr + recv_gain * (sample_0 - recv_drop)
-    e_field = electric_finish(e_field, drive, wire_of(curr_cell_1), cells)
+    spread_1 = jnp.where(lane_hot, curr_cell_1[:, :, None], 0.0)
+    wire_plane = jnp.einsum("scr,scl->rl", row_hot, spread_1, precision=highest)
+    ez_plane = e_field[2].reshape(plane_rows, lanes) + (
+        drive[2].reshape(plane_rows, lanes) + -TIME_STEP * wire_plane
+    ) / eps_cell.reshape(plane_rows, lanes)
+    picked = jnp.einsum("scr,rl->scl", row_hot, ez_plane, precision=highest)
+    sample_1 = jnp.sum(jnp.where(lane_hot, picked, 0.0), axis=2)
     polarization = polar_next
-    sample_1 = sample(e_field)
 
     back = jnp.stack([sample_0, sample_1], axis=1)
-    back, e_field, h_field, polarization = lax.optimization_barrier((back, e_field, h_field, polarization))
+    back, drive, wire_plane, h_field, polarization = lax.optimization_barrier((back, drive, wire_plane, h_field, polarization))
+    e_field = electric_finish(e_field, drive, wire_plane.reshape(grid_shape), cells)
     returned = from_slots(exchange(back))
     seg_sample_0, seg_sample_1 = returned[0], returned[1]
     curr_1 = curr_0 + gain_row * (seg_sample_0 - drop_0)

time: 131 us -> 139 us (1.061)
  starting transfers between devices: 58.8 us -> 65.4 us
  local copies, waits for them, and re-layouts: 14.3 us -> 20.9 us
  waiting for transfers between devices: 15.9 us -> 9.48 us
  other arithmetic: 22.2 us -> 24.2 us
    all_to_all x3, waiting for transfers between devices: 12.5 us -> 5.9 us  [exchange(): return lax.all_to_all(blocks, 'gy', split_axis=0, concat_axis=0, tiled=True)]
    dot_general x0 -> x2, matrix products: none -> 3.86 us  [the longest x1 2.3 us: on_device(): wire_plane = jnp.einsum('scr,scl->rl', row_hot, spread_1, precision=highest)]
    ppermute x8, starting transfers between devices: 21.2 us -> 24.6 us  [passed_along(): lax.ppermute(value, axis, [(source, source + steps) for source in range(f...]
    all_to_all x3, starting transfers between devices: 37.6 us -> 40.8 us  [exchange(): return lax.all_to_all(blocks, 'gy', split_axis=0, concat_axis=0, tiled=True)]
    dot_general x2 -> x1, matrix products: 5.25 us -> 2.3 us  [wire_of(): jnp.einsum('scr,scl->rl', row_hot, spread, precision=highest)]
    dot_general x2 -> x1, matrix products: 4.72 us -> 2.25 us  [sample(): jnp.einsum('scr,rl->scl', row_hot, e_now[2].reshape(plane_rows, lanes), p...]
    another operation x0 -> x1, local copies, waits for them, and re-layouts: none -> 1.62 us  [on_device(): drive[2].reshape(plane_rows, lanes) + -TIME_STEP * wire_plane]
    all_to_all x1, other arithmetic: 0.6 us -> 2.03 us  [exchange(): return lax.all_to_all(blocks, 'gy', split_axis=0, concat_axis=0, tiled=True)]
  transfers between devices with their start and end apart: 11 -> 11, of which waited for: 4 -> 3; matrix products, arithmetic and copies ran while one was open for 18% -> 24% of each run, Pallas kernels for 0% -> 0%
where the time goes in v13:
time: 139 us; the launch traced here: 137 us
  starting transfers between devices  65.4 us (47%)
  other arithmetic  24.2 us (17%)
  local copies, waits for them, and re-layouts  20.9 us (15%)
  matrix products  16 us (12%)
  waiting for transfers between devices  9.48 us (7%)
  between operations  1.5 us (1%)
    all_to_all x3, starting transfers between devices, exchange(): return lax.all_to_all(blocks, 'gy', split_axis=0, concat_axis=0, tiled=True)  40.8 us
    ppermute x8, starting transfers between devices, passed_along(): lax.ppermute(value, axis, [(source, source + steps) for source in range(f...  24.6 us
    all_to_all x3, waiting for transfers between devices, exchange(): return lax.all_to_all(blocks, 'gy', split_axis=0, concat_axis=0, tiled=True)  5.9 us
    reduce_sum x1, other arithmetic, electric_base(): change = jnp.sum(polar_new - polarization, axis=0)  3.8 us
    ppermute x8, waiting for transfers between devices, passed_along(): lax.ppermute(value, axis, [(source, source + steps) for source in range(f...  3.58 us
  transfers between devices with their start and end apart: 11, of which 3 were waited for; matrix products, arithmetic and copies ran while one was open for 24% of the time, Pallas kernels for 0%

profile of v13, /device:TPU:16, one launch (start us, length us, event | category | flops | bytes accessed | tf_op | source)
XLA Modules:
  0.0 137.4 jit_solution(5219835235420447922)
XLA Ops:
  0.7 1.0 slice.262
  1.7 1.3 collective-permute-start
  3.0 0.8 slice.271
  3.9 3.9 %collective-permute-start.1 = (f32[2,1,4,2048]{3,2,1,0:T(4,128)S(1)}, f32[2,1,4,2048]{3,2,1,0:T(4,128)S(1)}, u32[]{:S(2)}, u32[]{:S(2)}) collective-permute-start(f32[2,1,4,2048]{3,2,1,0:T(4,128)S(1)} %slice.271), channel_id=1, source_target_pairs={{32,0},{64,32},{96,64},{128,96},{160,128},{192,160},{224,192},{256... | collective-permute-start | bytes 196616 | tf_op jit(solution)/shard_map/ppermute | solution.py:15
  7.7 0.8 slice.259
  8.5 1.0 convert_reduce_fusion.1
  9.5 0.7 multiply_add_fusion.5
  10.2 0.7 convert_element_type.35
  11.2 1.5 %fusion.9 = f32[1,4,4,2048]{3,0,2,1:T(1,128)S(1)} fusion(s32[4,4,2048]{2,1,0:T(4,128)} %param.23, f32[8]{0:T(128)} %param.25), kind=kOutput, calls=%fused_computation.23 | convolution fusion | flops 3407872 | bytes 262176 | tf_op jit(solution)/shard_map/m,mxyz->xyz/dot_general | solution.py:133
  12.7 0.7 bitcast_multiply_fusion
  13.4 1.5 %convolution_bitcast_fusion.1 = f32[4,4,4,2048]{3,0,2,1:T(4,128)S(1)} fusion(s32[4,4,2048]{2,1,0:T(4,128)} %param.23, f32[4,8]{1,0:T(4,128)S(1)} %copy-done), kind=kOutput, calls=%fused_computation.2 | convolution fusion | flops 12845056 | bytes 655488 | tf_op jit(solution)/shard_map/pm,mxyz->pxyz/dot_general | solution.py:135
  15.3 0.6 fusion
  16.4 1.9 %multiply_add_fusion.1 = (f32[4,3,4,4,2048]{4,3,2,1,0:T(4,128)S(1)}, f32[3,4,4,2048]{3,2,1,0:T(4,128)}) fusion(f32[4,3,4,4,2048]{4,3,2,1,0:T(4,128)S(1)} %copy-done.4, f32[3,4,4,2048]{3,2,1,0:T(4,128)S(1)} %copy-done.1, f32[4,4,4,2048]{3,2,1,0:T(4,128)S(1)} %copy.56, f32[4,4,4,2048]{3,2,1,0:T(4,128)S(1)} %copy.55), kind=kLoop, calls=%fused_computation.11 | loop fusion | flops 1867776 | bytes 4980736 | tf_op jit(solution)/shard_map/add | solution.py:60
  18.3 1.0 fusion.7
  19.6 1.1 fusion.144
  21.0 1.2 fusion.68
  22.3 0.6 slice.284
  22.9 0.7 slice.277
  23.6 0.7 reshape.242
  24.3 18.0 %all-to-all-start = ((f32[32,1,128]{2,1,0:T(1,128)}), f32[32,1,128]{2,1,0:T(1,128)}, u32[]{:S(2)}, u32[]{:S(2)}) async-start(f32[32,1,128]{2,1,0:T(1,128)} %reshape.242), calls=%async_computation | async-start | bytes 32768 | tf_op jit(solution)/shard_map/all_to_all | solution.py:113
  42.3 3.6 %collective-permute-start.2 = (f32[2,4,1,2048]{3,2,1,0:T(1,128)}, f32[2,4,1,2048]{3,2,1,0:T(1,128)S(1)}, u32[]{:S(2)}, u32[]{:S(2)}) collective-permute-start(f32[2,4,1,2048]{3,2,1,0:T(1,128)} %slice.277), channel_id=1, source_target_pairs={{0,1},{1,2},{2,3},{3,4},{4,5},{5,6},{6,7},{7,8},{8,9},{9,10},{10,1... | collective-permute-start | bytes 196616 | tf_op jit(solution)/shard_map/ppermute | solution.py:15
  46.0 2.1 %collective-permute-start.3 = (f32[2,1,4,2048]{3,2,1,0:T(4,128)}, f32[2,1,4,2048]{3,2,1,0:T(4,128)}, u32[]{:S(2)}, u32[]{:S(2)}) collective-permute-start(f32[2,1,4,2048]{3,2,1,0:T(4,128)} %slice.284), channel_id=1, source_target_pairs={{0,32},{32,64},{64,96},{96,128},{128,160},{160,192},{192,224},{224... | collective-permute-start | bytes 196616 | tf_op jit(solution)/shard_map/ppermute | solution.py:15
  48.1 1.2 fusion.8
  49.4 0.7 reshape.226
  50.1 0.7 reshape.233
  50.8 0.7 reshape_squeeze.7
  51.6 3.9 %all-to-all-done = f32[32,1,128]{2,1,0:T(1,128)} async-done(((f32[32,1,128]{2,1,0:T(1,128)}), f32[32,1,128]{2,1,0:T(1,128)}, u32[]{:S(2)}, u32[]{:S(2)}) %all-to-all-start) | async-done | bytes 16416 | tf_op jit(solution)/shard_map/all_to_all | solution.py:113
  56.1 2.0 %reduce.4 = f32[32,128]{1,0:T(8,128)} reduce(f32[32,1,128]{2,1,0:T(1,128)} %all-to-all-done, f32[]{:T(128)} %broadcast.199), dimensions={1}, to_apply=%all_to_all.9.reduce_sub_computation | reduce | bytes 32772 | tf_op jit(solution)/shard_map/all_to_all | solution.py:113
  58.1 1.4 %reshape.243 = f32[32,4,32]{2,1,0:T(4,128)} reshape(f32[32,128]{1,0:T(8,128)} %reduce.4) | data formatting | bytes 32768 | tf_op jit(solution)/shard_map/optimization_barrier | solution.py:139
  59.6 0.9 slice_bitcast_fusion.5
  60.5 1.0 fusion.54
  61.8 0.6 fusion.145
  62.4 0.6 copy.60
  63.0 0.6 compare_convert_fusion
  63.6 0.6 add_select_fusion.1
  64.3 1.4 %copy.58 = f32[32,32]{0,1:T(8,128)} copy(f32[32,32]{1,0:T(8,128)} %compare_convert_fusion) | data formatting | bytes 8192 | tf_op jit(solution)/shard_map/convert_element_type | solution.py:150
  65.7 1.4 %copy.57 = s32[32,32]{0,1:T(8,128)} copy(s32[32,32]{1,0:T(8,128)} %get-tuple-element.79) | data formatting | bytes 8192 | tf_op jit(solution)/shard_map/jit(floor_divide)/jit(_where)/select_n | solution.py:149
  67.0 0.7 slice.290
  67.7 1.6 %reshape_squeeze.8 = f32[256,128]{1,0:T(8,128)} reshape(f32[1,4,4,2048]{3,2,1,0:T(4,128)} %slice.290) | data formatting | bytes 262144 | tf_op jit(solution)/shard_map/reshape;squeeze | solution.py:166
  69.3 1.1 fusion.14
  70.5 2.3 %fusion.4 = f32[32,32]{1,0:T(8,128)S(1)} fusion(f32[256,128,1]{1,0,2:T(8,128)S(1)} %copy-done.13, f32[32,32,256]{2,0,1:T(8,128)S(1)} %fusion.14, s32[32,32]{1,0:T(8,128)} %get-tuple-element.78), kind=kOutput, calls=%fused_computation.14 | convolution fusion | flops 403045376 | bytes 1187840 | tf_op jit(solution)/shard_map/scr,rl->scl/dot_general | solution.py:154
  73.2 2.3 %convolution_bitcast_fusion.3 = f32[256,128]{1,0:T(8,128)S(1)} fusion(f32[32,32,128]{2,1,0:T(8,128)S(1)} %fusion.28, f32[32,32]{0,1:T(8,128)S(1)} %copy-done.19, s32[32,32]{0,1:T(8,128)S(1)} %copy-done.21), kind=kOutput, calls=%fused_computation.18 | convolution fusion | flops 403177472 | bytes 663552 | tf_op jit(solution)/shard_map/scr,scl->rl/dot_general | solution.py:164
  75.5 1.6 %fusion.5 = f32[32,32]{1,0:T(8,128)S(1)} fusion(f32[32,32,256]{2,0,1:T(8,128)S(1)} %fusion.14, s32[32,32]{1,0:T(8,128)S(1)} %copy-done.15, f32[256,128]{1,0:T(8,128)S(1)} %copy-done.12, f32[256,128]{1,0:T(8,128)S(1)} %copy-done.11, f32[256,128]{1,0:T(8,128)S(1)} %copy-done.14, f32[256,128]{1,0:T(8,128)S(1)} %convolution_bitcast_fusion.3), kind=kOutput, calls=%fused_computation.15 | convolution fusion | flops 403176448 | bytes 1581056 | tf_op jit(solution)/shard_map/scr,rl->scl/dot_general | solution.py:168
  77.1 0.6 copy.64
  77.7 8.1 %all-to-all-start.1 = ((f32[32,2,32]{2,1,0:T(2,128)}), f32[32,2,32]{2,1,0:T(2,128)}, u32[]{:S(2)}, u32[]{:S(2)}) async-start(f32[32,2,32]{2,1,0:T(2,128)} %copy.64), calls=%async_computation.1 | async-start | bytes 65536 | tf_op jit(solution)/shard_map/all_to_all | solution.py:113
  85.8 0.7 broadcast_multiply_fusion
  86.5 0.9 mul.216
  87.5 0.7 copy-done.3
  88.2 1.1 divide_add_fusion.1
  89.3 3.8 %subtract_reduce_fusion = (f32[3,4,4,2048]{3,2,1,0:T(4,128)}, f32[4,3,4,4,2048]{4,3,2,1,0:T(4,128)}) fusion(f32[4,3,4,4,2048]{4,3,2,1,0:T(4,128)S(1)} %get-tuple-element.48, f32[3,4,4,2048]{3,2,1,0:T(4,128)S(1)} %bitcast.240, f32[4,4,4,2048]{3,2,1,0:T(4,128)} %copy-done.2, f32[4,4,4,2048]{3,2,1,0:T(4,128)S(1)} %copy.55), kind=kLoop, calls=%fused_computation.8 | loop fusion | flops 1867776 | bytes 4980736 | tf_op jit(solution)/shard_map/reduce_sum | solution.py:63
  93.3 7.0 %collective-permute-start.4 = (f32[2,1,4,2048]{3,2,1,0:T(4,128)S(1)}, f32[2,1,4,2048]{3,2,1,0:T(4,128)S(1)}, u32[]{:S(2)}, u32[]{:S(2)}) collective-permute-start(f32[2,1,4,2048]{3,2,1,0:T(4,128)S(1)} %slice.345), channel_id=1, source_target_pairs={{32,0},{64,32},{96,64},{128,96},{160,128},{192,160},{224,192},{256... | collective-permute-start | bytes 196616 | tf_op jit(solution)/shard_map/ppermute | solution.py:15
  100.3 1.3 collective-permute-start.5
  101.6 0.8 copy.65
  102.4 0.7 fusion.2
  103.6 0.7 fusion.135
  104.2 1.0 fusion.1
  105.3 0.7 transpose_reshape.3
  106.0 14.7 %all-to-all-start.2 = ((f32[32,1,32]{2,1,0:T(1,128)}), f32[32,1,32]{2,1,0:T(1,128)S(1)}, u32[]{:S(2)}, u32[]{:S(2)}) async-start(f32[32,1,32]{2,1,0:T(1,128)} %transpose_reshape.3), calls=%async_computation.2 | async-start | bytes 32768 | tf_op jit(solution)/shard_map/all_to_all | solution.py:113
  121.4 1.9 %collective-permute-start.7 = (f32[2,1,4,2048]{3,2,1,0:T(4,128)S(1)}, f32[2,1,4,2048]{3,2,1,0:T(4,128)S(1)}, u32[]{:S(2)}, u32[]{:S(2)}) collective-permute-start(f32[2,1,4,2048]{3,2,1,0:T(4,128)S(1)} %pad_maximum_fusion.10), channel_id=1, source_target_pairs={{0,32},{32,64},{64,96},{96,128},{128,160},{160,192},{192,224},{224... | collective-permute-start | bytes 196616 | tf_op jit(solution)/shard_map/ppermute | solution.py:15
  123.5 3.5 %collective-permute-start.6 = (f32[2,4,1,2048]{3,2,1,0:T(1,128)S(1)}, f32[2,4,1,2048]{3,2,1,0:T(1,128)S(1)}, u32[]{:S(2)}, u32[]{:S(2)}) collective-permute-start(f32[2,4,1,2048]{3,2,1,0:T(1,128)S(1)} %slice.316), channel_id=1, source_target_pairs={{0,1},{1,2},{2,3},{3,4},{4,5},{5,6},{6,7},{7,8},{8,9},{9,10},{10,1... | collective-permute-start | bytes 196616 | tf_op jit(solution)/shard_map/ppermute | solution.py:15
  127.0 3.6 %collective-permute-done.7 = f32[2,1,4,2048]{3,2,1,0:T(4,128)S(1)} collective-permute-done((f32[2,1,4,2048]{3,2,1,0:T(4,128)S(1)}, f32[2,1,4,2048]{3,2,1,0:T(4,128)S(1)}, u32[]{:S(2)}, u32[]{:S(2)}) %collective-permute-start.7) | collective-permute-done | bytes 65568 | tf_op jit(solution)/shard_map/ppermute | solution.py:15
  131.9 2.0 %all-to-all-done.2 = f32[32,1,32]{2,1,0:T(1,128)S(1)} async-done(((f32[32,1,32]{2,1,0:T(1,128)}), f32[32,1,32]{2,1,0:T(1,128)S(1)}, u32[]{:S(2)}, u32[]{:S(2)}) %all-to-all-start.2) | async-done | bytes 4128 | tf_op jit(solution)/shard_map/all_to_all | solution.py:113
  134.2 2.3 %fusion.6 = f32[256,128]{1,0:T(8,128)S(1)} fusion(f32[32,32,128]{2,1,0:T(8,128)S(1)} %fusion.27, f32[32,32]{0,1:T(8,128)S(1)} %copy-done.20, s32[32,32]{0,1:T(8,128)S(1)} %copy-done.22), kind=kOutput, calls=%fused_computation.17 | convolution fusion | flops 403210240 | bytes 663552 | tf_op jit(solution)/shard_map/scr,scl->rl/dot_general | solution.py:159
  136.6 0.8 divide_add_fusion
  (131 shorter events, 6.2 us)
Async XLA Ops:
  0.6 12.7 %copy-start = (f32[4,8]{1,0:T(4,128)S(1)}, f32[4,8]{1,0:T(4,128)}, u32[]{:S(2)}) copy-start(f32[4,8]{1,0:T(4,128)} %param.27) | copy-start | bytes 388
  0.6 14.6 %copy-start.10 = (s32[4,4,2048]{2,1,0:T(4,128)S(1)}, s32[4,4,2048]{2,1,0:T(4,128)}, u32[]{:S(2)}) copy-start(s32[4,4,2048]{2,1,0:T(4,128)} %param.23) | copy-start | bytes 393220
  0.7 14.6 %copy-start.35 = (f32[4,8]{1,0:T(4,128)S(1)}, f32[4,8]{1,0:T(4,128)}, u32[]{:S(2)}) copy-start(f32[4,8]{1,0:T(4,128)} %param.26) | copy-start | bytes 388
  1.7 17.9 %collective-permute-start = (f32[2,4,1,2048]{3,2,1,0:T(1,128)S(1)}, f32[2,4,1,2048]{3,2,1,0:T(1,128)S(1)}, u32[]{:S(2)}, u32[]{:S(2)}) collective-permute-start(f32[2,4,1,2048]{3,2,1,0:T(1,128)S(1)} %slice.262), channel_id=1, source_target_pairs={{1,0},{2,1},{3,2},{4,3},{5,4},{6,5},{7,6},{8,7},{9,8},{10,9},{11,1... | collective-permute-start | bytes 196616 | tf_op jit(solution)/shard_map/ppermute | solution.py:15
  3.9 15.8 %collective-permute-start.1 = (f32[2,1,4,2048]{3,2,1,0:T(4,128)S(1)}, f32[2,1,4,2048]{3,2,1,0:T(4,128)S(1)}, u32[]{:S(2)}, u32[]{:S(2)}) collective-permute-start(f32[2,1,4,2048]{3,2,1,0:T(4,128)S(1)} %slice.271), channel_id=1, source_target_pairs={{32,0},{64,32},{96,64},{128,96},{160,128},{192,160},{224,192},{256... | collective-permute-start | bytes 196616 | tf_op jit(solution)/shard_map/ppermute | solution.py:15
  8.5 7.8 %copy-start.26 = (f32[1,511]{1,0:T(1,128)}, f32[1,511]{1,0:T(1,128)S(1)}, u32[]{:S(2)}) copy-start(f32[1,511]{1,0:T(1,128)S(1)} %slice.259) | copy-start | bytes 6136
  10.2 8.1 %copy-start.33 = (s32[512]{0:T(512)}, s32[512]{0:T(512)S(1)}, u32[]{:S(2)}) copy-start(s32[512]{0:T(512)S(1)} %multiply_add_fusion.5) | copy-start | bytes 6148
  14.8 1.4 %copy-start.24 = (f32[1,512]{1,0:T(1,128)S(1)}, f32[1,512]{1,0:T(1,128)}, u32[]{:S(2)}) copy-start(f32[1,512]{1,0:T(1,128)} %param.31) | copy-start | bytes 6148
  14.9 1.5 %copy-start.1 = (f32[3,4,4,2048]{3,2,1,0:T(4,128)S(1)}, f32[3,4,4,2048]{3,2,1,0:T(4,128)}, u32[]{:S(2)}) copy-start(f32[3,4,4,2048]{3,2,1,0:T(4,128)} %param.20) | copy-start | bytes 1179652
  14.9 1.5 %copy-start.4 = (f32[4,3,4,4,2048]{4,3,2,1,0:T(4,128)S(1)}, f32[4,3,4,4,2048]{4,3,2,1,0:T(4,128)}, u32[]{:S(2)}) copy-start(f32[4,3,4,4,2048]{4,3,2,1,0:T(4,128)} %param.22) | copy-start | bytes 4718596
  16.3 2.0 %copy-start.2 = (f32[4,4,4,2048]{3,2,1,0:T(4,128)}, f32[4,4,4,2048]{3,2,1,0:T(4,128)S(1)}, u32[]{:S(2)}) copy-start(f32[4,4,4,2048]{3,2,1,0:T(4,128)S(1)} %copy.56) | copy-start | bytes 1572868
  16.4 1.9 %copy-start.30 = (f32[1,512]{1,0:T(1,128)}, f32[1,512]{1,0:T(1,128)S(1)}, u32[]{:S(2)}) copy-start(f32[1,512]{1,0:T(1,128)S(1)} %fusion.119) | copy-start | bytes 6148
  16.4 1.9 %copy-start.25 = (f32[1,512]{1,0:T(1,128)S(1)}, f32[1,512]{1,0:T(1,128)}, u32[]{:S(2)}) copy-start(f32[1,512]{1,0:T(1,128)} %param.32) | copy-start | bytes 6148
  16.4 1.9 %copy-start.28 = (f32[1,512]{1,0:T(1,128)S(1)}, f32[1,512]{1,0:T(1,128)}, u32[]{:S(2)}) copy-start(f32[1,512]{1,0:T(1,128)} %param.30) | copy-start | bytes 6148
  16.4 1.9 %copy-start.37 = (f32[4]{0:T(128)S(1)}, f32[4]{0:T(128)}, u32[]{:S(2)}) copy-start(f32[4]{0:T(128)} %constant.109.clone) | copy-start | bytes 52
  24.3 31.2 %all-to-all-start = ((f32[32,1,128]{2,1,0:T(1,128)}), f32[32,1,128]{2,1,0:T(1,128)}, u32[]{:S(2)}, u32[]{:S(2)}) async-start(f32[32,1,128]{2,1,0:T(1,128)} %reshape.242), calls=%async_computation | async-start | bytes 32768 | tf_op jit(solution)/shard_map/all_to_all | solution.py:113
  42.3 17.2 %collective-permute-start.2 = (f32[2,4,1,2048]{3,2,1,0:T(1,128)}, f32[2,4,1,2048]{3,2,1,0:T(1,128)S(1)}, u32[]{:S(2)}, u32[]{:S(2)}) collective-permute-start(f32[2,4,1,2048]{3,2,1,0:T(1,128)} %slice.277), channel_id=1, source_target_pairs={{0,1},{1,2},{2,3},{3,4},{4,5},{5,6},{6,7},{7,8},{8,9},{9,10},{10,1... | collective-permute-start | bytes 196616 | tf_op jit(solution)/shard_map/ppermute | solution.py:15
  46.0 13.6 %collective-permute-start.3 = (f32[2,1,4,2048]{3,2,1,0:T(4,128)}, f32[2,1,4,2048]{3,2,1,0:T(4,128)}, u32[]{:S(2)}, u32[]{:S(2)}) collective-permute-start(f32[2,1,4,2048]{3,2,1,0:T(4,128)} %slice.284), channel_id=1, source_target_pairs={{0,32},{32,64},{64,96},{96,128},{128,160},{160,192},{192,224},{224... | collective-permute-start | bytes 196616 | tf_op jit(solution)/shard_map/ppermute | solution.py:15
  59.6 2.0 %copy-start.6 = (f32[3,4,4,2048]{3,2,1,0:T(4,128)S(1)}, f32[3,4,4,2048]{3,2,1,0:T(4,128)}, u32[]{:S(2)}) copy-start(f32[3,4,4,2048]{3,2,1,0:T(4,128)} %get-tuple-element.58) | copy-start | bytes 1179652
  59.6 2.0 %copy-start.8 = (f32[4,4,2048]{2,1,0:T(4,128)S(1)}, f32[4,4,2048]{2,1,0:T(4,128)}, u32[]{:S(2)}) copy-start(f32[4,4,2048]{2,1,0:T(4,128)} %bitcast_multiply_fusion) | copy-start | bytes 393220
  60.5 1.3 copy-start.17
  61.6 8.9 %copy-start.13 = (f32[256,128,1]{1,0,2:T(8,128)S(1)}, f32[256,128,1]{1,0,2:T(8,128)}, u32[]{:S(2)}) copy-start(f32[256,128,1]{1,0,2:T(8,128)} %reshape.233) | copy-start | bytes 393220
  69.3 3.4 %copy-start.18 = (f32[32,4,32]{2,0,1:T(8,128)S(1)}, f32[32,4,32]{2,0,1:T(8,128)}, u32[]{:S(2)}) copy-start(f32[32,4,32]{2,0,1:T(8,128)} %copy.60) | copy-start | bytes 49156
  69.3 3.5 %copy-start.23 = (f32[32,1,32]{2,1,0:T(1,128)S(1)}, f32[32,1,32]{2,1,0:T(1,128)}, u32[]{:S(2)}) copy-start(f32[32,1,32]{2,1,0:T(1,128)} %get-tuple-element.76) | copy-start | bytes 12292
  69.3 3.5 %copy-start.15 = (s32[32,32]{1,0:T(8,128)S(1)}, s32[32,32]{1,0:T(8,128)}, u32[]{:S(2)}) copy-start(s32[32,32]{1,0:T(8,128)} %get-tuple-element.78) | copy-start | bytes 12292
  69.3 3.8 %copy-start.19 = (f32[32,32]{0,1:T(8,128)S(1)}, f32[32,32]{0,1:T(8,128)}, u32[]{:S(2)}) copy-start(f32[32,32]{0,1:T(8,128)} %copy.58) | copy-start | bytes 12292
  69.3 3.8 %copy-start.21 = (s32[32,32]{0,1:T(8,128)S(1)}, s32[32,32]{0,1:T(8,128)}, u32[]{:S(2)}) copy-start(s32[32,32]{0,1:T(8,128)} %copy.57) | copy-start | bytes 12292
  72.7 2.7 %copy-start.11 = (f32[256,128]{1,0:T(8,128)S(1)}, f32[256,128]{1,0:T(8,128)}, u32[]{:S(2)}) copy-start(f32[256,128]{1,0:T(8,128)} %reshape.226) | copy-start | bytes 393220
  72.8 2.7 %copy-start.12 = (f32[256,128]{1,0:T(8,128)S(1)}, f32[256,128]{1,0:T(8,128)}, u32[]{:S(2)}) copy-start(f32[256,128]{1,0:T(8,128)} %reshape_squeeze.7) | copy-start | bytes 393220
  72.8 2.7 %copy-start.14 = (f32[256,128]{1,0:T(8,128)S(1)}, f32[256,128]{1,0:T(8,128)}, u32[]{:S(2)}) copy-start(f32[256,128]{1,0:T(8,128)} %reshape_squeeze.8) | copy-start | bytes 393220
  77.7 23.8 %all-to-all-start.1 = ((f32[32,2,32]{2,1,0:T(2,128)}), f32[32,2,32]{2,1,0:T(2,128)}, u32[]{:S(2)}, u32[]{:S(2)}) async-start(f32[32,2,32]{2,1,0:T(2,128)} %copy.64), calls=%async_computation.1 | async-start | bytes 65536 | tf_op jit(solution)/shard_map/all_to_all | solution.py:113
  87.5 0.7 copy-start.3
  89.3 13.1 %copy-start.34 = (s32[512]{0:T(512)S(1)}, s32[512]{0:T(512)}, u32[]{:S(2)}) copy-start(s32[512]{0:T(512)} %copy-done.33) | copy-start | bytes 6148
  93.1 10.1 %copy-start.27 = (f32[1,511]{1,0:T(1,128)S(1)}, f32[1,511]{1,0:T(1,128)}, u32[]{:S(2)}) copy-start(f32[1,511]{1,0:T(1,128)} %copy-done.26) | copy-start | bytes 6136
  93.1 10.1 %copy-start.29 = (f32[1,512]{1,0:T(1,128)S(1)}, f32[1,512]{1,0:T(1,128)}, u32[]{:S(2)}) copy-start(f32[1,512]{1,0:T(1,128)} %param.30) | copy-start | bytes 6148
  93.1 10.1 %copy-start.32 = (f32[1,512]{1,0:T(1,128)S(1)}, f32[1,512]{1,0:T(1,128)}, u32[]{:S(2)}) copy-start(f32[1,512]{1,0:T(1,128)} %param.33) | copy-start | bytes 6148
  93.1 10.3 %copy-start.31 = (f32[1,512]{1,0:T(1,128)S(1)}, f32[1,512]{1,0:T(1,128)}, u32[]{:S(2)}) copy-start(f32[1,512]{1,0:T(1,128)} %copy-done.30) | copy-start | bytes 6148
  93.3 27.4 %collective-permute-start.4 = (f32[2,1,4,2048]{3,2,1,0:T(4,128)S(1)}, f32[2,1,4,2048]{3,2,1,0:T(4,128)S(1)}, u32[]{:S(2)}, u32[]{:S(2)}) collective-permute-start(f32[2,1,4,2048]{3,2,1,0:T(4,128)S(1)} %slice.345), channel_id=1, source_target_pairs={{32,0},{64,32},{96,64},{128,96},{160,128},{192,160},{224,192},{256... | collective-permute-start | bytes 196616 | tf_op jit(solution)/shard_map/ppermute | solution.py:15
  100.3 20.4 %collective-permute-start.5 = (f32[2,4,1,2048]{3,2,1,0:T(1,128)S(1)}, f32[2,4,1,2048]{3,2,1,0:T(1,128)S(1)}, u32[]{:S(2)}, u32[]{:S(2)}) collective-permute-start(f32[2,4,1,2048]{3,2,1,0:T(1,128)S(1)} %slice.306), channel_id=1, source_target_pairs={{1,0},{2,1},{3,2},{4,3},{5,4},{6,5},{7,6},{8,7},{9,8},{10,9},{11,1... | collective-permute-start | bytes 196616 | tf_op jit(solution)/shard_map/ppermute | solution.py:15
  104.2 17.1 %copy-start.36 = (f32[1,512]{1,0:T(1,128)}, f32[1,512]{1,0:T(1,128)S(1)}, u32[]{:S(2)}) copy-start(f32[1,512]{1,0:T(1,128)S(1)} %get-tuple-element.52) | copy-start | bytes 6148
  106.0 27.9 %all-to-all-start.2 = ((f32[32,1,32]{2,1,0:T(1,128)}), f32[32,1,32]{2,1,0:T(1,128)S(1)}, u32[]{:S(2)}, u32[]{:S(2)}) async-start(f32[32,1,32]{2,1,0:T(1,128)} %transpose_reshape.3), calls=%async_computation.2 | async-start | bytes 32768 | tf_op jit(solution)/shard_map/all_to_all | solution.py:113
  121.4 9.2 %collective-permute-start.7 = (f32[2,1,4,2048]{3,2,1,0:T(4,128)S(1)}, f32[2,1,4,2048]{3,2,1,0:T(4,128)S(1)}, u32[]{:S(2)}, u32[]{:S(2)}) collective-permute-start(f32[2,1,4,2048]{3,2,1,0:T(4,128)S(1)} %pad_maximum_fusion.10), channel_id=1, source_target_pairs={{0,32},{32,64},{64,96},{96,128},{128,160},{160,192},{192,224},{224... | collective-permute-start | bytes 196616 | tf_op jit(solution)/shard_map/ppermute | solution.py:15
  123.4 7.6 %copy-start.7 = (f32[3,4,4,2048]{3,2,1,0:T(4,128)}, f32[3,4,4,2048]{3,2,1,0:T(4,128)S(1)}, u32[]{:S(2)}) copy-start(f32[3,4,4,2048]{3,2,1,0:T(4,128)S(1)} %pad_maximum_fusion.1) | copy-start | bytes 1179652
  123.5 7.1 %collective-permute-start.6 = (f32[2,4,1,2048]{3,2,1,0:T(1,128)S(1)}, f32[2,4,1,2048]{3,2,1,0:T(1,128)S(1)}, u32[]{:S(2)}, u32[]{:S(2)}) collective-permute-start(f32[2,4,1,2048]{3,2,1,0:T(1,128)S(1)} %slice.316), channel_id=1, source_target_pairs={{0,1},{1,2},{2,3},{3,4},{4,5},{5,6},{6,7},{7,8},{8,9},{9,10},{10,1... | collective-permute-start | bytes 196616 | tf_op jit(solution)/shard_map/ppermute | solution.py:15
  130.7 1.0 copy-start.5
  130.7 1.0 copy-start.9
  131.0 2.8 %copy-start.16 = (s32[32,32]{1,0:T(8,128)S(1)}, s32[32,32]{1,0:T(8,128)}, u32[]{:S(2)}) copy-start(s32[32,32]{1,0:T(8,128)} %get-tuple-element.78) | copy-start | bytes 12292
  131.0 3.2 %copy-start.20 = (f32[32,32]{0,1:T(8,128)S(1)}, f32[32,32]{0,1:T(8,128)}, u32[]{:S(2)}) copy-start(f32[32,32]{0,1:T(8,128)} %copy.58) | copy-start | bytes 12292
  131.1 3.2 %copy-start.22 = (s32[32,32]{0,1:T(8,128)S(1)}, s32[32,32]{0,1:T(8,128)}, u32[]{:S(2)}) copy-start(s32[32,32]{0,1:T(8,128)} %copy.57) | copy-start | bytes 12292

commit v14 on v10

--- a/solution.py
+++ b/solution.py
@@ -136,7 +136,6 @@
     cells = (eps_cell, sigma_cell, strength_cell, decay_cell)
 
     drive, polar_next = electric_base(e_field, h_field, polarization, cells)
-    incoming, drive = lax.optimization_barrier((incoming, drive))
 
     recv_cells = incoming[:, 0, :].astype(jnp.int32)
     is_valid = recv_cells >= 0

time: 131 us -> 119 us (0.908)
  other arithmetic: 22.2 us -> 15.3 us
  waiting for transfers between devices: 15.9 us -> 10.1 us
  starting transfers between devices: 58.8 us -> 64.4 us
  local copies, waits for them, and re-layouts: 14.3 us -> 11.7 us
    all_to_all x3, waiting for transfers between devices: 12.5 us -> 7 us  [exchange(): return lax.all_to_all(blocks, 'gy', split_axis=0, concat_axis=0, tiled=True)]
    ppermute x8, starting transfers between devices: 21.2 us -> 25.7 us  [passed_along(): lax.ppermute(value, axis, [(source, source + steps) for source in range(f...]
    unnamed x65 -> x68, local copies, waits for them, and re-layouts: 2.68 us -> 1.38 us
  transfers between devices with their start and end apart: 11 -> 11, of which waited for: 4 -> 4; matrix products, arithmetic and copies ran while one was open for 18% -> 26% of each run, Pallas kernels for 0% -> 0%
where the time goes in v14:
time: 119 us; the launch traced here: 118 us
  starting transfers between devices  64.4 us (54%)
  matrix products  15.3 us (13%)
  other arithmetic  15.3 us (13%)
  local copies, waits for them, and re-layouts  11.7 us (10%)
  waiting for transfers between devices  10.1 us (8%)
  between operations  1.55 us (1%)
    all_to_all x3, starting transfers between devices, exchange(): return lax.all_to_all(blocks, 'gy', split_axis=0, concat_axis=0, tiled=True)  38.7 us
    ppermute x8, starting transfers between devices, passed_along(): lax.ppermute(value, axis, [(source, source + steps) for source in range(f...  25.7 us
    all_to_all x3, waiting for transfers between devices, exchange(): return lax.all_to_all(blocks, 'gy', split_axis=0, concat_axis=0, tiled=True)  7 us
    dot_general x2, matrix products, wire_of(): jnp.einsum('scr,scl->rl', row_hot, spread, precision=highest)  5.25 us
    dot_general x2, matrix products, sample(): jnp.einsum('scr,rl->scl', row_hot, e_now[2].reshape(plane_rows, lanes), p...  4.01 us
    reduce_sum x1, other arithmetic, electric_base(): change = jnp.sum(polar_new - polarization, axis=0)  3.71 us
    ppermute x8, waiting for transfers between devices, passed_along(): lax.ppermute(value, axis, [(source, source + steps) for source in range(f...  3.14 us
    add x1, other arithmetic, electric_base(): decay_cell[:, None] * polarization  2.75 us
  transfers between devices with their start and end apart: 11, of which 4 were waited for; matrix products, arithmetic and copies ran while one was open for 26% of the time, Pallas kernels for 0%

profile of v14, /device:TPU:16, one launch (start us, length us, event | category | flops | bytes accessed | tf_op | source)
XLA Modules:
  0.0 118.3 jit_solution(12278861189653157866)
XLA Ops:
  0.7 1.0 slice.261
  1.7 1.3 %collective-permute-start = (f32[2,4,1,2048]{3,2,1,0:T(1,128)S(1)}, f32[2,4,1,2048]{3,2,1,0:T(1,128)S(1)}, u32[]{:S(2)}, u32[]{:S(2)}) collective-permute-start(f32[2,4,1,2048]{3,2,1,0:T(1,128)S(1)} %slice.261), channel_id=1, source_target_pairs={{1,0},{2,1},{3,2},{4,3},{5,4},{6,5},{7,6},{8,7},{9,8},{10,9},{11,1... | collective-permute-start | bytes 196616 | tf_op jit(solution)/shard_map/ppermute | solution.py:15
  3.0 0.8 slice.270
  3.9 3.9 %collective-permute-start.1 = (f32[2,1,4,2048]{3,2,1,0:T(4,128)S(1)}, f32[2,1,4,2048]{3,2,1,0:T(4,128)S(1)}, u32[]{:S(2)}, u32[]{:S(2)}) collective-permute-start(f32[2,1,4,2048]{3,2,1,0:T(4,128)S(1)} %slice.270), channel_id=1, source_target_pairs={{32,0},{64,32},{96,64},{128,96},{160,128},{192,160},{224,192},{256... | collective-permute-start | bytes 196616 | tf_op jit(solution)/shard_map/ppermute | solution.py:15
  7.7 1.5 %convolution_bitcast_fusion.1 = f32[4,4,4,2048]{3,0,2,1:T(4,128)S(1)} fusion(s32[4,4,2048]{2,1,0:T(4,128)} %param.23, f32[4,8]{1,0:T(4,128)S(1)} %copy-done), kind=kOutput, calls=%fused_computation.2 | convolution fusion | flops 12845056 | bytes 655488 | tf_op jit(solution)/shard_map/pm,mxyz->pxyz/dot_general | solution.py:135
  9.3 0.3 copy.58
  9.7 0.6 fusion
  10.3 0.3 copy.59
  10.7 0.2 convert_reduce_fusion.1
  11.0 0.3 convert_reduce_fusion
  11.4 0.6 fusion.10
  12.1 2.8 %multiply_add_fusion.1 = (f32[4,3,4,4,2048]{4,3,2,1,0:T(4,128)}, f32[3,4,4,2048]{3,2,1,0:T(4,128)}) fusion(f32[4,3,4,4,2048]{4,3,2,1,0:T(4,128)S(1)} %copy-done.2, f32[3,4,4,2048]{3,2,1,0:T(4,128)S(1)} %copy-done.1, f32[4,4,4,2048]{3,2,1,0:T(4,128)S(1)} %copy.59, f32[4,4,4,2048]{3,2,1,0:T(4,128)S(1)} %copy.58), kind=kLoop, calls=%fused_computation.11 | loop fusion | flops 1867776 | bytes 4980736 | tf_op jit(solution)/shard_map/add | solution.py:60
  14.9 1.0 fusion.8
  16.2 0.2 fusion.137
  16.4 0.1 slice.329
  16.5 0.1 slice.330
  16.7 0.2 fusion.69
  17.0 0.7 reshape.239
  17.7 17.9 %all-to-all-start = ((f32[32,1,128]{2,1,0:T(1,128)}), f32[32,1,128]{2,1,0:T(1,128)S(1)}, u32[]{:S(2)}, u32[]{:S(2)}) async-start(f32[32,1,128]{2,1,0:T(1,128)} %reshape.239), calls=%async_computation | async-start | bytes 32768 | tf_op jit(solution)/shard_map/all_to_all | solution.py:113
  35.6 0.6 fusion.9
  36.2 0.7 copy.86
  36.9 0.7 slice.277
  37.6 0.6 slice.284
  38.2 4.3 %collective-permute-start.2 = (f32[2,4,1,2048]{3,2,1,0:T(1,128)}, f32[2,4,1,2048]{3,2,1,0:T(1,128)}, u32[]{:S(2)}, u32[]{:S(2)}) collective-permute-start(f32[2,4,1,2048]{3,2,1,0:T(1,128)} %slice.277), channel_id=1, source_target_pairs={{0,1},{1,2},{2,3},{3,4},{4,5},{5,6},{6,7},{7,8},{8,9},{9,10},{10,1... | collective-permute-start | bytes 196616 | tf_op jit(solution)/shard_map/ppermute | solution.py:15
  42.5 2.1 %collective-permute-start.3 = (f32[2,1,4,2048]{3,2,1,0:T(4,128)}, f32[2,1,4,2048]{3,2,1,0:T(4,128)}, u32[]{:S(2)}, u32[]{:S(2)}) collective-permute-start(f32[2,1,4,2048]{3,2,1,0:T(4,128)} %slice.284), channel_id=1, source_target_pairs={{0,32},{32,64},{64,96},{96,128},{128,160},{160,192},{192,224},{224... | collective-permute-start | bytes 196616 | tf_op jit(solution)/shard_map/ppermute | solution.py:15
  44.6 0.7 reshape.225
  45.3 3.6 %all-to-all-done = f32[32,1,128]{2,1,0:T(1,128)S(1)} async-done(((f32[32,1,128]{2,1,0:T(1,128)}), f32[32,1,128]{2,1,0:T(1,128)S(1)}, u32[]{:S(2)}, u32[]{:S(2)}) %all-to-all-start) | async-done | bytes 16416 | tf_op jit(solution)/shard_map/all_to_all | solution.py:113
  48.9 0.5 broadcast.204
  49.4 0.6 reduce.4
  50.2 0.6 fusion.138
  51.0 0.3 fusion.15
  51.4 2.5 %fusion.4 = f32[32,32]{1,0:T(8,128)S(1)} fusion(f32[256,128,1]{1,0,2:T(8,128)} %reshape.225, f32[32,32,256]{2,0,1:T(8,128)S(1)} %fusion.15, s32[32,32]{1,0:T(8,128)S(1)} %get-tuple-element.74), kind=kOutput, calls=%fused_computation.14 | convolution fusion | flops 403045376 | bytes 1187840 | tf_op jit(solution)/shard_map/scr,rl->scl/dot_general | solution.py:153
  53.9 0.3 fusion.33
  54.2 3.0 %fusion.7 = f32[256,128]{1,0:T(8,128)} fusion(f32[32,32,128]{2,1,0:T(8,128)S(1)} %fusion.33, f32[32,32]{0,1:T(8,128)S(1)} %copy.56, s32[32,32]{0,1:T(8,128)S(1)} %copy.55), kind=kOutput, calls=%fused_computation.19 | convolution fusion | flops 403210240 | bytes 663552 | tf_op jit(solution)/shard_map/scr,scl->rl/dot_general | solution.py:158
  57.2 1.6 %mul.208 = f32[1,4,4,2048]{3,2,1,0:T(4,128)} reshape(f32[256,128]{1,0:T(8,128)} %fusion.7) | data formatting | bytes 262144 | tf_op jit(solution)/shard_map/mul | solution.py:69
  58.8 1.0 slice_bitcast_fusion.5
  59.8 1.0 fusion.55
  60.8 0.2 fusion.35
  61.3 1.5 %fusion.5 = f32[32,32]{1,0:T(8,128)S(1)} fusion(f32[256,128,1]{1,0,2:T(8,128)S(1)} %reshape.233, f32[32,32,256]{2,0,1:T(8,128)S(1)} %fusion.15, s32[32,32]{1,0:T(8,128)S(1)} %get-tuple-element.74), kind=kOutput, calls=%fused_computation.15 | convolution fusion | flops 403045376 | bytes 1187840 | tf_op jit(solution)/shard_map/scr,rl->scl/dot_general | solution.py:153
  62.8 0.6 copy.64
  63.5 7.7 %all-to-all-start.1 = ((f32[32,2,32]{2,1,0:T(2,128)}), f32[32,2,32]{2,1,0:T(2,128)S(1)}, u32[]{:S(2)}, u32[]{:S(2)}) async-start(f32[32,2,32]{2,1,0:T(2,128)} %copy.64), calls=%async_computation.1 | async-start | bytes 65536 | tf_op jit(solution)/shard_map/all_to_all | solution.py:113
  71.2 3.7 %subtract_reduce_fusion = (f32[3,4,4,2048]{3,2,1,0:T(4,128)S(1)}, f32[4,3,4,4,2048]{4,3,2,1,0:T(4,128)}) fusion(f32[4,3,4,4,2048]{4,3,2,1,0:T(4,128)} %get-tuple-element.42, f32[3,4,4,2048]{3,2,1,0:T(4,128)S(1)} %bitcast.237, f32[4,4,4,2048]{3,2,1,0:T(4,128)S(1)} %copy.59, f32[4,4,4,2048]{3,2,1,0:T(4,128)S(1)} %copy.58), kind=kLoop, calls=%fused_computation.8 | loop fusion | flops 1867776 | bytes 4980736 | tf_op jit(solution)/shard_map/reduce_sum | solution.py:63
  75.1 1.3 %collective-permute-start.5 = (f32[2,4,1,2048]{3,2,1,0:T(1,128)S(1)}, f32[2,4,1,2048]{3,2,1,0:T(1,128)S(1)}, u32[]{:S(2)}, u32[]{:S(2)}) collective-permute-start(f32[2,4,1,2048]{3,2,1,0:T(1,128)S(1)} %slice.305), channel_id=1, source_target_pairs={{1,0},{2,1},{3,2},{4,3},{5,4},{6,5},{7,6},{8,7},{9,8},{10,9},{11,1... | collective-permute-start | bytes 196616 | tf_op jit(solution)/shard_map/ppermute | solution.py:15
  76.4 7.0 %collective-permute-start.4 = (f32[2,1,4,2048]{3,2,1,0:T(4,128)S(1)}, f32[2,1,4,2048]{3,2,1,0:T(4,128)S(1)}, u32[]{:S(2)}, u32[]{:S(2)}) collective-permute-start(f32[2,1,4,2048]{3,2,1,0:T(4,128)S(1)} %slice.301), channel_id=1, source_target_pairs={{32,0},{64,32},{96,64},{128,96},{160,128},{192,160},{224,192},{256... | collective-permute-start | bytes 196616 | tf_op jit(solution)/shard_map/ppermute | solution.py:15
  83.4 1.2 all-to-all-done.1
  84.7 0.7 fusion.2
  85.8 0.7 fusion.129
  86.5 1.0 fusion.1
  87.5 0.7 transpose_reshape.3
  88.2 13.1 %all-to-all-start.2 = ((f32[32,1,32]{2,1,0:T(1,128)}), f32[32,1,32]{2,1,0:T(1,128)S(1)}, u32[]{:S(2)}, u32[]{:S(2)}) async-start(f32[32,1,32]{2,1,0:T(1,128)} %transpose_reshape.3), calls=%async_computation.2 | async-start | bytes 32768 | tf_op jit(solution)/shard_map/all_to_all | solution.py:113
  101.4 0.1 slice_bitcast_fusion.2
  101.7 0.1 slice.351
  101.8 0.2 fusion.82
  102.1 1.9 %collective-permute-start.7 = (f32[2,1,4,2048]{3,2,1,0:T(4,128)S(1)}, f32[2,1,4,2048]{3,2,1,0:T(4,128)S(1)}, u32[]{:S(2)}, u32[]{:S(2)}) collective-permute-start(f32[2,1,4,2048]{3,2,1,0:T(4,128)S(1)} %pad_maximum_fusion.10), channel_id=1, source_target_pairs={{0,32},{32,64},{64,96},{96,128},{128,160},{160,192},{192,224},{224... | collective-permute-start | bytes 196616 | tf_op jit(solution)/shard_map/ppermute | solution.py:15
  104.2 3.9 %collective-permute-start.6 = (f32[2,4,1,2048]{3,2,1,0:T(1,128)S(1)}, f32[2,4,1,2048]{3,2,1,0:T(1,128)S(1)}, u32[]{:S(2)}, u32[]{:S(2)}) collective-permute-start(f32[2,4,1,2048]{3,2,1,0:T(1,128)S(1)} %slice.315), channel_id=1, source_target_pairs={{0,1},{1,2},{2,3},{3,4},{4,5},{5,6},{6,7},{7,8},{8,9},{9,10},{10,1... | collective-permute-start | bytes 196616 | tf_op jit(solution)/shard_map/ppermute | solution.py:15
  108.1 3.1 %collective-permute-done.7 = f32[2,1,4,2048]{3,2,1,0:T(4,128)S(1)} collective-permute-done((f32[2,1,4,2048]{3,2,1,0:T(4,128)S(1)}, f32[2,1,4,2048]{3,2,1,0:T(4,128)S(1)}, u32[]{:S(2)}, u32[]{:S(2)}) %collective-permute-start.7) | collective-permute-done | bytes 65568 | tf_op jit(solution)/shard_map/ppermute | solution.py:15
  111.4 0.3 fusion.43
  111.7 0.1 fusion.77
  111.9 0.4 copy-done.8
  112.3 0.2 fusion.37
  112.5 2.3 %all-to-all-done.2 = f32[32,1,32]{2,1,0:T(1,128)S(1)} async-done(((f32[32,1,32]{2,1,0:T(1,128)}), f32[32,1,32]{2,1,0:T(1,128)S(1)}, u32[]{:S(2)}, u32[]{:S(2)}) %all-to-all-start.2) | async-done | bytes 4128 | tf_op jit(solution)/shard_map/all_to_all | solution.py:113
  114.7 0.3 fusion.32
  115.1 2.3 %fusion.6 = f32[256,128]{1,0:T(8,128)S(1)} fusion(f32[32,32,128]{2,1,0:T(8,128)S(1)} %fusion.32, f32[32,32]{0,1:T(8,128)S(1)} %copy.56, s32[32,32]{0,1:T(8,128)S(1)} %copy.55), kind=kOutput, calls=%fused_computation.17 | convolution fusion | flops 403210240 | bytes 663552 | tf_op jit(solution)/shard_map/scr,scl->rl/dot_general | solution.py:158
  117.5 0.8 divide_add_fusion
  (117 shorter events, 2.3 us)
Async XLA Ops:
  0.6 7.1 %copy-start = (f32[4,8]{1,0:T(4,128)S(1)}, f32[4,8]{1,0:T(4,128)}, u32[]{:S(2)}) copy-start(f32[4,8]{1,0:T(4,128)} %param.27) | copy-start | bytes 388
  0.6 9.0 %copy-start.9 = (s32[4,4,2048]{2,1,0:T(4,128)S(1)}, s32[4,4,2048]{2,1,0:T(4,128)}, u32[]{:S(2)}) copy-start(s32[4,4,2048]{2,1,0:T(4,128)} %param.23) | copy-start | bytes 393220
  0.7 9.0 %copy-start.27 = (f32[4,8]{1,0:T(4,128)S(1)}, f32[4,8]{1,0:T(4,128)}, u32[]{:S(2)}) copy-start(f32[4,8]{1,0:T(4,128)} %param.26) | copy-start | bytes 388
  1.7 14.5 %collective-permute-start = (f32[2,4,1,2048]{3,2,1,0:T(1,128)S(1)}, f32[2,4,1,2048]{3,2,1,0:T(1,128)S(1)}, u32[]{:S(2)}, u32[]{:S(2)}) collective-permute-start(f32[2,4,1,2048]{3,2,1,0:T(1,128)S(1)} %slice.261), channel_id=1, source_target_pairs={{1,0},{2,1},{3,2},{4,3},{5,4},{6,5},{7,6},{8,7},{9,8},{10,9},{11,1... | collective-permute-start | bytes 196616 | tf_op jit(solution)/shard_map/ppermute | solution.py:15
  3.9 12.3 %collective-permute-start.1 = (f32[2,1,4,2048]{3,2,1,0:T(4,128)S(1)}, f32[2,1,4,2048]{3,2,1,0:T(4,128)S(1)}, u32[]{:S(2)}, u32[]{:S(2)}) collective-permute-start(f32[2,1,4,2048]{3,2,1,0:T(4,128)S(1)} %slice.270), channel_id=1, source_target_pairs={{32,0},{64,32},{96,64},{128,96},{160,128},{192,160},{224,192},{256... | collective-permute-start | bytes 196616 | tf_op jit(solution)/shard_map/ppermute | solution.py:15
  9.2 1.4 %copy-start.17 = (s32[1,512,1]{1,2,0:T(1,128)S(1)}, s32[1,512,1]{1,2,0:T(1,128)}, u32[]{:S(2)}) copy-start(s32[1,512,1]{1,2,0:T(1,128)} %param.28) | copy-start | bytes 6148
  9.2 1.7 %copy-start.15 = (f32[1,512]{1,0:T(1,128)S(1)}, f32[1,512]{1,0:T(1,128)}, u32[]{:S(2)}) copy-start(f32[1,512]{1,0:T(1,128)} %param.31) | copy-start | bytes 6148
  9.3 1.8 %copy-start.29 = (s32[1,512]{1,0:T(1,128)S(1)}, s32[1,512]{1,0:T(1,128)}, u32[]{:S(2)}) copy-start(s32[1,512]{1,0:T(1,128)} %param.29) | copy-start | bytes 6148
  9.3 2.1 %copy-start.30 = (f32[8]{0:T(128)S(1)}, f32[8]{0:T(128)}, u32[]{:S(2)}) copy-start(f32[8]{0:T(128)} %param.25) | copy-start | bytes 100
  9.6 2.4 %copy-start.1 = (f32[3,4,4,2048]{3,2,1,0:T(4,128)S(1)}, f32[3,4,4,2048]{3,2,1,0:T(4,128)}, u32[]{:S(2)}) copy-start(f32[3,4,4,2048]{3,2,1,0:T(4,128)} %param.20) | copy-start | bytes 1179652
  9.7 2.4 %copy-start.2 = (f32[4,3,4,4,2048]{4,3,2,1,0:T(4,128)S(1)}, f32[4,3,4,4,2048]{4,3,2,1,0:T(4,128)}, u32[]{:S(2)}) copy-start(f32[4,3,4,4,2048]{4,3,2,1,0:T(4,128)} %param.22) | copy-start | bytes 4718596
  10.9 3.9 %copy-start.25 = (s32[512]{0:T(512)}, s32[512]{0:T(512)S(1)}, u32[]{:S(2)}) copy-start(s32[512]{0:T(512)S(1)} %multiply_add_fusion.6) | copy-start | bytes 6148
  11.0 1.0 copy-start.18
  12.0 48.8 %copy-start.7 = (f32[4,4,2048]{2,1,0:T(4,128)}, f32[4,4,2048]{2,1,0:T(4,128)S(1)}, u32[]{:S(2)}) copy-start(f32[4,4,2048]{2,1,0:T(4,128)S(1)} %bitcast_multiply_fusion) | copy-start | bytes 393220
  12.1 2.8 %copy-start.22 = (f32[1,512]{1,0:T(1,128)}, f32[1,512]{1,0:T(1,128)S(1)}, u32[]{:S(2)}) copy-start(f32[1,512]{1,0:T(1,128)S(1)} %fusion.113) | copy-start | bytes 6148
  12.1 2.8 %copy-start.16 = (f32[1,512]{1,0:T(1,128)S(1)}, f32[1,512]{1,0:T(1,128)}, u32[]{:S(2)}) copy-start(f32[1,512]{1,0:T(1,128)} %param.32) | copy-start | bytes 6148
  12.1 2.8 %copy-start.20 = (f32[1,512]{1,0:T(1,128)S(1)}, f32[1,512]{1,0:T(1,128)}, u32[]{:S(2)}) copy-start(f32[1,512]{1,0:T(1,128)} %param.30) | copy-start | bytes 6148
  12.1 2.8 %copy-start.32 = (f32[4]{0:T(128)S(1)}, f32[4]{0:T(128)}, u32[]{:S(2)}) copy-start(f32[4]{0:T(128)} %constant.108.clone) | copy-start | bytes 52
  14.9 1.3 %copy-start.11 = (f32[3,4,4,2048]{3,2,1,0:T(4,128)S(1)}, f32[3,4,4,2048]{3,2,1,0:T(4,128)}, u32[]{:S(2)}) copy-start(f32[3,4,4,2048]{3,2,1,0:T(4,128)} %param.21) | copy-start | bytes 1179652
  16.4 19.2 %copy-start.31 = (f32[8]{0:T(128)S(1)}, f32[8]{0:T(128)}, u32[]{:S(2)}) copy-start(f32[8]{0:T(128)} %param.24) | copy-start | bytes 100
  17.7 31.2 %all-to-all-start = ((f32[32,1,128]{2,1,0:T(1,128)}), f32[32,1,128]{2,1,0:T(1,128)S(1)}, u32[]{:S(2)}, u32[]{:S(2)}) async-start(f32[32,1,128]{2,1,0:T(1,128)} %reshape.239), calls=%async_computation | async-start | bytes 32768 | tf_op jit(solution)/shard_map/all_to_all | solution.py:113
  38.2 20.6 %collective-permute-start.2 = (f32[2,4,1,2048]{3,2,1,0:T(1,128)}, f32[2,4,1,2048]{3,2,1,0:T(1,128)}, u32[]{:S(2)}, u32[]{:S(2)}) collective-permute-start(f32[2,4,1,2048]{3,2,1,0:T(1,128)} %slice.277), channel_id=1, source_target_pairs={{0,1},{1,2},{2,3},{3,4},{4,5},{5,6},{6,7},{7,8},{8,9},{9,10},{10,1... | collective-permute-start | bytes 196616 | tf_op jit(solution)/shard_map/ppermute | solution.py:15
  42.5 16.3 %collective-permute-start.3 = (f32[2,1,4,2048]{3,2,1,0:T(4,128)}, f32[2,1,4,2048]{3,2,1,0:T(4,128)}, u32[]{:S(2)}, u32[]{:S(2)}) collective-permute-start(f32[2,1,4,2048]{3,2,1,0:T(4,128)} %slice.284), channel_id=1, source_target_pairs={{0,32},{32,64},{64,96},{96,128},{128,160},{160,192},{192,224},{224... | collective-permute-start | bytes 196616 | tf_op jit(solution)/shard_map/ppermute | solution.py:15
  51.0 2.8 %copy-start.12 = (f32[32,1,32]{2,1,0:T(1,128)S(1)}, f32[32,1,32]{2,1,0:T(1,128)}, u32[]{:S(2)}) copy-start(f32[32,1,32]{2,1,0:T(1,128)} %get-tuple-element.70) | copy-start | bytes 12292
  51.0 2.8 %copy-start.13 = (f32[32,1,32]{2,1,0:T(1,128)S(1)}, f32[32,1,32]{2,1,0:T(1,128)}, u32[]{:S(2)}) copy-start(f32[32,1,32]{2,1,0:T(1,128)} %get-tuple-element.71) | copy-start | bytes 12292
  51.0 2.9 %copy-start.14 = (f32[32,1,32]{2,1,0:T(1,128)S(1)}, f32[32,1,32]{2,1,0:T(1,128)}, u32[]{:S(2)}) copy-start(f32[32,1,32]{2,1,0:T(1,128)} %get-tuple-element.72) | copy-start | bytes 12292
  58.8 2.0 %copy-start.3 = (f32[3,4,4,2048]{3,2,1,0:T(4,128)S(1)}, f32[3,4,4,2048]{3,2,1,0:T(4,128)}, u32[]{:S(2)}) copy-start(f32[3,4,4,2048]{3,2,1,0:T(4,128)} %get-tuple-element.52) | copy-start | bytes 1179652
  59.8 1.3 %copy-start.10 = (f32[1,4,4,2048]{3,2,1,0:T(4,128)S(1)}, f32[1,4,4,2048]{3,2,1,0:T(4,128)}, u32[]{:S(2)}) copy-start(f32[1,4,4,2048]{3,2,1,0:T(4,128)} %mul.208) | copy-start | bytes 393220
  59.8 1.4 %copy-start.5 = (f32[1,4,4,2048]{3,2,1,0:T(4,128)S(1)}, f32[1,4,4,2048]{3,2,1,0:T(4,128)}, u32[]{:S(2)}) copy-start(f32[1,4,4,2048]{3,2,1,0:T(4,128)} %copy.86) | copy-start | bytes 393220
  63.5 21.1 %all-to-all-start.1 = ((f32[32,2,32]{2,1,0:T(2,128)}), f32[32,2,32]{2,1,0:T(2,128)S(1)}, u32[]{:S(2)}, u32[]{:S(2)}) async-start(f32[32,2,32]{2,1,0:T(2,128)} %copy.64), calls=%async_computation.1 | async-start | bytes 65536 | tf_op jit(solution)/shard_map/all_to_all | solution.py:113
  71.2 13.5 %copy-start.26 = (s32[512]{0:T(512)S(1)}, s32[512]{0:T(512)}, u32[]{:S(2)}) copy-start(s32[512]{0:T(512)} %copy-done.25) | copy-start | bytes 6148
  74.9 10.5 %copy-start.19 = (f32[1,511]{1,0:T(1,128)S(1)}, f32[1,511]{1,0:T(1,128)}, u32[]{:S(2)}) copy-start(f32[1,511]{1,0:T(1,128)} %copy-done.18) | copy-start | bytes 6136
  74.9 10.5 %copy-start.21 = (f32[1,512]{1,0:T(1,128)S(1)}, f32[1,512]{1,0:T(1,128)}, u32[]{:S(2)}) copy-start(f32[1,512]{1,0:T(1,128)} %param.30) | copy-start | bytes 6148
  74.9 10.6 %copy-start.23 = (f32[1,512]{1,0:T(1,128)S(1)}, f32[1,512]{1,0:T(1,128)}, u32[]{:S(2)}) copy-start(f32[1,512]{1,0:T(1,128)} %copy-done.22) | copy-start | bytes 6148
  75.0 10.6 %copy-start.24 = (f32[1,512]{1,0:T(1,128)S(1)}, f32[1,512]{1,0:T(1,128)}, u32[]{:S(2)}) copy-start(f32[1,512]{1,0:T(1,128)} %param.33) | copy-start | bytes 6148
  75.1 26.3 %collective-permute-start.5 = (f32[2,4,1,2048]{3,2,1,0:T(1,128)S(1)}, f32[2,4,1,2048]{3,2,1,0:T(1,128)S(1)}, u32[]{:S(2)}, u32[]{:S(2)}) collective-permute-start(f32[2,4,1,2048]{3,2,1,0:T(1,128)S(1)} %slice.305), channel_id=1, source_target_pairs={{1,0},{2,1},{3,2},{4,3},{5,4},{6,5},{7,6},{8,7},{9,8},{10,9},{11,1... | collective-permute-start | bytes 196616 | tf_op jit(solution)/shard_map/ppermute | solution.py:15
  76.4 25.0 %collective-permute-start.4 = (f32[2,1,4,2048]{3,2,1,0:T(4,128)S(1)}, f32[2,1,4,2048]{3,2,1,0:T(4,128)S(1)}, u32[]{:S(2)}, u32[]{:S(2)}) collective-permute-start(f32[2,1,4,2048]{3,2,1,0:T(4,128)S(1)} %slice.301), channel_id=1, source_target_pairs={{32,0},{64,32},{96,64},{128,96},{160,128},{192,160},{224,192},{256... | collective-permute-start | bytes 196616 | tf_op jit(solution)/shard_map/ppermute | solution.py:15
  86.5 15.5 %copy-start.28 = (f32[1,512]{1,0:T(1,128)}, f32[1,512]{1,0:T(1,128)S(1)}, u32[]{:S(2)}) copy-start(f32[1,512]{1,0:T(1,128)S(1)} %get-tuple-element.46) | copy-start | bytes 6148
  88.2 26.5 %all-to-all-start.2 = ((f32[32,1,32]{2,1,0:T(1,128)}), f32[32,1,32]{2,1,0:T(1,128)S(1)}, u32[]{:S(2)}, u32[]{:S(2)}) async-start(f32[32,1,32]{2,1,0:T(1,128)} %transpose_reshape.3), calls=%async_computation.2 | async-start | bytes 32768 | tf_op jit(solution)/shard_map/all_to_all | solution.py:113
  102.1 9.2 %collective-permute-start.7 = (f32[2,1,4,2048]{3,2,1,0:T(4,128)S(1)}, f32[2,1,4,2048]{3,2,1,0:T(4,128)S(1)}, u32[]{:S(2)}, u32[]{:S(2)}) collective-permute-start(f32[2,1,4,2048]{3,2,1,0:T(4,128)S(1)} %pad_maximum_fusion.10), channel_id=1, source_target_pairs={{0,32},{32,64},{64,96},{96,128},{128,160},{160,192},{192,224},{224... | collective-permute-start | bytes 196616 | tf_op jit(solution)/shard_map/ppermute | solution.py:15
  104.1 7.6 %copy-start.4 = (f32[3,4,4,2048]{3,2,1,0:T(4,128)}, f32[3,4,4,2048]{3,2,1,0:T(4,128)S(1)}, u32[]{:S(2)}) copy-start(f32[3,4,4,2048]{3,2,1,0:T(4,128)S(1)} %pad_maximum_fusion.1) | copy-start | bytes 1179652
  104.2 7.1 %collective-permute-start.6 = (f32[2,4,1,2048]{3,2,1,0:T(1,128)S(1)}, f32[2,4,1,2048]{3,2,1,0:T(1,128)S(1)}, u32[]{:S(2)}, u32[]{:S(2)}) collective-permute-start(f32[2,4,1,2048]{3,2,1,0:T(1,128)S(1)} %slice.315), channel_id=1, source_target_pairs={{0,1},{1,2},{2,3},{3,4},{4,5},{5,6},{6,7},{7,8},{8,9},{9,10},{10,1... | collective-permute-start | bytes 196616 | tf_op jit(solution)/shard_map/ppermute | solution.py:15
  111.3 0.9 copy-start.8
  114.7 2.8 %copy-start.6 = (f32[1,4,4,2048]{3,2,1,0:T(4,128)S(1)}, f32[1,4,4,2048]{3,2,1,0:T(4,128)}, u32[]{:S(2)}) copy-start(f32[1,4,4,2048]{3,2,1,0:T(4,128)} %copy.86) | copy-start | bytes 393220
